TPU v7x, 256 devices: a whole 4x4x8 slice. The times are simulated.
256 devices in a mesh: row: 64 (over x, z_hi, y), col: 4 (over z_lo, core).
Axes of the slice: x: 4, y: 4, z: 8 (z_hi: 4, z_lo: 2; z = z_hi * 2 + z_lo), core: 2. Of those that a mesh axis runs over, the one named last changes fastest.
Arguments:
- img_hidden: bfloat16 [8, 1536, 2432], P(None, 'row', 'col'), may hold values from -6 to 6
- txt_hidden: bfloat16 [8, 128, 2432], P(None, 'row', 'col'), may hold values from -6 to 6
- latent: float32 [8, 1536, 64], P(None, 'row'), may hold values from -6 to 6
- img_mod: float32 [8, 5, 2432], replicated, may hold values from -4 to 4
- txt_mod: float32 [8, 2, 2432], replicated, may hold values from -4 to 4
- qkv_weight: bfloat16 [3, 2432, 2048], P(None, None, 'col'), may hold values from -0.125 to 0.125
- txt_kv_weight: bfloat16 [2, 2432, 2048], P(None, None, 'col'), may hold values from -0.125 to 0.125
- out_weight: bfloat16 [2048, 2432], P('col', 'row'), may hold values from -0.125 to 0.125
- final_weight: bfloat16 [2432, 64], P('col'), may hold values from -0.125 to 0.125
- qk_gains: float32 [3, 64], replicated, may hold values from 1.5 to 9
- txt_len: int32 [8], replicated, may hold values from 1 to 128, as said below
- step_idx: int32 [8], replicated, may hold values from 1 to 28
Outputs:
- advanced: float32 [8, 1536, 64], P(None, 'row')
- denoised: float32 [8, 1536, 64], P(None, 'row')
Inputs may be any that keep to these rules, and one draw needn't show every extreme that they name: `txt_len`: some request has all 128 text tokens live.
All inputs are finite; a program needn't handle non-finite values.
Results may differ from a plain program's by a relative error of at most 0.0044.
The roundings to bfloat16 on the way count: a program that leaves them out, or rounds other values in their place, can miss the bound.
Values may be sent and summed in bfloat16 or wider, within the bound.
No kernel may reach another device: no remote copies, remote signals or barrier semaphores. Data moves between devices by JAX's collectives and lax.ppermute only.
A program may use at most 128 MiB of HBM per device.

v0:
```python
import jax
import jax.numpy as jnp
from jax import lax
from jax.sharding import PartitionSpec as P

D = 2432
HD = 64
STEPS = 28


eps_norm = 1e-06
neg_fill = -1e30


def layer_norm(values):
    average = jnp.mean(values, -1, keepdims=True)
    centred = values - average
    variance = jnp.mean(centred * centred, -1, keepdims=True)
    return centred * lax.rsqrt(variance + eps_norm)


def rms_heads(values, scaling):
    reshaped = values.reshape(values.shape[:-1] + (values.shape[-1] // HD, HD))
    inverse = lax.rsqrt(jnp.mean(reshaped * reshaped, -1, keepdims=True) + eps_norm)
    return (reshaped * inverse * scaling).astype(jnp.bfloat16)


def sigma_at(indices):
    fraction = indices.astype(jnp.float32) / STEPS
    return 3.0 * fraction / (1.0 + 2.0 * fraction)


def attend_all(queries, key_rows, value_rows, allowed):
    scores = jnp.einsum(
        "rqhd,rkhd->rqhk", queries, key_rows, preferred_element_type=jnp.float32
    ) * HD ** (-0.5)
    scores = jnp.where(allowed[:, None, None, :], scores, neg_fill)
    top_score = jnp.max(scores, -1, keepdims=True)
    exp_scores = jnp.where(allowed[:, None, None, :], jnp.exp(scores - top_score), 0.0)
    row_total = jnp.sum(exp_scores, -1)
    weighted = jnp.einsum(
        "rqhk,rkhd->rqhd",
        exp_scores.astype(jnp.bfloat16),
        value_rows,
        preferred_element_type=jnp.float32,
    )
    return (weighted / row_total[..., None]).astype(jnp.bfloat16)


def per_device(
    img_hidden,
    txt_hidden,
    latent,
    img_mod,
    txt_mod,
    qkv_weight,
    txt_kv_weight,
    out_weight,
    final_weight,
    qk_gains,
    txt_len,
    step_idx,
):
    requests = img_hidden.shape[0]
    patches = img_hidden.shape[1]
    text_rows = txt_hidden.shape[1]
    cols_local = qkv_weight.shape[2]
    heads_local = cols_local // HD
    block_len = patches + text_rows
    img_full, txt_full = (
        lax.all_gather(img_hidden, "col", axis=2, tiled=True),
        lax.all_gather(txt_hidden, "col", axis=2, tiled=True),
    )
    img_wide = img_full.astype(jnp.float32)
    normed = (layer_norm(img_wide) * (1.0 + img_mod[:, 1:2, :]) + img_mod[:, 0:1, :]).astype(
        jnp.bfloat16
    )
    flat_rows = normed.reshape(requests * patches, D)
    projected = jnp.einsum("td,cde->cte", flat_rows, qkv_weight, preferred_element_type=jnp.float32)
    queries = rms_heads(projected[0], qk_gains[0]).reshape(requests, patches, heads_local, HD)
    img_keys = rms_heads(projected[1], qk_gains[1]).reshape(requests, patches, heads_local, HD)
    img_values = projected[2].astype(jnp.bfloat16).reshape(requests, patches, heads_local, HD)
    text_normed = (
        layer_norm(txt_full.astype(jnp.float32)) * (1.0 + txt_mod[:, 1:2, :]) + txt_mod[:, 0:1, :]
    ).astype(jnp.bfloat16)
    text_proj = jnp.einsum(
        "rtd,cde->crte", text_normed, txt_kv_weight, preferred_element_type=jnp.float32
    )
    text_keys = rms_heads(text_proj[0], qk_gains[2])
    text_values = text_proj[1].astype(jnp.bfloat16).reshape(requests, text_rows, heads_local, HD)
    key_rows = jnp.concatenate([img_keys, text_keys], 1)
    value_rows = jnp.concatenate([img_values, text_values], 1)
    key_flat = key_rows.reshape(requests, block_len, cols_local)
    value_flat = value_rows.reshape(requests, block_len, cols_local)
    all_keys, all_values = (
        lax.all_gather(key_flat, "row", axis=1, tiled=True),
        lax.all_gather(value_flat, "row", axis=1, tiled=True),
    )
    key_count = all_keys.shape[1]
    positions = jnp.arange(key_count, dtype=jnp.int32)
    gathered_keys = all_keys.reshape(requests, key_count, heads_local, HD)
    gathered_values = all_values.reshape(requests, key_count, heads_local, HD)
    within = positions % block_len
    source = positions // block_len
    text_pos = source * text_rows + within - patches
    attended = attend_all(
        queries,
        gathered_keys,
        gathered_values,
        (within[None, :] < patches) | (text_pos[None, :] < txt_len[:, None]),
    ).reshape(requests * patches, cols_local)
    partial_value = jnp.dot(
        attended,
        lax.all_gather(out_weight, "row", axis=1, tiled=True),
        preferred_element_type=jnp.float32,
    )
    slab_width = img_hidden.shape[2]
    col_index = lax.axis_index("col")
    shared_sum = lax.psum_scatter(partial_value, "col", scatter_dimension=1, tiled=True)
    col_mods = lax.dynamic_slice_in_dim(img_mod, col_index * slab_width, slab_width, 2)
    mixed = img_hidden.astype(jnp.float32) + col_mods[:, 2:3, :] * shared_sum.reshape(
        requests, patches, slab_width
    )
    row_sums, squares = lax.psum((jnp.sum(mixed, -1), jnp.sum(mixed * mixed, -1)), "col")
    row_mean = row_sums / D
    spread = squares / D - row_mean * row_mean
    scaled = (mixed - row_mean[..., None]) * lax.rsqrt(spread[..., None] + eps_norm)
    modulated = (scaled * (1.0 + col_mods[:, 4:5, :]) + col_mods[:, 3:4, :]).astype(jnp.bfloat16)
    velocity = lax.psum(
        jnp.dot(
            modulated.reshape(requests * patches, slab_width),
            final_weight,
            preferred_element_type=jnp.float32,
        ),
        "col",
    )
    velocity = velocity.reshape(requests, patches, latent.shape[2])
    sigma_now = sigma_at(step_idx)[:, None, None]
    sigma_next = sigma_at(step_idx - 1)[:, None, None]
    advanced = latent + (sigma_next - sigma_now) * velocity
    denoised = latent - sigma_now * velocity
    return (advanced, denoised)


def solution(mesh):
    in_specs = (
        P(None, "row", "col"),
        P(None, "row", "col"),
        P(None, "row", None),
        P(),
        P(),
        P(None, None, "col"),
        P(None, None, "col"),
        P("col", "row"),
        P("col", None),
        P(),
        P(),
        P(),
    )
    out_specs = (P(None, "row", None), P(None, "row", None))
    return jax.shard_map(
        per_device, mesh=mesh, in_specs=in_specs, out_specs=out_specs, check_vma=False
    )
```

profile of v0, /device:TPU:1, one launch (start us, length us, event | category | flops | bytes accessed | tf_op | source)
XLA Modules:
  0.0 487.1 jit_solution(12438980188880885017)
XLA Ops:
  7.2 0.7 all-gather.9.cloned.1.call-update
  8.0 1.0 copy.78
  9.0 12.9 %all_gather.16 = bf16[8,2,2432]{0,1,2:T(2,128)(2,1)S(1)} all-gather(bf16[8,2,608]{0,1,2:T(2,128)(2,1)S(1)} %copy.78), channel_id=1, replica_groups=mesh['row'=64,'col'=4] {'col'}, dimensions={2}, use_global_device_ids=true | all-gather | bytes 97280 | tf_op jit(solution)/shard_map/all_gather | solution.py:72
  21.9 1.1 copy.79
  23.3 1.1 fusion.73
  24.4 3.2 fusion.24
  28.1 0.8 copy.76
  28.9 35.2 %all_gather.15 = bf16[8,24,2432]{1,0,2:T(8,128)(2,1)} all-gather(bf16[8,24,608]{1,0,2:T(8,128)(2,1)S(1)} %copy.76), channel_id=1, replica_groups=mesh['row'=64,'col'=4] {'col'}, dimensions={2}, use_global_device_ids=true | all-gather | bytes 1167360 | tf_op jit(solution)/shard_map/all_gather | solution.py:71
  64.1 4.8 copy.77
  69.6 0.9 add_bitcast_fusion
  70.5 0.6 fusion.20
  71.1 4.8 convolution_bitcast_fusion.1
  76.2 0.8 copy-done.2
  78.3 0.7 pad_maximum_fusion.1
  79.1 1.0 slice.80
  80.2 0.7 pad_maximum_fusion
  81.2 1.1 reshape_squeeze.11
  82.7 13.0 %all-gather.9.cloned.1.call-done = bf16[64,38,512]{2,1,0:T(8,128)(2,1)} async-done(((bf16[1,38,512]{2,1,0:T(8,128)(2,1)}), bf16[64,38,512]{2,1,0:T(8,128)(2,1)}) %all-gather.9.cloned.1.call-update) | async-done | bytes 2490384 | tf_op jit(solution)/shard_map/all_gather | solution.py:114
  95.8 2.8 reshape.196
  98.5 137.7 %all-gather.7.cloned.1.call-done = bf16[8,1664,512]{2,0,1:T(8,128)(2,1)} async-done(((bf16[8,26,512]{2,0,1:T(8,128)(2,1)}), bf16[8,1664,512]{2,0,1:T(8,128)(2,1)}) %all-gather.7.cloned.1.call-update) | async-done | bytes 13631504 | tf_op jit(solution)/shard_map/all_gather | solution.py:96
  236.3 19.4 %copy.87 = bf16[8,1664,512]{1,2,0:T(8,128)(2,1)} copy(bf16[8,1664,512]{2,0,1:T(8,128)(2,1)} %all-gather.7.cloned.1.call-done) | data formatting | bytes 27262976 | tf_op jit(solution)/shard_map/all_gather | solution.py:96
  255.7 8.9 %fusion.74 = (f32[8,24,8]{1,2,0:T(8,128)S(1)}, bf16[8,24,8,1664]{3,1,2,0:T(8,128)(2,1)}) fusion(pred[8,1664]{1,0:T(8,128)(4,1)S(1)} %compare_or_fusion, bf16[8,1664,8,64]{1,3,2,0:T(8,128)(2,1)} %bitcast.107, f32[8,24,8,64]{3,2,1,0:T(8,128)} %reshape_squeeze.11, f32[64]{0:T(128)S(1)} %get-tuple-element.23, f32[8,24,8]{1,2,0:T(8,128)S(1)} %copy.89), kind=kOutput, calls=%fused_computation.107 | convolution fusion | flops 342787712 | bytes 19162368 | tf_op jit(solution)/shard_map/sub | solution.py:39
  264.6 122.3 %all-gather.5.cloned.1.call-done = bf16[8,1664,512]{2,0,1:T(8,128)(2,1)} async-done(((bf16[8,26,512]{2,0,1:T(8,128)(2,1)}), bf16[8,1664,512]{2,0,1:T(8,128)(2,1)}) %all-gather.5.cloned.1.call-update) | async-done | bytes 13631504 | tf_op jit(solution)/shard_map/all_gather | solution.py:97
  386.9 19.4 %copy.83 = bf16[8,1664,512]{1,2,0:T(8,128)(2,1)} copy(bf16[8,1664,512]{2,0,1:T(8,128)(2,1)} %all-gather.5.cloned.1.call-done) | data formatting | bytes 27262976 | tf_op jit(solution)/shard_map/all_gather | solution.py:97
  406.3 8.4 %fusion.30 = bf16[8,24,8,64]{3,1,2,0:T(8,128)(2,1)S(1)} fusion(bf16[8,1664,8,64]{1,3,2,0:T(8,128)(2,1)} %bitcast.108, bf16[8,24,8,1664]{3,1,2,0:T(8,128)(2,1)} %get-tuple-element.27, f32[8,24,8]{1,2,0:T(8,128)S(1)} %get-tuple-element.26), kind=kOutput, calls=%fused_computation.28 | convolution fusion | flops 327352320 | bytes 18946048 | tf_op jit(solution)/shard_map/rqhk,rkhd->rqhd/dot_general | solution.py:41
  415.1 2.3 convolution_bitcast_fusion
  417.4 0.9 dynamic-slice_bitcast_fusion.1
  418.2 42.7 %reduce-scatter.4.cloned.1.call-done = f32[608,192]{1,0:T(8,128)} async-done(((f32[2432,192]{1,0:T(8,128)}), f32[608,192]{1,0:T(8,128)}) %reduce-scatter.4.cloned.1.call-update) | async-done | bytes 466960
  461.0 1.3 copy.96
  462.4 5.5 %all-reduce = (f32[8,24]{1,0:T(8,128)S(1)}, f32[8,24]{1,0:T(8,128)S(1)}) all-reduce(f32[8,24]{1,0:T(8,128)S(1)} %get-tuple-element.3, f32[8,24]{1,0:T(8,128)S(1)} %get-tuple-element.2), channel_id=1, replica_groups=mesh['row'=64,'col'=4] {'col'}, use_global_device_ids=true, to_apply=%region_13.14 | all-reduce | flops 384 | bytes 3072 | tf_op jit(solution)/shard_map/psum | solution.py:124
  468.4 11.5 %psum.23 = f32[8,24,64]{2,1,0:T(8,128)S(1)} all-reduce(f32[8,24,64]{2,1,0:T(8,128)S(1)} %bitcast.118), channel_id=1, replica_groups=mesh['row'=64,'col'=4] {'col'}, use_global_device_ids=true, to_apply=%region_14.15 | all-reduce | flops 12288 | bytes 98304 | tf_op jit(solution)/shard_map/psum | solution.py:129
  479.9 0.8 multiply_subtract_fusion
  (67 shorter events, 4.7 us)
Async XLA Ops:
  7.2 461.0 %copy-start = (bf16[608,64]{0,1:T(8,128)(2,1)S(1)}, bf16[608,64]{0,1:T(8,128)(2,1)}, u32[]{:S(2)}) copy-start(bf16[608,64]{0,1:T(8,128)(2,1)} %param.20) | copy-start | bytes 233476
  7.2 20.8 %copy-start.4 = (f32[3,64]{1,0:T(4,128)S(1)}, f32[3,64]{1,0:T(4,128)}, u32[]{:S(2)}) copy-start(f32[3,64]{1,0:T(4,128)} %param.21) | copy-start | bytes 2308
  7.2 20.9 %copy-start.1 = (bf16[8,24,608]{2,1,0:T(8,128)(2,1)S(1)}, bf16[8,24,608]{2,1,0:T(8,128)(2,1)}, u32[]{:S(2)}) copy-start(bf16[8,24,608]{2,1,0:T(8,128)(2,1)} %param.12) | copy-start | bytes 700420
  7.2 88.6 %all-gather.9.cloned.1.call-start = ((), (), s32[]{:S(2)}) async-start(), calls=%async_computation.3 | async-start | bytes 2662400 | tf_op jit(solution)/shard_map/all_gather | solution.py:114
  7.9 228.3 %all-gather.7.cloned.1.call-start = ((), (), s32[]{:S(2)}) async-start(), calls=%async_computation.2 | async-start | bytes 13844480 | tf_op jit(solution)/shard_map/all_gather | solution.py:96
  76.0 1.0 copy-start.2
  77.0 5.7 %copy-start.5 = (s32[8]{0:T(128)S(1)}, s32[8]{0:T(128)}, u32[]{:S(2)}) copy-start(s32[8]{0:T(128)} %param.22) | copy-start | bytes 100
  79.0 307.9 %all-gather.5.cloned.1.call-start = ((), (), s32[]{:S(2)}) async-start(), calls=%async_computation.1 | async-start | bytes 13844480 | tf_op jit(solution)/shard_map/all_gather | solution.py:97
  80.9 380.0 %reduce-scatter.4.cloned.1.call-start = ((), (), s32[]{:S(2)}) async-start(), calls=%async_computation.4 | async-start | bytes 3112960
  414.8 3.5 copy-start.6
  415.0 64.8 %copy-start.3 = (f32[8,24,64]{2,1,0:T(8,128)S(1)}, f32[8,24,64]{2,1,0:T(8,128)}, u32[]{:S(2)}) copy-start(f32[8,24,64]{2,1,0:T(8,128)} %param.14) | copy-start | bytes 147460
Sparse Core Ops, SparseCore 0:
  11.3 84.3 all-gather.8
  99.0 137.1 all-gather.6
  239.6 147.2 all-gather.4
  417.5 43.4 reduce-scatter.3
where the time goes:
time: 489 us; the launch traced here: 487 us
  waiting for transfers between devices  317 us (65%)
  blocking collectives  65 us (13%)
  local copies, waits for them, and re-layouts  56.6 us (12%)
  matrix products  27.8 us (6%)
  between operations  14.2 us (3%)
  other arithmetic  6.71 us (1%)
    all_gather x1, waiting for transfers between devices, per_device(): lax.all_gather(key_flat, 'row', axis=1, tiled=True)  138 us
    all_gather x1, waiting for transfers between devices, per_device(): lax.all_gather(value_flat, 'row', axis=1, tiled=True)  122 us
    unnamed x5, waiting for transfers between devices  43.4 us
    all_gather x1, blocking collectives, per_device(): lax.all_gather(img_hidden, 'col', axis=2, tiled=True)  35.2 us
    all_gather x1, local copies, waits for them, and re-layouts, per_device(): lax.all_gather(key_flat, 'row', axis=1, tiled=True)  19.4 us
    all_gather x1, local copies, waits for them, and re-layouts, per_device(): lax.all_gather(value_flat, 'row', axis=1, tiled=True)  19.4 us
    all_gather x1, waiting for transfers between devices, per_device(): lax.all_gather(out_weight, 'row', axis=1, tiled=True)  13 us
    all_gather x1, blocking collectives, per_device(): lax.all_gather(txt_hidden, 'col', axis=2, tiled=True)  12.9 us
  transfers between devices with their start and end apart: 4, of which 4 were waited for; matrix products, arithmetic and copies ran while one was open for 12% of the time, Pallas kernels for 0%

commit v1 on v0

v1 whole, which is shorter than its diff:
```python
import jax
import jax.numpy as jnp
from jax import lax
from jax.sharding import Mesh
from jax.sharding import PartitionSpec as P

D = 2432
HD = 64
STEPS = 28
REQ = 8

ROW = ("rq", "rm")

eps_norm = 1e-06
neg_fill = -1e30


def layer_norm(values):
    average = jnp.mean(values, -1, keepdims=True)
    centred = values - average
    variance = jnp.mean(centred * centred, -1, keepdims=True)
    return centred * lax.rsqrt(variance + eps_norm)


def rms_heads(values, scaling):
    reshaped = values.reshape(values.shape[:-1] + (values.shape[-1] // HD, HD))
    inverse = lax.rsqrt(jnp.mean(reshaped * reshaped, -1, keepdims=True) + eps_norm)
    return (reshaped * inverse * scaling).astype(jnp.bfloat16)


def sigma_at(indices):
    fraction = indices.astype(jnp.float32) / STEPS
    return 3.0 * fraction / (1.0 + 2.0 * fraction)


def gather_features(local):
    stacked = lax.all_gather(local, "col", axis=0, tiled=False)
    slabs = stacked.shape[0]
    moved = jnp.moveaxis(stacked, 0, -2)
    return moved.reshape(local.shape[:-1] + (slabs * local.shape[-1],))


def attend_one(queries, keys, values, allowed):
    scores = jnp.einsum(
        "qhd,khd->hqk", queries, keys, preferred_element_type=jnp.float32
    ) * HD ** (-0.5)
    scores = jnp.where(allowed[None, None, :], scores, neg_fill)
    top_score = jnp.max(scores, -1, keepdims=True)
    exp_scores = jnp.where(allowed[None, None, :], jnp.exp(scores - top_score), 0.0)
    row_total = jnp.sum(exp_scores, -1)
    weighted = jnp.einsum(
        "hqk,khd->qhd",
        exp_scores.astype(jnp.bfloat16),
        values,
        preferred_element_type=jnp.float32,
    )
    return (weighted / jnp.transpose(row_total)[..., None]).astype(jnp.bfloat16)


def per_device(
    img_hidden,
    txt_hidden,
    latent,
    img_mod,
    txt_mod,
    qkv_weight,
    txt_kv_weight,
    out_weight,
    final_weight,
    qk_gains,
    txt_len,
    step_idx,
):
    requests = img_hidden.shape[0]
    patches = img_hidden.shape[1]
    text_rows = txt_hidden.shape[1]
    cols_local = qkv_weight.shape[2]
    heads_local = cols_local // HD
    block_len = patches + text_rows
    groups = lax.axis_size("rq")
    members = lax.axis_size("rm")

    weight_t = lax.all_gather(jnp.transpose(out_weight), ROW, axis=0, tiled=True)

    img_full = gather_features(img_hidden)
    txt_full = gather_features(txt_hidden)
    img_wide = img_full.astype(jnp.float32)
    normed = (layer_norm(img_wide) * (1.0 + img_mod[:, 1:2, :]) + img_mod[:, 0:1, :]).astype(
        jnp.bfloat16
    )
    flat_rows = normed.reshape(requests * patches, D)
    projected = jnp.einsum("td,cde->cte", flat_rows, qkv_weight, preferred_element_type=jnp.float32)
    queries = rms_heads(projected[0], qk_gains[0]).reshape(requests, patches, cols_local)
    img_keys = rms_heads(projected[1], qk_gains[1]).reshape(requests, patches, cols_local)
    img_values = projected[2].astype(jnp.bfloat16).reshape(requests, patches, cols_local)
    text_normed = (
        layer_norm(txt_full.astype(jnp.float32)) * (1.0 + txt_mod[:, 1:2, :]) + txt_mod[:, 0:1, :]
    ).astype(jnp.bfloat16)
    text_proj = jnp.einsum(
        "rtd,cde->crte", text_normed, txt_kv_weight, preferred_element_type=jnp.float32
    )
    text_keys = rms_heads(text_proj[0], qk_gains[2]).reshape(requests, text_rows, cols_local)
    text_values = text_proj[1].astype(jnp.bfloat16)
    key_rows = jnp.concatenate([img_keys, text_keys], 1)
    value_rows = jnp.concatenate([img_values, text_values], 1)
    kv_rows = jnp.stack([key_rows, value_rows], 1)

    group_queries = lax.all_to_all(queries, "rq", 0, 0, tiled=True)
    group_kv = lax.all_to_all(kv_rows, "rq", 0, 0, tiled=True)
    all_kv = lax.all_gather(group_kv, "rm", axis=0, tiled=False)

    key_count = members * groups * block_len
    keys = all_kv[:, :, 0].reshape(key_count, heads_local, HD)
    values = all_kv[:, :, 1].reshape(key_count, heads_local, HD)

    request = lax.axis_index("rq")
    positions = jnp.arange(key_count, dtype=jnp.int32)
    within = positions % block_len
    source_block = positions // block_len
    member_of = source_block // groups
    group_of = source_block % groups
    source_row = group_of * members + member_of
    text_pos = source_row * text_rows + within - patches
    live_text = text_pos < lax.dynamic_index_in_dim(txt_len, request, keepdims=False)
    allowed = (within < patches) | live_text

    attended = attend_one(
        group_queries.reshape(groups * patches, heads_local, HD), keys, values, allowed
    ).reshape(groups, patches, cols_local)
    attended = lax.all_to_all(attended, "rq", 0, 0, tiled=True).reshape(
        requests * patches, cols_local
    )

    partial_value = lax.dot_general(
        attended,
        weight_t,
        (((1,), (1,)), ((), ())),
        preferred_element_type=jnp.float32,
    )
    slab_width = img_hidden.shape[2]
    col_index = lax.axis_index("col")
    shared_sum = lax.psum_scatter(partial_value, "col", scatter_dimension=1, tiled=True)
    col_mods = lax.dynamic_slice_in_dim(img_mod, col_index * slab_width, slab_width, 2)
    mixed = img_hidden.astype(jnp.float32) + col_mods[:, 2:3, :] * shared_sum.reshape(
        requests, patches, slab_width
    )
    row_sums, squares = lax.psum((jnp.sum(mixed, -1), jnp.sum(mixed * mixed, -1)), "col")
    row_mean = row_sums / D
    spread = squares / D - row_mean * row_mean
    scaled = (mixed - row_mean[..., None]) * lax.rsqrt(spread[..., None] + eps_norm)
    modulated = (scaled * (1.0 + col_mods[:, 4:5, :]) + col_mods[:, 3:4, :]).astype(jnp.bfloat16)
    velocity = lax.psum(
        jnp.dot(
            modulated.reshape(requests * patches, slab_width),
            final_weight,
            preferred_element_type=jnp.float32,
        ),
        "col",
    )
    velocity = velocity.reshape(requests, patches, latent.shape[2])
    sigma_now = sigma_at(step_idx)[:, None, None]
    sigma_next = sigma_at(step_idx - 1)[:, None, None]
    advanced = latent + (sigma_next - sigma_now) * velocity
    denoised = latent - sigma_now * velocity
    return (advanced, denoised)


def solution(mesh):
    rows = mesh.shape["row"]
    cols = mesh.shape["col"]
    split = Mesh(mesh.devices.reshape(REQ, rows // REQ, cols), ("rq", "rm", "col"))
    in_specs = (
        P(None, ROW, "col"),
        P(None, ROW, "col"),
        P(None, ROW, None),
        P(),
        P(),
        P(None, None, "col"),
        P(None, None, "col"),
        P("col", ROW),
        P("col", None),
        P(),
        P(),
        P(),
    )
    out_specs = (P(None, ROW, None), P(None, ROW, None))
    return jax.shard_map(
        per_device, mesh=split, in_specs=in_specs, out_specs=out_specs, check_vma=False
    )
```

time: 489 us -> 300 us (0.61)
  waiting for transfers between devices: 317 us -> 125 us
  other arithmetic: 6.71 us -> 19.7 us
  starting transfers between devices: 0.34 us -> 11.3 us
  blocking collectives: 65 us -> 57 us
  matrix products: 27.8 us -> 21.3 us
  local copies, waits for them, and re-layouts: 56.6 us -> 50.3 us
    all_gather x3 -> x2, waiting for transfers between devices: 273 us -> 82.1 us  [the longest x1 66.5 us: per_device(): all_kv = lax.all_gather(group_kv, 'rm', axis=0, tiled=False)]
    all_gather x4 -> x0, local copies, waits for them, and re-layouts: 44.8 us -> none  [the longest x1 19.4 us: per_device(): lax.all_gather(key_flat, 'row', axis=1, tiled=True)]
    all_gather x2, blocking collectives: 48 us -> 18.6 us  [gather_features(): stacked = lax.all_gather(local, 'col', axis=0, tiled=False)]
    slice x1 -> x2, local copies, waits for them, and re-layouts: 1.02 us -> 25.4 us  [the longest x1 25.3 us: per_device(): values = all_kv[:, :, 1].reshape(key_count, heads_local, HD)]
    all_to_all x0 -> x1, blocking collectives: none -> 21.4 us  [per_device(): group_kv = lax.all_to_all(kv_rows, 'rq', 0, 0, tiled=True)]
    sub x1, other arithmetic: 0.01 us -> 12.9 us  [attend_one(): scores - top_score]
    all_to_all x0 -> x2, starting transfers between devices: none -> 11.2 us  [the longest x1 7.66 us: per_device(): lax.all_to_all(attended, 'rq', 0, 0, tiled=True)]
    another operation x1 -> x3, local copies, waits for them, and re-layouts: 1.06 us -> 10.4 us  [the longest x1 5.69 us: per_device(): values = all_kv[:, :, 1].reshape(key_count, heads_local, HD)]
  transfers between devices with their start and end apart: 4 -> 5, of which waited for: 4 -> 4; matrix products, arithmetic and copies ran while one was open for 12% -> 23% of each run, Pallas kernels for 0% -> 0%
where the time goes in v1:
time: 300 us; the launch traced here: 299 us
  waiting for transfers between devices  125 us (42%)
  blocking collectives  57 us (19%)
  local copies, waits for them, and re-layouts  50.3 us (17%)
  matrix products  21.3 us (7%)
  other arithmetic  19.7 us (7%)
  between operations  14.2 us (5%)
  starting transfers between devices  11.3 us (4%)
    all_gather x1, waiting for transfers between devices, per_device(): all_kv = lax.all_gather(group_kv, 'rm', axis=0, tiled=False)  66.5 us
    unnamed x4, waiting for transfers between devices  34.8 us
    slice x1, local copies, waits for them, and re-layouts, per_device(): values = all_kv[:, :, 1].reshape(key_count, heads_local, HD)  25.3 us
    all_to_all x1, blocking collectives, per_device(): group_kv = lax.all_to_all(kv_rows, 'rq', 0, 0, tiled=True)  21.4 us
    all_gather x2, blocking collectives, gather_features(): stacked = lax.all_gather(local, 'col', axis=0, tiled=False)  18.6 us
    all_gather x1, waiting for transfers between devices, per_device(): lax.all_gather(jnp.transpose(out_weight), ROW, axis=0, tiled=True)  15.6 us
    sub x1, other arithmetic, attend_one(): scores - top_score  12.9 us
    psum x1, blocking collectives, per_device(): lax.psum(jnp.dot(modulated.reshape(requests * patches, slab_width), final...  11.4 us
  transfers between devices with their start and end apart: 5, of which 4 were waited for; matrix products, arithmetic and copies ran while one was open for 23% of the time, Pallas kernels for 0%

profile of v1, /device:TPU:1, one launch (start us, length us, event | category | flops | bytes accessed | tf_op | source)
XLA Modules:
  0.0 299.0 jit_solution(12010077146269406684)
XLA Ops:
  7.2 8.6 %all-gather.1 = bf16[32,2,608]{2,1,0:T(2,128)(2,1)S(1)} all-gather(bf16[8,2,608]{2,1,0:T(2,128)(2,1)} %param.13), channel_id=3, replica_groups=mesh['rq'=8,'rm'=8,'col'=4] {'col'}, dimensions={0}, use_global_device_ids=true | all-gather | bytes 97280 | tf_op jit(solution)/shard_map/all_gather | solution.py:37
  16.1 10.0 %all-gather = bf16[32,24,608]{2,1,0:T(8,128)(2,1)S(1)} all-gather(bf16[8,24,608]{2,1,0:T(8,128)(2,1)} %param.12), channel_id=2, replica_groups=mesh['rq'=8,'rm'=8,'col'=4] {'col'}, dimensions={0}, use_global_device_ids=true | all-gather | bytes 1167360 | tf_op jit(solution)/shard_map/all_gather | solution.py:37
  27.9 3.2 %fusion.28 = f32[2,8,2,512]{3,1,0,2:T(8,128)S(1)} fusion(bf16[2,2432,512]{2,1,0:T(8,128)(2,1)} %param.18, f32[8,2,2432]{2,0,1:T(8,128)S(1)} %reshape.182, f32[8,2432]{1,0:T(8,128)S(1)} %get-tuple-element.30, f32[8,2432]{1,0:T(8,128)S(1)} %get-tuple-element.31, f32[8,2]{0,1:T(2,128)S(1)} %copy.88, f32[8,2]{0,1:T(2,128)S(1)} %copy.85), kind=kOutput, calls=%fused_computation.26 | convolution fusion | flops 79886336 | bytes 5357696 | tf_op jit(solution)/shard_map/rtd,cde->crte/dot_general | solution.py:99
  31.2 2.6 copy.80
  33.8 2.2 reshape.181
  36.0 0.9 add_bitcast_fusion
  37.5 4.8 %convolution_bitcast_fusion.1 = f32[3,192,512]{2,1,0:T(8,128)S(1)} fusion(bf16[3,2432,512]{2,1,0:T(8,128)(2,1)} %param.17, bf16[192,2432]{1,0:T(8,128)(2,1)S(1)} %fusion.12), kind=kOutput, calls=%fused_computation.22 | convolution fusion | flops 1434451968 | bytes 9584640 | tf_op jit(solution)/shard_map/td,cde->cte/dot_general | solution.py:92
  44.6 21.4 %all_to_all.15 = bf16[8,2,26,512]{3,1,2,0:T(2,128)(2,1)} all-to-all(bf16[8,2,26,512]{3,1,2,0:T(2,128)(2,1)S(1)} %copy.93), channel_id=1, replica_groups=mesh['rq'=8,'rm'=8,'col'=4] {'rq'}, dimensions={0} | all-to-all | bytes 851968 | tf_op jit(solution)/shard_map/all_to_all | solution.py:109
  66.2 0.7 all-gather.9.cloned.1.call-update
  67.8 0.7 multiply_convert_fusion
  68.6 3.6 %all-to-all-start.1 = ((bf16[8,24,512]{2,1,0:T(8,128)(2,1)}), bf16[8,24,512]{2,1,0:T(8,128)(2,1)S(1)}, u32[]{:S(2)}, u32[]{:S(2)}) async-start(bf16[8,24,512]{2,1,0:T(8,128)(2,1)} %multiply_convert_fusion), calls=%async_computation.1 | async-start | bytes 393216 | tf_op jit(solution)/shard_map/all_to_all | solution.py:108
  72.7 0.7 fusion.60
  73.4 8.2 %all-to-all-done.1 = bf16[8,24,512]{2,1,0:T(8,128)(2,1)S(1)} async-done(((bf16[8,24,512]{2,1,0:T(8,128)(2,1)}), bf16[8,24,512]{2,1,0:T(8,128)(2,1)S(1)}, u32[]{:S(2)}, u32[]{:S(2)}) %all-to-all-start.1) | async-done | bytes 196640 | tf_op jit(solution)/shard_map/all_to_all | solution.py:108
  81.6 1.0 reshape.175
  82.6 66.5 %all-gather.7.cloned.1.call-done = bf16[64,2,26,512]{3,1,2,0:T(2,128)(2,1)} async-done(((bf16[8,2,26,512]{3,1,2,0:T(2,128)(2,1)}), bf16[64,2,26,512]{3,1,2,0:T(2,128)(2,1)}) %all-gather.7.cloned.1.call-update) | async-done | bytes 3407888 | tf_op jit(solution)/shard_map/all_gather | solution.py:110
  149.1 25.3 %slice_reduce_fusion.1 = (bf16[8,8,26,512]{3,2,1,0:T(8,128)(2,1)}, bf16[8,8,26,512]{3,2,1,0:T(8,128)(2,1)}) fusion(bf16[8,8,2,26,512]{4,2,3,1,0:T(2,128)(2,1)} %bitcast.118), kind=kLoop, calls=%fused_computation.13 | loop fusion | bytes 6815744 | tf_op jit(solution)/shard_map/slice | solution.py:114
  174.5 4.3 %reshape_squeeze.19 = bf16[1664,8,64]{2,1,0:T(8,128)(2,1)S(1)} reshape(bf16[8,8,26,512]{3,2,1,0:T(8,128)(2,1)} %get-tuple-element.3) | data formatting | bytes 3407872 | tf_op jit(solution)/shard_map/reshape;squeeze | solution.py:113
  178.8 5.7 %reshape_squeeze.17 = bf16[1664,8,64]{2,1,0:T(8,128)(2,1)} reshape(bf16[8,8,26,512]{3,2,1,0:T(8,128)(2,1)} %get-tuple-element.2) | data formatting | bytes 3407872 | tf_op jit(solution)/shard_map/reshape;squeeze | solution.py:114
  184.4 6.4 %fusion.10 = f32[8,192,1664]{2,1,0:T(8,128)} fusion(bf16[1664,8,64]{2,1,0:T(8,128)(2,1)S(1)} %reshape_squeeze.19, bf16[192,8,64]{2,1,0:T(8,128)(2,1)} %reshape.175), kind=kOutput, calls=%fused_computation.15 | convolution fusion | flops 327155712 | bytes 12124160 | tf_op jit(solution)/shard_map/qhd,khd->hqk/dot_general | solution.py:44
  190.9 12.9 %fusion.67 = (f32[8,192]{1,0:T(8,128)S(1)}, bf16[8,192,1664]{2,1,0:T(8,128)(2,1)}) fusion(f32[8,192,1664]{2,1,0:T(8,128)} %fusion.10, pred[1664]{0:T(1024)(128)(4,1)S(1)} %fusion.60), kind=kOutput, calls=%fused_computation.113 | output fusion | flops 20448896 | bytes 15343232 | tf_op jit(solution)/shard_map/sub | solution.py:49
  203.8 4.4 %fusion.23 = bf16[192,8,64]{0,2,1:T(8,128)(2,1)S(1)} fusion(bf16[8,192,1664]{2,1,0:T(8,128)(2,1)} %get-tuple-element.29, bf16[1664,8,64]{2,1,0:T(8,128)(2,1)S(1)} %copy-done.1, f32[192,8]{0,1:T(8,128)S(1)} %bitcast.132), kind=kOutput, calls=%fused_computation.25 | convolution fusion | flops 327352320 | bytes 7018496 | tf_op jit(solution)/shard_map/hqk,khd->qhd/dot_general | solution.py:51
  208.5 0.9 reshape.176
  209.4 7.7 %all-to-all-start.2 = ((bf16[8,24,512]{2,1,0:T(8,128)(2,1)}), bf16[8,24,512]{2,1,0:T(8,128)(2,1)S(1)}, u32[]{:S(2)}, u32[]{:S(2)}) async-start(bf16[8,24,512]{2,1,0:T(8,128)(2,1)} %reshape.176), calls=%async_computation.2 | async-start | bytes 393216 | tf_op jit(solution)/shard_map/all_to_all | solution.py:130
  217.1 15.6 %all-gather.9.cloned.1.call-done = bf16[64,38,512]{2,1,0:T(8,128)(2,1)} async-done(((bf16[1,38,512]{2,1,0:T(8,128)(2,1)}), bf16[64,38,512]{2,1,0:T(8,128)(2,1)}) %all-gather.9.cloned.1.call-update) | async-done | bytes 2490384 | tf_op jit(solution)/shard_map/all_gather | solution.py:83
  232.7 2.8 reshape.191
  235.5 2.3 convolution_bitcast_fusion
  237.8 0.9 dynamic-slice_bitcast_fusion.1
  238.7 34.1 %reduce-scatter.4.cloned.1.call-done = f32[608,192]{1,0:T(8,128)} async-done(((f32[2432,192]{1,0:T(8,128)}), f32[608,192]{1,0:T(8,128)}) %reduce-scatter.4.cloned.1.call-update) | async-done | bytes 466960
  272.9 1.3 copy.106
  274.3 5.5 %all-reduce = (f32[8,24]{1,0:T(8,128)S(1)}, f32[8,24]{1,0:T(8,128)S(1)}) all-reduce(f32[8,24]{1,0:T(8,128)S(1)} %get-tuple-element.5, f32[8,24]{1,0:T(8,128)S(1)} %get-tuple-element.4), channel_id=1, replica_groups=mesh['rq'=8,'rm'=8,'col'=4] {'col'}, use_global_device_ids=true, to_apply=%region_13.14 | all-reduce | flops 384 | bytes 3072 | tf_op jit(solution)/shard_map/psum | solution.py:147
  280.3 11.4 %psum.23 = f32[8,24,64]{2,1,0:T(8,128)S(1)} all-reduce(f32[8,24,64]{2,1,0:T(8,128)S(1)} %bitcast.130), channel_id=1, replica_groups=mesh['rq'=8,'rm'=8,'col'=4] {'col'}, use_global_device_ids=true, to_apply=%region_14.15 | all-reduce | flops 12288 | bytes 98304 | tf_op jit(solution)/shard_map/psum | solution.py:152
  291.8 0.8 multiply_subtract_fusion
  (86 shorter events, 7.4 us)
Async XLA Ops:
  7.2 272.9 %copy-start = (bf16[608,64]{0,1:T(8,128)(2,1)S(1)}, bf16[608,64]{0,1:T(8,128)(2,1)}, u32[]{:S(2)}) copy-start(bf16[608,64]{0,1:T(8,128)(2,1)} %param.20) | copy-start | bytes 233476
  7.2 141.9 %all-gather.7.cloned.1.call-start = ((), (), s32[]{:S(2)}) async-start(), calls=%async_computation.4 | async-start | bytes 3833856 | tf_op jit(solution)/shard_map/all_gather | solution.py:110
  15.9 11.8 %copy-start.3 = (f32[8,2,2432]{2,1,0:T(2,128)S(1)}, f32[8,2,2432]{2,1,0:T(2,128)}, u32[]{:S(2)}) copy-start(f32[8,2,2432]{2,1,0:T(2,128)} %param.16) | copy-start | bytes 466948
  37.4 5.4 %copy-start.5 = (f32[3,64]{1,0:T(4,128)S(1)}, f32[3,64]{1,0:T(4,128)}, u32[]{:S(2)}) copy-start(f32[3,64]{1,0:T(4,128)} %param.21) | copy-start | bytes 2308
  44.6 27.5 %copy-start.6 = (s32[8]{0:T(128)S(1)}, s32[8]{0:T(128)}, u32[]{:S(2)}) copy-start(s32[8]{0:T(128)} %param.22) | copy-start | bytes 100
  66.1 166.6 %all-gather.9.cloned.1.call-start = ((), (), s32[]{:S(2)}) async-start(), calls=%async_computation.5 | async-start | bytes 2662400 | tf_op jit(solution)/shard_map/all_gather | solution.py:83
  68.6 13.0 %all-to-all-start.1 = ((bf16[8,24,512]{2,1,0:T(8,128)(2,1)}), bf16[8,24,512]{2,1,0:T(8,128)(2,1)S(1)}, u32[]{:S(2)}, u32[]{:S(2)}) async-start(bf16[8,24,512]{2,1,0:T(8,128)(2,1)} %multiply_convert_fusion), calls=%async_computation.1 | async-start | bytes 393216 | tf_op jit(solution)/shard_map/all_to_all | solution.py:108
  190.9 12.9 %copy-start.1 = (bf16[1664,8,64]{2,1,0:T(8,128)(2,1)S(1)}, bf16[1664,8,64]{2,1,0:T(8,128)(2,1)}, u32[]{:S(2)}) copy-start(bf16[1664,8,64]{2,1,0:T(8,128)(2,1)} %reshape_squeeze.17) | copy-start | bytes 5111812
  209.4 26.1 %all-to-all-start.2 = ((bf16[8,24,512]{2,1,0:T(8,128)(2,1)}), bf16[8,24,512]{2,1,0:T(8,128)(2,1)S(1)}, u32[]{:S(2)}, u32[]{:S(2)}) async-start(bf16[8,24,512]{2,1,0:T(8,128)(2,1)} %reshape.176), calls=%async_computation.2 | async-start | bytes 393216 | tf_op jit(solution)/shard_map/all_to_all | solution.py:130
  217.1 55.8 %reduce-scatter.4.cloned.1.call-start = ((), (), s32[]{:S(2)}) async-start(), calls=%async_computation.6 | async-start | bytes 3112960
  235.5 3.2 %copy-start.7 = (s32[8]{0:T(128)S(1)}, s32[8]{0:T(128)}, u32[]{:S(2)}) copy-start(s32[8]{0:T(128)} %param.23) | copy-start | bytes 100
  237.7 36.4 %copy-start.2 = (bf16[8,24,608]{2,1,0:T(8,128)(2,1)S(1)}, bf16[8,24,608]{2,1,0:T(8,128)(2,1)}, u32[]{:S(2)}) copy-start(bf16[8,24,608]{2,1,0:T(8,128)(2,1)} %param.12) | copy-start | bytes 700420
  237.7 54.0 %copy-start.4 = (f32[8,24,64]{2,1,0:T(8,128)S(1)}, f32[8,24,64]{2,1,0:T(8,128)}, u32[]{:S(2)}) copy-start(f32[8,24,64]{2,1,0:T(8,128)} %param.14) | copy-start | bytes 147460
Sparse Core Ops, SparseCore 0:
  66.2 82.8 all-gather.6
  152.4 80.2 all-gather.8
  237.9 34.9 reduce-scatter.3

commit v2 on v1

--- a/solution.py
+++ b/solution.py
@@ -41,20 +41,13 @@
 
 
 def attend_one(queries, keys, values, allowed):
-    scores = jnp.einsum(
-        "qhd,khd->hqk", queries, keys, preferred_element_type=jnp.float32
-    ) * HD ** (-0.5)
-    scores = jnp.where(allowed[None, None, :], scores, neg_fill)
+    scores = jnp.dot(queries, keys.T, preferred_element_type=jnp.float32) * HD ** (-0.5)
+    scores = jnp.where(allowed[None, :], scores, neg_fill)
     top_score = jnp.max(scores, -1, keepdims=True)
-    exp_scores = jnp.where(allowed[None, None, :], jnp.exp(scores - top_score), 0.0)
-    row_total = jnp.sum(exp_scores, -1)
-    weighted = jnp.einsum(
-        "hqk,khd->qhd",
-        exp_scores.astype(jnp.bfloat16),
-        values,
-        preferred_element_type=jnp.float32,
-    )
-    return (weighted / jnp.transpose(row_total)[..., None]).astype(jnp.bfloat16)
+    exp_scores = jnp.where(allowed[None, :], jnp.exp(scores - top_score), 0.0)
+    row_total = jnp.sum(exp_scores, -1, keepdims=True)
+    weighted = jnp.dot(exp_scores.astype(jnp.bfloat16), values, preferred_element_type=jnp.float32)
+    return (weighted / row_total).astype(jnp.bfloat16)
 
 
 def per_device(
@@ -77,8 +70,6 @@
     cols_local = qkv_weight.shape[2]
     heads_local = cols_local // HD
     block_len = patches + text_rows
-    groups = lax.axis_size("rq")
-    members = lax.axis_size("rm")
 
     weight_t = lax.all_gather(jnp.transpose(out_weight), ROW, axis=0, tiled=True)
 
@@ -103,33 +94,33 @@
     text_values = text_proj[1].astype(jnp.bfloat16)
     key_rows = jnp.concatenate([img_keys, text_keys], 1)
     value_rows = jnp.concatenate([img_values, text_values], 1)
-    kv_rows = jnp.stack([key_rows, value_rows], 1)
 
-    group_queries = lax.all_to_all(queries, "rq", 0, 0, tiled=True)
-    group_kv = lax.all_to_all(kv_rows, "rq", 0, 0, tiled=True)
-    all_kv = lax.all_gather(group_kv, "rm", axis=0, tiled=False)
+    def by_head(values, length):
+        split = values.reshape(requests, length, heads_local, HD)
+        return jnp.transpose(split, (0, 2, 1, 3)).reshape(requests * heads_local, length, HD)
 
-    key_count = members * groups * block_len
-    keys = all_kv[:, :, 0].reshape(key_count, heads_local, HD)
-    values = all_kv[:, :, 1].reshape(key_count, heads_local, HD)
+    bundle = jnp.concatenate(
+        [by_head(queries, patches), by_head(key_rows, block_len), by_head(value_rows, block_len)], 1
+    )
+    bundle = lax.all_to_all(bundle, ROW, 0, 0, tiled=True)
+    sources = bundle.shape[0]
+    head_queries = bundle[:, :patches].reshape(sources * patches, HD)
+    keys = bundle[:, patches : patches + block_len].reshape(sources * block_len, HD)
+    values = bundle[:, patches + block_len :].reshape(sources * block_len, HD)
 
     request = lax.axis_index("rq")
-    positions = jnp.arange(key_count, dtype=jnp.int32)
+    positions = jnp.arange(sources * block_len, dtype=jnp.int32)
     within = positions % block_len
-    source_block = positions // block_len
-    member_of = source_block // groups
-    group_of = source_block % groups
-    source_row = group_of * members + member_of
+    source_row = positions // block_len
     text_pos = source_row * text_rows + within - patches
     live_text = text_pos < lax.dynamic_index_in_dim(txt_len, request, keepdims=False)
     allowed = (within < patches) | live_text
 
-    attended = attend_one(
-        group_queries.reshape(groups * patches, heads_local, HD), keys, values, allowed
-    ).reshape(groups, patches, cols_local)
-    attended = lax.all_to_all(attended, "rq", 0, 0, tiled=True).reshape(
-        requests * patches, cols_local
-    )
+    attended = attend_one(head_queries, keys, values, allowed).reshape(sources, patches, HD)
+    attended = lax.all_to_all(attended, ROW, 0, 0, tiled=True)
+    attended = jnp.transpose(
+        attended.reshape(requests, heads_local, patches, HD), (0, 2, 1, 3)
+    ).reshape(requests * patches, cols_local)
 
     partial_value = lax.dot_general(
         attended,

time: 300 us -> 190 us (0.63)
  waiting for transfers between devices: 125 us -> 61.6 us
  local copies, waits for them, and re-layouts: 50.3 us -> 19.4 us
  other arithmetic: 19.7 us -> 8.78 us
  matrix products: 21.3 us -> 14.8 us
    all_gather x1 -> x0, waiting for transfers between devices: 66.5 us -> none  [per_device(): all_kv = lax.all_gather(group_kv, 'rm', axis=0, tiled=False)]
    all_to_all x2 -> x1, waiting for transfers between devices: 8.19 us -> 31.5 us  [per_device(): bundle = lax.all_to_all(bundle, ROW, 0, 0, tiled=True)]
    slice x1 -> x7, local copies, waits for them, and re-layouts: 25.3 us -> 2.98 us  [the longest x1 1.31 us: per_device(): values = bundle[:, patches + block_len:].reshape(sources * block_len, HD)]
    all_gather x1, waiting for transfers between devices: 15.6 us -> 0.02 us  [per_device(): lax.all_gather(jnp.transpose(out_weight), ROW, axis=0, tiled=True)]
    sub x1 -> x0, other arithmetic: 12.9 us -> none  [attend_one(): scores - top_score]
    another operation x3, local copies, waits for them, and re-layouts: 10.4 us -> 0.41 us  [rms_heads(): reshaped = values.reshape(values.shape[:-1] + (values.shape[-1] // HD, HD))]
    dot_general x2, matrix products: 10.8 us -> 4.33 us  [the longest x1 2.4 us: attend_one(): jnp.dot(exp_scores.astype(jnp.bfloat16), values, preferred_element_type=j...]
    unnamed x4 -> x3, waiting for transfers between devices: 34.8 us -> 30 us
  transfers between devices with their start and end apart: 5 -> 3, of which waited for: 4 -> 2; matrix products, arithmetic and copies ran while one was open for 23% -> 19% of each run, Pallas kernels for 0% -> 0%
where the time goes in v2:
time: 190 us; the launch traced here: 189 us
  waiting for transfers between devices  61.6 us (32%)
  blocking collectives  57.2 us (30%)
  local copies, waits for them, and re-layouts  19.4 us (10%)
  matrix products  14.8 us (8%)
  between operations  14.6 us (8%)
  starting transfers between devices  12.8 us (7%)
  other arithmetic  8.78 us (5%)
    all_to_all x1, waiting for transfers between devices, per_device(): bundle = lax.all_to_all(bundle, ROW, 0, 0, tiled=True)  31.5 us
    unnamed x3, waiting for transfers between devices  30 us
    all_to_all x1, blocking collectives, per_device(): attended = lax.all_to_all(attended, ROW, 0, 0, tiled=True)  21.7 us
    all_gather x2, blocking collectives, gather_features(): stacked = lax.all_gather(local, 'col', axis=0, tiled=False)  18.6 us
    all_to_all x1, starting transfers between devices, per_device(): bundle = lax.all_to_all(bundle, ROW, 0, 0, tiled=True)  12.6 us
    psum x1, blocking collectives, per_device(): lax.psum(jnp.dot(modulated.reshape(requests * patches, slab_width), final...  11.4 us
    psum x1, blocking collectives, per_device(): lax.psum((jnp.sum(mixed, -1), jnp.sum(mixed * mixed, -1)), 'col')  5.49 us
    dot_general x1, matrix products, per_device(): jnp.einsum('td,cde->cte', flat_rows, qkv_weight, preferred_element_type=j...  4.8 us
  transfers between devices with their start and end apart: 3, of which 2 were waited for; matrix products, arithmetic and copies ran while one was open for 19% of the time, Pallas kernels for 0%

profile of v2, /device:TPU:1, one launch (start us, length us, event | category | flops | bytes accessed | tf_op | source)
XLA Modules:
  0.0 189.2 jit_solution(925703248106274510)
XLA Ops:
  7.2 0.7 all-gather.5.cloned.1.call-update
  7.9 8.6 %all-gather.1 = bf16[32,2,608]{2,1,0:T(2,128)(2,1)S(1)} all-gather(bf16[8,2,608]{2,1,0:T(2,128)(2,1)} %param.13), channel_id=3, replica_groups=mesh['rq'=8,'rm'=8,'col'=4] {'col'}, dimensions={0}, use_global_device_ids=true | all-gather | bytes 97280 | tf_op jit(solution)/shard_map/all_gather | solution.py:37
  16.8 10.0 %all-gather = bf16[32,24,608]{2,1,0:T(8,128)(2,1)S(1)} all-gather(bf16[8,24,608]{2,1,0:T(8,128)(2,1)} %param.12), channel_id=2, replica_groups=mesh['rq'=8,'rm'=8,'col'=4] {'col'}, dimensions={0}, use_global_device_ids=true | all-gather | bytes 1167360 | tf_op jit(solution)/shard_map/all_gather | solution.py:37
  27.2 0.4 multiply_reduce_fusion
  28.6 3.2 %fusion.14 = f32[2,8,2,512]{3,1,0,2:T(8,128)S(1)} fusion(bf16[2,2432,512]{2,1,0:T(8,128)(2,1)} %param.18, f32[8,2,2432]{2,0,1:T(8,128)S(1)} %reshape.205, f32[8,2432]{1,0:T(8,128)S(1)} %get-tuple-element.30, f32[8,2432]{1,0:T(8,128)S(1)} %get-tuple-element.31, f32[8,2]{0,1:T(2,128)S(1)} %copy.88, f32[8,2]{0,1:T(2,128)S(1)} %copy.85), kind=kOutput, calls=%fused_computation.18 | convolution fusion | flops 79886336 | bytes 5357696 | tf_op jit(solution)/shard_map/rtd,cde->crte/dot_general | solution.py:90
  31.8 2.5 %copy.76 = f32[8,24,4,608]{3,2,1,0:T(4,128)} copy(f32[8,24,4,608]{3,1,0,2:T(8,128)S(1)} %convert_bitcast_fusion) | data formatting | bytes 3735552 | tf_op jit(solution)/shard_map/convert_element_type | solution.py:78
  34.3 2.2 %reshape.204 = f32[192,2432]{1,0:T(8,128)S(1)} reshape(f32[8,24,4,608]{3,2,1,0:T(4,128)} %copy.76) | data formatting | bytes 3735552 | tf_op jit(solution)/shard_map/convert_element_type | solution.py:78
  36.6 0.9 add_bitcast_fusion
  37.6 0.5 fusion.13
  38.1 4.8 %convolution_bitcast_fusion.1 = f32[3,192,512]{2,1,0:T(8,128)S(1)} fusion(bf16[3,2432,512]{2,1,0:T(8,128)(2,1)} %param.17, bf16[192,2432]{1,0:T(8,128)(2,1)S(1)} %fusion.13), kind=kOutput, calls=%fused_computation.16 | convolution fusion | flops 1434451968 | bytes 9584640 | tf_op jit(solution)/shard_map/td,cde->cte/dot_general | solution.py:83
  46.3 2.3 %copy.93 = bf16[64,76,64]{1,2,0:T(8,128)(2,1)} copy(bf16[64,76,64]{2,0,1:T(8,128)(2,1)S(1)} %pad_maximum_fusion) | data formatting | bytes 1245184 | tf_op jit(solution)/shard_map/concatenate | solution.py:102
  48.6 12.6 %all-to-all-start = ((bf16[64,76,64]{1,2,0:T(8,128)(2,1)}), bf16[64,76,64]{1,2,0:T(8,128)(2,1)S(1)}, u32[]{:S(2)}, u32[]{:S(2)}) async-start(bf16[64,76,64]{1,2,0:T(8,128)(2,1)} %copy.93), calls=%async_computation | async-start | bytes 2097152 | tf_op jit(solution)/shard_map/all_to_all | solution.py:105
  61.4 0.6 dynamic_slice.8
  62.0 0.7 fusion.42
  62.6 31.5 %all-to-all-done = bf16[64,76,64]{1,2,0:T(8,128)(2,1)S(1)} async-done(((bf16[64,76,64]{1,2,0:T(8,128)(2,1)}), bf16[64,76,64]{1,2,0:T(8,128)(2,1)S(1)}, u32[]{:S(2)}, u32[]{:S(2)}) %all-to-all-start) | async-done | bytes 622624 | tf_op jit(solution)/shard_map/all_to_all | solution.py:105
  94.2 0.6 fusion.45
  94.8 1.3 copy.96
  96.1 1.2 reshape.197
  97.3 0.4 copy.94
  97.7 0.5 copy.95
  98.4 1.9 %fusion.47 = (f32[1536]{0:T(1024)S(1)}, f32[1536,1664]{1,0:T(8,128)S(1)}) fusion(bf16[1536,64]{1,0:T(8,128)(2,1)S(1)} %bitcast.123, bf16[1664,64]{1,0:T(8,128)(2,1)S(1)} %reshape.196, pred[1664]{0:T(1024)(128)(4,1)S(1)} %fusion.42), kind=kOutput, calls=%fused_computation.93 | convolution fusion | flops 334821888 | bytes 10641024 | tf_op jit(solution)/shard_map/dot_general | solution.py:44
  100.3 1.8 fusion
  102.1 2.4 %fusion.10 = bf16[1536,64]{0,1:T(8,128)(2,1)S(1)} fusion(bf16[1664,64]{1,0:T(8,128)(2,1)S(1)} %reshape.197, f32[1536,1664]{1,0:T(8,128)S(1)} %get-tuple-element.29, f32[1536]{0:T(1024)S(1)} %get-tuple-element.28, pred[1664]{0:T(1024)(128)(4,1)S(1)} %fusion.42, f32[1536]{0:T(1024)S(1)} %fusion), kind=kOutput, calls=%fused_computation.10 | convolution fusion | flops 335020032 | bytes 10647168 | tf_op jit(solution)/shard_map/dot_general | solution.py:49
  105.0 21.7 %all_to_all.10 = bf16[64,2,768]{2,1,0:T(2,128)(2,1)S(1)} all-to-all(bf16[64,2,768]{2,1,0:T(2,128)(2,1)S(1)} %reshape.219), channel_id=1, replica_groups=mesh['rq'=8,'rm'=8,'col'=4] {'rq','rm'}, dimensions={0} | all-to-all | bytes 393216 | tf_op jit(solution)/shard_map/all_to_all | solution.py:120
  127.3 2.8 %reshape.213 = bf16[2432,512]{1,0:T(8,128)(2,1)S(1)} reshape(bf16[64,38,512]{2,1,0:T(8,128)(2,1)} %all-gather.5.cloned.1.call-done) | data formatting | bytes 4980736
  130.1 2.3 %convolution_bitcast_fusion = f32[2432,192]{1,0:T(8,128)} fusion(bf16[192,512]{1,0:T(8,128)(2,1)S(1)} %reshape.200, bf16[2432,512]{1,0:T(8,128)(2,1)S(1)} %reshape.213), kind=kOutput, calls=%fused_computation.8 | convolution fusion | flops 478150656 | bytes 4554752
  132.4 0.9 dynamic-slice_bitcast_fusion.1
  133.4 29.3 %reduce-scatter.4.cloned.1.call-done = f32[608,192]{1,0:T(8,128)} async-done(((f32[2432,192]{1,0:T(8,128)}), f32[608,192]{1,0:T(8,128)}) %reduce-scatter.4.cloned.1.call-update) | async-done | bytes 466960
  162.7 1.3 copy.103
  164.2 5.5 %all-reduce = (f32[8,24]{1,0:T(8,128)S(1)}, f32[8,24]{1,0:T(8,128)S(1)}) all-reduce(f32[8,24]{1,0:T(8,128)S(1)} %get-tuple-element.3, f32[8,24]{1,0:T(8,128)S(1)} %get-tuple-element.2), channel_id=1, replica_groups=mesh['rq'=8,'rm'=8,'col'=4] {'col'}, use_global_device_ids=true, to_apply=%region_13.14 | all-reduce | flops 384 | bytes 3072 | tf_op jit(solution)/shard_map/psum | solution.py:138
  170.2 11.4 %psum.23 = f32[8,24,64]{2,1,0:T(8,128)S(1)} all-reduce(f32[8,24,64]{2,1,0:T(8,128)S(1)} %bitcast.133), channel_id=1, replica_groups=mesh['rq'=8,'rm'=8,'col'=4] {'col'}, use_global_device_ids=true, to_apply=%region_14.15 | all-reduce | flops 12288 | bytes 98304 | tf_op jit(solution)/shard_map/psum | solution.py:143
  181.6 0.8 multiply_subtract_fusion
  (80 shorter events, 7.1 us)
Async XLA Ops:
  7.2 162.8 %copy-start = (bf16[608,64]{0,1:T(8,128)(2,1)S(1)}, bf16[608,64]{0,1:T(8,128)(2,1)}, u32[]{:S(2)}) copy-start(bf16[608,64]{0,1:T(8,128)(2,1)} %param.20) | copy-start | bytes 233476
  7.2 120.1 %all-gather.5.cloned.1.call-start = ((), (), s32[]{:S(2)}) async-start(), calls=%async_computation.3 | async-start | bytes 2662400 | tf_op jit(solution)/shard_map/all_gather | solution.py:74
  26.8 1.0 copy-start.3
  31.8 4.8 %copy-start.2 = (f32[2,8,2,512]{3,1,0,2:T(8,128)}, f32[2,8,2,512]{3,1,0,2:T(8,128)S(1)}, u32[]{:S(2)}) copy-start(f32[2,8,2,512]{3,1,0,2:T(8,128)S(1)} %fusion.14) | copy-start | bytes 196612
  42.9 0.8 slice-start
  42.9 0.8 copy-start.5
  46.3 15.1 %copy-start.6 = (s32[8]{0:T(128)S(1)}, s32[8]{0:T(128)}, u32[]{:S(2)}) copy-start(s32[8]{0:T(128)} %param.22) | copy-start | bytes 100
  48.6 45.6 %all-to-all-start = ((bf16[64,76,64]{1,2,0:T(8,128)(2,1)}), bf16[64,76,64]{1,2,0:T(8,128)(2,1)S(1)}, u32[]{:S(2)}, u32[]{:S(2)}) async-start(bf16[64,76,64]{1,2,0:T(8,128)(2,1)} %copy.93), calls=%async_computation | async-start | bytes 2097152 | tf_op jit(solution)/shard_map/all_to_all | solution.py:105
  61.1 101.6 %reduce-scatter.4.cloned.1.call-start = ((), (), s32[]{:S(2)}) async-start(), calls=%async_computation.4 | async-start | bytes 3112960
  132.4 1.0 copy-start.7
  132.4 31.6 %copy-start.1 = (bf16[8,24,608]{2,1,0:T(8,128)(2,1)S(1)}, bf16[8,24,608]{2,1,0:T(8,128)(2,1)}, u32[]{:S(2)}) copy-start(bf16[8,24,608]{2,1,0:T(8,128)(2,1)} %param.12) | copy-start | bytes 700420
  132.4 49.2 %copy-start.4 = (f32[8,24,64]{2,1,0:T(8,128)S(1)}, f32[8,24,64]{2,1,0:T(8,128)}, u32[]{:S(2)}) copy-start(f32[8,24,64]{2,1,0:T(8,128)} %param.14) | copy-start | bytes 147460
Sparse Core Ops, SparseCore 0:
  11.3 92.9 all-gather.4
  132.5 30.1 reduce-scatter.3

commit v3 on v2

--- a/solution.py
+++ b/solution.py
@@ -73,6 +73,7 @@
 
     weight_t = lax.all_gather(jnp.transpose(out_weight), ROW, axis=0, tiled=True)
 
+    full_final = lax.all_gather(final_weight, "col", axis=0, tiled=True)
     img_full = gather_features(img_hidden)
     txt_full = gather_features(txt_hidden)
     img_wide = img_full.astype(jnp.float32)
@@ -128,31 +129,30 @@
         (((1,), (1,)), ((), ())),
         preferred_element_type=jnp.float32,
     )
-    slab_width = img_hidden.shape[2]
+    cols = lax.axis_size("col")
     col_index = lax.axis_index("col")
-    shared_sum = lax.psum_scatter(partial_value, "col", scatter_dimension=1, tiled=True)
-    col_mods = lax.dynamic_slice_in_dim(img_mod, col_index * slab_width, slab_width, 2)
-    mixed = img_hidden.astype(jnp.float32) + col_mods[:, 2:3, :] * shared_sum.reshape(
-        requests, patches, slab_width
+    shared_sum = lax.psum_scatter(partial_value, "col", scatter_dimension=0, tiled=True)
+    own_requests = requests // cols
+    first = col_index * own_requests
+    own_mods = lax.dynamic_slice_in_dim(img_mod, first, own_requests, 0)
+    own_hidden = lax.dynamic_slice_in_dim(img_wide, first, own_requests, 0)
+    mixed = own_hidden + own_mods[:, 2:3, :] * shared_sum.reshape(own_requests, patches, D)
+    modulated = (layer_norm(mixed) * (1.0 + own_mods[:, 4:5, :]) + own_mods[:, 3:4, :]).astype(
+        jnp.bfloat16
     )
-    row_sums, squares = lax.psum((jnp.sum(mixed, -1), jnp.sum(mixed * mixed, -1)), "col")
-    row_mean = row_sums / D
-    spread = squares / D - row_mean * row_mean
-    scaled = (mixed - row_mean[..., None]) * lax.rsqrt(spread[..., None] + eps_norm)
-    modulated = (scaled * (1.0 + col_mods[:, 4:5, :]) + col_mods[:, 3:4, :]).astype(jnp.bfloat16)
-    velocity = lax.psum(
-        jnp.dot(
-            modulated.reshape(requests * patches, slab_width),
-            final_weight,
-            preferred_element_type=jnp.float32,
-        ),
-        "col",
-    )
-    velocity = velocity.reshape(requests, patches, latent.shape[2])
-    sigma_now = sigma_at(step_idx)[:, None, None]
-    sigma_next = sigma_at(step_idx - 1)[:, None, None]
-    advanced = latent + (sigma_next - sigma_now) * velocity
-    denoised = latent - sigma_now * velocity
+    velocity = jnp.dot(
+        modulated.reshape(own_requests * patches, D),
+        full_final,
+        preferred_element_type=jnp.float32,
+    ).reshape(own_requests, patches, latent.shape[2])
+    own_latent = lax.dynamic_slice_in_dim(latent, first, own_requests, 0)
+    own_steps = lax.dynamic_slice_in_dim(step_idx, first, own_requests, 0)
+    sigma_now = sigma_at(own_steps)[:, None, None]
+    sigma_next = sigma_at(own_steps - 1)[:, None, None]
+    advanced = own_latent + (sigma_next - sigma_now) * velocity
+    denoised = own_latent - sigma_now * velocity
+    both = lax.all_gather(jnp.stack([advanced, denoised]), "col", axis=1, tiled=True)
+    advanced, denoised = both[0], both[1]
     return (advanced, denoised)
 
 

time: 190 us -> 203 us (1.068)
  local copies, waits for them, and re-layouts: 19.4 us -> 32.8 us
  other arithmetic: 8.78 us -> 16.9 us
  waiting for transfers between devices: 61.6 us -> 54.5 us
  blocking collectives: 57.2 us -> 52.9 us
  matrix products: 14.8 us -> 17.5 us
    unnamed x3 -> x2, waiting for transfers between devices: 30 us -> 0.7 us
    psum x2 -> x0, blocking collectives: 16.9 us -> none  [the longest x1 11.4 us: per_device(): lax.psum(jnp.dot(modulated.reshape(requests * patches, slab_width), final...]
    all_gather x0 -> x2, blocking collectives: none -> 15.3 us  [the longest x1 9.43 us: per_device(): full_final = lax.all_gather(final_weight, 'col', axis=0, tiled=True)]
    reduce_scatter x0 -> x1, waiting for transfers between devices: none -> 11.6 us  [per_device(): lax.psum_scatter(partial_value, 'col', scatter_dimension=0, tiled=True)]
    all_to_all x1, waiting for transfers between devices: 31.5 us -> 42.2 us  [per_device(): bundle = lax.all_to_all(bundle, ROW, 0, 0, tiled=True)]
    dot_general x1 -> x2, matrix products: 0.21 us -> 5.01 us  [the longest x1 3.95 us: per_device(): lax.dot_general(attended, weight_t, (((1,), (1,)), ((), ())), preferred_e...]
    mul x2, local copies, waits for them, and re-layouts: 0.39 us -> 3.2 us  [rms_heads(): reshaped * reshaped]
    rsqrt x4, local copies, waits for them, and re-layouts: 0.27 us -> 3.01 us  [rms_heads(): lax.rsqrt(jnp.mean(reshaped * reshaped, -1, keepdims=True) + eps_norm)]
  transfers between devices with their start and end apart: 3 -> 3, of which waited for: 2 -> 2; matrix products, arithmetic and copies ran while one was open for 19% -> 28% of each run, Pallas kernels for 0% -> 0%
where the time goes in v3:
time: 203 us; the launch traced here: 202 us
  waiting for transfers between devices  54.5 us (27%)
  blocking collectives  52.9 us (26%)
  local copies, waits for them, and re-layouts  32.8 us (16%)
  matrix products  17.5 us (9%)
  other arithmetic  16.9 us (8%)
  between operations  14.5 us (7%)
  starting transfers between devices  12.8 us (6%)
    all_to_all x1, waiting for transfers between devices, per_device(): bundle = lax.all_to_all(bundle, ROW, 0, 0, tiled=True)  42.2 us
    all_to_all x1, blocking collectives, per_device(): attended = lax.all_to_all(attended, ROW, 0, 0, tiled=True)  19.1 us
    all_gather x2, blocking collectives, gather_features(): stacked = lax.all_gather(local, 'col', axis=0, tiled=False)  18.6 us
    all_to_all x1, starting transfers between devices, per_device(): bundle = lax.all_to_all(bundle, ROW, 0, 0, tiled=True)  12.6 us
    reduce_scatter x1, waiting for transfers between devices, per_device(): lax.psum_scatter(partial_value, 'col', scatter_dimension=0, tiled=True)  11.6 us
    all_gather x1, blocking collectives, per_device(): full_final = lax.all_gather(final_weight, 'col', axis=0, tiled=True)  9.43 us
    all_gather x1, blocking collectives, per_device(): lax.all_gather(jnp.stack([advanced, denoised]), 'col', axis=1, tiled=True)  5.86 us
    convert_element_type x3, local copies, waits for them, and re-layouts, per_device(): img_wide = img_full.astype(jnp.float32)  5.81 us
  transfers between devices with their start and end apart: 3, of which 2 were waited for; matrix products, arithmetic and copies ran while one was open for 28% of the time, Pallas kernels for 0%

profile of v3, /device:TPU:1, one launch (start us, length us, event | category | flops | bytes accessed | tf_op | source)
XLA Modules:
  0.0 202.0 jit_solution(4776180282703177053)
XLA Ops:
  7.9 8.6 %all-gather.1 = bf16[32,2,608]{2,1,0:T(2,128)(2,1)S(1)} all-gather(bf16[8,2,608]{2,1,0:T(2,128)(2,1)} %param.13), channel_id=3, replica_groups=mesh['rq'=8,'rm'=8,'col'=4] {'col'}, dimensions={0}, use_global_device_ids=true | all-gather | bytes 97280 | tf_op jit(solution)/shard_map/all_gather | solution.py:37
  16.8 10.0 %all-gather = bf16[32,24,608]{2,1,0:T(8,128)(2,1)S(1)} all-gather(bf16[8,24,608]{2,1,0:T(8,128)(2,1)} %param.12), channel_id=2, replica_groups=mesh['rq'=8,'rm'=8,'col'=4] {'col'}, dimensions={0}, use_global_device_ids=true | all-gather | bytes 1167360 | tf_op jit(solution)/shard_map/all_gather | solution.py:37
  26.8 1.4 convert_bitcast_fusion
  29.8 3.4 %fusion.14 = f32[2,8,2,512]{3,1,0,2:T(8,128)S(1)} fusion(bf16[2,2432,512]{2,1,0:T(8,128)(2,1)} %param.18, f32[8,2,2432]{2,0,1:T(8,128)S(1)} %reshape.212, f32[8,2432]{1,0:T(8,128)S(1)} %get-tuple-element.28, f32[8,2432]{1,0:T(8,128)S(1)} %get-tuple-element.29, f32[8,2]{0,1:T(2,128)S(1)} %copy.93, f32[8,2]{0,1:T(2,128)S(1)} %copy.90), kind=kOutput, calls=%fused_computation.17 | convolution fusion | flops 79886336 | bytes 5357696 | tf_op jit(solution)/shard_map/rtd,cde->crte/dot_general | solution.py:91
  33.2 1.3 copy.80
  34.5 2.3 %reshape.211 = f32[192,2432]{1,0:T(8,128)} reshape(f32[8,24,4,608]{3,2,1,0:T(4,128)S(1)} %copy.80) | data formatting | bytes 3735552 | tf_op jit(solution)/shard_map/convert_element_type | solution.py:79
  37.8 2.0 fusion.13
  39.8 4.8 %convolution_bitcast_fusion = f32[3,192,512]{2,1,0:T(8,128)S(1)} fusion(bf16[3,2432,512]{2,1,0:T(8,128)(2,1)} %param.17, bf16[192,2432]{1,0:T(8,128)(2,1)S(1)} %fusion.13), kind=kOutput, calls=%fused_computation.15 | convolution fusion | flops 1434451968 | bytes 9584640 | tf_op jit(solution)/shard_map/td,cde->cte/dot_general | solution.py:84
  44.7 1.1 slice_multiply_fusion.1
  48.4 1.2 copy.85
  50.5 1.2 reshape_squeeze.9
  51.7 2.0 copy.82
  53.7 1.1 reduce_sum.92
  55.4 1.4 rsqrt.60
  59.5 1.2 fusion.20
  61.2 2.3 %copy.98 = bf16[64,76,64]{1,2,0:T(8,128)(2,1)} copy(bf16[64,76,64]{2,0,1:T(8,128)(2,1)S(1)} %pad_maximum_fusion) | data formatting | bytes 1245184 | tf_op jit(solution)/shard_map/concatenate | solution.py:103
  63.4 12.6 %all-to-all-start = ((bf16[64,76,64]{1,2,0:T(8,128)(2,1)}), bf16[64,76,64]{1,2,0:T(8,128)(2,1)S(1)}, u32[]{:S(2)}, u32[]{:S(2)}) async-start(bf16[64,76,64]{1,2,0:T(8,128)(2,1)} %copy.98), calls=%async_computation | async-start | bytes 2097152 | tf_op jit(solution)/shard_map/all_to_all | solution.py:106
  77.5 42.2 %all-to-all-done = bf16[64,76,64]{1,2,0:T(8,128)(2,1)S(1)} async-done(((bf16[64,76,64]{1,2,0:T(8,128)(2,1)}), bf16[64,76,64]{1,2,0:T(8,128)(2,1)S(1)}, u32[]{:S(2)}, u32[]{:S(2)}) %all-to-all-start) | async-done | bytes 622624 | tf_op jit(solution)/shard_map/all_to_all | solution.py:106
  119.7 1.9 fusion.50
  121.6 1.7 copy.101
  124.6 1.7 copy.100
  126.5 1.9 fusion.52
  128.5 1.8 fusion
  130.3 2.4 %fusion.10 = bf16[1536,64]{0,1:T(8,128)(2,1)S(1)} fusion(bf16[1664,64]{1,0:T(8,128)(2,1)S(1)} %copy-done.4, f32[1536,1664]{1,0:T(8,128)S(1)} %get-tuple-element.27, f32[1536]{0:T(1024)S(1)} %get-tuple-element.26, pred[1664]{0:T(1024)(128)(4,1)S(1)} %fusion.46, f32[1536]{0:T(1024)S(1)} %fusion), kind=kOutput, calls=%fused_computation.9 | convolution fusion | flops 335020032 | bytes 10647168 | tf_op jit(solution)/shard_map/dot_general | solution.py:49
  133.2 19.1 %all_to_all.10 = bf16[64,2,768]{2,1,0:T(2,128)(2,1)S(1)} all-to-all(bf16[64,2,768]{2,1,0:T(2,128)(2,1)S(1)} %reshape.229), channel_id=1, replica_groups=mesh['rq'=8,'rm'=8,'col'=4] {'rq','rm'}, dimensions={0} | all-to-all | bytes 393216 | tf_op jit(solution)/shard_map/all_to_all | solution.py:121
  152.9 4.2 %reshape.221 = bf16[2432,512]{1,0:T(8,128)(2,1)} reshape(bf16[64,38,512]{2,1,0:T(8,128)(2,1)} %all-gather.6.cloned.1.call-done) | data formatting | bytes 4980736
  157.1 4.0 %fusion.53 = f32[192,2432]{1,0:T(8,128)} fusion(bf16[192,512]{1,0:T(8,128)(2,1)S(1)} %reshape.208, bf16[2432,512]{1,0:T(8,128)(2,1)} %reshape.221), kind=kOutput, calls=%fused_computation.102 | convolution fusion | flops 478150656 | bytes 4554752 | tf_op jit(solution)/shard_map/dot_general | solution.py:126
  161.1 2.3 %reshape.210 = f32[8,24,2432]{2,1,0:T(8,128)} reshape(f32[8,24,4,608]{3,2,1,0:T(4,128)S(1)} %copy.80) | data formatting | bytes 3735552 | tf_op jit(solution)/shard_map/convert_element_type | solution.py:79
  163.4 9.4 %all-gather.3 = bf16[4,608,64]{1,2,0:T(8,128)(2,1)S(1)} all-gather(bf16[1,608,64]{1,2,0:T(8,128)(2,1)S(1)} %bitcast.135), channel_id=1, replica_groups=mesh['rq'=8,'rm'=8,'col'=4] {'col'}, dimensions={0}, use_global_device_ids=true | all-gather | bytes 389120 | tf_op jit(solution)/shard_map/all_gather | solution.py:76
  174.4 11.6 %reduce-scatter.2.cloned.1.call-done = f32[48,2432]{1,0:T(8,128)} async-done(((f32[192,2432]{1,0:T(8,128)}), f32[48,2432]{1,0:T(8,128)}) %reduce-scatter.2.cloned.1.call-update) | async-done | bytes 466960 | tf_op jit(solution)/shard_map/reduce_scatter | solution.py:134
  186.0 1.3 fusion.49
  188.6 5.9 %all_gather.27 = f32[2,8,24,64]{3,2,1,0:T(8,128)S(1)} all-gather(f32[2,2,24,64]{3,2,1,0:T(8,128)S(1)} %pad_maximum_fusion.1), channel_id=1, replica_groups=mesh['rq'=8,'rm'=8,'col'=4] {'col'}, dimensions={1}, use_global_device_ids=true | all-gather | bytes 122880 | tf_op jit(solution)/shard_map/all_gather | solution.py:154
  (90 shorter events, 18.6 us)
Async XLA Ops:
  7.2 145.7 %all-gather.6.cloned.1.call-start = ((), (), s32[]{:S(2)}) async-start(), calls=%async_computation.4 | async-start | bytes 2662400 | tf_op jit(solution)/shard_map/all_gather | solution.py:74
  26.8 2.3 %copy-start.5 = (f32[8,2,2432]{2,1,0:T(2,128)S(1)}, f32[8,2,2432]{2,1,0:T(2,128)}, u32[]{:S(2)}) copy-start(f32[8,2,2432]{2,1,0:T(2,128)} %param.16) | copy-start | bytes 466948
  29.8 3.4 %copy-start = (f32[8,24,4,608]{3,1,0,2:T(8,128)S(1)}, f32[8,24,4,608]{3,1,0,2:T(8,128)}, u32[]{:S(2)}) copy-start(f32[8,24,4,608]{3,1,0,2:T(8,128)} %convert_bitcast_fusion) | copy-start | bytes 5603332
  33.2 3.6 %copy-start.3 = (f32[2,8,2,512]{3,1,0,2:T(8,128)}, f32[2,8,2,512]{3,1,0,2:T(8,128)S(1)}, u32[]{:S(2)}) copy-start(f32[2,8,2,512]{3,1,0,2:T(8,128)S(1)} %fusion.14) | copy-start | bytes 196612
  44.6 2.8 %slice-start = ((f32[2,8,2,512]{3,1,0,2:T(8,128)}), f32[1,8,2,512]{3,1,0,2:T(8,128)S(1)}, s32[]{:S(2)}) async-start(f32[2,8,2,512]{3,1,0,2:T(8,128)} %copy-done.3), calls=%async_computation.5 | async-start | bytes 65536 | tf_op jit(solution)/shard_map/slice | solution.py:94
  44.6 2.9 %copy-start.8 = (f32[3,64]{1,0:T(4,128)S(1)}, f32[3,64]{1,0:T(4,128)}, u32[]{:S(2)}) copy-start(f32[3,64]{1,0:T(4,128)} %param.21) | copy-start | bytes 2308
  47.5 0.7 copy-start.2
  56.7 4.0 %copy-start.1 = (bf16[8,24,8,64]{3,2,1,0:T(8,128)(2,1)S(1)}, bf16[8,24,8,64]{3,2,1,0:T(8,128)(2,1)}, u32[]{:S(2)}) copy-start(bf16[8,24,8,64]{3,2,1,0:T(8,128)(2,1)} %convert_element_type.99) | copy-start | bytes 589828
  56.7 4.0 %copy-start.6 = (bf16[8,2,8,64]{3,2,0,1:T(8,128)(2,1)S(1)}, bf16[8,2,8,64]{3,2,0,1:T(8,128)(2,1)}, u32[]{:S(2)}) copy-start(bf16[8,2,8,64]{3,2,0,1:T(8,128)(2,1)} %convert_element_type.100) | copy-start | bytes 49156
  61.2 15.1 %copy-start.10 = (s32[8]{0:T(128)S(1)}, s32[8]{0:T(128)}, u32[]{:S(2)}) copy-start(s32[8]{0:T(128)} %param.22) | copy-start | bytes 100
  63.4 56.3 %all-to-all-start = ((bf16[64,76,64]{1,2,0:T(8,128)(2,1)}), bf16[64,76,64]{1,2,0:T(8,128)(2,1)S(1)}, u32[]{:S(2)}, u32[]{:S(2)}) async-start(bf16[64,76,64]{1,2,0:T(8,128)(2,1)} %copy.98), calls=%async_computation | async-start | bytes 2097152 | tf_op jit(solution)/shard_map/all_to_all | solution.py:106
  76.0 110.0 %reduce-scatter.2.cloned.1.call-start = ((), (), s32[]{:S(2)}) async-start(), calls=%async_computation.3 | async-start | bytes 2334720 | tf_op jit(solution)/shard_map/reduce_scatter | solution.py:134
  128.5 1.8 copy-start.4
  161.1 2.3 %copy-start.7 = (bf16[608,64]{0,1:T(8,128)(2,1)S(1)}, bf16[608,64]{0,1:T(8,128)(2,1)}, u32[]{:S(2)}) copy-start(bf16[608,64]{0,1:T(8,128)(2,1)} %param.20) | copy-start | bytes 233476
  161.1 12.2 %copy-start.9 = (s32[8]{0:T(128)S(1)}, s32[8]{0:T(128)}, u32[]{:S(2)}) copy-start(s32[8]{0:T(128)} %param.23) | copy-start | bytes 100
Sparse Core Ops, SparseCore 0:
  11.3 102.5 all-gather.5
  161.2 24.7 reduce-scatter.1

commit v4 on v3

--- a/solution.py
+++ b/solution.py
@@ -33,13 +33,6 @@
     return 3.0 * fraction / (1.0 + 2.0 * fraction)
 
 
-def gather_features(local):
-    stacked = lax.all_gather(local, "col", axis=0, tiled=False)
-    slabs = stacked.shape[0]
-    moved = jnp.moveaxis(stacked, 0, -2)
-    return moved.reshape(local.shape[:-1] + (slabs * local.shape[-1],))
-
-
 def attend_one(queries, keys, values, allowed):
     scores = jnp.dot(queries, keys.T, preferred_element_type=jnp.float32) * HD ** (-0.5)
     scores = jnp.where(allowed[None, :], scores, neg_fill)
@@ -73,9 +66,20 @@
 
     weight_t = lax.all_gather(jnp.transpose(out_weight), ROW, axis=0, tiled=True)
 
-    full_final = lax.all_gather(final_weight, "col", axis=0, tiled=True)
-    img_full = gather_features(img_hidden)
-    txt_full = gather_features(txt_hidden)
+    img_rows = img_hidden.reshape(requests * patches, -1)
+    txt_rows = txt_hidden.reshape(requests * text_rows, -1)
+    packed = jnp.concatenate([img_rows, txt_rows, jnp.transpose(final_weight)], 0)
+    packed = lax.all_gather(packed, "col", axis=0, tiled=False)
+    slabs = packed.shape[0]
+
+    def joined(part):
+        return jnp.moveaxis(part, 0, -2).reshape(part.shape[1], slabs * part.shape[2])
+
+    img_count = requests * patches
+    txt_count = requests * text_rows
+    img_full = joined(packed[:, :img_count]).reshape(requests, patches, D)
+    txt_full = joined(packed[:, img_count : img_count + txt_count]).reshape(requests, text_rows, D)
+    final_slabs = packed[:, img_count + txt_count :]
     img_wide = img_full.astype(jnp.float32)
     normed = (layer_norm(img_wide) * (1.0 + img_mod[:, 1:2, :]) + img_mod[:, 0:1, :]).astype(
         jnp.bfloat16
@@ -100,14 +104,13 @@
         split = values.reshape(requests, length, heads_local, HD)
         return jnp.transpose(split, (0, 2, 1, 3)).reshape(requests * heads_local, length, HD)
 
-    bundle = jnp.concatenate(
-        [by_head(queries, patches), by_head(key_rows, block_len), by_head(value_rows, block_len)], 1
-    )
+    head_queries = lax.all_to_all(by_head(queries, patches), ROW, 0, 0, tiled=True)
+    bundle = jnp.concatenate([by_head(key_rows, block_len), by_head(value_rows, block_len)], 1)
     bundle = lax.all_to_all(bundle, ROW, 0, 0, tiled=True)
     sources = bundle.shape[0]
-    head_queries = bundle[:, :patches].reshape(sources * patches, HD)
-    keys = bundle[:, patches : patches + block_len].reshape(sources * block_len, HD)
-    values = bundle[:, patches + block_len :].reshape(sources * block_len, HD)
+    head_queries = head_queries.reshape(sources * patches, HD)
+    keys = bundle[:, :block_len].reshape(sources * block_len, HD)
+    values = bundle[:, block_len:].reshape(sources * block_len, HD)
 
     request = lax.axis_index("rq")
     positions = jnp.arange(sources * block_len, dtype=jnp.int32)
@@ -140,9 +143,10 @@
     modulated = (layer_norm(mixed) * (1.0 + own_mods[:, 4:5, :]) + own_mods[:, 3:4, :]).astype(
         jnp.bfloat16
     )
-    velocity = jnp.dot(
-        modulated.reshape(own_requests * patches, D),
-        full_final,
+    velocity = jnp.einsum(
+        "tcf,cof->to",
+        modulated.reshape(own_requests * patches, slabs, D // slabs),
+        final_slabs,
         preferred_element_type=jnp.float32,
     ).reshape(own_requests, patches, latent.shape[2])
     own_latent = lax.dynamic_slice_in_dim(latent, first, own_requests, 0)

time: 203 us -> 233 us (1.15)
  blocking collectives: 52.9 us -> 24.5 us
  local copies, waits for them, and re-layouts: 32.8 us -> 59 us
  other arithmetic: 16.9 us -> 32 us
  starting transfers between devices: 12.8 us -> 24.3 us
  waiting for transfers between devices: 54.5 us -> 58.9 us
    all_to_all x1, waiting for transfers between devices: 42.2 us -> 11.4 us  [per_device(): bundle = lax.all_to_all(bundle, ROW, 0, 0, tiled=True)]
    all_gather x3 -> x0, blocking collectives: 28 us -> none  [the longest x2 18.6 us: gather_features(): stacked = lax.all_gather(local, 'col', axis=0, tiled=False)]
    all_gather x0 -> x1, waiting for transfers between devices: none -> 24.8 us  [per_device(): packed = lax.all_gather(packed, 'col', axis=0, tiled=False)]
    unnamed x28 -> x25, local copies, waits for them, and re-layouts: 5.2 us -> 17.8 us
    all_to_all x0 -> x1, starting transfers between devices: none -> 11.7 us  [per_device(): lax.all_to_all(by_head(queries, patches), ROW, 0, 0, tiled=True)]
    reduce_scatter x1, waiting for transfers between devices: 11.6 us -> 21.9 us  [per_device(): lax.psum_scatter(partial_value, 'col', scatter_dimension=0, tiled=True)]
    reshape x3, local copies, waits for them, and re-layouts: 1.2 us -> 4.71 us  [the longest x1 1.98 us: per_device(): keys = bundle[:, :block_len].reshape(sources * block_len, HD)]
    slice x4 -> x1, local copies, waits for them, and re-layouts: 5.74 us -> 2.32 us  [per_device(): keys = bundle[:, :block_len].reshape(sources * block_len, HD)]
  transfers between devices with their start and end apart: 3 -> 5, of which waited for: 2 -> 3; matrix products, arithmetic and copies ran while one was open for 28% -> 40% of each run, Pallas kernels for 0% -> 0%
where the time goes in v4:
time: 233 us; the launch traced here: 231 us
  local copies, waits for them, and re-layouts  59 us (25%)
  waiting for transfers between devices  58.9 us (25%)
  other arithmetic  32 us (14%)
  blocking collectives  24.5 us (11%)
  starting transfers between devices  24.3 us (10%)
  matrix products  18.4 us (8%)
  between operations  14 us (6%)
    all_gather x1, waiting for transfers between devices, per_device(): packed = lax.all_gather(packed, 'col', axis=0, tiled=False)  24.8 us
    reduce_scatter x1, waiting for transfers between devices, per_device(): lax.psum_scatter(partial_value, 'col', scatter_dimension=0, tiled=True)  21.9 us
    all_to_all x1, blocking collectives, per_device(): attended = lax.all_to_all(attended, ROW, 0, 0, tiled=True)  18.6 us
    unnamed x25, local copies, waits for them, and re-layouts  17.8 us
    all_to_all x1, starting transfers between devices, per_device(): bundle = lax.all_to_all(bundle, ROW, 0, 0, tiled=True)  12.4 us
    all_to_all x1, starting transfers between devices, per_device(): lax.all_to_all(by_head(queries, patches), ROW, 0, 0, tiled=True)  11.7 us
    all_to_all x1, waiting for transfers between devices, per_device(): bundle = lax.all_to_all(bundle, ROW, 0, 0, tiled=True)  11.4 us
    convert_element_type x3, local copies, waits for them, and re-layouts, per_device(): img_wide = img_full.astype(jnp.float32)  7.36 us
  transfers between devices with their start and end apart: 5, of which 3 were waited for; matrix products, arithmetic and copies ran while one was open for 40% of the time, Pallas kernels for 0%

profile of v4, /device:TPU:1, one launch (start us, length us, event | category | flops | bytes accessed | tf_op | source)
XLA Modules:
  0.0 231.0 jit_solution(5811243940051838765)
XLA Ops:
  15.3 24.8 %all-gather.5.cloned.1.call-done = bf16[1088,608]{1,0:T(8,128)(2,1)} async-done(((bf16[272,608]{1,0:T(8,128)(2,1)}), bf16[1088,608]{1,0:T(8,128)(2,1)}) %all-gather.5.cloned.1.call-update) | async-done | bytes 1323024 | tf_op jit(solution)/shard_map/all_gather | solution.py:72
  43.3 2.6 %convert_bitcast_fusion = f32[192,4,608]{2,0,1:T(8,128)} fusion(bf16[4,272,608]{2,1,0:T(8,128)(2,1)} %bitcast.114), kind=kLoop, calls=%fused_computation.10 | loop fusion | flops 466944 | bytes 2801664 | tf_op jit(solution)/shard_map/convert_element_type | solution.py:83
  46.5 2.8 %copy.53 = f32[192,4,608]{2,1,0:T(4,128)S(1)} copy(f32[192,4,608]{2,0,1:T(8,128)} %convert_bitcast_fusion) | data formatting | bytes 3735552 | tf_op jit(solution)/shard_map/convert_element_type | solution.py:83
  49.3 2.3 reshape.233
  53.2 3.2 %fusion.16 = f32[2,8,2,512]{3,1,0,2:T(8,128)S(1)} fusion(bf16[2,2432,512]{2,1,0:T(8,128)(2,1)} %param.18, bf16[8,2,2432,1]{2,1,0,3:T(2,128)(2,1)S(1)} %fusion.29), kind=kOutput, calls=%fused_computation.19 | convolution fusion | flops 79691776 | bytes 5124096 | tf_op jit(solution)/shard_map/rtd,cde->crte/dot_general | solution.py:95
  57.7 2.0 fusion.15
  59.7 4.8 %convolution_bitcast_fusion = f32[3,192,512]{2,1,0:T(8,128)S(1)} fusion(bf16[3,2432,512]{2,1,0:T(8,128)(2,1)} %param.17, bf16[192,2432]{1,0:T(8,128)(2,1)S(1)} %fusion.15), kind=kOutput, calls=%fused_computation.18 | convolution fusion | flops 1434451968 | bytes 9584640 | tf_op jit(solution)/shard_map/td,cde->cte/dot_general | solution.py:88
  66.8 2.1 reshape_squeeze.10
  68.8 2.0 copy.58
  72.8 2.0 reshape_squeeze.9
  74.8 2.0 copy.55
  78.0 2.2 fusion.23
  80.2 1.9 reshape.245
  82.2 11.7 %all-to-all-start = ((bf16[64,2,768]{2,1,0:T(2,128)(2,1)}), bf16[64,2,768]{2,1,0:T(2,128)(2,1)S(1)}, u32[]{:S(2)}, u32[]{:S(2)}) async-start(bf16[64,2,768]{2,1,0:T(2,128)(2,1)} %reshape.245), calls=%async_computation | async-start | bytes 393216 | tf_op jit(solution)/shard_map/all_to_all | solution.py:107
  102.5 1.9 convert_element_type.99
  108.2 2.8 %reshape.243 = bf16[64,2,1664]{2,1,0:T(2,128)(2,1)} reshape(bf16[64,52,64]{2,1,0:T(8,128)(2,1)} %copy.66) | data formatting | bytes 851968
  111.1 12.4 %all-to-all-start.1 = ((bf16[64,2,1664]{2,1,0:T(2,128)(2,1)}), bf16[64,2,1664]{2,1,0:T(2,128)(2,1)}, u32[]{:S(2)}, u32[]{:S(2)}) async-start(bf16[64,2,1664]{2,1,0:T(2,128)(2,1)} %reshape.243), calls=%async_computation.1 | async-start | bytes 851968 | tf_op jit(solution)/shard_map/all_to_all | solution.py:109
  127.0 11.4 %all-to-all-done.1 = bf16[64,2,1664]{2,1,0:T(2,128)(2,1)} async-done(((bf16[64,2,1664]{2,1,0:T(2,128)(2,1)}), bf16[64,2,1664]{2,1,0:T(2,128)(2,1)}, u32[]{:S(2)}, u32[]{:S(2)}) %all-to-all-start.1) | async-done | bytes 426016 | tf_op jit(solution)/shard_map/all_to_all | solution.py:109
  138.4 2.9 %reshape.244 = bf16[64,52,64]{2,1,0:T(8,128)(2,1)} reshape(bf16[64,2,1664]{2,1,0:T(2,128)(2,1)} %all-to-all-done.1) | data formatting | bytes 851968
  141.3 2.3 %fusion.44 = (bf16[64,26,64]{2,1,0:T(8,128)(2,1)}, bf16[64,26,64]{2,1,0:T(8,128)(2,1)}) fusion(bf16[64,52,64]{2,1,0:T(8,128)(2,1)} %reshape.244), kind=kLoop, calls=%fused_computation.98 | loop fusion | bytes 851968 | tf_op jit(solution)/shard_map/slice | solution.py:112
  143.7 2.0 reshape.227
  145.6 2.0 reshape.226
  147.6 3.0 %fusion.46 = (f32[1536]{0:T(1024)S(1)}, f32[1536,1664]{1,0:T(8,128)S(1)}) fusion(bf16[1536,64]{1,0:T(8,128)(2,1)} %bitcast.118, bf16[1664,64]{1,0:T(8,128)(2,1)} %reshape.226, pred[1664]{0:T(1024)(128)(4,1)S(1)} %copy-done.6), kind=kOutput, calls=%fused_computation.100 | convolution fusion | flops 334821888 | bytes 10641024 | tf_op jit(solution)/shard_map/dot_general | solution.py:37
  152.5 2.4 %fusion.10 = bf16[1536,64]{0,1:T(8,128)(2,1)S(1)} fusion(bf16[1664,64]{1,0:T(8,128)(2,1)S(1)} %copy-done.3, f32[1536,1664]{1,0:T(8,128)S(1)} %get-tuple-element.27, f32[1536]{0:T(1024)S(1)} %get-tuple-element.26, pred[1664]{0:T(1024)(128)(4,1)S(1)} %copy-done.7, f32[1536]{0:T(1024)S(1)} %fusion), kind=kOutput, calls=%fused_computation.12 | convolution fusion | flops 335020032 | bytes 10647168 | tf_op jit(solution)/shard_map/dot_general | solution.py:42
  157.1 18.6 %all_to_all.15 = bf16[64,2,768]{2,1,0:T(2,128)(2,1)} all-to-all(bf16[64,2,768]{2,1,0:T(2,128)(2,1)S(1)} %reshape.247), channel_id=1, replica_groups=mesh['rq'=8,'rm'=8,'col'=4] {'rq','rm'}, dimensions={0} | all-to-all | bytes 393216 | tf_op jit(solution)/shard_map/all_to_all | solution.py:124
  175.7 2.0 reshape.248
  177.7 1.8 copy.99
  180.9 4.2 %reshape.237 = bf16[2432,512]{1,0:T(8,128)(2,1)} reshape(bf16[64,38,512]{2,1,0:T(8,128)(2,1)} %all-gather.7.cloned.1.call-done) | data formatting | bytes 4980736
  185.1 4.0 %fusion.49 = f32[192,2432]{1,0:T(8,128)} fusion(bf16[192,512]{1,0:T(8,128)(2,1)S(1)} %reshape.230, bf16[2432,512]{1,0:T(8,128)(2,1)} %reshape.237), kind=kOutput, calls=%fused_computation.101 | convolution fusion | flops 478150656 | bytes 4554752 | tf_op jit(solution)/shard_map/dot_general | solution.py:129
  190.8 2.3 reshape.232
  193.1 21.9 %reduce-scatter.2.cloned.1.call-done = f32[48,2432]{1,0:T(8,128)} async-done(((f32[192,2432]{1,0:T(8,128)}), f32[48,2432]{1,0:T(8,128)}) %reduce-scatter.2.cloned.1.call-update) | async-done | bytes 466960 | tf_op jit(solution)/shard_map/reduce_scatter | solution.py:137
  218.0 5.8 %all_gather.15 = f32[2,8,24,64]{3,2,1,0:T(8,128)S(1)} all-gather(f32[2,2,24,64]{3,2,1,0:T(8,128)S(1)} %pad_maximum_fusion.2), channel_id=1, replica_groups=mesh['rq'=8,'rm'=8,'col'=4] {'col'}, dimensions={1}, use_global_device_ids=true | all-gather | bytes 122880 | tf_op jit(solution)/shard_map/all_gather | solution.py:158
  (86 shorter events, 46.7 us)
Async XLA Ops:
  7.2 32.9 %all-gather.5.cloned.1.call-start = ((), (), s32[]{:S(2)}) async-start(), calls=%async_computation.5 | async-start | bytes 1740800 | tf_op jit(solution)/shard_map/all_gather | solution.py:72
  9.7 171.1 %all-gather.7.cloned.1.call-start = ((), (), s32[]{:S(2)}) async-start(), calls=%async_computation.6 | async-start | bytes 2662400 | tf_op jit(solution)/shard_map/all_gather | solution.py:67
  40.0 5.8 %copy-start = (bf16[1088,608]{1,0:T(8,128)(2,1)S(1)}, bf16[1088,608]{1,0:T(8,128)(2,1)}, u32[]{:S(2)}) copy-start(bf16[1088,608]{1,0:T(8,128)(2,1)} %all-gather.5.cloned.1.call-done) | copy-start | bytes 3969028
  53.2 4.6 %copy-start.4 = (f32[8,2432]{1,0:T(8,128)S(1)}, f32[8,2432]{1,0:T(8,128)}, u32[]{:S(2)}) copy-start(f32[8,2432]{1,0:T(8,128)} %get-tuple-element.15) | copy-start | bytes 233476
  53.2 4.6 %copy-start.5 = (f32[8,2432]{1,0:T(8,128)S(1)}, f32[8,2432]{1,0:T(8,128)}, u32[]{:S(2)}) copy-start(f32[8,2432]{1,0:T(8,128)} %get-tuple-element.16) | copy-start | bytes 233476
  56.4 0.6 copy-start.2
  64.5 1.0 copy-start.1
  68.8 9.2 %copy-start.8 = (f32[64]{0:T(128)S(1)}, f32[64]{0:T(128)}, u32[]{:S(2)}) copy-start(f32[64]{0:T(128)} %get-tuple-element.23) | copy-start | bytes 772
  82.2 28.9 %all-to-all-start = ((bf16[64,2,768]{2,1,0:T(2,128)(2,1)}), bf16[64,2,768]{2,1,0:T(2,128)(2,1)S(1)}, u32[]{:S(2)}, u32[]{:S(2)}) async-start(bf16[64,2,768]{2,1,0:T(2,128)(2,1)} %reshape.245), calls=%async_computation | async-start | bytes 393216 | tf_op jit(solution)/shard_map/all_to_all | solution.py:107
  111.1 27.4 %all-to-all-start.1 = ((bf16[64,2,1664]{2,1,0:T(2,128)(2,1)}), bf16[64,2,1664]{2,1,0:T(2,128)(2,1)}, u32[]{:S(2)}, u32[]{:S(2)}) async-start(bf16[64,2,1664]{2,1,0:T(2,128)(2,1)} %reshape.243), calls=%async_computation.1 | async-start | bytes 851968 | tf_op jit(solution)/shard_map/all_to_all | solution.py:109
  123.5 91.5 %reduce-scatter.2.cloned.1.call-start = ((), (), s32[]{:S(2)}) async-start(), calls=%async_computation.4 | async-start | bytes 2334720 | tf_op jit(solution)/shard_map/reduce_scatter | solution.py:137
  127.0 20.6 %copy-start.6 = (pred[1664]{0:T(1024)(128)(4,1)S(1)}, pred[1664]{0:T(1024)(128)(4,1)}, u32[]{:S(2)}) copy-start(pred[1664]{0:T(1024)(128)(4,1)} %fusion.41) | copy-start | bytes 4996
  150.7 1.8 copy-start.3
  150.7 1.8 copy-start.7
Sparse Core Ops, SparseCore 0:
  9.8 30.1 all-gather.4
  43.3 79.9 all-gather.6
  189.2 25.7 reduce-scatter.1

commit v5 on v3

--- a/solution.py
+++ b/solution.py
@@ -73,11 +73,19 @@
 
     weight_t = lax.all_gather(jnp.transpose(out_weight), ROW, axis=0, tiled=True)
 
-    full_final = lax.all_gather(final_weight, "col", axis=0, tiled=True)
     img_full = gather_features(img_hidden)
-    txt_full = gather_features(txt_hidden)
-    img_wide = img_full.astype(jnp.float32)
-    normed = (layer_norm(img_wide) * (1.0 + img_mod[:, 1:2, :]) + img_mod[:, 0:1, :]).astype(
+    txt_rows = txt_hidden.reshape(requests * text_rows, -1)
+    packed = jnp.concatenate([txt_rows, jnp.transpose(final_weight)], 0)
+    packed = lax.all_gather(packed, "col", axis=0, tiled=False)
+    slabs = packed.shape[0]
+    txt_count = requests * text_rows
+    txt_full = (
+        jnp.moveaxis(packed[:, :txt_count], 0, -2)
+        .reshape(txt_count, D)
+        .reshape(requests, text_rows, D)
+    )
+    final_slabs = packed[:, txt_count:]
+    normed = (layer_norm(img_full.astype(jnp.float32)) * (1.0 + img_mod[:, 1:2, :]) + img_mod[:, 0:1, :]).astype(
         jnp.bfloat16
     )
     flat_rows = normed.reshape(requests * patches, D)
@@ -135,14 +143,15 @@
     own_requests = requests // cols
     first = col_index * own_requests
     own_mods = lax.dynamic_slice_in_dim(img_mod, first, own_requests, 0)
-    own_hidden = lax.dynamic_slice_in_dim(img_wide, first, own_requests, 0)
+    own_hidden = lax.dynamic_slice_in_dim(img_full, first, own_requests, 0).astype(jnp.float32)
     mixed = own_hidden + own_mods[:, 2:3, :] * shared_sum.reshape(own_requests, patches, D)
     modulated = (layer_norm(mixed) * (1.0 + own_mods[:, 4:5, :]) + own_mods[:, 3:4, :]).astype(
         jnp.bfloat16
     )
-    velocity = jnp.dot(
-        modulated.reshape(own_requests * patches, D),
-        full_final,
+    velocity = jnp.einsum(
+        "tcf,cof->to",
+        modulated.reshape(own_requests * patches, slabs, D // slabs),
+        final_slabs,
         preferred_element_type=jnp.float32,
     ).reshape(own_requests, patches, latent.shape[2])
     own_latent = lax.dynamic_slice_in_dim(latent, first, own_requests, 0)

time: 203 us -> 192 us (0.946)
  blocking collectives: 52.9 us -> 45.8 us
  local copies, waits for them, and re-layouts: 32.8 us -> 28.6 us
  waiting for transfers between devices: 54.5 us -> 58 us
  other arithmetic: 16.9 us -> 14.5 us
    reduce_scatter x1, waiting for transfers between devices: 11.6 us -> 23.9 us  [per_device(): lax.psum_scatter(partial_value, 'col', scatter_dimension=0, tiled=True)]
    all_to_all x1, waiting for transfers between devices: 42.2 us -> 33.4 us  [per_device(): bundle = lax.all_to_all(bundle, ROW, 0, 0, tiled=True)]
    all_gather x2 -> x1, blocking collectives: 18.6 us -> 9.99 us  [gather_features(): stacked = lax.all_gather(local, 'col', axis=0, tiled=False)]
    mul x2, local copies, waits for them, and re-layouts: 3.2 us -> 0.4 us  [rms_heads(): reshaped * reshaped]
    rsqrt x4, local copies, waits for them, and re-layouts: 3.01 us -> 0.9 us  [rms_heads(): lax.rsqrt(jnp.mean(reshaped * reshaped, -1, keepdims=True) + eps_norm)]
    unnamed x28 -> x23, local copies, waits for them, and re-layouts: 5.2 us -> 3.96 us
    convert_element_type x3 -> x2, local copies, waits for them, and re-layouts: 5.81 us -> 4.77 us  [per_device(): img_full.astype(jnp.float32)]
  transfers between devices with their start and end apart: 3 -> 3, of which waited for: 2 -> 2; matrix products, arithmetic and copies ran while one was open for 28% -> 25% of each run, Pallas kernels for 0% -> 0%
where the time goes in v5:
time: 192 us; the launch traced here: 191 us
  waiting for transfers between devices  58 us (30%)
  blocking collectives  45.8 us (24%)
  local copies, waits for them, and re-layouts  28.6 us (15%)
  matrix products  16.4 us (9%)
  other arithmetic  14.5 us (8%)
  between operations  14.5 us (8%)
  starting transfers between devices  12.8 us (7%)
    all_to_all x1, waiting for transfers between devices, per_device(): bundle = lax.all_to_all(bundle, ROW, 0, 0, tiled=True)  33.4 us
    reduce_scatter x1, waiting for transfers between devices, per_device(): lax.psum_scatter(partial_value, 'col', scatter_dimension=0, tiled=True)  23.9 us
    all_to_all x1, blocking collectives, per_device(): attended = lax.all_to_all(attended, ROW, 0, 0, tiled=True)  20.7 us
    all_to_all x1, starting transfers between devices, per_device(): bundle = lax.all_to_all(bundle, ROW, 0, 0, tiled=True)  12.5 us
    all_gather x1, blocking collectives, gather_features(): stacked = lax.all_gather(local, 'col', axis=0, tiled=False)  9.99 us
    all_gather x1, blocking collectives, per_device(): packed = lax.all_gather(packed, 'col', axis=0, tiled=False)  9.27 us
    all_gather x1, blocking collectives, per_device(): lax.all_gather(jnp.stack([advanced, denoised]), 'col', axis=1, tiled=True)  5.84 us
    dot_general x1, matrix products, per_device(): jnp.einsum('td,cde->cte', flat_rows, qkv_weight, preferred_element_type=j...  4.8 us
  transfers between devices with their start and end apart: 3, of which 2 were waited for; matrix products, arithmetic and copies ran while one was open for 25% of the time, Pallas kernels for 0%

profile of v5, /device:TPU:1, one launch (start us, length us, event | category | flops | bytes accessed | tf_op | source)
XLA Modules:
  0.0 190.6 jit_solution(15054088263402779681)
XLA Ops:
  8.7 0.9 pad_maximum_fusion.1
  9.6 9.3 %all-gather.1 = bf16[320,608]{1,0:T(8,128)(2,1)S(1)} all-gather(bf16[80,608]{1,0:T(8,128)(2,1)S(1)} %pad_maximum_fusion.1), channel_id=3, replica_groups=mesh['rq'=8,'rm'=8,'col'=4] {'col'}, dimensions={0}, use_global_device_ids=true | all-gather | bytes 486400 | tf_op jit(solution)/shard_map/all_gather | solution.py:79
  19.9 10.0 %all-gather = bf16[32,24,608]{2,1,0:T(8,128)(2,1)S(1)} all-gather(bf16[8,24,608]{2,1,0:T(8,128)(2,1)} %param.12), channel_id=2, replica_groups=mesh['rq'=8,'rm'=8,'col'=4] {'col'}, dimensions={0}, use_global_device_ids=true | all-gather | bytes 1167360 | tf_op jit(solution)/shard_map/all_gather | solution.py:37
  31.6 3.2 %fusion.14 = f32[2,8,2,512]{3,1,0,2:T(8,128)S(1)} fusion(bf16[2,2432,512]{2,1,0:T(8,128)(2,1)} %param.18, bf16[8,2,2432,1]{2,1,0,3:T(2,128)(2,1)S(1)} %fusion.27), kind=kOutput, calls=%fused_computation.16 | convolution fusion | flops 79691776 | bytes 5124096 | tf_op jit(solution)/shard_map/rtd,cde->crte/dot_general | solution.py:99
  35.4 2.5 %copy.59 = f32[8,24,4,608]{3,2,1,0:T(4,128)} copy(f32[8,24,4,608]{3,1,0,2:T(8,128)S(1)} %bitcast_convert_fusion) | data formatting | bytes 3735552 | tf_op jit(solution)/shard_map/convert_element_type | solution.py:88
  37.9 2.2 %reshape.231 = f32[192,2432]{1,0:T(8,128)S(1)} reshape(f32[8,24,4,608]{3,2,1,0:T(4,128)} %copy.59) | data formatting | bytes 3735552 | tf_op jit(solution)/shard_map/convert_element_type | solution.py:88
  40.1 0.9 add_bitcast_fusion
  41.6 4.8 %convolution_bitcast_fusion = f32[3,192,512]{2,1,0:T(8,128)S(1)} fusion(bf16[3,2432,512]{2,1,0:T(8,128)(2,1)} %param.17, bf16[192,2432]{1,0:T(8,128)(2,1)S(1)} %fusion.13), kind=kOutput, calls=%fused_computation.14 | convolution fusion | flops 1434451968 | bytes 9584640 | tf_op jit(solution)/shard_map/td,cde->cte/dot_general | solution.py:92
  47.4 1.0 convert_element_type.90
  51.0 0.9 fusion.21
  52.7 1.2 fusion.19
  54.4 2.3 %copy.72 = bf16[64,76,64]{1,2,0:T(8,128)(2,1)} copy(bf16[64,76,64]{2,0,1:T(8,128)(2,1)S(1)} %pad_maximum_fusion) | data formatting | bytes 1245184 | tf_op jit(solution)/shard_map/concatenate | solution.py:111
  56.7 12.5 %all-to-all-start = ((bf16[64,76,64]{1,2,0:T(8,128)(2,1)}), bf16[64,76,64]{1,2,0:T(8,128)(2,1)S(1)}, u32[]{:S(2)}, u32[]{:S(2)}) async-start(bf16[64,76,64]{1,2,0:T(8,128)(2,1)} %copy.72), calls=%async_computation | async-start | bytes 2097152 | tf_op jit(solution)/shard_map/all_to_all | solution.py:114
  70.7 33.4 %all-to-all-done = bf16[64,76,64]{1,2,0:T(8,128)(2,1)S(1)} async-done(((bf16[64,76,64]{1,2,0:T(8,128)(2,1)}), bf16[64,76,64]{1,2,0:T(8,128)(2,1)S(1)}, u32[]{:S(2)}, u32[]{:S(2)}) %all-to-all-start) | async-done | bytes 622624 | tf_op jit(solution)/shard_map/all_to_all | solution.py:114
  104.1 1.6 fusion.42
  105.8 2.5 %copy.75 = bf16[64,26,64]{2,1,0:T(8,128)(2,1)} copy(bf16[64,26,64]{1,2,0:T(8,128)(2,1)} %get-tuple-element.9) | data formatting | bytes 425984 | tf_op jit(solution)/shard_map/slice | solution.py:118
  108.3 2.0 %reshape.226 = bf16[1664,64]{1,0:T(8,128)(2,1)} reshape(bf16[64,26,64]{2,1,0:T(8,128)(2,1)} %copy.75) | data formatting | bytes 425984 | tf_op jit(solution)/shard_map/reshape | solution.py:118
  111.3 1.9 %fusion.44 = (f32[1536]{0:T(1024)S(1)}, f32[1536,1664]{1,0:T(8,128)S(1)}) fusion(bf16[1536,64]{1,0:T(8,128)(2,1)S(1)} %bitcast.120, bf16[1664,64]{1,0:T(8,128)(2,1)S(1)} %reshape.225, pred[1664]{0:T(1024)(128)(4,1)S(1)} %fusion.40), kind=kOutput, calls=%fused_computation.98 | convolution fusion | flops 334821888 | bytes 10641024 | tf_op jit(solution)/shard_map/dot_general | solution.py:44
  113.3 1.8 fusion
  115.1 2.4 %fusion.10 = bf16[1536,64]{0,1:T(8,128)(2,1)S(1)} fusion(bf16[1664,64]{1,0:T(8,128)(2,1)S(1)} %copy-done.3, f32[1536,1664]{1,0:T(8,128)S(1)} %get-tuple-element.25, f32[1536]{0:T(1024)S(1)} %get-tuple-element.24, pred[1664]{0:T(1024)(128)(4,1)S(1)} %fusion.40, f32[1536]{0:T(1024)S(1)} %fusion), kind=kOutput, calls=%fused_computation.9 | convolution fusion | flops 335020032 | bytes 10647168 | tf_op jit(solution)/shard_map/dot_general | solution.py:49
  118.0 20.7 %all_to_all.10 = bf16[64,2,768]{2,1,0:T(2,128)(2,1)S(1)} all-to-all(bf16[64,2,768]{2,1,0:T(2,128)(2,1)S(1)} %reshape.242), channel_id=1, replica_groups=mesh['rq'=8,'rm'=8,'col'=4] {'rq','rm'}, dimensions={0} | all-to-all | bytes 393216 | tf_op jit(solution)/shard_map/all_to_all | solution.py:129
  139.0 0.9 reshape.229
  139.9 2.8 %reshape.236 = bf16[2432,512]{1,0:T(8,128)(2,1)S(1)} reshape(bf16[64,38,512]{2,1,0:T(8,128)(2,1)} %all-gather.5.cloned.1.call-done) | data formatting | bytes 4980736
  142.7 3.2 %fusion.47 = f32[192,2432]{1,0:T(8,128)} fusion(bf16[192,512]{1,0:T(8,128)(2,1)} %reshape.229, bf16[2432,512]{1,0:T(8,128)(2,1)S(1)} %reshape.236), kind=kOutput, calls=%fused_computation.99 | convolution fusion | flops 478150656 | bytes 4554752 | tf_op jit(solution)/shard_map/dot_general | solution.py:134
  145.9 0.8 copy.58
  147.5 1.0 dynamic-slice_bitcast_fusion.1
  148.4 23.9 %reduce-scatter.2.cloned.1.call-done = f32[48,2432]{1,0:T(8,128)} async-done(((f32[192,2432]{1,0:T(8,128)}), f32[48,2432]{1,0:T(8,128)}) %reduce-scatter.2.cloned.1.call-update) | async-done | bytes 466960 | tf_op jit(solution)/shard_map/reduce_scatter | solution.py:142
  172.4 1.2 fusion.28
  173.5 1.2 multiply_reduce_fusion.1
  174.8 1.2 add_convert_fusion
  176.3 1.0 add_bitcast_fusion.1
  177.3 5.8 %all_gather.23 = f32[2,8,24,64]{3,2,1,0:T(8,128)S(1)} all-gather(f32[2,2,24,64]{3,2,1,0:T(8,128)S(1)} %pad_maximum_fusion.2), channel_id=1, replica_groups=mesh['rq'=8,'rm'=8,'col'=4] {'col'}, dimensions={1}, use_global_device_ids=true | all-gather | bytes 122880 | tf_op jit(solution)/shard_map/all_gather | solution.py:163
  (88 shorter events, 15.1 us)
Async XLA Ops:
  7.2 132.7 %all-gather.5.cloned.1.call-start = ((), (), s32[]{:S(2)}) async-start(), calls=%async_computation.4 | async-start | bytes 2662400 | tf_op jit(solution)/shard_map/all_gather | solution.py:74
  18.8 0.8 copy-start.1
  29.9 0.9 copy-start.4
  46.4 2.0 %copy-start.5 = (f32[1,8,2,512]{3,1,0,2:T(8,128)S(1)}, f32[1,8,2,512]{3,1,0,2:T(8,128)}, u32[]{:S(2)}) copy-start(f32[1,8,2,512]{3,1,0,2:T(8,128)} %slice.93) | copy-start | bytes 98308
  46.5 2.0 %copy-start.7 = (f32[3,64]{1,0:T(4,128)S(1)}, f32[3,64]{1,0:T(4,128)}, u32[]{:S(2)}) copy-start(f32[3,64]{1,0:T(4,128)} %param.21) | copy-start | bytes 2308
  50.8 3.2 %copy-start = (bf16[8,24,8,64]{3,2,1,0:T(8,128)(2,1)S(1)}, bf16[8,24,8,64]{3,2,1,0:T(8,128)(2,1)}, u32[]{:S(2)}) copy-start(bf16[8,24,8,64]{3,2,1,0:T(8,128)(2,1)} %convert_element_type.90) | copy-start | bytes 589828
  50.9 3.1 %copy-start.6 = (bf16[8,2,8,64]{3,2,0,1:T(8,128)(2,1)S(1)}, bf16[8,2,8,64]{3,2,0,1:T(8,128)(2,1)}, u32[]{:S(2)}) copy-start(bf16[8,2,8,64]{3,2,0,1:T(8,128)(2,1)} %convert_element_type.91) | copy-start | bytes 49156
  54.4 15.1 %copy-start.9 = (s32[8]{0:T(128)S(1)}, s32[8]{0:T(128)}, u32[]{:S(2)}) copy-start(s32[8]{0:T(128)} %param.22) | copy-start | bytes 100
  56.7 47.5 %all-to-all-start = ((bf16[64,76,64]{1,2,0:T(8,128)(2,1)}), bf16[64,76,64]{1,2,0:T(8,128)(2,1)S(1)}, u32[]{:S(2)}, u32[]{:S(2)}) async-start(bf16[64,76,64]{1,2,0:T(8,128)(2,1)} %copy.72), calls=%async_computation | async-start | bytes 2097152 | tf_op jit(solution)/shard_map/all_to_all | solution.py:114
  69.2 103.1 %reduce-scatter.2.cloned.1.call-start = ((), (), s32[]{:S(2)}) async-start(), calls=%async_computation.3 | async-start | bytes 2334720 | tf_op jit(solution)/shard_map/reduce_scatter | solution.py:142
  113.3 1.8 copy-start.3
  145.8 1.5 copy-start.8
  146.6 29.6 %copy-start.2 = (bf16[320,608]{1,0:T(8,128)(2,1)S(1)}, bf16[320,608]{1,0:T(8,128)(2,1)}, u32[]{:S(2)}) copy-start(bf16[320,608]{1,0:T(8,128)(2,1)} %copy-done.1) | copy-start | bytes 1167364
Sparse Core Ops, SparseCore 0:
  11.3 100.3 all-gather.4
  146.0 26.3 reduce-scatter.1

commit v6 on v5

--- a/solution.py
+++ b/solution.py
@@ -111,8 +111,10 @@
     bundle = jnp.concatenate(
         [by_head(queries, patches), by_head(key_rows, block_len), by_head(value_rows, block_len)], 1
     )
+    sources, bundle_rows = bundle.shape[0], bundle.shape[1]
+    bundle = bundle.reshape(sources, bundle_rows // 2, 2 * HD)
     bundle = lax.all_to_all(bundle, ROW, 0, 0, tiled=True)
-    sources = bundle.shape[0]
+    bundle = bundle.reshape(sources, bundle_rows, HD)
     head_queries = bundle[:, :patches].reshape(sources * patches, HD)
     keys = bundle[:, patches : patches + block_len].reshape(sources * block_len, HD)
     values = bundle[:, patches + block_len :].reshape(sources * block_len, HD)

time: 192 us -> 176 us (0.917)
  waiting for transfers between devices: 58 us -> 47.5 us
  local copies, waits for them, and re-layouts: 28.6 us -> 24.7 us
    all_to_all x1, waiting for transfers between devices: 33.4 us -> 22.9 us  [per_device(): bundle = lax.all_to_all(bundle, ROW, 0, 0, tiled=True)]
    slice x1 -> x0, local copies, waits for them, and re-layouts: 2.52 us -> none  [per_device(): values = bundle[:, patches + block_len:].reshape(sources * block_len, HD)]
    reshape x0 -> x2, local copies, waits for them, and re-layouts: none -> 2.28 us  [the longest x1 1.63 us: per_device(): bundle = bundle.reshape(sources, bundle_rows // 2, 2 * HD)]
    unnamed x23 -> x21, local copies, waits for them, and re-layouts: 3.96 us -> 3.95 us
where the time goes in v6:
time: 176 us; the launch traced here: 175 us
  waiting for transfers between devices  47.5 us (27%)
  blocking collectives  44.4 us (25%)
  local copies, waits for them, and re-layouts  24.7 us (14%)
  matrix products  16.4 us (9%)
  other arithmetic  14.5 us (8%)
  between operations  14.5 us (8%)
  starting transfers between devices  12.8 us (7%)
    reduce_scatter x1, waiting for transfers between devices, per_device(): lax.psum_scatter(partial_value, 'col', scatter_dimension=0, tiled=True)  23.9 us
    all_to_all x1, waiting for transfers between devices, per_device(): bundle = lax.all_to_all(bundle, ROW, 0, 0, tiled=True)  22.9 us
    all_to_all x1, blocking collectives, per_device(): attended = lax.all_to_all(attended, ROW, 0, 0, tiled=True)  19.3 us
    all_to_all x1, starting transfers between devices, per_device(): bundle = lax.all_to_all(bundle, ROW, 0, 0, tiled=True)  12.5 us
    all_gather x1, blocking collectives, gather_features(): stacked = lax.all_gather(local, 'col', axis=0, tiled=False)  9.99 us
    all_gather x1, blocking collectives, per_device(): packed = lax.all_gather(packed, 'col', axis=0, tiled=False)  9.27 us
    all_gather x1, blocking collectives, per_device(): lax.all_gather(jnp.stack([advanced, denoised]), 'col', axis=1, tiled=True)  5.82 us
    dot_general x1, matrix products, per_device(): jnp.einsum('td,cde->cte', flat_rows, qkv_weight, preferred_element_type=j...  4.8 us
  transfers between devices with their start and end apart: 3, of which 2 were waited for; matrix products, arithmetic and copies ran while one was open for 25% of the time, Pallas kernels for 0%

profile of v6, /device:TPU:1, one launch (start us, length us, event | category | flops | bytes accessed | tf_op | source)
XLA Modules:
  0.0 174.9 jit_solution(7360343964602564225)
XLA Ops:
  8.7 0.9 pad_maximum_fusion.1
  9.6 9.3 %all-gather.1 = bf16[320,608]{1,0:T(8,128)(2,1)S(1)} all-gather(bf16[80,608]{1,0:T(8,128)(2,1)S(1)} %pad_maximum_fusion.1), channel_id=3, replica_groups=mesh['rq'=8,'rm'=8,'col'=4] {'col'}, dimensions={0}, use_global_device_ids=true | all-gather | bytes 486400 | tf_op jit(solution)/shard_map/all_gather | solution.py:79
  19.9 10.0 %all-gather = bf16[32,24,608]{2,1,0:T(8,128)(2,1)S(1)} all-gather(bf16[8,24,608]{2,1,0:T(8,128)(2,1)} %param.12), channel_id=2, replica_groups=mesh['rq'=8,'rm'=8,'col'=4] {'col'}, dimensions={0}, use_global_device_ids=true | all-gather | bytes 1167360 | tf_op jit(solution)/shard_map/all_gather | solution.py:37
  31.6 3.2 %fusion.14 = f32[2,8,2,512]{3,1,0,2:T(8,128)S(1)} fusion(bf16[2,2432,512]{2,1,0:T(8,128)(2,1)} %param.18, bf16[8,2,2432,1]{2,1,0,3:T(2,128)(2,1)S(1)} %fusion.27), kind=kOutput, calls=%fused_computation.16 | convolution fusion | flops 79691776 | bytes 5124096 | tf_op jit(solution)/shard_map/rtd,cde->crte/dot_general | solution.py:99
  35.4 2.5 %copy.56 = f32[8,24,4,608]{3,2,1,0:T(4,128)} copy(f32[8,24,4,608]{3,1,0,2:T(8,128)S(1)} %bitcast_convert_fusion) | data formatting | bytes 3735552 | tf_op jit(solution)/shard_map/convert_element_type | solution.py:88
  37.9 2.2 %reshape.239 = f32[192,2432]{1,0:T(8,128)S(1)} reshape(f32[8,24,4,608]{3,2,1,0:T(4,128)} %copy.56) | data formatting | bytes 3735552 | tf_op jit(solution)/shard_map/convert_element_type | solution.py:88
  40.1 0.9 add_bitcast_fusion
  41.6 4.8 %convolution_bitcast_fusion = f32[3,192,512]{2,1,0:T(8,128)S(1)} fusion(bf16[3,2432,512]{2,1,0:T(8,128)(2,1)} %param.17, bf16[192,2432]{1,0:T(8,128)(2,1)S(1)} %fusion.13), kind=kOutput, calls=%fused_computation.14 | convolution fusion | flops 1434451968 | bytes 9584640 | tf_op jit(solution)/shard_map/td,cde->cte/dot_general | solution.py:92
  47.4 1.0 convert_element_type.90
  51.0 0.9 fusion.21
  52.7 1.2 fusion.19
  54.4 0.8 copy.69
  55.2 1.6 reshape.230
  56.9 12.5 %all-to-all-start = ((bf16[64,38,128]{2,1,0:T(8,128)(2,1)}), bf16[64,38,128]{2,1,0:T(8,128)(2,1)S(1)}, u32[]{:S(2)}, u32[]{:S(2)}) async-start(bf16[64,38,128]{2,1,0:T(8,128)(2,1)} %reshape.230), calls=%async_computation | async-start | bytes 1310720 | tf_op jit(solution)/shard_map/all_to_all | solution.py:116
  70.9 22.9 %all-to-all-done = bf16[64,38,128]{2,1,0:T(8,128)(2,1)S(1)} async-done(((bf16[64,38,128]{2,1,0:T(8,128)(2,1)}), bf16[64,38,128]{2,1,0:T(8,128)(2,1)S(1)}, u32[]{:S(2)}, u32[]{:S(2)}) %all-to-all-start) | async-done | bytes 622624 | tf_op jit(solution)/shard_map/all_to_all | solution.py:116
  94.5 1.0 fusion.42
  95.6 1.2 reshape.234
  97.0 1.9 %fusion.44 = (f32[1536]{0:T(1024)S(1)}, f32[1536,1664]{1,0:T(8,128)S(1)}) fusion(bf16[1536,64]{1,0:T(8,128)(2,1)S(1)} %bitcast.118, bf16[1664,64]{1,0:T(8,128)(2,1)S(1)} %reshape.233, pred[1664]{0:T(1024)(128)(4,1)S(1)} %fusion.40), kind=kOutput, calls=%fused_computation.98 | convolution fusion | flops 334821888 | bytes 10641024 | tf_op jit(solution)/shard_map/dot_general | solution.py:44
  98.9 1.8 %fusion = f32[1536]{0:T(1024)S(1)} fusion(f32[1536,1664]{1,0:T(8,128)S(1)} %get-tuple-element.25, f32[1536]{0:T(1024)S(1)} %get-tuple-element.24, pred[1664]{0:T(1024)(128)(4,1)S(1)} %fusion.40), kind=kLoop, calls=%fused_computation.2 | loop fusion | flops 7666176 | bytes 10237568 | tf_op jit(solution)/shard_map/reduce_sum | solution.py:48
  100.7 2.4 %fusion.10 = bf16[1536,64]{0,1:T(8,128)(2,1)S(1)} fusion(bf16[1664,64]{1,0:T(8,128)(2,1)S(1)} %reshape.234, f32[1536,1664]{1,0:T(8,128)S(1)} %get-tuple-element.25, f32[1536]{0:T(1024)S(1)} %get-tuple-element.24, pred[1664]{0:T(1024)(128)(4,1)S(1)} %fusion.40, f32[1536]{0:T(1024)S(1)} %fusion), kind=kOutput, calls=%fused_computation.9 | convolution fusion | flops 335020032 | bytes 10647168 | tf_op jit(solution)/shard_map/dot_general | solution.py:49
  103.6 19.3 %all_to_all.10 = bf16[64,2,768]{2,1,0:T(2,128)(2,1)S(1)} all-to-all(bf16[64,2,768]{2,1,0:T(2,128)(2,1)S(1)} %reshape.250), channel_id=1, replica_groups=mesh['rq'=8,'rm'=8,'col'=4] {'rq','rm'}, dimensions={0} | all-to-all | bytes 393216 | tf_op jit(solution)/shard_map/all_to_all | solution.py:131
  123.2 0.9 reshape.237
  124.2 2.8 %reshape.244 = bf16[2432,512]{1,0:T(8,128)(2,1)S(1)} reshape(bf16[64,38,512]{2,1,0:T(8,128)(2,1)} %all-gather.5.cloned.1.call-done) | data formatting | bytes 4980736
  127.0 3.2 %fusion.47 = f32[192,2432]{1,0:T(8,128)} fusion(bf16[192,512]{1,0:T(8,128)(2,1)} %reshape.237, bf16[2432,512]{1,0:T(8,128)(2,1)S(1)} %reshape.244), kind=kOutput, calls=%fused_computation.99 | convolution fusion | flops 478150656 | bytes 4554752 | tf_op jit(solution)/shard_map/dot_general | solution.py:136
  130.2 0.8 copy.55
  131.7 1.0 dynamic-slice_bitcast_fusion.1
  132.7 23.9 %reduce-scatter.2.cloned.1.call-done = f32[48,2432]{1,0:T(8,128)} async-done(((f32[192,2432]{1,0:T(8,128)}), f32[48,2432]{1,0:T(8,128)}) %reduce-scatter.2.cloned.1.call-update) | async-done | bytes 466960 | tf_op jit(solution)/shard_map/reduce_scatter | solution.py:144
  156.6 1.2 fusion.28
  157.8 1.2 multiply_reduce_fusion.1
  159.1 1.2 add_convert_fusion
  160.6 1.0 add_bitcast_fusion.1
  161.5 5.8 %all_gather.23 = f32[2,8,24,64]{3,2,1,0:T(8,128)S(1)} all-gather(f32[2,2,24,64]{3,2,1,0:T(8,128)S(1)} %pad_maximum_fusion.2), channel_id=1, replica_groups=mesh['rq'=8,'rm'=8,'col'=4] {'col'}, dimensions={1}, use_global_device_ids=true | all-gather | bytes 122880 | tf_op jit(solution)/shard_map/all_gather | solution.py:165
  (86 shorter events, 14.9 us)
Async XLA Ops:
  7.2 117.0 %all-gather.5.cloned.1.call-start = ((), (), s32[]{:S(2)}) async-start(), calls=%async_computation.4 | async-start | bytes 2662400 | tf_op jit(solution)/shard_map/all_gather | solution.py:74
  18.8 0.8 copy-start.1
  29.9 0.9 copy-start.3
  46.4 2.0 %copy-start.4 = (f32[1,8,2,512]{3,1,0,2:T(8,128)S(1)}, f32[1,8,2,512]{3,1,0,2:T(8,128)}, u32[]{:S(2)}) copy-start(f32[1,8,2,512]{3,1,0,2:T(8,128)} %slice.93) | copy-start | bytes 98308
  46.5 2.0 %copy-start.6 = (f32[3,64]{1,0:T(4,128)S(1)}, f32[3,64]{1,0:T(4,128)}, u32[]{:S(2)}) copy-start(f32[3,64]{1,0:T(4,128)} %param.21) | copy-start | bytes 2308
  50.8 3.2 %copy-start = (bf16[8,24,8,64]{3,2,1,0:T(8,128)(2,1)S(1)}, bf16[8,24,8,64]{3,2,1,0:T(8,128)(2,1)}, u32[]{:S(2)}) copy-start(bf16[8,24,8,64]{3,2,1,0:T(8,128)(2,1)} %convert_element_type.90) | copy-start | bytes 589828
  50.9 3.1 %copy-start.5 = (bf16[8,2,8,64]{3,2,0,1:T(8,128)(2,1)S(1)}, bf16[8,2,8,64]{3,2,0,1:T(8,128)(2,1)}, u32[]{:S(2)}) copy-start(bf16[8,2,8,64]{3,2,0,1:T(8,128)(2,1)} %convert_element_type.91) | copy-start | bytes 49156
  54.4 15.3 %copy-start.8 = (s32[8]{0:T(128)S(1)}, s32[8]{0:T(128)}, u32[]{:S(2)}) copy-start(s32[8]{0:T(128)} %param.22) | copy-start | bytes 100
  56.9 37.0 %all-to-all-start = ((bf16[64,38,128]{2,1,0:T(8,128)(2,1)}), bf16[64,38,128]{2,1,0:T(8,128)(2,1)S(1)}, u32[]{:S(2)}, u32[]{:S(2)}) async-start(bf16[64,38,128]{2,1,0:T(8,128)(2,1)} %reshape.230), calls=%async_computation | async-start | bytes 1310720 | tf_op jit(solution)/shard_map/all_to_all | solution.py:116
  69.4 87.2 %reduce-scatter.2.cloned.1.call-start = ((), (), s32[]{:S(2)}) async-start(), calls=%async_computation.3 | async-start | bytes 2334720 | tf_op jit(solution)/shard_map/reduce_scatter | solution.py:144
  130.1 1.5 copy-start.7
  130.9 29.6 %copy-start.2 = (bf16[320,608]{1,0:T(8,128)(2,1)S(1)}, bf16[320,608]{1,0:T(8,128)(2,1)}, u32[]{:S(2)}) copy-start(bf16[320,608]{1,0:T(8,128)(2,1)} %copy-done.1) | copy-start | bytes 1167364
Sparse Core Ops, SparseCore 0:
  11.3 91.9 all-gather.4
  130.3 26.3 reduce-scatter.1

commit v7 on v6

--- a/solution.py
+++ b/solution.py
@@ -38,6 +38,21 @@
     slabs = stacked.shape[0]
     moved = jnp.moveaxis(stacked, 0, -2)
     return moved.reshape(local.shape[:-1] + (slabs * local.shape[-1],))
+
+
+def halving_scatter(partial, cols, col_index):
+    rows = partial.shape[0] // cols
+    chunks = partial.reshape((2, 2, rows) + partial.shape[1:])
+    low = col_index % 2
+    high = col_index // 2
+    keep = lax.dynamic_index_in_dim(chunks, low, 1, keepdims=False)
+    send = lax.dynamic_index_in_dim(chunks, 1 - low, 1, keepdims=False)
+    pairs = [(i, i ^ 1) for i in range(cols)]
+    halves = keep + lax.ppermute(send, "col", pairs)
+    keep = lax.dynamic_index_in_dim(halves, high, 0, keepdims=False)
+    send = lax.dynamic_index_in_dim(halves, 1 - high, 0, keepdims=False)
+    pairs = [(i, i ^ 2) for i in range(cols)]
+    return keep + lax.ppermute(send, "col", pairs)
 
 
 def attend_one(queries, keys, values, allowed):
@@ -141,7 +156,7 @@
     )
     cols = lax.axis_size("col")
     col_index = lax.axis_index("col")
-    shared_sum = lax.psum_scatter(partial_value, "col", scatter_dimension=0, tiled=True)
+    shared_sum = halving_scatter(partial_value, cols, col_index)
     own_requests = requests // cols
     first = col_index * own_requests
     own_mods = lax.dynamic_slice_in_dim(img_mod, first, own_requests, 0)

time: 176 us -> 172 us (0.977)
  blocking collectives: 44.4 us -> 25.9 us
  starting transfers between devices: 12.8 us -> 26.8 us
  other arithmetic: 14.5 us -> 17 us
    reduce_scatter x1 -> x0, waiting for transfers between devices: 23.9 us -> none  [per_device(): lax.psum_scatter(partial_value, 'col', scatter_dimension=0, tiled=True)]
    all_to_all x1 -> x0, blocking collectives: 19.3 us -> none  [per_device(): attended = lax.all_to_all(attended, ROW, 0, 0, tiled=True)]
    ppermute x0 -> x2, waiting for transfers between devices: none -> 12.4 us  [the longest x1 10.3 us: halving_scatter(): return keep + lax.ppermute(send, 'col', pairs)]
    all_to_all x0 -> x1, waiting for transfers between devices: none -> 11.9 us  [per_device(): attended = lax.all_to_all(attended, ROW, 0, 0, tiled=True)]
    all_to_all x0 -> x1, starting transfers between devices: none -> 8.45 us  [per_device(): attended = lax.all_to_all(attended, ROW, 0, 0, tiled=True)]
    ppermute x0 -> x2, starting transfers between devices: none -> 5.8 us  [the longest x1 5.8 us: halving_scatter(): halves = keep + lax.ppermute(send, 'col', pairs)]
    convert_element_type x2 -> x1, local copies, waits for them, and re-layouts: 4.77 us -> 2.29 us  [per_device(): img_full.astype(jnp.float32)]
    unnamed x21 -> x23, local copies, waits for them, and re-layouts: 3.95 us -> 5.28 us
  transfers between devices with their start and end apart: 3 -> 5, of which waited for: 2 -> 4; matrix products, arithmetic and copies ran while one was open for 25% -> 26% of each run, Pallas kernels for 0% -> 0%
where the time goes in v7:
time: 172 us; the launch traced here: 171 us
  waiting for transfers between devices  48.4 us (28%)
  starting transfers between devices  26.8 us (16%)
  blocking collectives  25.9 us (15%)
  local copies, waits for them, and re-layouts  23.7 us (14%)
  other arithmetic  17 us (10%)
  matrix products  15.2 us (9%)
  between operations  14.6 us (8%)
    all_to_all x1, waiting for transfers between devices, per_device(): bundle = lax.all_to_all(bundle, ROW, 0, 0, tiled=True)  23.4 us
    all_to_all x1, starting transfers between devices, per_device(): bundle = lax.all_to_all(bundle, ROW, 0, 0, tiled=True)  12.5 us
    all_to_all x1, waiting for transfers between devices, per_device(): attended = lax.all_to_all(attended, ROW, 0, 0, tiled=True)  11.9 us
    ppermute x1, waiting for transfers between devices, halving_scatter(): return keep + lax.ppermute(send, 'col', pairs)  10.3 us
    all_gather x1, blocking collectives, gather_features(): stacked = lax.all_gather(local, 'col', axis=0, tiled=False)  9.99 us
    all_gather x1, blocking collectives, per_device(): packed = lax.all_gather(packed, 'col', axis=0, tiled=False)  9.27 us
    all_to_all x1, starting transfers between devices, per_device(): attended = lax.all_to_all(attended, ROW, 0, 0, tiled=True)  8.45 us
    all_gather x1, blocking collectives, per_device(): lax.all_gather(jnp.stack([advanced, denoised]), 'col', axis=1, tiled=True)  6.63 us
  transfers between devices with their start and end apart: 5, of which 4 were waited for; matrix products, arithmetic and copies ran while one was open for 26% of the time, Pallas kernels for 0%

profile of v7, /device:TPU:1, one launch (start us, length us, event | category | flops | bytes accessed | tf_op | source)
XLA Modules:
  0.0 171.5 jit_solution(1650609526607530369)
XLA Ops:
  9.6 9.3 %all-gather.1 = bf16[320,608]{1,0:T(8,128)(2,1)S(1)} all-gather(bf16[80,608]{1,0:T(8,128)(2,1)S(1)} %pad_maximum_fusion.1), channel_id=3, replica_groups=mesh['rq'=8,'rm'=8,'col'=4] {'col'}, dimensions={0}, use_global_device_ids=true | all-gather | bytes 486400 | tf_op jit(solution)/shard_map/all_gather | solution.py:94
  19.3 10.0 %all-gather = bf16[32,24,608]{2,1,0:T(8,128)(2,1)S(1)} all-gather(bf16[8,24,608]{2,1,0:T(8,128)(2,1)} %param.12), channel_id=2, replica_groups=mesh['rq'=8,'rm'=8,'col'=4] {'col'}, dimensions={0}, use_global_device_ids=true | all-gather | bytes 1167360 | tf_op jit(solution)/shard_map/all_gather | solution.py:37
  29.3 1.0 copy_bitcast_fusion
  30.3 1.1 convert_reduce_fusion
  31.4 1.4 multiply_reduce_fusion
  33.6 3.2 %fusion.16 = f32[2,8,2,512]{3,1,0,2:T(8,128)S(1)} fusion(bf16[2,2432,512]{2,1,0:T(8,128)(2,1)} %param.18, bf16[8,2,2432,1]{2,1,0,3:T(2,128)(2,1)S(1)} %fusion.29), kind=kOutput, calls=%fused_computation.18 | convolution fusion | flops 79691776 | bytes 5124096 | tf_op jit(solution)/shard_map/rtd,cde->crte/dot_general | solution.py:114
  37.4 2.3 %reshape.239 = f32[192,2432]{1,0:T(8,128)} reshape(f32[8,24,4,608]{3,2,1,0:T(4,128)S(1)} %get-tuple-element.11) | data formatting | bytes 3735552 | tf_op jit(solution)/shard_map/convert_element_type | solution.py:103
  40.7 2.0 %fusion.15 = bf16[192,2432]{1,0:T(8,128)(2,1)S(1)} fusion(f32[192,2432]{1,0:T(8,128)} %reshape.239, f32[8,2432]{1,0:T(8,128)S(1)} %get-tuple-element.16, f32[8,2432]{1,0:T(8,128)S(1)} %get-tuple-element.15, f32[192]{0:T(256)S(1)} %rsqrt.61, f32[192]{0:T(256)S(1)} %div.72), kind=kLoop, calls=%fused_computation.14 | loop fusion | flops 2334720 | bytes 2958848 | tf_op jit(solution)/shard_map/convert_element_type | solution.py:103
  42.7 4.8 %convolution_bitcast_fusion = f32[3,192,512]{2,1,0:T(8,128)S(1)} fusion(bf16[3,2432,512]{2,1,0:T(8,128)(2,1)} %param.17, bf16[192,2432]{1,0:T(8,128)(2,1)S(1)} %fusion.15), kind=kOutput, calls=%fused_computation.16 | convolution fusion | flops 1434451968 | bytes 9584640 | tf_op jit(solution)/shard_map/td,cde->cte/dot_general | solution.py:107
  48.5 1.0 convert_element_type.90
  53.8 1.2 fusion.21
  56.3 1.6 reshape.231
  57.9 12.5 %all-to-all-start = ((bf16[64,38,128]{2,1,0:T(8,128)(2,1)}), bf16[64,38,128]{2,1,0:T(8,128)(2,1)S(1)}, u32[]{:S(2)}, u32[]{:S(2)}) async-start(bf16[64,38,128]{2,1,0:T(8,128)(2,1)} %reshape.231), calls=%async_computation | async-start | bytes 1310720 | tf_op jit(solution)/shard_map/all_to_all | solution.py:131
  71.8 23.4 %all-to-all-done = bf16[64,38,128]{2,1,0:T(8,128)(2,1)S(1)} async-done(((bf16[64,38,128]{2,1,0:T(8,128)(2,1)}), bf16[64,38,128]{2,1,0:T(8,128)(2,1)S(1)}, u32[]{:S(2)}, u32[]{:S(2)}) %all-to-all-start) | async-done | bytes 622624 | tf_op jit(solution)/shard_map/all_to_all | solution.py:131
  95.9 1.0 fusion.45
  96.9 1.2 reshape.235
  98.3 1.9 %fusion.47 = (f32[1536]{0:T(1024)S(1)}, f32[1536,1664]{1,0:T(8,128)S(1)}) fusion(bf16[1536,64]{1,0:T(8,128)(2,1)S(1)} %bitcast.133, bf16[1664,64]{1,0:T(8,128)(2,1)S(1)} %reshape.234, pred[1664]{0:T(1024)(128)(4,1)S(1)} %fusion.42), kind=kOutput, calls=%fused_computation.105 | convolution fusion | flops 334821888 | bytes 10641024 | tf_op jit(solution)/shard_map/dot_general | solution.py:59
  100.2 1.8 %fusion = f32[1536]{0:T(1024)S(1)} fusion(f32[1536,1664]{1,0:T(8,128)S(1)} %get-tuple-element.27, f32[1536]{0:T(1024)S(1)} %get-tuple-element.26, pred[1664]{0:T(1024)(128)(4,1)S(1)} %fusion.42), kind=kLoop, calls=%fused_computation.2 | loop fusion | flops 7666176 | bytes 10237568 | tf_op jit(solution)/shard_map/reduce_sum | solution.py:63
  102.1 2.4 %fusion.12 = bf16[1536,64]{0,1:T(8,128)(2,1)S(1)} fusion(bf16[1664,64]{1,0:T(8,128)(2,1)S(1)} %reshape.235, f32[1536,1664]{1,0:T(8,128)S(1)} %get-tuple-element.27, f32[1536]{0:T(1024)S(1)} %get-tuple-element.26, pred[1664]{0:T(1024)(128)(4,1)S(1)} %fusion.42, f32[1536]{0:T(1024)S(1)} %fusion), kind=kOutput, calls=%fused_computation.11 | convolution fusion | flops 335020032 | bytes 10647168 | tf_op jit(solution)/shard_map/dot_general | solution.py:64
  105.6 8.5 %all-to-all-start.1 = ((bf16[64,2,768]{2,1,0:T(2,128)(2,1)}), bf16[64,2,768]{2,1,0:T(2,128)(2,1)S(1)}, u32[]{:S(2)}, u32[]{:S(2)}) async-start(bf16[64,2,768]{2,1,0:T(2,128)(2,1)} %reshape.252), calls=%async_computation.1 | async-start | bytes 393216 | tf_op jit(solution)/shard_map/all_to_all | solution.py:146
  114.1 11.9 %all-to-all-done.1 = bf16[64,2,768]{2,1,0:T(2,128)(2,1)S(1)} async-done(((bf16[64,2,768]{2,1,0:T(2,128)(2,1)}), bf16[64,2,768]{2,1,0:T(2,128)(2,1)S(1)}, u32[]{:S(2)}, u32[]{:S(2)}) %all-to-all-start.1) | async-done | bytes 196640 | tf_op jit(solution)/shard_map/all_to_all | solution.py:146
  126.3 0.9 dot_general.26
  127.3 2.8 %reshape.248 = bf16[2432,512,1,1]{1,0,2,3:T(8,128)(2,1)S(1)} reshape(bf16[64,38,512]{2,1,0:T(8,128)(2,1)} %all-gather.5.cloned.1.call-done) | data formatting | bytes 4980736
  130.0 1.9 %fusion.7 = f32[2,2,48,2432]{3,2,1,0:T(8,128)S(1)} fusion(bf16[2,2,48,512]{3,2,1,0:T(8,128)(2,1)} %dot_general.26, bf16[2432,512,1,1]{1,0,2,3:T(8,128)(2,1)S(1)} %reshape.248), kind=kOutput, calls=%fused_computation.8 | convolution fusion | flops 478150656 | bytes 4554752 | tf_op jit(solution)/shard_map/dot_general | solution.py:151
  131.9 1.3 copy-done
  133.3 5.8 %collective-permute-start = (f32[2,48,2432]{2,1,0:T(8,128)S(1)}, f32[2,48,2432]{2,1,0:T(8,128)S(1)}, u32[]{:S(2)}, u32[]{:S(2)}) collective-permute-start(f32[2,48,2432]{2,1,0:T(8,128)S(1)} %dynamic-slice_bitcast_fusion), channel_id=1, source_target_pairs={{0,1},{1,0},{2,3},{3,2},{4,5},{5,4},{6,7},{7,6},{8,9},{9,8},{10,11... | collective-permute-start | bytes 2801672 | tf_op jit(solution)/shard_map/ppermute | solution.py:51
  139.1 2.1 %collective-permute-done = f32[2,48,2432]{2,1,0:T(8,128)S(1)} collective-permute-done((f32[2,48,2432]{2,1,0:T(8,128)S(1)}, f32[2,48,2432]{2,1,0:T(8,128)S(1)}, u32[]{:S(2)}, u32[]{:S(2)}) %collective-permute-start) | collective-permute-done | bytes 933920 | tf_op jit(solution)/shard_map/ppermute | solution.py:51
  141.2 1.3 bitcast_add_fusion.1
  144.1 1.0 dynamic-slice_bitcast_fusion.3
  145.1 10.3 %collective-permute-done.1 = f32[48,2432]{1,0:T(8,128)S(1)} collective-permute-done((f32[48,2432]{1,0:T(8,128)}, f32[48,2432]{1,0:T(8,128)S(1)}, u32[]{:S(2)}, u32[]{:S(2)}) %collective-permute-start.1) | collective-permute-done | bytes 466976 | tf_op jit(solution)/shard_map/ppermute | solution.py:55
  156.3 1.0 add_bitcast_fusion.1
  157.3 6.6 %all_gather.23 = f32[2,8,24,64]{3,2,1,0:T(8,128)S(1)} all-gather(f32[2,2,24,64]{3,2,1,0:T(8,128)S(1)} %pad_maximum_fusion.2), channel_id=1, replica_groups=mesh['rq'=8,'rm'=8,'col'=4] {'col'}, dimensions={1}, use_global_device_ids=true | all-gather | bytes 122880 | tf_op jit(solution)/shard_map/all_gather | solution.py:180
  (92 shorter events, 18.5 us)
Async XLA Ops:
  7.2 120.1 %all-gather.5.cloned.1.call-start = ((), (), s32[]{:S(2)}) async-start(), calls=%async_computation.2 | async-start | bytes 2662400 | tf_op jit(solution)/shard_map/all_gather | solution.py:89
  18.8 10.4 %copy-start.2 = (bf16[320,608]{1,0:T(8,128)(2,1)}, bf16[320,608]{1,0:T(8,128)(2,1)S(1)}, u32[]{:S(2)}) copy-start(bf16[320,608]{1,0:T(8,128)(2,1)S(1)} %all-gather.1) | copy-start | bytes 1167364
  29.3 3.6 %copy-start.4 = (f32[8,2,2432]{2,1,0:T(2,128)S(1)}, f32[8,2,2432]{2,1,0:T(2,128)}, u32[]{:S(2)}) copy-start(f32[8,2,2432]{2,1,0:T(2,128)} %param.16) | copy-start | bytes 466948
  47.5 2.0 %copy-start.5 = (f32[1,8,2,512]{3,1,0,2:T(8,128)S(1)}, f32[1,8,2,512]{3,1,0,2:T(8,128)}, u32[]{:S(2)}) copy-start(f32[1,8,2,512]{3,1,0,2:T(8,128)} %slice.93) | copy-start | bytes 98308
  47.5 2.0 %copy-start.7 = (f32[3,64]{1,0:T(4,128)S(1)}, f32[3,64]{1,0:T(4,128)}, u32[]{:S(2)}) copy-start(f32[3,64]{1,0:T(4,128)} %param.21) | copy-start | bytes 2308
  51.9 3.2 %copy-start.1 = (bf16[8,24,8,64]{3,2,1,0:T(8,128)(2,1)S(1)}, bf16[8,24,8,64]{3,2,1,0:T(8,128)(2,1)}, u32[]{:S(2)}) copy-start(bf16[8,24,8,64]{3,2,1,0:T(8,128)(2,1)} %convert_element_type.90) | copy-start | bytes 589828
  52.0 3.1 %copy-start.6 = (bf16[8,2,8,64]{3,2,0,1:T(8,128)(2,1)S(1)}, bf16[8,2,8,64]{3,2,0,1:T(8,128)(2,1)}, u32[]{:S(2)}) copy-start(bf16[8,2,8,64]{3,2,0,1:T(8,128)(2,1)} %convert_element_type.91) | copy-start | bytes 49156
  55.5 15.0 %copy-start.9 = (s32[8]{0:T(128)S(1)}, s32[8]{0:T(128)}, u32[]{:S(2)}) copy-start(s32[8]{0:T(128)} %param.22) | copy-start | bytes 100
  57.9 37.2 %all-to-all-start = ((bf16[64,38,128]{2,1,0:T(8,128)(2,1)}), bf16[64,38,128]{2,1,0:T(8,128)(2,1)S(1)}, u32[]{:S(2)}, u32[]{:S(2)}) async-start(bf16[64,38,128]{2,1,0:T(8,128)(2,1)} %reshape.231), calls=%async_computation | async-start | bytes 1310720 | tf_op jit(solution)/shard_map/all_to_all | solution.py:131
  105.6 20.4 %all-to-all-start.1 = ((bf16[64,2,768]{2,1,0:T(2,128)(2,1)}), bf16[64,2,768]{2,1,0:T(2,128)(2,1)S(1)}, u32[]{:S(2)}, u32[]{:S(2)}) async-start(bf16[64,2,768]{2,1,0:T(2,128)(2,1)} %reshape.252), calls=%async_computation.1 | async-start | bytes 393216 | tf_op jit(solution)/shard_map/all_to_all | solution.py:146
  131.9 1.3 copy-start
  133.3 7.9 %collective-permute-start = (f32[2,48,2432]{2,1,0:T(8,128)S(1)}, f32[2,48,2432]{2,1,0:T(8,128)S(1)}, u32[]{:S(2)}, u32[]{:S(2)}) collective-permute-start(f32[2,48,2432]{2,1,0:T(8,128)S(1)} %dynamic-slice_bitcast_fusion), channel_id=1, source_target_pairs={{0,1},{1,0},{2,3},{3,2},{4,5},{5,4},{6,7},{7,6},{8,9},{9,8},{10,11... | collective-permute-start | bytes 2801672 | tf_op jit(solution)/shard_map/ppermute | solution.py:51
  139.1 4.9 %copy-start.8 = (s32[8]{0:T(128)S(1)}, s32[8]{0:T(128)}, u32[]{:S(2)}) copy-start(s32[8]{0:T(128)} %param.23) | copy-start | bytes 100
  143.3 12.1 %collective-permute-start.1 = (f32[48,2432]{1,0:T(8,128)}, f32[48,2432]{1,0:T(8,128)S(1)}, u32[]{:S(2)}, u32[]{:S(2)}) collective-permute-start(f32[48,2432]{1,0:T(8,128)} %dynamic-slice_bitcast_fusion.1), channel_id=1, source_target_pairs={{0,2},{1,3},{2,0},{3,1},{4,6},{5,7},{6,4},{7,5},{8,10},{9,11},{10,... | collective-permute-start | bytes 1400840 | tf_op jit(solution)/shard_map/ppermute | solution.py:55
  144.0 12.3 %copy-start.3 = (bf16[320,608]{1,0:T(8,128)(2,1)S(1)}, bf16[320,608]{1,0:T(8,128)(2,1)}, u32[]{:S(2)}) copy-start(bf16[320,608]{1,0:T(8,128)(2,1)} %copy-done.2) | copy-start | bytes 1167364
Sparse Core Ops, SparseCore 0:
  11.3 93.6 all-gather.4

commit v8 on v7

--- a/solution.py
+++ b/solution.py
@@ -53,6 +53,28 @@
     send = lax.dynamic_index_in_dim(halves, 1 - high, 0, keepdims=False)
     pairs = [(i, i ^ 2) for i in range(cols)]
     return keep + lax.ppermute(send, "col", pairs)
+
+
+def doubling_gather(block):
+    rows = lax.axis_size(ROW)
+    index = lax.axis_index(ROW)
+    bits = rows.bit_length() - 1
+    order = [3, 2, 5, 1, 4, 0][:bits] if bits == 6 else list(range(bits))
+    buffer = block[None]
+    for bit in order:
+        pairs = [(i, i ^ (1 << bit)) for i in range(rows)]
+        received = lax.ppermute(buffer, ROW, pairs)
+        upper = (index >> bit) % 2 == 1
+        buffer = jnp.where(
+            upper,
+            jnp.stack([received, buffer]),
+            jnp.stack([buffer, received]),
+        )
+    done = list(reversed(order))
+    buffer = buffer.reshape((2,) * bits + block.shape)
+    perm = [done.index(bit) for bit in reversed(range(bits))]
+    buffer = jnp.transpose(buffer, perm + [bits, bits + 1])
+    return buffer.reshape((rows * block.shape[0],) + block.shape[1:])
 
 
 def attend_one(queries, keys, values, allowed):
@@ -86,7 +108,7 @@
     heads_local = cols_local // HD
     block_len = patches + text_rows
 
-    weight_t = lax.all_gather(jnp.transpose(out_weight), ROW, axis=0, tiled=True)
+    weight_t = doubling_gather(jnp.transpose(out_weight))
 
     img_full = gather_features(img_hidden)
     txt_rows = txt_hidden.reshape(requests * text_rows, -1)

time: 172 us -> 185 us (1.076)
  starting transfers between devices: 26.8 us -> 41.5 us
  between operations: 14.6 us -> 1.35 us
  local copies, waits for them, and re-layouts: 23.7 us -> 28.3 us
  waiting for transfers between devices: 48.4 us -> 52.6 us
  matrix products: 15.2 us -> 19.2 us
  blocking collectives: 25.9 us -> 23.6 us
    ppermute x0 -> x6, waiting for transfers between devices: none -> 28.9 us  [doubling_gather(): received = lax.ppermute(buffer, ROW, pairs)]
    all_to_all x1, waiting for transfers between devices: 23.4 us -> 0.01 us  [per_device(): bundle = lax.all_to_all(bundle, ROW, 0, 0, tiled=True)]
    ppermute x0 -> x6, starting transfers between devices: none -> 18 us  [doubling_gather(): received = lax.ppermute(buffer, ROW, pairs)]
    all_to_all x1, starting transfers between devices: 12.5 us -> 6.38 us  [per_device(): bundle = lax.all_to_all(bundle, ROW, 0, 0, tiled=True)]
    all_to_all x1, starting transfers between devices: 8.45 us -> 12.9 us  [per_device(): attended = lax.all_to_all(attended, ROW, 0, 0, tiled=True)]
    dot_general x1, matrix products: 2.4 us -> 5.62 us  [attend_one(): jnp.dot(exp_scores.astype(jnp.bfloat16), values, preferred_element_type=j...]
    ppermute x0 -> x2, local copies, waits for them, and re-layouts: none -> 2.7 us  [doubling_gather(): received = lax.ppermute(buffer, ROW, pairs)]
    select_n x0 -> x2, local copies, waits for them, and re-layouts: none -> 2.47 us  [doubling_gather(): jnp.where(upper, jnp.stack([received, buffer]), jnp.stack([buffer, receiv...]
  transfers between devices with their start and end apart: 5 -> 10, of which waited for: 4 -> 6; matrix products, arithmetic and copies ran while one was open for 26% -> 26% of each run, Pallas kernels for 0% -> 0%
where the time goes in v8:
time: 185 us; the launch traced here: 184 us
  waiting for transfers between devices  52.6 us (28%)
  starting transfers between devices  41.5 us (22%)
  local copies, waits for them, and re-layouts  28.3 us (15%)
  blocking collectives  23.6 us (13%)
  matrix products  19.2 us (10%)
  other arithmetic  17.2 us (9%)
    ppermute x6, waiting for transfers between devices, doubling_gather(): received = lax.ppermute(buffer, ROW, pairs)  28.9 us
    ppermute x6, starting transfers between devices, doubling_gather(): received = lax.ppermute(buffer, ROW, pairs)  18 us
    all_to_all x1, starting transfers between devices, per_device(): attended = lax.all_to_all(attended, ROW, 0, 0, tiled=True)  12.9 us
    all_to_all x1, waiting for transfers between devices, per_device(): attended = lax.all_to_all(attended, ROW, 0, 0, tiled=True)  11.7 us
    all_gather x1, blocking collectives, gather_features(): stacked = lax.all_gather(local, 'col', axis=0, tiled=False)  9.99 us
    ppermute x1, waiting for transfers between devices, halving_scatter(): return keep + lax.ppermute(send, 'col', pairs)  9.54 us
    all_gather x1, blocking collectives, per_device(): packed = lax.all_gather(packed, 'col', axis=0, tiled=False)  6.99 us
    all_gather x1, blocking collectives, per_device(): lax.all_gather(jnp.stack([advanced, denoised]), 'col', axis=1, tiled=True)  6.63 us
  transfers between devices with their start and end apart: 10, of which 6 were waited for; matrix products, arithmetic and copies ran while one was open for 26% of the time, Pallas kernels for 0%

profile of v8, /device:TPU:1, one launch (start us, length us, event | category | flops | bytes accessed | tf_op | source)
XLA Modules:
  0.0 183.6 jit_solution(16910051753117760047)
XLA Ops:
  0.6 7.8 %collective-permute-start = (bf16[1,38,512]{2,1,0:T(8,128)(2,1)}, bf16[1,38,512]{2,1,0:T(8,128)(2,1)S(1)}, u32[]{:S(2)}, u32[]{:S(2)}) collective-permute-start(bf16[1,38,512]{2,1,0:T(8,128)(2,1)} %bitcast.194), channel_id=1, source_target_pairs={{0,32},{4,36},{8,40},{12,44},{16,48},{20,52},{24,56},{28,60},{32,0... | collective-permute-start | bytes 116744 | tf_op jit(solution)/shard_map/ppermute | solution.py:66
  10.1 7.0 %all-gather.1 = bf16[320,608]{1,0:T(8,128)(2,1)S(1)} all-gather(bf16[80,608]{1,0:T(8,128)(2,1)S(1)} %pad_maximum_fusion.1), channel_id=3, replica_groups=mesh['rq'=8,'rm'=8,'col'=4] {'col'}, dimensions={0}, use_global_device_ids=true | all-gather | bytes 486400 | tf_op jit(solution)/shard_map/all_gather | solution.py:116
  18.1 10.0 %all-gather = bf16[32,24,608]{2,1,0:T(8,128)(2,1)S(1)} all-gather(bf16[8,24,608]{2,1,0:T(8,128)(2,1)} %param.12), channel_id=2, replica_groups=mesh['rq'=8,'rm'=8,'col'=4] {'col'}, dimensions={0}, use_global_device_ids=true | all-gather | bytes 1167360 | tf_op jit(solution)/shard_map/all_gather | solution.py:37
  28.1 2.0 %copy_bitcast_fusion.1 = (bf16[8,24,4,608]{3,2,1,0:T(4,128)(2,1)}, f32[8,24,4,608]{3,2,1,0:T(4,128)S(1)}) fusion(bf16[4,8,24,608]{3,2,1,0:T(8,128)(2,1)S(1)} %bitcast.168), kind=kLoop, calls=%fused_computation.25 | loop fusion | flops 466944 | bytes 3735552 | tf_op jit(solution)/shard_map/transpose | solution.py:39
  31.3 1.3 multiply_reduce_fusion
  33.5 3.2 %fusion.17 = f32[2,8,2,512]{3,1,0,2:T(8,128)S(1)} fusion(bf16[2,2432,512]{2,1,0:T(8,128)(2,1)} %param.18, bf16[8,2,2432,1]{2,1,0,3:T(2,128)(2,1)S(1)} %fusion.32), kind=kOutput, calls=%fused_computation.23 | convolution fusion | flops 79691776 | bytes 5124096 | tf_op jit(solution)/shard_map/rtd,cde->crte/dot_general | solution.py:136
  36.7 2.3 %reshape.1444 = f32[192,2432]{1,0:T(8,128)} reshape(f32[8,24,4,608]{3,2,1,0:T(4,128)S(1)} %get-tuple-element.11) | data formatting | bytes 3735552 | tf_op jit(solution)/shard_map/convert_element_type | solution.py:125
  40.0 2.0 %fusion.16 = bf16[192,2432]{1,0:T(8,128)(2,1)S(1)} fusion(f32[192,2432]{1,0:T(8,128)} %reshape.1444, f32[8,2432]{1,0:T(8,128)S(1)} %get-tuple-element.20, f32[8,2432]{1,0:T(8,128)S(1)} %get-tuple-element.19, f32[192]{0:T(256)S(1)} %rsqrt.61, f32[192]{0:T(256)S(1)} %div.72), kind=kLoop, calls=%fused_computation.16 | loop fusion | flops 2334720 | bytes 2958848 | tf_op jit(solution)/shard_map/convert_element_type | solution.py:125
  42.0 4.8 %convolution_bitcast_fusion = f32[3,192,512]{2,1,0:T(8,128)S(1)} fusion(bf16[3,2432,512]{2,1,0:T(8,128)(2,1)} %param.17, bf16[192,2432]{1,0:T(8,128)(2,1)S(1)} %fusion.16), kind=kOutput, calls=%fused_computation.18 | convolution fusion | flops 1434451968 | bytes 9584640 | tf_op jit(solution)/shard_map/td,cde->cte/dot_general | solution.py:129
  51.2 5.4 %collective-permute-done.1 = bf16[2,1,38,512]{3,2,0,1:T(8,128)(2,1)S(1)} collective-permute-done((bf16[2,1,38,512]{3,2,0,1:T(8,128)(2,1)S(1)}, bf16[2,1,38,512]{3,2,0,1:T(8,128)(2,1)S(1)}, u32[]{:S(2)}, u32[]{:S(2)}) %collective-permute-start.1) | collective-permute-done | bytes 77856 | tf_op jit(solution)/shard_map/ppermute | solution.py:66
  56.7 3.0 %collective-permute-start.2 = (bf16[2,2,1,38,512]{4,3,1,0,2:T(8,128)(2,1)S(1)}, bf16[2,2,1,38,512]{4,3,1,0,2:T(8,128)(2,1)S(1)}, u32[]{:S(2)}, u32[]{:S(2)}) collective-permute-start(bf16[2,2,1,38,512]{4,3,1,0,2:T(8,128)(2,1)S(1)} %maximum_select_fusion.7), channel_id=1, source_target_pairs={{0,128},{4,132},{8,136},{12,140},{16,144},{20,148},{24,152},{28,15... | collective-permute-start | bytes 466952 | tf_op jit(solution)/shard_map/ppermute | solution.py:66
  60.8 1.6 reshape.1435
  62.4 6.4 %all-to-all-start = ((bf16[64,38,128]{2,1,0:T(8,128)(2,1)}), bf16[64,38,128]{2,1,0:T(8,128)(2,1)S(1)}, u32[]{:S(2)}, u32[]{:S(2)}) async-start(bf16[64,38,128]{2,1,0:T(8,128)(2,1)} %reshape.1435), calls=%async_computation | async-start | bytes 1310720 | tf_op jit(solution)/shard_map/all_to_all | solution.py:153
  68.9 2.6 %collective-permute-start.3 = (bf16[2,2,2,1,38,512]{5,4,2,1,0,3:T(8,128)(2,1)S(1)}, bf16[2,2,2,1,38,512]{5,4,2,1,0,3:T(8,128)(2,1)S(1)}, u32[]{:S(2)}, u32[]{:S(2)}) collective-permute-start(bf16[2,2,2,1,38,512]{5,4,2,1,0,3:T(8,128)(2,1)S(1)} %maximum_select_fusion.5), channel_id=1, source_target_pairs={{0,8},{4,12},{8,0},{12,4},{16,24},{20,28},{24,16},{28,20},{32,40},... | collective-permute-start | bytes 933896 | tf_op jit(solution)/shard_map/ppermute | solution.py:66
  71.6 13.0 %collective-permute-done.3 = bf16[2,2,2,1,38,512]{5,4,2,1,0,3:T(8,128)(2,1)S(1)} collective-permute-done((bf16[2,2,2,1,38,512]{5,4,2,1,0,3:T(8,128)(2,1)S(1)}, bf16[2,2,2,1,38,512]{5,4,2,1,0,3:T(8,128)(2,1)S(1)}, u32[]{:S(2)}, u32[]{:S(2)}) %collective-permute-start.3) | collective-permute-done | bytes 311328 | tf_op jit(solution)/shard_map/ppermute | solution.py:66
  85.2 1.5 collective-permute-start.4
  88.0 10.5 %collective-permute-done.4 = bf16[2,2,2,2,1,38,512]{6,3,5,4,2,1,0:T(2,128)(2,1)} collective-permute-done((bf16[2,2,2,2,1,38,512]{6,3,5,4,2,1,0:T(2,128)(2,1)S(1)}, bf16[2,2,2,2,1,38,512]{6,3,5,4,2,1,0:T(2,128)(2,1)}, u32[]{:S(2)}, u32[]{:S(2)}) %collective-permute-start.4) | collective-permute-done | bytes 622624 | tf_op jit(solution)/shard_map/ppermute | solution.py:66
  99.9 2.0 %copy.113 = bf16[2,2,2,2,2,1,38,512]{7,4,6,5,3,2,1,0:T(2,128)(2,1)} copy(bf16[2,2,2,2,2,1,38,512]{7,6,4,3,2,1,5,0:T(8,128)(2,1)S(1)} %maximum_select_fusion.1) | data formatting | bytes 2490368 | tf_op jit(solution)/shard_map/jit(_where)/select_n | solution.py:68
  101.9 1.8 collective-permute-start.5
  106.8 1.9 %fusion.56 = (f32[1536]{0:T(1024)S(1)}, f32[1536,1664]{1,0:T(8,128)S(1)}) fusion(bf16[1536,64]{1,0:T(8,128)(2,1)S(1)} %bitcast.177, bf16[1664,64]{1,0:T(8,128)(2,1)S(1)} %reshape.1438, pred[1664]{0:T(1024)(128)(4,1)S(1)} %fusion.51), kind=kOutput, calls=%fused_computation.128 | convolution fusion | flops 334821888 | bytes 10641024 | tf_op jit(solution)/shard_map/dot_general | solution.py:81
  108.7 1.8 fusion
  110.5 2.1 %copy-done = f32[1536,1664]{1,0:T(8,128)} copy-done((f32[1536,1664]{1,0:T(8,128)}, f32[1536,1664]{1,0:T(8,128)S(1)}, u32[]{:S(2)}) %copy-start) | copy-done | bytes 10223640
  112.8 5.6 %fusion.13 = bf16[1536,64]{0,1:T(8,128)(2,1)S(1)} fusion(bf16[1664,64]{1,0:T(8,128)(2,1)S(1)} %reshape.1439, f32[1536,1664]{1,0:T(8,128)} %copy-done, f32[1536]{0:T(1024)S(1)} %get-tuple-element.36, pred[1664]{0:T(1024)(128)(4,1)S(1)} %fusion.51, f32[1536]{0:T(1024)S(1)} %fusion), kind=kOutput, calls=%fused_computation.13 | convolution fusion | flops 335020032 | bytes 10647168 | tf_op jit(solution)/shard_map/dot_general | solution.py:86
  119.6 12.9 %all-to-all-start.1 = ((bf16[64,2,768]{2,1,0:T(2,128)(2,1)}), bf16[64,2,768]{2,1,0:T(2,128)(2,1)S(1)}, u32[]{:S(2)}, u32[]{:S(2)}) async-start(bf16[64,2,768]{2,1,0:T(2,128)(2,1)} %reshape.1455), calls=%async_computation.1 | async-start | bytes 393216 | tf_op jit(solution)/shard_map/all_to_all | solution.py:168
  132.7 11.7 %all-to-all-done.1 = bf16[64,2,768]{2,1,0:T(2,128)(2,1)S(1)} async-done(((bf16[64,2,768]{2,1,0:T(2,128)(2,1)}), bf16[64,2,768]{2,1,0:T(2,128)(2,1)S(1)}, u32[]{:S(2)}, u32[]{:S(2)}) %all-to-all-start.1) | async-done | bytes 196640 | tf_op jit(solution)/shard_map/all_to_all | solution.py:168
  145.0 1.5 copy.158
  147.4 2.2 %reshape.1451 = bf16[2432,512,1,1]{1,0,2,3:T(8,128)(2,1)} reshape(bf16[2,2,2,2,2,2,38,512]{7,6,5,4,3,2,1,0:T(8,128)(2,1)S(1)} %copy.116) | data formatting | bytes 4980736 | tf_op jit(solution)/shard_map/reshape | solution.py:77
  149.6 2.7 %fusion.8 = f32[2,2,48,2432]{3,2,1,0:T(8,128)S(1)} fusion(bf16[2,2,48,512]{3,2,1,0:T(8,128)(2,1)S(1)} %dot_general.26, bf16[2432,512,1,1]{1,0,2,3:T(8,128)(2,1)} %reshape.1451), kind=kOutput, calls=%fused_computation.10 | convolution fusion | flops 478150656 | bytes 4554752 | tf_op jit(solution)/shard_map/dot_general | solution.py:173
  153.3 3.4 %collective-permute-start.6 = (f32[2,48,2432]{2,1,0:T(8,128)}, f32[2,48,2432]{2,1,0:T(8,128)}, u32[]{:S(2)}, u32[]{:S(2)}) collective-permute-start(f32[2,48,2432]{2,1,0:T(8,128)} %dynamic-slice_bitcast_fusion), channel_id=1, source_target_pairs={{0,1},{1,0},{2,3},{3,2},{4,5},{5,4},{6,7},{7,6},{8,9},{9,8},{10,11... | collective-permute-start | bytes 2801672 | tf_op jit(solution)/shard_map/ppermute | solution.py:51
  156.7 2.5 %collective-permute-done.6 = f32[2,48,2432]{2,1,0:T(8,128)} collective-permute-done((f32[2,48,2432]{2,1,0:T(8,128)}, f32[2,48,2432]{2,1,0:T(8,128)}, u32[]{:S(2)}, u32[]{:S(2)}) %collective-permute-start.6) | collective-permute-done | bytes 933920 | tf_op jit(solution)/shard_map/ppermute | solution.py:51
  164.9 9.5 %collective-permute-done.7 = f32[48,2432]{1,0:T(8,128)S(1)} collective-permute-done((f32[48,2432]{1,0:T(8,128)}, f32[48,2432]{1,0:T(8,128)S(1)}, u32[]{:S(2)}, u32[]{:S(2)}) %collective-permute-start.7) | collective-permute-done | bytes 466976 | tf_op jit(solution)/shard_map/ppermute | solution.py:55
  176.3 6.6 %all_gather.19 = f32[2,8,24,64]{3,2,1,0:T(8,128)S(1)} all-gather(f32[2,2,24,64]{3,2,1,0:T(8,128)S(1)} %pad_maximum_fusion.2), channel_id=1, replica_groups=mesh['rq'=8,'rm'=8,'col'=4] {'col'}, dimensions={1}, use_global_device_ids=true | all-gather | bytes 122880 | tf_op jit(solution)/shard_map/all_gather | solution.py:202
  (124 shorter events, 29.6 us)
Async XLA Ops:
  0.6 49.3 %collective-permute-start = (bf16[1,38,512]{2,1,0:T(8,128)(2,1)}, bf16[1,38,512]{2,1,0:T(8,128)(2,1)S(1)}, u32[]{:S(2)}, u32[]{:S(2)}) collective-permute-start(bf16[1,38,512]{2,1,0:T(8,128)(2,1)} %bitcast.194), channel_id=1, source_target_pairs={{0,32},{4,36},{8,40},{12,44},{16,48},{20,52},{24,56},{28,60},{32,0... | collective-permute-start | bytes 116744 | tf_op jit(solution)/shard_map/ppermute | solution.py:66
  17.1 0.7 copy-start.5
  30.2 2.5 %copy-start.9 = (f32[8,2,2432]{2,1,0:T(2,128)S(1)}, f32[8,2,2432]{2,1,0:T(2,128)}, u32[]{:S(2)}) copy-start(f32[8,2,2432]{2,1,0:T(2,128)} %param.16) | copy-start | bytes 466948
  36.6 2.3 %copy-start.7 = (f32[2,8,2,512]{3,1,0,2:T(8,128)}, f32[2,8,2,512]{3,1,0,2:T(8,128)S(1)}, u32[]{:S(2)}) copy-start(f32[2,8,2,512]{3,1,0,2:T(8,128)S(1)} %fusion.17) | copy-start | bytes 196612
  46.8 0.8 slice-start
  46.8 0.8 copy-start.10
  49.1 0.8 copy-start.8
  49.9 6.7 %collective-permute-start.1 = (bf16[2,1,38,512]{3,2,0,1:T(8,128)(2,1)S(1)}, bf16[2,1,38,512]{3,2,0,1:T(8,128)(2,1)S(1)}, u32[]{:S(2)}, u32[]{:S(2)}) collective-permute-start(bf16[2,1,38,512]{3,2,0,1:T(8,128)(2,1)S(1)} %maximum_select_fusion.9), channel_id=1, source_target_pairs={{0,16},{4,20},{8,24},{12,28},{16,0},{20,4},{24,8},{28,12},{32,48},... | collective-permute-start | bytes 233480 | tf_op jit(solution)/shard_map/ppermute | solution.py:66
  56.7 12.2 %collective-permute-start.2 = (bf16[2,2,1,38,512]{4,3,1,0,2:T(8,128)(2,1)S(1)}, bf16[2,2,1,38,512]{4,3,1,0,2:T(8,128)(2,1)S(1)}, u32[]{:S(2)}, u32[]{:S(2)}) collective-permute-start(bf16[2,2,1,38,512]{4,3,1,0,2:T(8,128)(2,1)S(1)} %maximum_select_fusion.7), channel_id=1, source_target_pairs={{0,128},{4,132},{8,136},{12,140},{16,144},{20,148},{24,152},{28,15... | collective-permute-start | bytes 466952 | tf_op jit(solution)/shard_map/ppermute | solution.py:66
  62.4 41.3 %all-to-all-start = ((bf16[64,38,128]{2,1,0:T(8,128)(2,1)}), bf16[64,38,128]{2,1,0:T(8,128)(2,1)S(1)}, u32[]{:S(2)}, u32[]{:S(2)}) async-start(bf16[64,38,128]{2,1,0:T(8,128)(2,1)} %reshape.1435), calls=%async_computation | async-start | bytes 1310720 | tf_op jit(solution)/shard_map/all_to_all | solution.py:153
  68.9 17.7 %copy-start.12 = (s32[8]{0:T(128)S(1)}, s32[8]{0:T(128)}, u32[]{:S(2)}) copy-start(s32[8]{0:T(128)} %param.22) | copy-start | bytes 100
  68.9 15.6 %collective-permute-start.3 = (bf16[2,2,2,1,38,512]{5,4,2,1,0,3:T(8,128)(2,1)S(1)}, bf16[2,2,2,1,38,512]{5,4,2,1,0,3:T(8,128)(2,1)S(1)}, u32[]{:S(2)}, u32[]{:S(2)}) collective-permute-start(bf16[2,2,2,1,38,512]{5,4,2,1,0,3:T(8,128)(2,1)S(1)} %maximum_select_fusion.5), channel_id=1, source_target_pairs={{0,8},{4,12},{8,0},{12,4},{16,24},{20,28},{24,16},{28,20},{32,40},... | collective-permute-start | bytes 933896 | tf_op jit(solution)/shard_map/ppermute | solution.py:66
  85.2 13.4 %collective-permute-start.4 = (bf16[2,2,2,2,1,38,512]{6,3,5,4,2,1,0:T(2,128)(2,1)S(1)}, bf16[2,2,2,2,1,38,512]{6,3,5,4,2,1,0:T(2,128)(2,1)}, u32[]{:S(2)}, u32[]{:S(2)}) collective-permute-start(bf16[2,2,2,2,1,38,512]{6,3,5,4,2,1,0:T(2,128)(2,1)S(1)} %copy.111), channel_id=1, source_target_pairs={{0,64},{4,68},{8,72},{12,76},{16,80},{20,84},{24,88},{28,92},{32,9... | collective-permute-start | bytes 1867784 | tf_op jit(solution)/shard_map/ppermute | solution.py:66
  101.9 43.0 %collective-permute-start.5 = (bf16[2,2,2,2,2,1,38,512]{7,4,6,5,3,2,1,0:T(2,128)(2,1)}, bf16[2,2,2,2,2,1,38,512]{7,4,6,5,3,2,1,0:T(2,128)(2,1)}, u32[]{:S(2)}, u32[]{:S(2)}) collective-permute-start(bf16[2,2,2,2,2,1,38,512]{7,4,6,5,3,2,1,0:T(2,128)(2,1)} %copy.113), channel_id=1, source_target_pairs={{0,4},{4,0},{8,12},{12,8},{16,20},{20,16},{24,28},{28,24},{32,36},... | collective-permute-start | bytes 3735560 | tf_op jit(solution)/shard_map/ppermute | solution.py:66
  108.7 3.9 %copy-start = (f32[1536,1664]{1,0:T(8,128)}, f32[1536,1664]{1,0:T(8,128)S(1)}, u32[]{:S(2)}) copy-start(f32[1536,1664]{1,0:T(8,128)S(1)} %get-tuple-element.37) | copy-start | bytes 30670852
  108.7 3.9 %copy-start.4 = (bf16[64,26,64]{2,1,0:T(8,128)(2,1)S(1)}, bf16[64,26,64]{2,1,0:T(8,128)(2,1)}, u32[]{:S(2)}) copy-start(bf16[64,26,64]{2,1,0:T(8,128)(2,1)} %get-tuple-element.5) | copy-start | bytes 638980
  119.6 24.8 %all-to-all-start.1 = ((bf16[64,2,768]{2,1,0:T(2,128)(2,1)}), bf16[64,2,768]{2,1,0:T(2,128)(2,1)S(1)}, u32[]{:S(2)}, u32[]{:S(2)}) async-start(bf16[64,2,768]{2,1,0:T(2,128)(2,1)} %reshape.1455), calls=%async_computation.1 | async-start | bytes 393216 | tf_op jit(solution)/shard_map/all_to_all | solution.py:168
  153.3 9.8 %copy-start.1 = (bf16[8,24,4,608]{3,2,1,0:T(4,128)(2,1)S(1)}, bf16[8,24,4,608]{3,2,1,0:T(4,128)(2,1)}, u32[]{:S(2)}) copy-start(bf16[8,24,4,608]{3,2,1,0:T(4,128)(2,1)} %get-tuple-element.10) | copy-start | bytes 2801668
  153.3 5.9 %collective-permute-start.6 = (f32[2,48,2432]{2,1,0:T(8,128)}, f32[2,48,2432]{2,1,0:T(8,128)}, u32[]{:S(2)}, u32[]{:S(2)}) collective-permute-start(f32[2,48,2432]{2,1,0:T(8,128)} %dynamic-slice_bitcast_fusion), channel_id=1, source_target_pairs={{0,1},{1,0},{2,3},{3,2},{4,5},{5,4},{6,7},{7,6},{8,9},{9,8},{10,11... | collective-permute-start | bytes 2801672 | tf_op jit(solution)/shard_map/ppermute | solution.py:51
  160.5 0.9 copy-start.2
  161.4 2.3 %copy-start.11 = (s32[8]{0:T(128)S(1)}, s32[8]{0:T(128)}, u32[]{:S(2)}) copy-start(s32[8]{0:T(128)} %param.23) | copy-start | bytes 100
  162.3 12.1 %copy-start.3 = (f32[2,48,2432]{2,1,0:T(8,128)S(1)}, f32[2,48,2432]{2,1,0:T(8,128)}, u32[]{:S(2)}) copy-start(f32[2,48,2432]{2,1,0:T(8,128)} %copy-done.2) | copy-start | bytes 2801668
  162.3 12.1 %collective-permute-start.7 = (f32[48,2432]{1,0:T(8,128)}, f32[48,2432]{1,0:T(8,128)S(1)}, u32[]{:S(2)}, u32[]{:S(2)}) collective-permute-start(f32[48,2432]{1,0:T(8,128)} %dynamic-slice_bitcast_fusion.1), channel_id=1, source_target_pairs={{0,2},{1,3},{2,0},{3,1},{4,6},{5,7},{6,4},{7,5},{8,10},{9,11},{10,... | collective-permute-start | bytes 1400840 | tf_op jit(solution)/shard_map/ppermute | solution.py:55
  164.8 10.5 %copy-start.6 = (bf16[320,608]{1,0:T(8,128)(2,1)S(1)}, bf16[320,608]{1,0:T(8,128)(2,1)}, u32[]{:S(2)}) copy-start(bf16[320,608]{1,0:T(8,128)(2,1)} %copy-done.5) | copy-start | bytes 1167364

commit v9 on v7

--- a/solution.py
+++ b/solution.py
@@ -33,8 +33,28 @@
     return 3.0 * fraction / (1.0 + 2.0 * fraction)
 
 
+def doubling_gather(block, axis, order):
+    size = lax.axis_size(axis)
+    index = lax.axis_index(axis)
+    bits = len(order)
+    buffer = block[None]
+    for bit in order:
+        pairs = [(i, i ^ (1 << bit)) for i in range(size)]
+        received = lax.ppermute(buffer, axis, pairs)
+        upper = (index >> bit) % 2 == 1
+        buffer = jnp.where(upper, jnp.stack([received, buffer]), jnp.stack([buffer, received]))
+    done = list(reversed(order))
+    buffer = buffer.reshape((2,) * bits + block.shape)
+    perm = [done.index(bit) for bit in reversed(range(bits))]
+    buffer = jnp.transpose(buffer, perm + list(range(bits, bits + block.ndim)))
+    return buffer.reshape((size,) + block.shape)
+
+
+COL_ORDER = [1, 0]
+
+
 def gather_features(local):
-    stacked = lax.all_gather(local, "col", axis=0, tiled=False)
+    stacked = doubling_gather(local, "col", COL_ORDER)
     slabs = stacked.shape[0]
     moved = jnp.moveaxis(stacked, 0, -2)
     return moved.reshape(local.shape[:-1] + (slabs * local.shape[-1],))
@@ -91,7 +111,7 @@
     img_full = gather_features(img_hidden)
     txt_rows = txt_hidden.reshape(requests * text_rows, -1)
     packed = jnp.concatenate([txt_rows, jnp.transpose(final_weight)], 0)
-    packed = lax.all_gather(packed, "col", axis=0, tiled=False)
+    packed = doubling_gather(packed, "col", COL_ORDER)
     slabs = packed.shape[0]
     txt_count = requests * text_rows
     txt_full = (
@@ -177,7 +197,8 @@
     sigma_next = sigma_at(own_steps - 1)[:, None, None]
     advanced = own_latent + (sigma_next - sigma_now) * velocity
     denoised = own_latent - sigma_now * velocity
-    both = lax.all_gather(jnp.stack([advanced, denoised]), "col", axis=1, tiled=True)
+    both = doubling_gather(jnp.stack([advanced, denoised]), "col", COL_ORDER)
+    both = jnp.moveaxis(both, 0, 1).reshape((2, requests) + both.shape[3:])
     advanced, denoised = both[0], both[1]
     return (advanced, denoised)
 

time: 172 us -> 154 us (0.90)
  blocking collectives: 25.9 us -> 0 us
  starting transfers between devices: 26.8 us -> 35 us
  other arithmetic: 17 us -> 12.3 us
  local copies, waits for them, and re-layouts: 23.7 us -> 27.7 us
    all_gather x3 -> x0, blocking collectives: 25.9 us -> none  [the longest x1 9.99 us: gather_features(): stacked = lax.all_gather(local, 'col', axis=0, tiled=False)]
    ppermute x0 -> x6, starting transfers between devices: none -> 12.4 us  [doubling_gather(): received = lax.ppermute(buffer, axis, pairs)]
    ppermute x0 -> x6, waiting for transfers between devices: none -> 3.48 us  [doubling_gather(): received = lax.ppermute(buffer, axis, pairs)]
    all_to_all x1, starting transfers between devices: 8.45 us -> 5.18 us  [per_device(): attended = lax.all_to_all(attended, ROW, 0, 0, tiled=True)]
    ppermute x1, starting transfers between devices: 5.8 us -> 2.86 us  [halving_scatter(): halves = keep + lax.ppermute(send, 'col', pairs)]
    convert_element_type x1 -> x2, local copies, waits for them, and re-layouts: 2.29 us -> 4.77 us  [per_device(): img_full.astype(jnp.float32)]
    unnamed x23 -> x17, local copies, waits for them, and re-layouts: 5.28 us -> 5.85 us
  transfers between devices with their start and end apart: 5 -> 11, of which waited for: 4 -> 7; matrix products, arithmetic and copies ran while one was open for 26% -> 28% of each run, Pallas kernels for 0% -> 0%
where the time goes in v9:
time: 154 us; the launch traced here: 153 us
  waiting for transfers between devices  48.4 us (31%)
  starting transfers between devices  35 us (23%)
  local copies, waits for them, and re-layouts  27.7 us (18%)
  matrix products  15.2 us (10%)
  between operations  14.6 us (9%)
  other arithmetic  12.3 us (8%)
    all_to_all x1, waiting for transfers between devices, per_device(): bundle = lax.all_to_all(bundle, ROW, 0, 0, tiled=True)  21.7 us
    all_to_all x1, starting transfers between devices, per_device(): bundle = lax.all_to_all(bundle, ROW, 0, 0, tiled=True)  13.8 us
    ppermute x6, starting transfers between devices, doubling_gather(): received = lax.ppermute(buffer, axis, pairs)  12.4 us
    all_to_all x1, waiting for transfers between devices, per_device(): attended = lax.all_to_all(attended, ROW, 0, 0, tiled=True)  12.3 us
    ppermute x1, waiting for transfers between devices, halving_scatter(): return keep + lax.ppermute(send, 'col', pairs)  8.77 us
    unnamed x17, local copies, waits for them, and re-layouts  5.85 us
    all_to_all x1, starting transfers between devices, per_device(): attended = lax.all_to_all(attended, ROW, 0, 0, tiled=True)  5.18 us
    dot_general x1, matrix products, per_device(): jnp.einsum('td,cde->cte', flat_rows, qkv_weight, preferred_element_type=j...  4.82 us
  transfers between devices with their start and end apart: 11, of which 7 were waited for; matrix products, arithmetic and copies ran while one was open for 28% of the time, Pallas kernels for 0%

profile of v9, /device:TPU:1, one launch (start us, length us, event | category | flops | bytes accessed | tf_op | source)
XLA Modules:
  0.0 153.2 jit_solution(6359378732305521279)
XLA Ops:
  9.0 2.6 %collective-permute-start.2 = (bf16[1,80,608]{2,1,0:T(8,128)(2,1)S(1)}, bf16[1,80,608]{2,1,0:T(8,128)(2,1)S(1)}, u32[]{:S(2)}, u32[]{:S(2)}) collective-permute-start(bf16[1,80,608]{2,1,0:T(8,128)(2,1)S(1)} %get-tuple-element.23), channel_id=1, source_target_pairs={{0,2},{1,3},{2,0},{3,1},{4,6},{5,7},{6,4},{7,5},{8,10},{9,11},{10,... | collective-permute-start | bytes 291848 | tf_op jit(solution)/shard_map/ppermute | solution.py:43
  11.6 1.1 fusion.56
  14.6 3.6 %collective-permute-start.3 = (bf16[2,1,80,608]{3,2,0,1:T(8,128)(2,1)S(1)}, bf16[2,1,80,608]{3,2,0,1:T(8,128)(2,1)S(1)}, u32[]{:S(2)}, u32[]{:S(2)}) collective-permute-start(bf16[2,1,80,608]{3,2,0,1:T(8,128)(2,1)S(1)} %maximum_select_fusion.4), channel_id=1, source_target_pairs={{0,1},{1,0},{2,3},{3,2},{4,5},{5,4},{6,7},{7,6},{8,9},{9,8},{10,11... | collective-permute-start | bytes 583688 | tf_op jit(solution)/shard_map/ppermute | solution.py:43
  18.8 2.8 %collective-permute-start.1 = (bf16[2,1,8,24,608]{4,3,2,0,1:T(8,128)(2,1)S(1)}, bf16[2,1,8,24,608]{4,3,2,0,1:T(8,128)(2,1)S(1)}, u32[]{:S(2)}, u32[]{:S(2)}) collective-permute-start(bf16[2,1,8,24,608]{4,3,2,0,1:T(8,128)(2,1)S(1)} %maximum_select_fusion.1), channel_id=1, source_target_pairs={{0,1},{1,0},{2,3},{3,2},{4,5},{5,4},{6,7},{7,6},{8,9},{9,8},{10,11... | collective-permute-start | bytes 1400840 | tf_op jit(solution)/shard_map/ppermute | solution.py:43
  23.5 3.2 %fusion.16 = f32[2,8,2,512]{3,1,0,2:T(8,128)S(1)} fusion(bf16[2,2432,512]{2,1,0:T(8,128)(2,1)} %param.18, bf16[8,2,2432,1]{2,1,0,3:T(2,128)(2,1)S(1)} %fusion.33), kind=kOutput, calls=%fused_computation.18 | convolution fusion | flops 79691776 | bytes 5124096 | tf_op jit(solution)/shard_map/rtd,cde->crte/dot_general | solution.py:134
  28.3 2.5 %copy.93 = f32[8,24,4,608]{3,2,1,0:T(4,128)} copy(f32[8,24,4,608]{3,1,0,2:T(8,128)S(1)} %bitcast_convert_fusion) | data formatting | bytes 3735552 | tf_op jit(solution)/shard_map/convert_element_type | solution.py:123
  30.8 2.2 %reshape.751 = f32[192,2432]{1,0:T(8,128)S(1)} reshape(f32[8,24,4,608]{3,2,1,0:T(4,128)} %copy.93) | data formatting | bytes 3735552 | tf_op jit(solution)/shard_map/convert_element_type | solution.py:123
  33.6 4.8 %convolution_bitcast_fusion = f32[3,192,512]{2,1,0:T(8,128)S(1)} fusion(bf16[3,2432,512]{2,1,0:T(8,128)(2,1)} %param.17, bf16[192,2432]{1,0:T(8,128)(2,1)S(1)} %fusion.15), kind=kOutput, calls=%fused_computation.16 | convolution fusion | flops 1434451968 | bytes 9584640 | tf_op jit(solution)/shard_map/td,cde->cte/dot_general | solution.py:127
  38.7 1.0 convert_element_type.90
  41.9 1.2 fusion.21
  44.4 1.6 %reshape.742 = bf16[64,38,128]{2,1,0:T(8,128)(2,1)} reshape(bf16[64,76,64]{2,1,0:T(8,128)(2,1)S(1)} %copy.112) | data formatting | bytes 1245184 | tf_op jit(solution)/shard_map/reshape | solution.py:150
  46.0 13.8 %all-to-all-start = ((bf16[64,38,128]{2,1,0:T(8,128)(2,1)}), bf16[64,38,128]{2,1,0:T(8,128)(2,1)S(1)}, u32[]{:S(2)}, u32[]{:S(2)}) async-start(bf16[64,38,128]{2,1,0:T(8,128)(2,1)} %reshape.742), calls=%async_computation | async-start | bytes 1310720 | tf_op jit(solution)/shard_map/all_to_all | solution.py:151
  61.0 21.7 %all-to-all-done = bf16[64,38,128]{2,1,0:T(8,128)(2,1)S(1)} async-done(((bf16[64,38,128]{2,1,0:T(8,128)(2,1)}), bf16[64,38,128]{2,1,0:T(8,128)(2,1)S(1)}, u32[]{:S(2)}, u32[]{:S(2)}) %all-to-all-start) | async-done | bytes 622624 | tf_op jit(solution)/shard_map/all_to_all | solution.py:151
  83.5 1.0 fusion.54
  84.5 1.2 reshape.746
  85.9 1.9 %fusion.57 = (f32[1536]{0:T(1024)S(1)}, f32[1536,1664]{1,0:T(8,128)S(1)}) fusion(bf16[1536,64]{1,0:T(8,128)(2,1)S(1)} %bitcast.173, bf16[1664,64]{1,0:T(8,128)(2,1)S(1)} %reshape.745, pred[1664]{0:T(1024)(128)(4,1)S(1)} %fusion.52), kind=kOutput, calls=%fused_computation.122 | convolution fusion | flops 334821888 | bytes 10641024 | tf_op jit(solution)/shard_map/dot_general | solution.py:79
  87.8 1.8 %fusion = f32[1536]{0:T(1024)S(1)} fusion(f32[1536,1664]{1,0:T(8,128)S(1)} %get-tuple-element.31, f32[1536]{0:T(1024)S(1)} %get-tuple-element.30, pred[1664]{0:T(1024)(128)(4,1)S(1)} %fusion.52), kind=kLoop, calls=%fused_computation.2 | loop fusion | flops 7666176 | bytes 10237568 | tf_op jit(solution)/shard_map/reduce_sum | solution.py:83
  89.6 2.4 %fusion.12 = bf16[1536,64]{0,1:T(8,128)(2,1)S(1)} fusion(bf16[1664,64]{1,0:T(8,128)(2,1)S(1)} %reshape.746, f32[1536,1664]{1,0:T(8,128)S(1)} %get-tuple-element.31, f32[1536]{0:T(1024)S(1)} %get-tuple-element.30, pred[1664]{0:T(1024)(128)(4,1)S(1)} %fusion.52, f32[1536]{0:T(1024)S(1)} %fusion), kind=kOutput, calls=%fused_computation.11 | convolution fusion | flops 335020032 | bytes 10647168 | tf_op jit(solution)/shard_map/dot_general | solution.py:84
  93.2 5.2 %all-to-all-start.1 = ((bf16[64,2,768]{2,1,0:T(2,128)(2,1)}), bf16[64,2,768]{2,1,0:T(2,128)(2,1)S(1)}, u32[]{:S(2)}, u32[]{:S(2)}) async-start(bf16[64,2,768]{2,1,0:T(2,128)(2,1)} %reshape.762), calls=%async_computation.1 | async-start | bytes 393216 | tf_op jit(solution)/shard_map/all_to_all | solution.py:166
  98.4 12.3 %all-to-all-done.1 = bf16[64,2,768]{2,1,0:T(2,128)(2,1)S(1)} async-done(((bf16[64,2,768]{2,1,0:T(2,128)(2,1)}), bf16[64,2,768]{2,1,0:T(2,128)(2,1)S(1)}, u32[]{:S(2)}, u32[]{:S(2)}) %all-to-all-start.1) | async-done | bytes 196640 | tf_op jit(solution)/shard_map/all_to_all | solution.py:166
  111.1 1.0 dot_general.26
  112.1 2.8 %reshape.758 = bf16[2432,512,1,1]{1,0,2,3:T(8,128)(2,1)S(1)} reshape(bf16[64,38,512]{2,1,0:T(8,128)(2,1)} %all-gather.3.cloned.1.call-done) | data formatting | bytes 4980736
  114.8 1.9 %fusion.7 = f32[2,2,48,2432]{3,2,1,0:T(8,128)S(1)} fusion(bf16[2,2,48,512]{3,2,1,0:T(8,128)(2,1)} %dot_general.26, bf16[2432,512,1,1]{1,0,2,3:T(8,128)(2,1)S(1)} %reshape.758), kind=kOutput, calls=%fused_computation.8 | convolution fusion | flops 478150656 | bytes 4554752 | tf_op jit(solution)/shard_map/dot_general | solution.py:171
  116.8 1.3 copy-done
  118.1 2.9 %collective-permute-start.4 = (f32[2,48,2432]{2,1,0:T(8,128)S(1)}, f32[2,48,2432]{2,1,0:T(8,128)S(1)}, u32[]{:S(2)}, u32[]{:S(2)}) collective-permute-start(f32[2,48,2432]{2,1,0:T(8,128)S(1)} %dynamic-slice_bitcast_fusion), channel_id=1, source_target_pairs={{0,1},{1,0},{2,3},{3,2},{4,5},{5,4},{6,7},{7,6},{8,9},{9,8},{10,11... | collective-permute-start | bytes 2801672 | tf_op jit(solution)/shard_map/ppermute | solution.py:71
  120.9 2.1 %collective-permute-done.4 = f32[2,48,2432]{2,1,0:T(8,128)S(1)} collective-permute-done((f32[2,48,2432]{2,1,0:T(8,128)S(1)}, f32[2,48,2432]{2,1,0:T(8,128)S(1)}, u32[]{:S(2)}, u32[]{:S(2)}) %collective-permute-start.4) | collective-permute-done | bytes 933920 | tf_op jit(solution)/shard_map/ppermute | solution.py:71
  123.1 1.3 bitcast_add_fusion.1
  126.0 1.0 dynamic-slice_bitcast_fusion.3
  128.5 8.8 %collective-permute-done.5 = f32[48,2432]{1,0:T(8,128)S(1)} collective-permute-done((f32[48,2432]{1,0:T(8,128)}, f32[48,2432]{1,0:T(8,128)S(1)}, u32[]{:S(2)}, u32[]{:S(2)}) %collective-permute-start.5) | collective-permute-done | bytes 466976 | tf_op jit(solution)/shard_map/ppermute | solution.py:75
  138.2 1.0 add_bitcast_fusion.1
  140.1 2.1 %collective-permute-done.6 = f32[1,2,2,24,64]{4,3,2,1,0:T(8,128)S(1)} collective-permute-done((f32[1,2,2,24,64]{4,3,2,1,0:T(8,128)S(1)}, f32[1,2,2,24,64]{4,3,2,1,0:T(8,128)S(1)}, u32[]{:S(2)}, u32[]{:S(2)}) %collective-permute-start.6) | collective-permute-done | bytes 24608 | tf_op jit(solution)/shard_map/ppermute | solution.py:43
  142.2 2.4 %collective-permute-start.7 = (f32[2,1,2,2,24,64]{5,4,3,2,0,1:T(8,128)S(1)}, f32[2,1,2,2,24,64]{5,4,3,2,0,1:T(8,128)S(1)}, u32[]{:S(2)}, u32[]{:S(2)}) collective-permute-start(f32[2,1,2,2,24,64]{5,4,3,2,0,1:T(8,128)S(1)} %maximum_select_fusion.6), channel_id=1, source_target_pairs={{0,1},{1,0},{2,3},{3,2},{4,5},{5,4},{6,7},{7,6},{8,9},{9,8},{10,11... | collective-permute-start | bytes 147464 | tf_op jit(solution)/shard_map/ppermute | solution.py:43
  (108 shorter events, 22.2 us)
Async XLA Ops:
  7.2 11.5 %copy-start.4 = (bf16[8,24,608]{2,1,0:T(8,128)(2,1)S(1)}, bf16[8,24,608]{2,1,0:T(8,128)(2,1)}, u32[]{:S(2)}) copy-start(bf16[8,24,608]{2,1,0:T(8,128)(2,1)} %param.12) | copy-start | bytes 700420
  7.2 104.9 %all-gather.3.cloned.1.call-start = ((), (), s32[]{:S(2)}) async-start(), calls=%async_computation.2 | async-start | bytes 2662400 | tf_op jit(solution)/shard_map/all_gather | solution.py:109
  9.0 5.6 %collective-permute-start.2 = (bf16[1,80,608]{2,1,0:T(8,128)(2,1)S(1)}, bf16[1,80,608]{2,1,0:T(8,128)(2,1)S(1)}, u32[]{:S(2)}, u32[]{:S(2)}) collective-permute-start(bf16[1,80,608]{2,1,0:T(8,128)(2,1)S(1)} %get-tuple-element.23), channel_id=1, source_target_pairs={{0,2},{1,3},{2,0},{3,1},{4,6},{5,7},{6,4},{7,5},{8,10},{9,11},{10,... | collective-permute-start | bytes 291848 | tf_op jit(solution)/shard_map/ppermute | solution.py:43
  11.5 7.2 %collective-permute-start = (bf16[1,8,24,608]{3,2,1,0:T(8,128)(2,1)}, bf16[1,8,24,608]{3,2,1,0:T(8,128)(2,1)S(1)}, u32[]{:S(2)}, u32[]{:S(2)}) collective-permute-start(bf16[1,8,24,608]{3,2,1,0:T(8,128)(2,1)} %bitcast.184), channel_id=1, source_target_pairs={{0,2},{1,3},{2,0},{3,1},{4,6},{5,7},{6,4},{7,5},{8,10},{9,11},{10,... | collective-permute-start | bytes 700424 | tf_op jit(solution)/shard_map/ppermute | solution.py:43
  14.6 7.1 %collective-permute-start.3 = (bf16[2,1,80,608]{3,2,0,1:T(8,128)(2,1)S(1)}, bf16[2,1,80,608]{3,2,0,1:T(8,128)(2,1)S(1)}, u32[]{:S(2)}, u32[]{:S(2)}) collective-permute-start(bf16[2,1,80,608]{3,2,0,1:T(8,128)(2,1)S(1)} %maximum_select_fusion.4), channel_id=1, source_target_pairs={{0,1},{1,0},{2,3},{3,2},{4,5},{5,4},{6,7},{7,6},{8,9},{9,8},{10,11... | collective-permute-start | bytes 583688 | tf_op jit(solution)/shard_map/ppermute | solution.py:43
  18.8 8.3 %collective-permute-start.1 = (bf16[2,1,8,24,608]{4,3,2,0,1:T(8,128)(2,1)S(1)}, bf16[2,1,8,24,608]{4,3,2,0,1:T(8,128)(2,1)S(1)}, u32[]{:S(2)}, u32[]{:S(2)}) collective-permute-start(bf16[2,1,8,24,608]{4,3,2,0,1:T(8,128)(2,1)S(1)} %maximum_select_fusion.1), channel_id=1, source_target_pairs={{0,1},{1,0},{2,3},{3,2},{4,5},{5,4},{6,7},{7,6},{8,9},{9,8},{10,11... | collective-permute-start | bytes 1400840 | tf_op jit(solution)/shard_map/ppermute | solution.py:43
  21.9 0.8 copy-start.2
  41.3 1.8 %copy-start.1 = (bf16[8,24,8,64]{3,2,1,0:T(8,128)(2,1)S(1)}, bf16[8,24,8,64]{3,2,1,0:T(8,128)(2,1)}, u32[]{:S(2)}) copy-start(bf16[8,24,8,64]{3,2,1,0:T(8,128)(2,1)} %convert_element_type.90) | copy-start | bytes 589828
  43.5 16.2 %copy-start.6 = (s32[8]{0:T(128)S(1)}, s32[8]{0:T(128)}, u32[]{:S(2)}) copy-start(s32[8]{0:T(128)} %param.22) | copy-start | bytes 100
  46.0 36.7 %all-to-all-start = ((bf16[64,38,128]{2,1,0:T(8,128)(2,1)}), bf16[64,38,128]{2,1,0:T(8,128)(2,1)S(1)}, u32[]{:S(2)}, u32[]{:S(2)}) async-start(bf16[64,38,128]{2,1,0:T(8,128)(2,1)} %reshape.742), calls=%async_computation | async-start | bytes 1310720 | tf_op jit(solution)/shard_map/all_to_all | solution.py:151
  93.2 17.5 %all-to-all-start.1 = ((bf16[64,2,768]{2,1,0:T(2,128)(2,1)}), bf16[64,2,768]{2,1,0:T(2,128)(2,1)S(1)}, u32[]{:S(2)}, u32[]{:S(2)}) async-start(bf16[64,2,768]{2,1,0:T(2,128)(2,1)} %reshape.762), calls=%async_computation.1 | async-start | bytes 393216 | tf_op jit(solution)/shard_map/all_to_all | solution.py:166
  116.8 1.3 copy-start
  118.0 7.9 %copy-start.5 = (s32[8]{0:T(128)S(1)}, s32[8]{0:T(128)}, u32[]{:S(2)}) copy-start(s32[8]{0:T(128)} %param.23) | copy-start | bytes 100
  118.1 5.0 %collective-permute-start.4 = (f32[2,48,2432]{2,1,0:T(8,128)S(1)}, f32[2,48,2432]{2,1,0:T(8,128)S(1)}, u32[]{:S(2)}, u32[]{:S(2)}) collective-permute-start(f32[2,48,2432]{2,1,0:T(8,128)S(1)} %dynamic-slice_bitcast_fusion), channel_id=1, source_target_pairs={{0,1},{1,0},{2,3},{3,2},{4,5},{5,4},{6,7},{7,6},{8,9},{9,8},{10,11... | collective-permute-start | bytes 2801672 | tf_op jit(solution)/shard_map/ppermute | solution.py:71
  125.2 12.1 %collective-permute-start.5 = (f32[48,2432]{1,0:T(8,128)}, f32[48,2432]{1,0:T(8,128)S(1)}, u32[]{:S(2)}, u32[]{:S(2)}) collective-permute-start(f32[48,2432]{1,0:T(8,128)} %dynamic-slice_bitcast_fusion.1), channel_id=1, source_target_pairs={{0,2},{1,3},{2,0},{3,1},{4,6},{5,7},{6,4},{7,5},{8,10},{9,11},{10,... | collective-permute-start | bytes 1400840 | tf_op jit(solution)/shard_map/ppermute | solution.py:75
  128.5 9.7 %copy-start.3 = (bf16[2,2,80,608]{3,2,1,0:T(8,128)(2,1)S(1)}, bf16[2,2,80,608]{3,2,1,0:T(8,128)(2,1)}, u32[]{:S(2)}) copy-start(bf16[2,2,80,608]{3,2,1,0:T(8,128)(2,1)} %copy-done.2) | copy-start | bytes 1167364
  139.2 3.0 %collective-permute-start.6 = (f32[1,2,2,24,64]{4,3,2,1,0:T(8,128)S(1)}, f32[1,2,2,24,64]{4,3,2,1,0:T(8,128)S(1)}, u32[]{:S(2)}, u32[]{:S(2)}) collective-permute-start(f32[1,2,2,24,64]{4,3,2,1,0:T(8,128)S(1)} %get-tuple-element.26), channel_id=1, source_target_pairs={{0,2},{1,3},{2,0},{3,1},{4,6},{5,7},{6,4},{7,5},{8,10},{9,11},{10,... | collective-permute-start | bytes 73736 | tf_op jit(solution)/shard_map/ppermute | solution.py:43
  142.2 3.4 %collective-permute-start.7 = (f32[2,1,2,2,24,64]{5,4,3,2,0,1:T(8,128)S(1)}, f32[2,1,2,2,24,64]{5,4,3,2,0,1:T(8,128)S(1)}, u32[]{:S(2)}, u32[]{:S(2)}) collective-permute-start(f32[2,1,2,2,24,64]{5,4,3,2,0,1:T(8,128)S(1)} %maximum_select_fusion.6), channel_id=1, source_target_pairs={{0,1},{1,0},{2,3},{3,2},{4,5},{5,4},{6,7},{7,6},{8,9},{9,8},{10,11... | collective-permute-start | bytes 147464 | tf_op jit(solution)/shard_map/ppermute | solution.py:43
Sparse Core Ops, SparseCore 0:
  11.8 86.0 all-gather.2

commit v10 on v9

--- a/solution.py
+++ b/solution.py
@@ -9,7 +9,7 @@
 STEPS = 28
 REQ = 8
 
-ROW = ("rq", "rm")
+ROW = ("x", "zh", "y")
 
 eps_norm = 1e-06
 neg_fill = -1e30
@@ -106,7 +106,10 @@
     heads_local = cols_local // HD
     block_len = patches + text_rows
 
-    weight_t = lax.all_gather(jnp.transpose(out_weight), ROW, axis=0, tiled=True)
+    staged = lax.all_gather(jnp.transpose(out_weight), "zh", axis=0, tiled=False)
+    staged = lax.all_gather(staged, "y", axis=0, tiled=False)
+    staged = lax.all_gather(staged, "x", axis=0, tiled=False)
+    weight_t = jnp.transpose(staged, (0, 2, 1, 3, 4)).reshape(-1, cols_local)
 
     img_full = gather_features(img_hidden)
     txt_rows = txt_hidden.reshape(requests * text_rows, -1)
@@ -154,7 +157,7 @@
     keys = bundle[:, patches : patches + block_len].reshape(sources * block_len, HD)
     values = bundle[:, patches + block_len :].reshape(sources * block_len, HD)
 
-    request = lax.axis_index("rq")
+    request = lax.axis_index(ROW) // (sources // requests)
     positions = jnp.arange(sources * block_len, dtype=jnp.int32)
     within = positions % block_len
     source_row = positions // block_len
@@ -206,7 +209,8 @@
 def solution(mesh):
     rows = mesh.shape["row"]
     cols = mesh.shape["col"]
-    split = Mesh(mesh.devices.reshape(REQ, rows // REQ, cols), ("rq", "rm", "col"))
+    side = round(rows ** (1 / 3))
+    split = Mesh(mesh.devices.reshape(side, side, side, cols), ROW + ("col",))
     in_specs = (
         P(None, ROW, "col"),
         P(None, ROW, "col"),

time: 154 us -> 172 us (1.12)
  blocking collectives: 0 us -> 30.6 us
  waiting for transfers between devices: 48.4 us -> 32.5 us
  local copies, waits for them, and re-layouts: 27.7 us -> 33.8 us
  starting transfers between devices: 35 us -> 30.5 us
  other arithmetic: 12.3 us -> 14.2 us
    all_gather x0 -> x2, blocking collectives: none -> 30.6 us  [the longest x1 16.4 us: per_device(): lax.all_gather(jnp.transpose(out_weight), 'zh', axis=0, tiled=False)]
    all_to_all x1, waiting for transfers between devices: 21.7 us -> 4.38 us  [per_device(): bundle = lax.all_to_all(bundle, ROW, 0, 0, tiled=True)]
    all_to_all x1, starting transfers between devices: 13.8 us -> 10.1 us  [per_device(): bundle = lax.all_to_all(bundle, ROW, 0, 0, tiled=True)]
    all_gather x0 -> x2, local copies, waits for them, and re-layouts: none -> 3.52 us  [the longest x1 2.36 us: per_device(): staged = lax.all_gather(staged, 'x', axis=0, tiled=False)]
    all_gather x1, waiting for transfers between devices: 0.01 us -> 3.16 us  [per_device(): staged = lax.all_gather(staged, 'x', axis=0, tiled=False)]
    unnamed x17 -> x20, local copies, waits for them, and re-layouts: 5.85 us -> 2.93 us
    reshape x0 -> x1, local copies, waits for them, and re-layouts: none -> 2.77 us  [per_device(): weight_t = jnp.transpose(staged, (0, 2, 1, 3, 4)).reshape(-1, cols_local)]
    all_to_all x1, starting transfers between devices: 5.18 us -> 7.69 us  [per_device(): attended = lax.all_to_all(attended, ROW, 0, 0, tiled=True)]
  transfers between devices with their start and end apart: 11 -> 11, of which waited for: 7 -> 8; matrix products, arithmetic and copies ran while one was open for 28% -> 15% of each run, Pallas kernels for 0% -> 0%
where the time goes in v10:
time: 172 us; the launch traced here: 171 us
  local copies, waits for them, and re-layouts  33.8 us (20%)
  waiting for transfers between devices  32.5 us (19%)
  blocking collectives  30.6 us (18%)
  starting transfers between devices  30.5 us (18%)
  matrix products  15.1 us (9%)
  between operations  14.7 us (9%)
  other arithmetic  14.2 us (8%)
    all_gather x1, blocking collectives, per_device(): lax.all_gather(jnp.transpose(out_weight), 'zh', axis=0, tiled=False)  16.4 us
    all_gather x1, blocking collectives, per_device(): staged = lax.all_gather(staged, 'y', axis=0, tiled=False)  14.3 us
    all_to_all x1, waiting for transfers between devices, per_device(): attended = lax.all_to_all(attended, ROW, 0, 0, tiled=True)  12.4 us
    ppermute x6, starting transfers between devices, doubling_gather(): received = lax.ppermute(buffer, axis, pairs)  10.6 us
    all_to_all x1, starting transfers between devices, per_device(): bundle = lax.all_to_all(bundle, ROW, 0, 0, tiled=True)  10.1 us
    all_to_all x1, starting transfers between devices, per_device(): attended = lax.all_to_all(attended, ROW, 0, 0, tiled=True)  7.69 us
    ppermute x1, waiting for transfers between devices, halving_scatter(): return keep + lax.ppermute(send, 'col', pairs)  7.35 us
    convert_element_type x2, local copies, waits for them, and re-layouts, per_device(): img_full.astype(jnp.float32)  4.81 us
  transfers between devices with their start and end apart: 11, of which 8 were waited for; matrix products, arithmetic and copies ran while one was open for 15% of the time, Pallas kernels for 0%

profile of v10, /device:TPU:1, one launch (start us, length us, event | category | flops | bytes accessed | tf_op | source)
XLA Modules:
  0.0 171.4 jit_solution(16528531041503353921)
XLA Ops:
  8.9 2.6 %collective-permute-start.2 = (bf16[1,80,608]{2,1,0:T(8,128)(2,1)S(1)}, bf16[1,80,608]{2,1,0:T(8,128)(2,1)S(1)}, u32[]{:S(2)}, u32[]{:S(2)}) collective-permute-start(bf16[1,80,608]{2,1,0:T(8,128)(2,1)S(1)} %get-tuple-element.23), channel_id=1, source_target_pairs={{0,2},{1,3},{2,0},{3,1},{4,6},{5,7},{6,4},{7,5},{8,10},{9,11},{10,... | collective-permute-start | bytes 291848 | tf_op jit(solution)/shard_map/ppermute | solution.py:43
  14.4 16.4 %all-gather.3 = bf16[4,38,512]{2,1,0:T(8,128)(2,1)} all-gather(bf16[1,38,512]{2,1,0:T(8,128)(2,1)} %bitcast.208), channel_id=2, replica_groups=mesh['x'=4,'zh'=4,'y'=4,'col'=4] {'zh'}, dimensions={0}, use_global_device_ids=true | all-gather | bytes 194560 | tf_op jit(solution)/shard_map/all_gather | solution.py:109
  30.9 3.9 %collective-permute-start.3 = (bf16[2,1,80,608]{3,2,0,1:T(8,128)(2,1)S(1)}, bf16[2,1,80,608]{3,2,0,1:T(8,128)(2,1)S(1)}, u32[]{:S(2)}, u32[]{:S(2)}) collective-permute-start(bf16[2,1,80,608]{3,2,0,1:T(8,128)(2,1)S(1)} %maximum_select_fusion.4), channel_id=1, source_target_pairs={{0,1},{1,0},{2,3},{3,2},{4,5},{5,4},{6,7},{7,6},{8,9},{9,8},{10,11... | collective-permute-start | bytes 583688 | tf_op jit(solution)/shard_map/ppermute | solution.py:43
  37.1 3.2 %fusion.16 = f32[2,8,2,512]{3,1,0,2:T(8,128)S(1)} fusion(bf16[2,2432,512]{2,1,0:T(8,128)(2,1)} %param.18, bf16[8,2,2432,1]{2,1,0,3:T(2,128)(2,1)S(1)} %fusion.33), kind=kOutput, calls=%fused_computation.18 | convolution fusion | flops 79691776 | bytes 5124096 | tf_op jit(solution)/shard_map/rtd,cde->crte/dot_general | solution.py:137
  41.8 2.6 %copy.95 = f32[8,24,4,608]{3,2,1,0:T(4,128)} copy(f32[8,24,4,608]{3,1,0,2:T(8,128)S(1)} %bitcast_convert_fusion) | data formatting | bytes 3735552 | tf_op jit(solution)/shard_map/convert_element_type | solution.py:126
  44.4 2.2 %reshape.755 = f32[192,2432]{1,0:T(8,128)S(1)} reshape(f32[8,24,4,608]{3,2,1,0:T(4,128)} %copy.95) | data formatting | bytes 3735552 | tf_op jit(solution)/shard_map/convert_element_type | solution.py:126
  47.2 4.8 %convolution_bitcast_fusion = f32[3,192,512]{2,1,0:T(8,128)S(1)} fusion(bf16[3,2432,512]{2,1,0:T(8,128)(2,1)} %param.17, bf16[192,2432]{1,0:T(8,128)(2,1)S(1)} %fusion.15), kind=kOutput, calls=%fused_computation.16 | convolution fusion | flops 1434451968 | bytes 9584640 | tf_op jit(solution)/shard_map/td,cde->cte/dot_general | solution.py:130
  57.5 1.6 reshape.745
  59.1 10.1 %all-to-all-start = ((bf16[64,38,128]{2,1,0:T(8,128)(2,1)}), bf16[64,38,128]{2,1,0:T(8,128)(2,1)S(1)}, u32[]{:S(2)}, u32[]{:S(2)}) async-start(bf16[64,38,128]{2,1,0:T(8,128)(2,1)} %reshape.745), calls=%async_computation | async-start | bytes 1310720 | tf_op jit(solution)/shard_map/all_to_all | solution.py:154
  69.3 14.3 %all-gather.1 = bf16[16,38,512]{2,1,0:T(8,128)(2,1)S(1)} all-gather(bf16[4,38,512]{2,1,0:T(8,128)(2,1)S(1)} %copy-done.5), channel_id=3, replica_groups=mesh['x'=4,'zh'=4,'y'=4,'col'=4] {'y'}, dimensions={0}, use_global_device_ids=true | all-gather | bytes 778240 | tf_op jit(solution)/shard_map/all_gather | solution.py:110
  83.5 1.2 copy.117
  86.0 4.4 %all-to-all-done = bf16[64,38,128]{2,1,0:T(8,128)(2,1)S(1)} async-done(((bf16[64,38,128]{2,1,0:T(8,128)(2,1)}), bf16[64,38,128]{2,1,0:T(8,128)(2,1)S(1)}, u32[]{:S(2)}, u32[]{:S(2)}) %all-to-all-start) | async-done | bytes 622624 | tf_op jit(solution)/shard_map/all_to_all | solution.py:154
  92.1 1.2 reshape.749
  93.5 1.9 %fusion.57 = (f32[1536]{0:T(1024)S(1)}, f32[1536,1664]{1,0:T(8,128)S(1)}) fusion(bf16[1536,64]{1,0:T(8,128)(2,1)S(1)} %bitcast.179, bf16[1664,64]{1,0:T(8,128)(2,1)S(1)} %reshape.748, pred[1664]{0:T(1024)(128)(4,1)S(1)} %fusion.52), kind=kOutput, calls=%fused_computation.122 | convolution fusion | flops 334821888 | bytes 10641024 | tf_op jit(solution)/shard_map/dot_general | solution.py:79
  95.5 1.8 %fusion = f32[1536]{0:T(1024)S(1)} fusion(f32[1536,1664]{1,0:T(8,128)S(1)} %get-tuple-element.31, f32[1536]{0:T(1024)S(1)} %get-tuple-element.30, pred[1664]{0:T(1024)(128)(4,1)S(1)} %fusion.52), kind=kLoop, calls=%fused_computation.2 | loop fusion | flops 7666176 | bytes 10237568 | tf_op jit(solution)/shard_map/reduce_sum | solution.py:83
  97.3 2.4 %fusion.12 = bf16[1536,64]{0,1:T(8,128)(2,1)S(1)} fusion(bf16[1664,64]{1,0:T(8,128)(2,1)S(1)} %reshape.749, f32[1536,1664]{1,0:T(8,128)S(1)} %get-tuple-element.31, f32[1536]{0:T(1024)S(1)} %get-tuple-element.30, pred[1664]{0:T(1024)(128)(4,1)S(1)} %fusion.52, f32[1536]{0:T(1024)S(1)} %fusion), kind=kOutput, calls=%fused_computation.11 | convolution fusion | flops 335020032 | bytes 10647168 | tf_op jit(solution)/shard_map/dot_general | solution.py:84
  100.8 7.7 %all-to-all-start.1 = ((bf16[64,2,768]{2,1,0:T(2,128)(2,1)}), bf16[64,2,768]{2,1,0:T(2,128)(2,1)S(1)}, u32[]{:S(2)}, u32[]{:S(2)}) async-start(bf16[64,2,768]{2,1,0:T(2,128)(2,1)} %reshape.770), calls=%async_computation.1 | async-start | bytes 393216 | tf_op jit(solution)/shard_map/all_to_all | solution.py:169
  108.5 12.4 %all-to-all-done.1 = bf16[64,2,768]{2,1,0:T(2,128)(2,1)S(1)} async-done(((bf16[64,2,768]{2,1,0:T(2,128)(2,1)}), bf16[64,2,768]{2,1,0:T(2,128)(2,1)S(1)}, u32[]{:S(2)}, u32[]{:S(2)}) %all-to-all-start.1) | async-done | bytes 196640 | tf_op jit(solution)/shard_map/all_to_all | solution.py:169
  122.3 3.2 %all-gather.6.cloned.1.call-done = bf16[16,4,38,512]{3,1,2,0:T(4,128)(2,1)} async-done(((bf16[4,4,38,512]{3,1,2,0:T(4,128)(2,1)}), bf16[16,4,38,512]{3,1,2,0:T(4,128)(2,1)}) %all-gather.6.cloned.1.call-update) | async-done | bytes 2490384 | tf_op jit(solution)/shard_map/all_gather | solution.py:111
  125.4 2.4 %copy.118 = bf16[16,4,38,512]{3,2,1,0:T(8,128)(2,1)S(1)} copy(bf16[16,4,38,512]{3,1,2,0:T(4,128)(2,1)} %all-gather.6.cloned.1.call-done) | data formatting | bytes 4980736 | tf_op jit(solution)/shard_map/all_gather | solution.py:111
  127.8 1.8 %copy.119 = bf16[4,4,4,38,512]{4,3,2,1,0:T(8,128)(2,1)} copy(bf16[4,4,4,38,512]{4,3,1,2,0:T(8,128)(2,1)S(1)} %bitcast.174) | data formatting | bytes 4980736 | tf_op jit(solution)/shard_map/transpose | solution.py:112
  129.6 2.8 %reshape.766 = bf16[2432,512,1,1]{1,0,2,3:T(8,128)(2,1)S(1)} reshape(bf16[4,4,4,38,512]{4,3,2,1,0:T(8,128)(2,1)} %copy.119) | data formatting | bytes 4980736 | tf_op jit(solution)/shard_map/reshape | solution.py:112
  132.3 1.9 %fusion.7 = f32[2,2,48,2432]{3,2,1,0:T(8,128)S(1)} fusion(bf16[2,2,48,512]{3,2,1,0:T(8,128)(2,1)} %dot_general.26, bf16[2432,512,1,1]{1,0,2,3:T(8,128)(2,1)S(1)} %reshape.766), kind=kOutput, calls=%fused_computation.8 | convolution fusion | flops 478150656 | bytes 4554752 | tf_op jit(solution)/shard_map/dot_general | solution.py:174
  134.2 1.2 copy-done
  136.3 2.1 %collective-permute-done.4 = f32[2,48,2432]{2,1,0:T(8,128)S(1)} collective-permute-done((f32[2,48,2432]{2,1,0:T(8,128)S(1)}, f32[2,48,2432]{2,1,0:T(8,128)S(1)}, u32[]{:S(2)}, u32[]{:S(2)}) %collective-permute-start.4) | collective-permute-done | bytes 933920 | tf_op jit(solution)/shard_map/ppermute | solution.py:71
  138.4 1.3 bitcast_add_fusion.1
  140.6 1.3 collective-permute-start.5
  143.7 1.7 reshape.739
  145.3 7.3 %collective-permute-done.5 = f32[48,2432]{1,0:T(8,128)S(1)} collective-permute-done((f32[48,2432]{1,0:T(8,128)}, f32[48,2432]{1,0:T(8,128)S(1)}, u32[]{:S(2)}, u32[]{:S(2)}) %collective-permute-start.5) | collective-permute-done | bytes 466976 | tf_op jit(solution)/shard_map/ppermute | solution.py:75
  157.4 1.4 collective-permute-start.6
  158.8 1.7 collective-permute-done.6
  160.4 2.4 %collective-permute-start.7 = (f32[2,1,2,2,24,64]{5,4,3,2,0,1:T(8,128)S(1)}, f32[2,1,2,2,24,64]{5,4,3,2,0,1:T(8,128)S(1)}, u32[]{:S(2)}, u32[]{:S(2)}) collective-permute-start(f32[2,1,2,2,24,64]{5,4,3,2,0,1:T(8,128)S(1)} %maximum_select_fusion.6), channel_id=1, source_target_pairs={{0,1},{1,0},{2,3},{3,2},{4,5},{5,4},{6,7},{7,6},{8,9},{9,8},{10,11... | collective-permute-start | bytes 147464 | tf_op jit(solution)/shard_map/ppermute | solution.py:43
  (117 shorter events, 29.9 us)
Async XLA Ops:
  7.2 27.7 %copy-start.4 = (bf16[8,24,608]{2,1,0:T(8,128)(2,1)S(1)}, bf16[8,24,608]{2,1,0:T(8,128)(2,1)}, u32[]{:S(2)}) copy-start(bf16[8,24,608]{2,1,0:T(8,128)(2,1)} %param.12) | copy-start | bytes 700420
  8.9 21.9 %collective-permute-start.2 = (bf16[1,80,608]{2,1,0:T(8,128)(2,1)S(1)}, bf16[1,80,608]{2,1,0:T(8,128)(2,1)S(1)}, u32[]{:S(2)}, u32[]{:S(2)}) collective-permute-start(bf16[1,80,608]{2,1,0:T(8,128)(2,1)S(1)} %get-tuple-element.23), channel_id=1, source_target_pairs={{0,2},{1,3},{2,0},{3,1},{4,6},{5,7},{6,4},{7,5},{8,10},{9,11},{10,... | collective-permute-start | bytes 291848 | tf_op jit(solution)/shard_map/ppermute | solution.py:43
  11.4 23.4 %collective-permute-start = (bf16[1,8,24,608]{3,2,1,0:T(8,128)(2,1)}, bf16[1,8,24,608]{3,2,1,0:T(8,128)(2,1)S(1)}, u32[]{:S(2)}, u32[]{:S(2)}) collective-permute-start(bf16[1,8,24,608]{3,2,1,0:T(8,128)(2,1)} %bitcast.190), channel_id=1, source_target_pairs={{0,2},{1,3},{2,0},{3,1},{4,6},{5,7},{6,4},{7,5},{8,10},{9,11},{10,... | collective-permute-start | bytes 700424 | tf_op jit(solution)/shard_map/ppermute | solution.py:43
  30.9 5.0 %collective-permute-start.3 = (bf16[2,1,80,608]{3,2,0,1:T(8,128)(2,1)S(1)}, bf16[2,1,80,608]{3,2,0,1:T(8,128)(2,1)S(1)}, u32[]{:S(2)}, u32[]{:S(2)}) collective-permute-start(bf16[2,1,80,608]{3,2,0,1:T(8,128)(2,1)S(1)} %maximum_select_fusion.4), channel_id=1, source_target_pairs={{0,1},{1,0},{2,3},{3,2},{4,5},{5,4},{6,7},{7,6},{8,9},{9,8},{10,11... | collective-permute-start | bytes 583688 | tf_op jit(solution)/shard_map/ppermute | solution.py:43
  35.0 5.7 %collective-permute-start.1 = (bf16[2,1,8,24,608]{4,3,2,0,1:T(8,128)(2,1)S(1)}, bf16[2,1,8,24,608]{4,3,2,0,1:T(8,128)(2,1)S(1)}, u32[]{:S(2)}, u32[]{:S(2)}) collective-permute-start(bf16[2,1,8,24,608]{4,3,2,0,1:T(8,128)(2,1)S(1)} %maximum_select_fusion.1), channel_id=1, source_target_pairs={{0,1},{1,0},{2,3},{3,2},{4,5},{5,4},{6,7},{7,6},{8,9},{9,8},{10,11... | collective-permute-start | bytes 1400840 | tf_op jit(solution)/shard_map/ppermute | solution.py:43
  36.0 4.3 %copy-start.2 = (bf16[2,2,80,608]{3,2,1,0:T(8,128)(2,1)}, bf16[2,2,80,608]{3,2,1,0:T(8,128)(2,1)S(1)}, u32[]{:S(2)}) copy-start(bf16[2,2,80,608]{3,2,1,0:T(8,128)(2,1)S(1)} %copy.107) | copy-start | bytes 1167364
  54.9 1.0 copy-start.1
  55.0 1.0 copy-start.6
  56.7 12.6 %copy-start.5 = (bf16[4,38,512]{2,1,0:T(8,128)(2,1)S(1)}, bf16[4,38,512]{2,1,0:T(8,128)(2,1)}, u32[]{:S(2)}) copy-start(bf16[4,38,512]{2,1,0:T(8,128)(2,1)} %all-gather.3) | copy-start | bytes 466948
  59.1 25.6 %copy-start.8 = (s32[8]{0:T(128)S(1)}, s32[8]{0:T(128)}, u32[]{:S(2)}) copy-start(s32[8]{0:T(128)} %param.22) | copy-start | bytes 100
  59.1 31.3 %all-to-all-start = ((bf16[64,38,128]{2,1,0:T(8,128)(2,1)}), bf16[64,38,128]{2,1,0:T(8,128)(2,1)S(1)}, u32[]{:S(2)}, u32[]{:S(2)}) async-start(bf16[64,38,128]{2,1,0:T(8,128)(2,1)} %reshape.745), calls=%async_computation | async-start | bytes 1310720 | tf_op jit(solution)/shard_map/all_to_all | solution.py:154
  69.2 56.2 %all-gather.6.cloned.1.call-start = ((), (), s32[]{:S(2)}) async-start(), calls=%async_computation.2 | async-start | bytes 3112960 | tf_op jit(solution)/shard_map/all_gather | solution.py:111
  100.8 20.1 %all-to-all-start.1 = ((bf16[64,2,768]{2,1,0:T(2,128)(2,1)}), bf16[64,2,768]{2,1,0:T(2,128)(2,1)S(1)}, u32[]{:S(2)}, u32[]{:S(2)}) async-start(bf16[64,2,768]{2,1,0:T(2,128)(2,1)} %reshape.770), calls=%async_computation.1 | async-start | bytes 393216 | tf_op jit(solution)/shard_map/all_to_all | solution.py:169
  134.2 1.3 copy-start
  135.5 6.3 %copy-start.7 = (s32[8]{0:T(128)S(1)}, s32[8]{0:T(128)}, u32[]{:S(2)}) copy-start(s32[8]{0:T(128)} %param.23) | copy-start | bytes 100
  135.6 2.9 %collective-permute-start.4 = (f32[2,48,2432]{2,1,0:T(8,128)S(1)}, f32[2,48,2432]{2,1,0:T(8,128)S(1)}, u32[]{:S(2)}, u32[]{:S(2)}) collective-permute-start(f32[2,48,2432]{2,1,0:T(8,128)S(1)} %dynamic-slice_bitcast_fusion), channel_id=1, source_target_pairs={{0,1},{1,0},{2,3},{3,2},{4,5},{5,4},{6,7},{7,6},{8,9},{9,8},{10,11... | collective-permute-start | bytes 2801672 | tf_op jit(solution)/shard_map/ppermute | solution.py:71
  140.6 12.1 %collective-permute-start.5 = (f32[48,2432]{1,0:T(8,128)}, f32[48,2432]{1,0:T(8,128)S(1)}, u32[]{:S(2)}, u32[]{:S(2)}) collective-permute-start(f32[48,2432]{1,0:T(8,128)} %dynamic-slice_bitcast_fusion.1), channel_id=1, source_target_pairs={{0,2},{1,3},{2,0},{3,1},{4,6},{5,7},{6,4},{7,5},{8,10},{9,11},{10,... | collective-permute-start | bytes 1400840 | tf_op jit(solution)/shard_map/ppermute | solution.py:75
  145.3 11.1 %copy-start.3 = (bf16[2,2,80,608]{3,2,1,0:T(8,128)(2,1)S(1)}, bf16[2,2,80,608]{3,2,1,0:T(8,128)(2,1)}, u32[]{:S(2)}) copy-start(bf16[2,2,80,608]{3,2,1,0:T(8,128)(2,1)} %copy-done.2) | copy-start | bytes 1167364
  157.4 3.0 %collective-permute-start.6 = (f32[1,2,2,24,64]{4,3,2,1,0:T(8,128)S(1)}, f32[1,2,2,24,64]{4,3,2,1,0:T(8,128)S(1)}, u32[]{:S(2)}, u32[]{:S(2)}) collective-permute-start(f32[1,2,2,24,64]{4,3,2,1,0:T(8,128)S(1)} %get-tuple-element.26), channel_id=1, source_target_pairs={{0,2},{1,3},{2,0},{3,1},{4,6},{5,7},{6,4},{7,5},{8,10},{9,11},{10,... | collective-permute-start | bytes 73736 | tf_op jit(solution)/shard_map/ppermute | solution.py:43
  160.4 3.4 %collective-permute-start.7 = (f32[2,1,2,2,24,64]{5,4,3,2,0,1:T(8,128)S(1)}, f32[2,1,2,2,24,64]{5,4,3,2,0,1:T(8,128)S(1)}, u32[]{:S(2)}, u32[]{:S(2)}) collective-permute-start(f32[2,1,2,2,24,64]{5,4,3,2,0,1:T(8,128)S(1)} %maximum_select_fusion.6), channel_id=1, source_target_pairs={{0,1},{1,0},{2,3},{3,2},{4,5},{5,4},{6,7},{7,6},{8,9},{9,8},{10,11... | collective-permute-start | bytes 147464 | tf_op jit(solution)/shard_map/ppermute | solution.py:43
Sparse Core Ops, SparseCore 0:
  84.8 40.5 all-gather.5

commit v11 on v9

--- a/solution.py
+++ b/solution.py
@@ -51,6 +51,7 @@
 
 
 COL_ORDER = [1, 0]
+ROW_ORDER = [3, 2, 5, 1, 4, 0]
 
 
 def gather_features(local):
@@ -106,7 +107,6 @@
     heads_local = cols_local // HD
     block_len = patches + text_rows
 
-    weight_t = lax.all_gather(jnp.transpose(out_weight), ROW, axis=0, tiled=True)
 
     img_full = gather_features(img_hidden)
     txt_rows = txt_hidden.reshape(requests * text_rows, -1)
@@ -148,7 +148,9 @@
     )
     sources, bundle_rows = bundle.shape[0], bundle.shape[1]
     bundle = bundle.reshape(sources, bundle_rows // 2, 2 * HD)
+    bundle, weight_block = lax.optimization_barrier((bundle, jnp.transpose(out_weight)))
     bundle = lax.all_to_all(bundle, ROW, 0, 0, tiled=True)
+    weight_t = doubling_gather(weight_block, ROW, ROW_ORDER).reshape(-1, cols_local)
     bundle = bundle.reshape(sources, bundle_rows, HD)
     head_queries = bundle[:, :patches].reshape(sources * patches, HD)
     keys = bundle[:, patches : patches + block_len].reshape(sources * block_len, HD)

time: 154 us -> 186 us (1.21)
  starting transfers between devices: 35 us -> 57.5 us
  between operations: 14.6 us -> 1.34 us
  local copies, waits for them, and re-layouts: 27.7 us -> 37.8 us
  waiting for transfers between devices: 48.4 us -> 53.8 us
  other arithmetic: 12.3 us -> 16 us
  matrix products: 15.2 us -> 18.4 us
    ppermute x6 -> x12, waiting for transfers between devices: 3.48 us -> 32.4 us  [doubling_gather(): received = lax.ppermute(buffer, axis, pairs)]
    all_to_all x1, waiting for transfers between devices: 21.7 us -> 0.01 us  [per_device(): bundle = lax.all_to_all(bundle, ROW, 0, 0, tiled=True)]
    ppermute x6 -> x12, starting transfers between devices: 12.4 us -> 27 us  [doubling_gather(): received = lax.ppermute(buffer, axis, pairs)]
    all_to_all x1, starting transfers between devices: 5.18 us -> 15.7 us  [per_device(): attended = lax.all_to_all(attended, ROW, 0, 0, tiled=True)]
    dot_general x1, matrix products: 2.4 us -> 5.62 us  [attend_one(): jnp.dot(exp_scores.astype(jnp.bfloat16), values, preferred_element_type=j...]
    another operation x0 -> x1, local copies, waits for them, and re-layouts: none -> 2.77 us  [per_device(): doubling_gather(weight_block, ROW, ROW_ORDER).reshape(-1, cols_local)]
    all_to_all x1, starting transfers between devices: 13.8 us -> 11 us  [per_device(): bundle = lax.all_to_all(bundle, ROW, 0, 0, tiled=True)]
    select_n x0 -> x2, local copies, waits for them, and re-layouts: none -> 2.49 us  [doubling_gather(): jnp.where(upper, jnp.stack([received, buffer]), jnp.stack([buffer, receiv...]
  transfers between devices with their start and end apart: 11 -> 16, of which waited for: 7 -> 10; matrix products, arithmetic and copies ran while one was open for 28% -> 19% of each run, Pallas kernels for 0% -> 0%
where the time goes in v11:
time: 186 us; the launch traced here: 185 us
  starting transfers between devices  57.5 us (31%)
  waiting for transfers between devices  53.8 us (29%)
  local copies, waits for them, and re-layouts  37.8 us (20%)
  matrix products  18.4 us (10%)
  other arithmetic  16 us (9%)
    ppermute x12, waiting for transfers between devices, doubling_gather(): received = lax.ppermute(buffer, axis, pairs)  32.4 us
    ppermute x12, starting transfers between devices, doubling_gather(): received = lax.ppermute(buffer, axis, pairs)  27 us
    all_to_all x1, starting transfers between devices, per_device(): attended = lax.all_to_all(attended, ROW, 0, 0, tiled=True)  15.7 us
    all_to_all x1, starting transfers between devices, per_device(): bundle = lax.all_to_all(bundle, ROW, 0, 0, tiled=True)  11 us
    all_to_all x1, waiting for transfers between devices, per_device(): attended = lax.all_to_all(attended, ROW, 0, 0, tiled=True)  10.6 us
    ppermute x1, waiting for transfers between devices, halving_scatter(): return keep + lax.ppermute(send, 'col', pairs)  8.63 us
    dot_general x1, matrix products, attend_one(): jnp.dot(exp_scores.astype(jnp.bfloat16), values, preferred_element_type=j...  5.62 us
    unnamed x26, local copies, waits for them, and re-layouts  5.08 us
  transfers between devices with their start and end apart: 16, of which 10 were waited for; matrix products, arithmetic and copies ran while one was open for 19% of the time, Pallas kernels for 0%

profile of v11, /device:TPU:1, one launch (start us, length us, event | category | flops | bytes accessed | tf_op | source)
XLA Modules:
  0.0 184.8 jit_solution(17476318359849672714)
XLA Ops:
  2.4 2.6 %collective-permute-start.2 = (bf16[1,80,608]{2,1,0:T(8,128)(2,1)S(1)}, bf16[1,80,608]{2,1,0:T(8,128)(2,1)S(1)}, u32[]{:S(2)}, u32[]{:S(2)}) collective-permute-start(bf16[1,80,608]{2,1,0:T(8,128)(2,1)S(1)} %get-tuple-element.35), channel_id=1, source_target_pairs={{0,2},{1,3},{2,0},{3,1},{4,6},{5,7},{6,4},{7,5},{8,10},{9,11},{10,... | collective-permute-start | bytes 291848 | tf_op jit(solution)/shard_map/ppermute | solution.py:43
  8.0 3.6 %collective-permute-start.3 = (bf16[2,1,80,608]{3,2,0,1:T(8,128)(2,1)S(1)}, bf16[2,1,80,608]{3,2,0,1:T(8,128)(2,1)S(1)}, u32[]{:S(2)}, u32[]{:S(2)}) collective-permute-start(bf16[2,1,80,608]{3,2,0,1:T(8,128)(2,1)S(1)} %maximum_select_fusion.11), channel_id=1, source_target_pairs={{0,1},{1,0},{2,3},{3,2},{4,5},{5,4},{6,7},{7,6},{8,9},{9,8},{10,11... | collective-permute-start | bytes 583688 | tf_op jit(solution)/shard_map/ppermute | solution.py:43
  12.2 2.8 %collective-permute-start.1 = (bf16[2,1,8,24,608]{4,3,2,0,1:T(8,128)(2,1)S(1)}, bf16[2,1,8,24,608]{4,3,2,0,1:T(8,128)(2,1)S(1)}, u32[]{:S(2)}, u32[]{:S(2)}) collective-permute-start(bf16[2,1,8,24,608]{4,3,2,0,1:T(8,128)(2,1)S(1)} %maximum_select_fusion.6), channel_id=1, source_target_pairs={{0,1},{1,0},{2,3},{3,2},{4,5},{5,4},{6,7},{7,6},{8,9},{9,8},{10,11... | collective-permute-start | bytes 1400840 | tf_op jit(solution)/shard_map/ppermute | solution.py:43
  16.4 3.2 %fusion.17 = f32[2,8,2,512]{3,1,0,2:T(8,128)S(1)} fusion(bf16[2,2432,512]{2,1,0:T(8,128)(2,1)} %param.18, bf16[8,2,2432,1]{2,1,0,3:T(2,128)(2,1)S(1)} %fusion.36), kind=kOutput, calls=%fused_computation.23 | convolution fusion | flops 79691776 | bytes 5124096 | tf_op jit(solution)/shard_map/rtd,cde->crte/dot_general | solution.py:134
  21.1 2.6 %copy.144 = f32[8,24,4,608]{3,2,1,0:T(4,128)} copy(f32[8,24,4,608]{3,1,0,2:T(8,128)S(1)} %bitcast_convert_fusion) | data formatting | bytes 3735552 | tf_op jit(solution)/shard_map/convert_element_type | solution.py:123
  23.7 2.2 %reshape.1952 = f32[192,2432]{1,0:T(8,128)S(1)} reshape(f32[8,24,4,608]{3,2,1,0:T(4,128)} %copy.144) | data formatting | bytes 3735552 | tf_op jit(solution)/shard_map/convert_element_type | solution.py:123
  26.5 4.8 %convolution_bitcast_fusion = f32[3,192,512]{2,1,0:T(8,128)S(1)} fusion(bf16[3,2432,512]{2,1,0:T(8,128)(2,1)} %param.17, bf16[192,2432]{1,0:T(8,128)(2,1)S(1)} %fusion.16), kind=kOutput, calls=%fused_computation.18 | convolution fusion | flops 1434451968 | bytes 9584640 | tf_op jit(solution)/shard_map/td,cde->cte/dot_general | solution.py:127
  38.4 6.2 %collective-permute-start.4 = (bf16[1,38,512]{2,1,0:T(8,128)(2,1)S(1)}, bf16[1,38,512]{2,1,0:T(8,128)(2,1)S(1)}, u32[]{:S(2)}, u32[]{:S(2)}) collective-permute-start(bf16[1,38,512]{2,1,0:T(8,128)(2,1)S(1)} %bitcast.246), channel_id=1, source_target_pairs={{0,32},{4,36},{8,40},{12,44},{16,48},{20,52},{24,56},{28,60},{32,0... | collective-permute-start | bytes 116744 | tf_op jit(solution)/shard_map/ppermute | solution.py:43
  44.6 1.9 %collective-permute-done.4 = bf16[1,38,512]{2,1,0:T(8,128)(2,1)S(1)} collective-permute-done((bf16[1,38,512]{2,1,0:T(8,128)(2,1)S(1)}, bf16[1,38,512]{2,1,0:T(8,128)(2,1)S(1)}, u32[]{:S(2)}, u32[]{:S(2)}) %collective-permute-start.4) | collective-permute-done | bytes 38944 | tf_op jit(solution)/shard_map/ppermute | solution.py:43
  47.7 5.4 %collective-permute-done.5 = bf16[2,1,38,512]{3,2,0,1:T(8,128)(2,1)S(1)} collective-permute-done((bf16[2,1,38,512]{3,2,0,1:T(8,128)(2,1)S(1)}, bf16[2,1,38,512]{3,2,0,1:T(8,128)(2,1)S(1)}, u32[]{:S(2)}, u32[]{:S(2)}) %collective-permute-start.5) | collective-permute-done | bytes 77856 | tf_op jit(solution)/shard_map/ppermute | solution.py:43
  53.2 2.9 %collective-permute-start.6 = (bf16[2,2,1,38,512]{4,3,1,0,2:T(8,128)(2,1)S(1)}, bf16[2,2,1,38,512]{4,3,1,0,2:T(8,128)(2,1)S(1)}, u32[]{:S(2)}, u32[]{:S(2)}) collective-permute-start(bf16[2,2,1,38,512]{4,3,1,0,2:T(8,128)(2,1)S(1)} %maximum_select_fusion.13), channel_id=1, source_target_pairs={{0,128},{4,132},{8,136},{12,140},{16,144},{20,148},{24,152},{28,15... | collective-permute-start | bytes 466952 | tf_op jit(solution)/shard_map/ppermute | solution.py:43
  56.1 11.0 %all-to-all-start = ((bf16[64,38,128]{2,1,0:T(8,128)(2,1)}), bf16[64,38,128]{2,1,0:T(8,128)(2,1)}, u32[]{:S(2)}, u32[]{:S(2)}) async-start(bf16[64,38,128]{2,1,0:T(8,128)(2,1)} %reshape.1943), calls=%async_computation | async-start | bytes 1310720 | tf_op jit(solution)/shard_map/all_to_all | solution.py:152
  67.2 2.5 %collective-permute-start.7 = (bf16[2,2,2,1,38,512]{5,4,2,1,0,3:T(8,128)(2,1)S(1)}, bf16[2,2,2,1,38,512]{5,4,2,1,0,3:T(8,128)(2,1)S(1)}, u32[]{:S(2)}, u32[]{:S(2)}) collective-permute-start(bf16[2,2,2,1,38,512]{5,4,2,1,0,3:T(8,128)(2,1)S(1)} %maximum_select_fusion.9), channel_id=1, source_target_pairs={{0,8},{4,12},{8,0},{12,4},{16,24},{20,28},{24,16},{28,20},{32,40},... | collective-permute-start | bytes 933896 | tf_op jit(solution)/shard_map/ppermute | solution.py:43
  69.8 9.7 %collective-permute-done.7 = bf16[2,2,2,1,38,512]{5,4,2,1,0,3:T(8,128)(2,1)S(1)} collective-permute-done((bf16[2,2,2,1,38,512]{5,4,2,1,0,3:T(8,128)(2,1)S(1)}, bf16[2,2,2,1,38,512]{5,4,2,1,0,3:T(8,128)(2,1)S(1)}, u32[]{:S(2)}, u32[]{:S(2)}) %collective-permute-start.7) | collective-permute-done | bytes 311328 | tf_op jit(solution)/shard_map/ppermute | solution.py:43
  83.1 11.4 %collective-permute-done.8 = bf16[2,2,2,2,1,38,512]{6,3,5,4,2,1,0:T(2,128)(2,1)S(1)} collective-permute-done((bf16[2,2,2,2,1,38,512]{6,3,5,4,2,1,0:T(2,128)(2,1)S(1)}, bf16[2,2,2,2,1,38,512]{6,3,5,4,2,1,0:T(2,128)(2,1)S(1)}, u32[]{:S(2)}, u32[]{:S(2)}) %collective-permute-start.8) | collective-permute-done | bytes 622624 | tf_op jit(solution)/shard_map/ppermute | solution.py:43
  94.9 2.0 %copy.172 = bf16[2,2,2,2,2,1,38,512]{7,4,6,5,3,2,1,0:T(2,128)(2,1)} copy(bf16[2,2,2,2,2,1,38,512]{7,6,4,3,2,1,5,0:T(8,128)(2,1)S(1)} %maximum_select_fusion.1) | data formatting | bytes 2490368 | tf_op jit(solution)/shard_map/jit(_where)/select_n | solution.py:45
  96.9 1.6 collective-permute-start.9
  98.5 1.8 reshape.1944
  102.7 1.9 %fusion.66 = (f32[1536]{0:T(1024)S(1)}, f32[1536,1664]{1,0:T(8,128)S(1)}) fusion(bf16[1536,64]{1,0:T(8,128)(2,1)S(1)} %bitcast.215, bf16[1664,64]{1,0:T(8,128)(2,1)S(1)} %reshape.1946, pred[1664]{0:T(1024)(128)(4,1)S(1)} %fusion.61), kind=kOutput, calls=%fused_computation.145 | convolution fusion | flops 334821888 | bytes 10641024 | tf_op jit(solution)/shard_map/dot_general | solution.py:80
  104.6 1.8 fusion
  106.4 2.1 %copy-done = f32[1536,1664]{1,0:T(8,128)} copy-done((f32[1536,1664]{1,0:T(8,128)}, f32[1536,1664]{1,0:T(8,128)S(1)}, u32[]{:S(2)}) %copy-start) | copy-done | bytes 10223640
  108.7 5.6 %fusion.13 = bf16[1536,64]{0,1:T(8,128)(2,1)S(1)} fusion(bf16[1664,64]{1,0:T(8,128)(2,1)S(1)} %reshape.1947, f32[1536,1664]{1,0:T(8,128)} %copy-done, f32[1536]{0:T(1024)S(1)} %get-tuple-element.44, pred[1664]{0:T(1024)(128)(4,1)S(1)} %fusion.61, f32[1536]{0:T(1024)S(1)} %fusion), kind=kOutput, calls=%fused_computation.13 | convolution fusion | flops 335020032 | bytes 10647168 | tf_op jit(solution)/shard_map/dot_general | solution.py:85
  115.5 15.7 %all-to-all-start.1 = ((bf16[64,2,768]{2,1,0:T(2,128)(2,1)}), bf16[64,2,768]{2,1,0:T(2,128)(2,1)S(1)}, u32[]{:S(2)}, u32[]{:S(2)}) async-start(bf16[64,2,768]{2,1,0:T(2,128)(2,1)} %reshape.1961), calls=%async_computation.1 | async-start | bytes 393216 | tf_op jit(solution)/shard_map/all_to_all | solution.py:168
  132.8 10.6 %all-to-all-done.1 = bf16[64,2,768]{2,1,0:T(2,128)(2,1)S(1)} async-done(((bf16[64,2,768]{2,1,0:T(2,128)(2,1)}), bf16[64,2,768]{2,1,0:T(2,128)(2,1)S(1)}, u32[]{:S(2)}, u32[]{:S(2)}) %all-to-all-start.1) | async-done | bytes 196640 | tf_op jit(solution)/shard_map/all_to_all | solution.py:168
  146.8 1.8 copy.175
  148.6 2.8 %reshape.1957 = bf16[2432,512,1,1]{1,0,2,3:T(8,128)(2,1)S(1)} reshape(bf16[2,2,2,2,2,2,38,512]{7,6,5,4,3,2,1,0:T(8,128)(2,1)} %copy.175) | data formatting | bytes 4980736 | tf_op jit(solution)/shard_map/reshape;reshape | solution.py:153
  151.4 1.9 %fusion.8 = f32[2,2,48,2432]{3,2,1,0:T(8,128)S(1)} fusion(bf16[2,2,48,512]{3,2,1,0:T(8,128)(2,1)} %dot_general.26, bf16[2432,512,1,1]{1,0,2,3:T(8,128)(2,1)S(1)} %reshape.1957), kind=kOutput, calls=%fused_computation.10 | convolution fusion | flops 478150656 | bytes 4554752 | tf_op jit(solution)/shard_map/dot_general | solution.py:173
  154.6 3.8 %collective-permute-start.10 = (f32[2,48,2432]{2,1,0:T(8,128)S(1)}, f32[2,48,2432]{2,1,0:T(8,128)S(1)}, u32[]{:S(2)}, u32[]{:S(2)}) collective-permute-start(f32[2,48,2432]{2,1,0:T(8,128)S(1)} %dynamic-slice_bitcast_fusion), channel_id=1, source_target_pairs={{0,1},{1,0},{2,3},{3,2},{4,5},{5,4},{6,7},{7,6},{8,9},{9,8},{10,11... | collective-permute-start | bytes 2801672 | tf_op jit(solution)/shard_map/ppermute | solution.py:72
  158.5 2.1 %collective-permute-done.10 = f32[2,48,2432]{2,1,0:T(8,128)S(1)} collective-permute-done((f32[2,48,2432]{2,1,0:T(8,128)S(1)}, f32[2,48,2432]{2,1,0:T(8,128)S(1)}, u32[]{:S(2)}, u32[]{:S(2)}) %collective-permute-start.10) | collective-permute-done | bytes 933920 | tf_op jit(solution)/shard_map/ppermute | solution.py:72
  166.2 8.6 %collective-permute-done.11 = f32[48,2432]{1,0:T(8,128)S(1)} collective-permute-done((f32[48,2432]{1,0:T(8,128)}, f32[48,2432]{1,0:T(8,128)S(1)}, u32[]{:S(2)}, u32[]{:S(2)}) %collective-permute-start.11) | collective-permute-done | bytes 466976 | tf_op jit(solution)/shard_map/ppermute | solution.py:76
  178.1 2.6 %collective-permute-done.12 = f32[1,2,2,24,64]{4,3,2,1,0:T(8,128)S(1)} collective-permute-done((f32[1,2,2,24,64]{4,3,2,1,0:T(8,128)S(1)}, f32[1,2,2,24,64]{4,3,2,1,0:T(8,128)S(1)}, u32[]{:S(2)}, u32[]{:S(2)}) %collective-permute-start.12) | collective-permute-done | bytes 24608 | tf_op jit(solution)/shard_map/ppermute | solution.py:43
  180.7 2.4 %collective-permute-start.13 = (f32[2,1,2,2,24,64]{5,4,3,2,0,1:T(8,128)S(1)}, f32[2,1,2,2,24,64]{5,4,3,2,0,1:T(8,128)S(1)}, u32[]{:S(2)}, u32[]{:S(2)}) collective-permute-start(f32[2,1,2,2,24,64]{5,4,3,2,0,1:T(8,128)S(1)} %maximum_select_fusion.15), channel_id=1, source_target_pairs={{0,1},{1,0},{2,3},{3,2},{4,5},{5,4},{6,7},{7,6},{8,9},{9,8},{10,11... | collective-permute-start | bytes 147464 | tf_op jit(solution)/shard_map/ppermute | solution.py:43
  (143 shorter events, 41.5 us)
Async XLA Ops:
  0.6 11.4 %copy-start.7 = (bf16[8,24,608]{2,1,0:T(8,128)(2,1)S(1)}, bf16[8,24,608]{2,1,0:T(8,128)(2,1)}, u32[]{:S(2)}) copy-start(bf16[8,24,608]{2,1,0:T(8,128)(2,1)} %param.12) | copy-start | bytes 700420
  2.4 5.5 %collective-permute-start.2 = (bf16[1,80,608]{2,1,0:T(8,128)(2,1)S(1)}, bf16[1,80,608]{2,1,0:T(8,128)(2,1)S(1)}, u32[]{:S(2)}, u32[]{:S(2)}) collective-permute-start(bf16[1,80,608]{2,1,0:T(8,128)(2,1)S(1)} %get-tuple-element.35), channel_id=1, source_target_pairs={{0,2},{1,3},{2,0},{3,1},{4,6},{5,7},{6,4},{7,5},{8,10},{9,11},{10,... | collective-permute-start | bytes 291848 | tf_op jit(solution)/shard_map/ppermute | solution.py:43
  4.9 7.2 %collective-permute-start = (bf16[1,8,24,608]{3,2,1,0:T(8,128)(2,1)}, bf16[1,8,24,608]{3,2,1,0:T(8,128)(2,1)S(1)}, u32[]{:S(2)}, u32[]{:S(2)}) collective-permute-start(bf16[1,8,24,608]{3,2,1,0:T(8,128)(2,1)} %bitcast.228), channel_id=1, source_target_pairs={{0,2},{1,3},{2,0},{3,1},{4,6},{5,7},{6,4},{7,5},{8,10},{9,11},{10,... | collective-permute-start | bytes 700424 | tf_op jit(solution)/shard_map/ppermute | solution.py:43
  8.0 7.1 %collective-permute-start.3 = (bf16[2,1,80,608]{3,2,0,1:T(8,128)(2,1)S(1)}, bf16[2,1,80,608]{3,2,0,1:T(8,128)(2,1)S(1)}, u32[]{:S(2)}, u32[]{:S(2)}) collective-permute-start(bf16[2,1,80,608]{3,2,0,1:T(8,128)(2,1)S(1)} %maximum_select_fusion.11), channel_id=1, source_target_pairs={{0,1},{1,0},{2,3},{3,2},{4,5},{5,4},{6,7},{7,6},{8,9},{9,8},{10,11... | collective-permute-start | bytes 583688 | tf_op jit(solution)/shard_map/ppermute | solution.py:43
  12.2 7.7 %collective-permute-start.1 = (bf16[2,1,8,24,608]{4,3,2,0,1:T(8,128)(2,1)S(1)}, bf16[2,1,8,24,608]{4,3,2,0,1:T(8,128)(2,1)S(1)}, u32[]{:S(2)}, u32[]{:S(2)}) collective-permute-start(bf16[2,1,8,24,608]{4,3,2,0,1:T(8,128)(2,1)S(1)} %maximum_select_fusion.6), channel_id=1, source_target_pairs={{0,1},{1,0},{2,3},{3,2},{4,5},{5,4},{6,7},{7,6},{8,9},{9,8},{10,11... | collective-permute-start | bytes 1400840 | tf_op jit(solution)/shard_map/ppermute | solution.py:43
  15.3 4.3 %copy-start.5 = (bf16[2,2,80,608]{3,2,1,0:T(8,128)(2,1)}, bf16[2,2,80,608]{3,2,1,0:T(8,128)(2,1)S(1)}, u32[]{:S(2)}) copy-start(bf16[2,2,80,608]{3,2,1,0:T(8,128)(2,1)S(1)} %copy.156) | copy-start | bytes 1167364
  34.2 1.0 copy-start.4
  34.3 1.0 copy-start.8
  36.0 2.5 %copy-start.9 = (bf16[512,38]{0,1:T(8,128)(2,1)S(1)}, bf16[512,38]{0,1:T(8,128)(2,1)}, u32[]{:S(2)}) copy-start(bf16[512,38]{0,1:T(8,128)(2,1)} %param.19) | copy-start | bytes 116740
  38.4 8.1 %collective-permute-start.4 = (bf16[1,38,512]{2,1,0:T(8,128)(2,1)S(1)}, bf16[1,38,512]{2,1,0:T(8,128)(2,1)S(1)}, u32[]{:S(2)}, u32[]{:S(2)}) collective-permute-start(bf16[1,38,512]{2,1,0:T(8,128)(2,1)S(1)} %bitcast.246), channel_id=1, source_target_pairs={{0,32},{4,36},{8,40},{12,44},{16,48},{20,52},{24,56},{28,60},{32,0... | collective-permute-start | bytes 116744 | tf_op jit(solution)/shard_map/ppermute | solution.py:43
  46.5 6.6 %collective-permute-start.5 = (bf16[2,1,38,512]{3,2,0,1:T(8,128)(2,1)S(1)}, bf16[2,1,38,512]{3,2,0,1:T(8,128)(2,1)S(1)}, u32[]{:S(2)}, u32[]{:S(2)}) collective-permute-start(bf16[2,1,38,512]{3,2,0,1:T(8,128)(2,1)S(1)} %maximum_select_fusion.16), channel_id=1, source_target_pairs={{0,16},{4,20},{8,24},{12,28},{16,0},{20,4},{24,8},{28,12},{32,48},... | collective-permute-start | bytes 233480 | tf_op jit(solution)/shard_map/ppermute | solution.py:43
  53.2 13.9 %collective-permute-start.6 = (bf16[2,2,1,38,512]{4,3,1,0,2:T(8,128)(2,1)S(1)}, bf16[2,2,1,38,512]{4,3,1,0,2:T(8,128)(2,1)S(1)}, u32[]{:S(2)}, u32[]{:S(2)}) collective-permute-start(bf16[2,2,1,38,512]{4,3,1,0,2:T(8,128)(2,1)S(1)} %maximum_select_fusion.13), channel_id=1, source_target_pairs={{0,128},{4,132},{8,136},{12,140},{16,144},{20,148},{24,152},{28,15... | collective-permute-start | bytes 466952 | tf_op jit(solution)/shard_map/ppermute | solution.py:43
  56.1 42.5 %all-to-all-start = ((bf16[64,38,128]{2,1,0:T(8,128)(2,1)}), bf16[64,38,128]{2,1,0:T(8,128)(2,1)}, u32[]{:S(2)}, u32[]{:S(2)}) async-start(bf16[64,38,128]{2,1,0:T(8,128)(2,1)} %reshape.1943), calls=%async_computation | async-start | bytes 1310720 | tf_op jit(solution)/shard_map/all_to_all | solution.py:152
  67.2 13.6 %copy-start.11 = (s32[8]{0:T(128)S(1)}, s32[8]{0:T(128)}, u32[]{:S(2)}) copy-start(s32[8]{0:T(128)} %param.22) | copy-start | bytes 100
  67.2 12.3 %collective-permute-start.7 = (bf16[2,2,2,1,38,512]{5,4,2,1,0,3:T(8,128)(2,1)S(1)}, bf16[2,2,2,1,38,512]{5,4,2,1,0,3:T(8,128)(2,1)S(1)}, u32[]{:S(2)}, u32[]{:S(2)}) collective-permute-start(bf16[2,2,2,1,38,512]{5,4,2,1,0,3:T(8,128)(2,1)S(1)} %maximum_select_fusion.9), channel_id=1, source_target_pairs={{0,8},{4,12},{8,0},{12,4},{16,24},{20,28},{24,16},{28,20},{32,40},... | collective-permute-start | bytes 933896 | tf_op jit(solution)/shard_map/ppermute | solution.py:43
  80.1 14.5 %collective-permute-start.8 = (bf16[2,2,2,2,1,38,512]{6,3,5,4,2,1,0:T(2,128)(2,1)S(1)}, bf16[2,2,2,2,1,38,512]{6,3,5,4,2,1,0:T(2,128)(2,1)S(1)}, u32[]{:S(2)}, u32[]{:S(2)}) collective-permute-start(bf16[2,2,2,2,1,38,512]{6,3,5,4,2,1,0:T(2,128)(2,1)S(1)} %copy.170), channel_id=1, source_target_pairs={{0,64},{4,68},{8,72},{12,76},{16,80},{20,84},{24,88},{28,92},{32,9... | collective-permute-start | bytes 1867784 | tf_op jit(solution)/shard_map/ppermute | solution.py:43
  96.9 47.9 %collective-permute-start.9 = (bf16[2,2,2,2,2,1,38,512]{7,4,6,5,3,2,1,0:T(2,128)(2,1)}, bf16[2,2,2,2,2,1,38,512]{7,4,6,5,3,2,1,0:T(2,128)(2,1)}, u32[]{:S(2)}, u32[]{:S(2)}) collective-permute-start(bf16[2,2,2,2,2,1,38,512]{7,4,6,5,3,2,1,0:T(2,128)(2,1)} %copy.172), channel_id=1, source_target_pairs={{0,4},{4,0},{8,12},{12,8},{16,20},{20,16},{24,28},{28,24},{32,36},... | collective-permute-start | bytes 3735560 | tf_op jit(solution)/shard_map/ppermute | solution.py:43
  104.6 3.9 %copy-start = (f32[1536,1664]{1,0:T(8,128)}, f32[1536,1664]{1,0:T(8,128)S(1)}, u32[]{:S(2)}) copy-start(f32[1536,1664]{1,0:T(8,128)S(1)} %get-tuple-element.45) | copy-start | bytes 30670852
  104.6 3.9 %copy-start.3 = (bf16[64,26,64]{2,1,0:T(8,128)(2,1)S(1)}, bf16[64,26,64]{2,1,0:T(8,128)(2,1)}, u32[]{:S(2)}) copy-start(bf16[64,26,64]{2,1,0:T(8,128)(2,1)} %get-tuple-element.9) | copy-start | bytes 638980
  115.5 27.9 %all-to-all-start.1 = ((bf16[64,2,768]{2,1,0:T(2,128)(2,1)}), bf16[64,2,768]{2,1,0:T(2,128)(2,1)S(1)}, u32[]{:S(2)}, u32[]{:S(2)}) async-start(bf16[64,2,768]{2,1,0:T(2,128)(2,1)} %reshape.1961), calls=%async_computation.1 | async-start | bytes 393216 | tf_op jit(solution)/shard_map/all_to_all | solution.py:168
  153.3 1.3 copy-start.1
  154.6 8.1 %copy-start.10 = (s32[8]{0:T(128)S(1)}, s32[8]{0:T(128)}, u32[]{:S(2)}) copy-start(s32[8]{0:T(128)} %param.23) | copy-start | bytes 100
  154.6 5.9 %collective-permute-start.10 = (f32[2,48,2432]{2,1,0:T(8,128)S(1)}, f32[2,48,2432]{2,1,0:T(8,128)S(1)}, u32[]{:S(2)}, u32[]{:S(2)}) collective-permute-start(f32[2,48,2432]{2,1,0:T(8,128)S(1)} %dynamic-slice_bitcast_fusion), channel_id=1, source_target_pairs={{0,1},{1,0},{2,3},{3,2},{4,5},{5,4},{6,7},{7,6},{8,9},{9,8},{10,11... | collective-permute-start | bytes 2801672 | tf_op jit(solution)/shard_map/ppermute | solution.py:72
  162.7 12.1 %collective-permute-start.11 = (f32[48,2432]{1,0:T(8,128)}, f32[48,2432]{1,0:T(8,128)S(1)}, u32[]{:S(2)}, u32[]{:S(2)}) collective-permute-start(f32[48,2432]{1,0:T(8,128)} %dynamic-slice_bitcast_fusion.1), channel_id=1, source_target_pairs={{0,2},{1,3},{2,0},{3,1},{4,6},{5,7},{6,4},{7,5},{8,10},{9,11},{10,... | collective-permute-start | bytes 1400840 | tf_op jit(solution)/shard_map/ppermute | solution.py:76
  166.2 9.8 %copy-start.2 = (bf16[8,24,2432]{2,1,0:T(8,128)(2,1)S(1)}, bf16[8,24,2432]{2,1,0:T(8,128)(2,1)}, u32[]{:S(2)}) copy-start(bf16[8,24,2432]{2,1,0:T(8,128)(2,1)} %reshape.1937) | copy-start | bytes 2801668
  166.2 10.5 %copy-start.6 = (bf16[2,2,80,608]{3,2,1,0:T(8,128)(2,1)S(1)}, bf16[2,2,80,608]{3,2,1,0:T(8,128)(2,1)}, u32[]{:S(2)}) copy-start(bf16[2,2,80,608]{3,2,1,0:T(8,128)(2,1)} %copy-done.5) | copy-start | bytes 1167364
  177.7 3.0 %collective-permute-start.12 = (f32[1,2,2,24,64]{4,3,2,1,0:T(8,128)S(1)}, f32[1,2,2,24,64]{4,3,2,1,0:T(8,128)S(1)}, u32[]{:S(2)}, u32[]{:S(2)}) collective-permute-start(f32[1,2,2,24,64]{4,3,2,1,0:T(8,128)S(1)} %get-tuple-element.40), channel_id=1, source_target_pairs={{0,2},{1,3},{2,0},{3,1},{4,6},{5,7},{6,4},{7,5},{8,10},{9,11},{10,... | collective-permute-start | bytes 73736 | tf_op jit(solution)/shard_map/ppermute | solution.py:43
  180.7 3.4 %collective-permute-start.13 = (f32[2,1,2,2,24,64]{5,4,3,2,0,1:T(8,128)S(1)}, f32[2,1,2,2,24,64]{5,4,3,2,0,1:T(8,128)S(1)}, u32[]{:S(2)}, u32[]{:S(2)}) collective-permute-start(f32[2,1,2,2,24,64]{5,4,3,2,0,1:T(8,128)S(1)} %maximum_select_fusion.15), channel_id=1, source_target_pairs={{0,1},{1,0},{2,3},{3,2},{4,5},{5,4},{6,7},{7,6},{8,9},{9,8},{10,11... | collective-permute-start | bytes 147464 | tf_op jit(solution)/shard_map/ppermute | solution.py:43

commit v12 on v9

--- a/solution.py
+++ b/solution.py
@@ -162,7 +162,9 @@
     live_text = text_pos < lax.dynamic_index_in_dim(txt_len, request, keepdims=False)
     allowed = (within < patches) | live_text
 
-    attended = attend_one(head_queries, keys, values, allowed).reshape(sources, patches, HD)
+    attended = attend_one(head_queries, keys, values, allowed).reshape(
+        sources, patches // 2, 2 * HD
+    )
     attended = lax.all_to_all(attended, ROW, 0, 0, tiled=True)
     attended = jnp.transpose(
         attended.reshape(requests, heads_local, patches, HD), (0, 2, 1, 3)

time: 154 us -> 155 us (level)
    unnamed x17 -> x15, local copies, waits for them, and re-layouts: 5.85 us -> 4.63 us
  transfers between devices with their start and end apart: 11 -> 11, of which waited for: 7 -> 7; matrix products, arithmetic and copies ran while one was open for 28% -> 27% of each run, Pallas kernels for 0% -> 0%
where the time goes in v12:
time: 155 us; the launch traced here: 154 us
  waiting for transfers between devices  49.9 us (32%)
  starting transfers between devices  34.9 us (23%)
  local copies, waits for them, and re-layouts  27.6 us (18%)
  matrix products  15.2 us (10%)
  between operations  14.6 us (9%)
  other arithmetic  12.3 us (8%)
    all_to_all x1, waiting for transfers between devices, per_device(): bundle = lax.all_to_all(bundle, ROW, 0, 0, tiled=True)  21.7 us
    all_to_all x1, starting transfers between devices, per_device(): bundle = lax.all_to_all(bundle, ROW, 0, 0, tiled=True)  13.8 us
    all_to_all x1, waiting for transfers between devices, per_device(): attended = lax.all_to_all(attended, ROW, 0, 0, tiled=True)  13.4 us
    ppermute x6, starting transfers between devices, doubling_gather(): received = lax.ppermute(buffer, axis, pairs)  12.2 us
    ppermute x1, waiting for transfers between devices, halving_scatter(): return keep + lax.ppermute(send, 'col', pairs)  8.93 us
    all_to_all x1, starting transfers between devices, per_device(): attended = lax.all_to_all(attended, ROW, 0, 0, tiled=True)  5.18 us
    dot_general x1, matrix products, per_device(): jnp.einsum('td,cde->cte', flat_rows, qkv_weight, preferred_element_type=j...  4.82 us
    convert_element_type x2, local copies, waits for them, and re-layouts, per_device(): img_full.astype(jnp.float32)  4.77 us
  transfers between devices with their start and end apart: 11, of which 7 were waited for; matrix products, arithmetic and copies ran while one was open for 27% of the time, Pallas kernels for 0%

profile of v12, /device:TPU:1, one launch (start us, length us, event | category | flops | bytes accessed | tf_op | source)
XLA Modules:
  0.0 154.4 jit_solution(5699620904787644947)
XLA Ops:
  9.0 2.6 %collective-permute-start.2 = (bf16[1,80,608]{2,1,0:T(8,128)(2,1)S(1)}, bf16[1,80,608]{2,1,0:T(8,128)(2,1)S(1)}, u32[]{:S(2)}, u32[]{:S(2)}) collective-permute-start(bf16[1,80,608]{2,1,0:T(8,128)(2,1)S(1)} %get-tuple-element.23), channel_id=1, source_target_pairs={{0,2},{1,3},{2,0},{3,1},{4,6},{5,7},{6,4},{7,5},{8,10},{9,11},{10,... | collective-permute-start | bytes 291848 | tf_op jit(solution)/shard_map/ppermute | solution.py:43
  11.6 1.1 fusion.56
  14.6 3.6 %collective-permute-start.3 = (bf16[2,1,80,608]{3,2,0,1:T(8,128)(2,1)S(1)}, bf16[2,1,80,608]{3,2,0,1:T(8,128)(2,1)S(1)}, u32[]{:S(2)}, u32[]{:S(2)}) collective-permute-start(bf16[2,1,80,608]{3,2,0,1:T(8,128)(2,1)S(1)} %maximum_select_fusion.4), channel_id=1, source_target_pairs={{0,1},{1,0},{2,3},{3,2},{4,5},{5,4},{6,7},{7,6},{8,9},{9,8},{10,11... | collective-permute-start | bytes 583688 | tf_op jit(solution)/shard_map/ppermute | solution.py:43
  18.8 2.8 %collective-permute-start.1 = (bf16[2,1,8,24,608]{4,3,2,0,1:T(8,128)(2,1)S(1)}, bf16[2,1,8,24,608]{4,3,2,0,1:T(8,128)(2,1)S(1)}, u32[]{:S(2)}, u32[]{:S(2)}) collective-permute-start(bf16[2,1,8,24,608]{4,3,2,0,1:T(8,128)(2,1)S(1)} %maximum_select_fusion.1), channel_id=1, source_target_pairs={{0,1},{1,0},{2,3},{3,2},{4,5},{5,4},{6,7},{7,6},{8,9},{9,8},{10,11... | collective-permute-start | bytes 1400840 | tf_op jit(solution)/shard_map/ppermute | solution.py:43
  23.5 3.2 %fusion.16 = f32[2,8,2,512]{3,1,0,2:T(8,128)S(1)} fusion(bf16[2,2432,512]{2,1,0:T(8,128)(2,1)} %param.18, bf16[8,2,2432,1]{2,1,0,3:T(2,128)(2,1)S(1)} %fusion.33), kind=kOutput, calls=%fused_computation.18 | convolution fusion | flops 79691776 | bytes 5124096 | tf_op jit(solution)/shard_map/rtd,cde->crte/dot_general | solution.py:134
  28.3 2.5 %copy.92 = f32[8,24,4,608]{3,2,1,0:T(4,128)} copy(f32[8,24,4,608]{3,1,0,2:T(8,128)S(1)} %bitcast_convert_fusion) | data formatting | bytes 3735552 | tf_op jit(solution)/shard_map/convert_element_type | solution.py:123
  30.8 2.2 %reshape.751 = f32[192,2432]{1,0:T(8,128)S(1)} reshape(f32[8,24,4,608]{3,2,1,0:T(4,128)} %copy.92) | data formatting | bytes 3735552 | tf_op jit(solution)/shard_map/convert_element_type | solution.py:123
  33.6 4.8 %convolution_bitcast_fusion = f32[3,192,512]{2,1,0:T(8,128)S(1)} fusion(bf16[3,2432,512]{2,1,0:T(8,128)(2,1)} %param.17, bf16[192,2432]{1,0:T(8,128)(2,1)S(1)} %fusion.15), kind=kOutput, calls=%fused_computation.16 | convolution fusion | flops 1434451968 | bytes 9584640 | tf_op jit(solution)/shard_map/td,cde->cte/dot_general | solution.py:127
  38.7 1.0 convert_element_type.90
  41.9 1.2 fusion.21
  44.4 1.6 %reshape.742 = bf16[64,38,128]{2,1,0:T(8,128)(2,1)} reshape(bf16[64,76,64]{2,1,0:T(8,128)(2,1)S(1)} %copy.111) | data formatting | bytes 1245184 | tf_op jit(solution)/shard_map/reshape | solution.py:150
  46.0 13.8 %all-to-all-start = ((bf16[64,38,128]{2,1,0:T(8,128)(2,1)}), bf16[64,38,128]{2,1,0:T(8,128)(2,1)S(1)}, u32[]{:S(2)}, u32[]{:S(2)}) async-start(bf16[64,38,128]{2,1,0:T(8,128)(2,1)} %reshape.742), calls=%async_computation | async-start | bytes 1310720 | tf_op jit(solution)/shard_map/all_to_all | solution.py:151
  61.0 21.7 %all-to-all-done = bf16[64,38,128]{2,1,0:T(8,128)(2,1)S(1)} async-done(((bf16[64,38,128]{2,1,0:T(8,128)(2,1)}), bf16[64,38,128]{2,1,0:T(8,128)(2,1)S(1)}, u32[]{:S(2)}, u32[]{:S(2)}) %all-to-all-start) | async-done | bytes 622624 | tf_op jit(solution)/shard_map/all_to_all | solution.py:151
  83.5 1.0 fusion.54
  84.5 1.2 reshape.746
  85.9 1.9 %fusion.57 = (f32[1536]{0:T(1024)S(1)}, f32[1536,1664]{1,0:T(8,128)S(1)}) fusion(bf16[1536,64]{1,0:T(8,128)(2,1)S(1)} %bitcast.169, bf16[1664,64]{1,0:T(8,128)(2,1)S(1)} %reshape.745, pred[1664]{0:T(1024)(128)(4,1)S(1)} %fusion.52), kind=kOutput, calls=%fused_computation.121 | convolution fusion | flops 334821888 | bytes 10641024 | tf_op jit(solution)/shard_map/dot_general | solution.py:79
  87.8 1.8 %fusion = f32[1536]{0:T(1024)S(1)} fusion(f32[1536,1664]{1,0:T(8,128)S(1)} %get-tuple-element.31, f32[1536]{0:T(1024)S(1)} %get-tuple-element.30, pred[1664]{0:T(1024)(128)(4,1)S(1)} %fusion.52), kind=kLoop, calls=%fused_computation.2 | loop fusion | flops 7666176 | bytes 10237568 | tf_op jit(solution)/shard_map/reduce_sum | solution.py:83
  89.6 2.4 %fusion.12 = bf16[1536,64]{0,1:T(8,128)(2,1)S(1)} fusion(bf16[1664,64]{1,0:T(8,128)(2,1)S(1)} %reshape.746, f32[1536,1664]{1,0:T(8,128)S(1)} %get-tuple-element.31, f32[1536]{0:T(1024)S(1)} %get-tuple-element.30, pred[1664]{0:T(1024)(128)(4,1)S(1)} %fusion.52, f32[1536]{0:T(1024)S(1)} %fusion), kind=kOutput, calls=%fused_computation.11 | convolution fusion | flops 335020032 | bytes 10647168 | tf_op jit(solution)/shard_map/dot_general | solution.py:84
  93.2 5.2 %all-to-all-start.1 = ((bf16[64,12,128]{2,1,0:T(8,128)(2,1)}), bf16[64,12,128]{2,1,0:T(8,128)(2,1)S(1)}, u32[]{:S(2)}, u32[]{:S(2)}) async-start(bf16[64,12,128]{2,1,0:T(8,128)(2,1)} %reshape.747), calls=%async_computation.1 | async-start | bytes 524288 | tf_op jit(solution)/shard_map/all_to_all | solution.py:168
  98.4 13.4 %all-to-all-done.1 = bf16[64,12,128]{2,1,0:T(8,128)(2,1)S(1)} async-done(((bf16[64,12,128]{2,1,0:T(8,128)(2,1)}), bf16[64,12,128]{2,1,0:T(8,128)(2,1)S(1)}, u32[]{:S(2)}, u32[]{:S(2)}) %all-to-all-start.1) | async-done | bytes 196640 | tf_op jit(solution)/shard_map/all_to_all | solution.py:168
  112.1 1.0 dot_general.26
  113.1 2.8 %reshape.758 = bf16[2432,512,1,1]{1,0,2,3:T(8,128)(2,1)S(1)} reshape(bf16[64,38,512]{2,1,0:T(8,128)(2,1)} %all-gather.3.cloned.1.call-done) | data formatting | bytes 4980736
  115.8 1.9 %fusion.7 = f32[2,2,48,2432]{3,2,1,0:T(8,128)S(1)} fusion(bf16[2,2,48,512]{3,2,1,0:T(8,128)(2,1)} %dot_general.26, bf16[2432,512,1,1]{1,0,2,3:T(8,128)(2,1)S(1)} %reshape.758), kind=kOutput, calls=%fused_computation.8 | convolution fusion | flops 478150656 | bytes 4554752 | tf_op jit(solution)/shard_map/dot_general | solution.py:173
  117.8 1.3 copy-done
  119.1 3.1 %collective-permute-start.4 = (f32[2,48,2432]{2,1,0:T(8,128)S(1)}, f32[2,48,2432]{2,1,0:T(8,128)S(1)}, u32[]{:S(2)}, u32[]{:S(2)}) collective-permute-start(f32[2,48,2432]{2,1,0:T(8,128)S(1)} %dynamic-slice_bitcast_fusion), channel_id=1, source_target_pairs={{0,1},{1,0},{2,3},{3,2},{4,5},{5,4},{6,7},{7,6},{8,9},{9,8},{10,11... | collective-permute-start | bytes 2801672 | tf_op jit(solution)/shard_map/ppermute | solution.py:71
  122.2 2.1 %collective-permute-done.4 = f32[2,48,2432]{2,1,0:T(8,128)S(1)} collective-permute-done((f32[2,48,2432]{2,1,0:T(8,128)S(1)}, f32[2,48,2432]{2,1,0:T(8,128)S(1)}, u32[]{:S(2)}, u32[]{:S(2)}) %collective-permute-start.4) | collective-permute-done | bytes 933920 | tf_op jit(solution)/shard_map/ppermute | solution.py:71
  124.3 1.3 bitcast_add_fusion.1
  127.1 1.0 dynamic-slice_bitcast_fusion.3
  129.6 8.9 %collective-permute-done.5 = f32[48,2432]{1,0:T(8,128)S(1)} collective-permute-done((f32[48,2432]{1,0:T(8,128)}, f32[48,2432]{1,0:T(8,128)S(1)}, u32[]{:S(2)}, u32[]{:S(2)}) %collective-permute-start.5) | collective-permute-done | bytes 466976 | tf_op jit(solution)/shard_map/ppermute | solution.py:75
  139.4 1.0 add_bitcast_fusion.1
  141.2 2.3 %collective-permute-done.6 = f32[1,2,2,24,64]{4,3,2,1,0:T(8,128)S(1)} collective-permute-done((f32[1,2,2,24,64]{4,3,2,1,0:T(8,128)S(1)}, f32[1,2,2,24,64]{4,3,2,1,0:T(8,128)S(1)}, u32[]{:S(2)}, u32[]{:S(2)}) %collective-permute-start.6) | collective-permute-done | bytes 24608 | tf_op jit(solution)/shard_map/ppermute | solution.py:43
  143.5 2.4 %collective-permute-start.7 = (f32[2,1,2,2,24,64]{5,4,3,2,0,1:T(8,128)S(1)}, f32[2,1,2,2,24,64]{5,4,3,2,0,1:T(8,128)S(1)}, u32[]{:S(2)}, u32[]{:S(2)}) collective-permute-start(f32[2,1,2,2,24,64]{5,4,3,2,0,1:T(8,128)S(1)} %maximum_select_fusion.6), channel_id=1, source_target_pairs={{0,1},{1,0},{2,3},{3,2},{4,5},{5,4},{6,7},{7,6},{8,9},{9,8},{10,11... | collective-permute-start | bytes 147464 | tf_op jit(solution)/shard_map/ppermute | solution.py:43
  (108 shorter events, 21.7 us)
Async XLA Ops:
  7.2 11.5 %copy-start.4 = (bf16[8,24,608]{2,1,0:T(8,128)(2,1)S(1)}, bf16[8,24,608]{2,1,0:T(8,128)(2,1)}, u32[]{:S(2)}) copy-start(bf16[8,24,608]{2,1,0:T(8,128)(2,1)} %param.12) | copy-start | bytes 700420
  7.2 105.9 %all-gather.3.cloned.1.call-start = ((), (), s32[]{:S(2)}) async-start(), calls=%async_computation.2 | async-start | bytes 2662400 | tf_op jit(solution)/shard_map/all_gather | solution.py:109
  9.0 5.6 %collective-permute-start.2 = (bf16[1,80,608]{2,1,0:T(8,128)(2,1)S(1)}, bf16[1,80,608]{2,1,0:T(8,128)(2,1)S(1)}, u32[]{:S(2)}, u32[]{:S(2)}) collective-permute-start(bf16[1,80,608]{2,1,0:T(8,128)(2,1)S(1)} %get-tuple-element.23), channel_id=1, source_target_pairs={{0,2},{1,3},{2,0},{3,1},{4,6},{5,7},{6,4},{7,5},{8,10},{9,11},{10,... | collective-permute-start | bytes 291848 | tf_op jit(solution)/shard_map/ppermute | solution.py:43
  11.5 7.2 %collective-permute-start = (bf16[1,8,24,608]{3,2,1,0:T(8,128)(2,1)}, bf16[1,8,24,608]{3,2,1,0:T(8,128)(2,1)S(1)}, u32[]{:S(2)}, u32[]{:S(2)}) collective-permute-start(bf16[1,8,24,608]{3,2,1,0:T(8,128)(2,1)} %bitcast.178), channel_id=1, source_target_pairs={{0,2},{1,3},{2,0},{3,1},{4,6},{5,7},{6,4},{7,5},{8,10},{9,11},{10,... | collective-permute-start | bytes 700424 | tf_op jit(solution)/shard_map/ppermute | solution.py:43
  14.6 7.1 %collective-permute-start.3 = (bf16[2,1,80,608]{3,2,0,1:T(8,128)(2,1)S(1)}, bf16[2,1,80,608]{3,2,0,1:T(8,128)(2,1)S(1)}, u32[]{:S(2)}, u32[]{:S(2)}) collective-permute-start(bf16[2,1,80,608]{3,2,0,1:T(8,128)(2,1)S(1)} %maximum_select_fusion.4), channel_id=1, source_target_pairs={{0,1},{1,0},{2,3},{3,2},{4,5},{5,4},{6,7},{7,6},{8,9},{9,8},{10,11... | collective-permute-start | bytes 583688 | tf_op jit(solution)/shard_map/ppermute | solution.py:43
  18.8 8.3 %collective-permute-start.1 = (bf16[2,1,8,24,608]{4,3,2,0,1:T(8,128)(2,1)S(1)}, bf16[2,1,8,24,608]{4,3,2,0,1:T(8,128)(2,1)S(1)}, u32[]{:S(2)}, u32[]{:S(2)}) collective-permute-start(bf16[2,1,8,24,608]{4,3,2,0,1:T(8,128)(2,1)S(1)} %maximum_select_fusion.1), channel_id=1, source_target_pairs={{0,1},{1,0},{2,3},{3,2},{4,5},{5,4},{6,7},{7,6},{8,9},{9,8},{10,11... | collective-permute-start | bytes 1400840 | tf_op jit(solution)/shard_map/ppermute | solution.py:43
  21.9 0.8 copy-start.2
  41.3 1.8 %copy-start.1 = (bf16[8,24,8,64]{3,2,1,0:T(8,128)(2,1)S(1)}, bf16[8,24,8,64]{3,2,1,0:T(8,128)(2,1)}, u32[]{:S(2)}) copy-start(bf16[8,24,8,64]{3,2,1,0:T(8,128)(2,1)} %convert_element_type.90) | copy-start | bytes 589828
  43.5 16.2 %copy-start.6 = (s32[8]{0:T(128)S(1)}, s32[8]{0:T(128)}, u32[]{:S(2)}) copy-start(s32[8]{0:T(128)} %param.22) | copy-start | bytes 100
  46.0 36.7 %all-to-all-start = ((bf16[64,38,128]{2,1,0:T(8,128)(2,1)}), bf16[64,38,128]{2,1,0:T(8,128)(2,1)S(1)}, u32[]{:S(2)}, u32[]{:S(2)}) async-start(bf16[64,38,128]{2,1,0:T(8,128)(2,1)} %reshape.742), calls=%async_computation | async-start | bytes 1310720 | tf_op jit(solution)/shard_map/all_to_all | solution.py:151
  93.2 18.6 %all-to-all-start.1 = ((bf16[64,12,128]{2,1,0:T(8,128)(2,1)}), bf16[64,12,128]{2,1,0:T(8,128)(2,1)S(1)}, u32[]{:S(2)}, u32[]{:S(2)}) async-start(bf16[64,12,128]{2,1,0:T(8,128)(2,1)} %reshape.747), calls=%async_computation.1 | async-start | bytes 524288 | tf_op jit(solution)/shard_map/all_to_all | solution.py:168
  117.7 1.3 copy-start
  119.0 8.0 %copy-start.5 = (s32[8]{0:T(128)S(1)}, s32[8]{0:T(128)}, u32[]{:S(2)}) copy-start(s32[8]{0:T(128)} %param.23) | copy-start | bytes 100
  119.1 5.2 %collective-permute-start.4 = (f32[2,48,2432]{2,1,0:T(8,128)S(1)}, f32[2,48,2432]{2,1,0:T(8,128)S(1)}, u32[]{:S(2)}, u32[]{:S(2)}) collective-permute-start(f32[2,48,2432]{2,1,0:T(8,128)S(1)} %dynamic-slice_bitcast_fusion), channel_id=1, source_target_pairs={{0,1},{1,0},{2,3},{3,2},{4,5},{5,4},{6,7},{7,6},{8,9},{9,8},{10,11... | collective-permute-start | bytes 2801672 | tf_op jit(solution)/shard_map/ppermute | solution.py:71
  126.4 12.1 %collective-permute-start.5 = (f32[48,2432]{1,0:T(8,128)}, f32[48,2432]{1,0:T(8,128)S(1)}, u32[]{:S(2)}, u32[]{:S(2)}) collective-permute-start(f32[48,2432]{1,0:T(8,128)} %dynamic-slice_bitcast_fusion.1), channel_id=1, source_target_pairs={{0,2},{1,3},{2,0},{3,1},{4,6},{5,7},{6,4},{7,5},{8,10},{9,11},{10,... | collective-permute-start | bytes 1400840 | tf_op jit(solution)/shard_map/ppermute | solution.py:75
  129.6 9.8 %copy-start.3 = (bf16[2,2,80,608]{3,2,1,0:T(8,128)(2,1)S(1)}, bf16[2,2,80,608]{3,2,1,0:T(8,128)(2,1)}, u32[]{:S(2)}) copy-start(bf16[2,2,80,608]{3,2,1,0:T(8,128)(2,1)} %copy-done.2) | copy-start | bytes 1167364
  140.4 3.0 %collective-permute-start.6 = (f32[1,2,2,24,64]{4,3,2,1,0:T(8,128)S(1)}, f32[1,2,2,24,64]{4,3,2,1,0:T(8,128)S(1)}, u32[]{:S(2)}, u32[]{:S(2)}) collective-permute-start(f32[1,2,2,24,64]{4,3,2,1,0:T(8,128)S(1)} %get-tuple-element.26), channel_id=1, source_target_pairs={{0,2},{1,3},{2,0},{3,1},{4,6},{5,7},{6,4},{7,5},{8,10},{9,11},{10,... | collective-permute-start | bytes 73736 | tf_op jit(solution)/shard_map/ppermute | solution.py:43
  143.5 3.4 %collective-permute-start.7 = (f32[2,1,2,2,24,64]{5,4,3,2,0,1:T(8,128)S(1)}, f32[2,1,2,2,24,64]{5,4,3,2,0,1:T(8,128)S(1)}, u32[]{:S(2)}, u32[]{:S(2)}) collective-permute-start(f32[2,1,2,2,24,64]{5,4,3,2,0,1:T(8,128)S(1)} %maximum_select_fusion.6), channel_id=1, source_target_pairs={{0,1},{1,0},{2,3},{3,2},{4,5},{5,4},{6,7},{7,6},{8,9},{9,8},{10,11... | collective-permute-start | bytes 147464 | tf_op jit(solution)/shard_map/ppermute | solution.py:43
Sparse Core Ops, SparseCore 0:
  11.8 86.0 all-gather.2

commit v13 on v9

--- a/solution.py
+++ b/solution.py
@@ -72,7 +72,8 @@
     keep = lax.dynamic_index_in_dim(halves, high, 0, keepdims=False)
     send = lax.dynamic_index_in_dim(halves, 1 - high, 0, keepdims=False)
     pairs = [(i, i ^ 2) for i in range(cols)]
-    return keep + lax.ppermute(send, "col", pairs)
+    received = lax.ppermute(send.astype(jnp.bfloat16), "col", pairs)
+    return keep + received.astype(jnp.float32)
 
 
 def attend_one(queries, keys, values, allowed):

time: 154 us -> 148 us (0.961)
  waiting for transfers between devices: 48.4 us -> 43.2 us
    ppermute x1, waiting for transfers between devices: 8.77 us -> 3.64 us  [halving_scatter(): received = lax.ppermute(send.astype(jnp.bfloat16), 'col', pairs)]
  transfers between devices with their start and end apart: 11 -> 11, of which waited for: 7 -> 7; matrix products, arithmetic and copies ran while one was open for 28% -> 29% of each run, Pallas kernels for 0% -> 0%
where the time goes in v13:
time: 148 us
  waiting for transfers between devices  43.2 us (29%)
  starting transfers between devices  35.3 us (24%)
  local copies, waits for them, and re-layouts  26.9 us (18%)
  matrix products  15.2 us (10%)
  between operations  14.6 us (10%)
  other arithmetic  12.3 us (8%)
    all_to_all x1, waiting for transfers between devices, per_device(): bundle = lax.all_to_all(bundle, ROW, 0, 0, tiled=True)  21.7 us
    all_to_all x1, starting transfers between devices, per_device(): bundle = lax.all_to_all(bundle, ROW, 0, 0, tiled=True)  13.8 us
    ppermute x6, starting transfers between devices, doubling_gather(): received = lax.ppermute(buffer, axis, pairs)  12.4 us
    all_to_all x1, waiting for transfers between devices, per_device(): attended = lax.all_to_all(attended, ROW, 0, 0, tiled=True)  12.3 us
    unnamed x17, local copies, waits for them, and re-layouts  5.86 us
    all_to_all x1, starting transfers between devices, per_device(): attended = lax.all_to_all(attended, ROW, 0, 0, tiled=True)  5.18 us
    dot_general x1, matrix products, per_device(): jnp.einsum('td,cde->cte', flat_rows, qkv_weight, preferred_element_type=j...  4.82 us
    convert_element_type x2, local copies, waits for them, and re-layouts, per_device(): img_full.astype(jnp.float32)  4.77 us
  transfers between devices with their start and end apart: 11, of which 7 were waited for; matrix products, arithmetic and copies ran while one was open for 29% of the time, Pallas kernels for 0%

profile of v13, /device:TPU:1, one launch (start us, length us, event | category | flops | bytes accessed | tf_op | source)
XLA Modules:
  0.0 147.6 jit_solution(15090746736018762126)
XLA Ops:
  9.0 2.6 %collective-permute-start.2 = (bf16[1,80,608]{2,1,0:T(8,128)(2,1)S(1)}, bf16[1,80,608]{2,1,0:T(8,128)(2,1)S(1)}, u32[]{:S(2)}, u32[]{:S(2)}) collective-permute-start(bf16[1,80,608]{2,1,0:T(8,128)(2,1)S(1)} %get-tuple-element.23), channel_id=1, source_target_pairs={{0,2},{1,3},{2,0},{3,1},{4,6},{5,7},{6,4},{7,5},{8,10},{9,11},{10,... | collective-permute-start | bytes 291848 | tf_op jit(solution)/shard_map/ppermute | solution.py:43
  11.6 1.1 fusion.57
  14.6 3.6 %collective-permute-start.3 = (bf16[2,1,80,608]{3,2,0,1:T(8,128)(2,1)S(1)}, bf16[2,1,80,608]{3,2,0,1:T(8,128)(2,1)S(1)}, u32[]{:S(2)}, u32[]{:S(2)}) collective-permute-start(bf16[2,1,80,608]{3,2,0,1:T(8,128)(2,1)S(1)} %maximum_select_fusion.4), channel_id=1, source_target_pairs={{0,1},{1,0},{2,3},{3,2},{4,5},{5,4},{6,7},{7,6},{8,9},{9,8},{10,11... | collective-permute-start | bytes 583688 | tf_op jit(solution)/shard_map/ppermute | solution.py:43
  18.8 2.8 %collective-permute-start.1 = (bf16[2,1,8,24,608]{4,3,2,0,1:T(8,128)(2,1)S(1)}, bf16[2,1,8,24,608]{4,3,2,0,1:T(8,128)(2,1)S(1)}, u32[]{:S(2)}, u32[]{:S(2)}) collective-permute-start(bf16[2,1,8,24,608]{4,3,2,0,1:T(8,128)(2,1)S(1)} %maximum_select_fusion.1), channel_id=1, source_target_pairs={{0,1},{1,0},{2,3},{3,2},{4,5},{5,4},{6,7},{7,6},{8,9},{9,8},{10,11... | collective-permute-start | bytes 1400840 | tf_op jit(solution)/shard_map/ppermute | solution.py:43
  23.5 3.2 %fusion.16 = f32[2,8,2,512]{3,1,0,2:T(8,128)S(1)} fusion(bf16[2,2432,512]{2,1,0:T(8,128)(2,1)} %param.18, bf16[8,2,2432,1]{2,1,0,3:T(2,128)(2,1)S(1)} %fusion.34), kind=kOutput, calls=%fused_computation.18 | convolution fusion | flops 79691776 | bytes 5124096 | tf_op jit(solution)/shard_map/rtd,cde->crte/dot_general | solution.py:135
  28.3 2.5 %copy.93 = f32[8,24,4,608]{3,2,1,0:T(4,128)} copy(f32[8,24,4,608]{3,1,0,2:T(8,128)S(1)} %bitcast_convert_fusion) | data formatting | bytes 3735552 | tf_op jit(solution)/shard_map/convert_element_type | solution.py:124
  30.8 2.2 %reshape.752 = f32[192,2432]{1,0:T(8,128)S(1)} reshape(f32[8,24,4,608]{3,2,1,0:T(4,128)} %copy.93) | data formatting | bytes 3735552 | tf_op jit(solution)/shard_map/convert_element_type | solution.py:124
  33.6 4.8 %convolution_bitcast_fusion = f32[3,192,512]{2,1,0:T(8,128)S(1)} fusion(bf16[3,2432,512]{2,1,0:T(8,128)(2,1)} %param.17, bf16[192,2432]{1,0:T(8,128)(2,1)S(1)} %fusion.15), kind=kOutput, calls=%fused_computation.16 | convolution fusion | flops 1434451968 | bytes 9584640 | tf_op jit(solution)/shard_map/td,cde->cte/dot_general | solution.py:128
  38.7 1.0 convert_element_type.99
  41.9 1.2 fusion.21
  44.4 1.6 %reshape.743 = bf16[64,38,128]{2,1,0:T(8,128)(2,1)} reshape(bf16[64,76,64]{2,1,0:T(8,128)(2,1)S(1)} %copy.112) | data formatting | bytes 1245184 | tf_op jit(solution)/shard_map/reshape | solution.py:151
  46.0 13.8 %all-to-all-start = ((bf16[64,38,128]{2,1,0:T(8,128)(2,1)}), bf16[64,38,128]{2,1,0:T(8,128)(2,1)S(1)}, u32[]{:S(2)}, u32[]{:S(2)}) async-start(bf16[64,38,128]{2,1,0:T(8,128)(2,1)} %reshape.743), calls=%async_computation | async-start | bytes 1310720 | tf_op jit(solution)/shard_map/all_to_all | solution.py:152
  61.0 21.7 %all-to-all-done = bf16[64,38,128]{2,1,0:T(8,128)(2,1)S(1)} async-done(((bf16[64,38,128]{2,1,0:T(8,128)(2,1)}), bf16[64,38,128]{2,1,0:T(8,128)(2,1)S(1)}, u32[]{:S(2)}, u32[]{:S(2)}) %all-to-all-start) | async-done | bytes 622624 | tf_op jit(solution)/shard_map/all_to_all | solution.py:152
  83.5 1.0 fusion.55
  84.5 1.2 reshape.747
  85.9 1.9 %fusion.58 = (f32[1536]{0:T(1024)S(1)}, f32[1536,1664]{1,0:T(8,128)S(1)}) fusion(bf16[1536,64]{1,0:T(8,128)(2,1)S(1)} %bitcast.173, bf16[1664,64]{1,0:T(8,128)(2,1)S(1)} %reshape.746, pred[1664]{0:T(1024)(128)(4,1)S(1)} %fusion.53), kind=kOutput, calls=%fused_computation.123 | convolution fusion | flops 334821888 | bytes 10641024 | tf_op jit(solution)/shard_map/dot_general | solution.py:80
  87.8 1.8 %fusion = f32[1536]{0:T(1024)S(1)} fusion(f32[1536,1664]{1,0:T(8,128)S(1)} %get-tuple-element.31, f32[1536]{0:T(1024)S(1)} %get-tuple-element.30, pred[1664]{0:T(1024)(128)(4,1)S(1)} %fusion.53), kind=kLoop, calls=%fused_computation.2 | loop fusion | flops 7666176 | bytes 10237568 | tf_op jit(solution)/shard_map/reduce_sum | solution.py:84
  89.6 2.4 %fusion.12 = bf16[1536,64]{0,1:T(8,128)(2,1)S(1)} fusion(bf16[1664,64]{1,0:T(8,128)(2,1)S(1)} %reshape.747, f32[1536,1664]{1,0:T(8,128)S(1)} %get-tuple-element.31, f32[1536]{0:T(1024)S(1)} %get-tuple-element.30, pred[1664]{0:T(1024)(128)(4,1)S(1)} %fusion.53, f32[1536]{0:T(1024)S(1)} %fusion), kind=kOutput, calls=%fused_computation.11 | convolution fusion | flops 335020032 | bytes 10647168 | tf_op jit(solution)/shard_map/dot_general | solution.py:85
  93.2 5.2 %all-to-all-start.1 = ((bf16[64,2,768]{2,1,0:T(2,128)(2,1)}), bf16[64,2,768]{2,1,0:T(2,128)(2,1)S(1)}, u32[]{:S(2)}, u32[]{:S(2)}) async-start(bf16[64,2,768]{2,1,0:T(2,128)(2,1)} %reshape.763), calls=%async_computation.1 | async-start | bytes 393216 | tf_op jit(solution)/shard_map/all_to_all | solution.py:167
  98.4 12.3 %all-to-all-done.1 = bf16[64,2,768]{2,1,0:T(2,128)(2,1)S(1)} async-done(((bf16[64,2,768]{2,1,0:T(2,128)(2,1)}), bf16[64,2,768]{2,1,0:T(2,128)(2,1)S(1)}, u32[]{:S(2)}, u32[]{:S(2)}) %all-to-all-start.1) | async-done | bytes 196640 | tf_op jit(solution)/shard_map/all_to_all | solution.py:167
  112.1 2.8 %reshape.759 = bf16[2432,512,1,1]{1,0,2,3:T(8,128)(2,1)S(1)} reshape(bf16[64,38,512]{2,1,0:T(8,128)(2,1)} %all-gather.3.cloned.1.call-done) | data formatting | bytes 4980736
  114.9 1.9 %fusion.7 = f32[2,2,48,2432]{3,2,1,0:T(8,128)S(1)} fusion(bf16[2,2,48,512]{3,2,1,0:T(8,128)(2,1)} %dot_general.26, bf16[2432,512,1,1]{1,0,2,3:T(8,128)(2,1)S(1)} %reshape.759), kind=kOutput, calls=%fused_computation.8 | convolution fusion | flops 478150656 | bytes 4554752 | tf_op jit(solution)/shard_map/dot_general | solution.py:172
  116.8 1.3 copy-done
  118.1 2.9 %collective-permute-start.4 = (f32[2,48,2432]{2,1,0:T(8,128)S(1)}, f32[2,48,2432]{2,1,0:T(8,128)S(1)}, u32[]{:S(2)}, u32[]{:S(2)}) collective-permute-start(f32[2,48,2432]{2,1,0:T(8,128)S(1)} %dynamic-slice_bitcast_fusion), channel_id=1, source_target_pairs={{0,1},{1,0},{2,3},{3,2},{4,5},{5,4},{6,7},{7,6},{8,9},{9,8},{10,11... | collective-permute-start | bytes 2801672 | tf_op jit(solution)/shard_map/ppermute | solution.py:71
  121.0 2.0 %collective-permute-done.4 = f32[2,48,2432]{2,1,0:T(8,128)S(1)} collective-permute-done((f32[2,48,2432]{2,1,0:T(8,128)S(1)}, f32[2,48,2432]{2,1,0:T(8,128)S(1)}, u32[]{:S(2)}, u32[]{:S(2)}) %collective-permute-start.4) | collective-permute-done | bytes 933920 | tf_op jit(solution)/shard_map/ppermute | solution.py:71
  123.1 1.3 bitcast_add_fusion.1
  124.4 1.1 collective-permute-start.5
  125.5 1.0 dynamic-slice_bitcast_fusion.2
  128.0 3.6 %collective-permute-done.5 = bf16[48,2432]{1,0:T(8,128)(2,1)S(1)} collective-permute-done((bf16[48,2432]{1,0:T(8,128)(2,1)S(1)}, bf16[48,2432]{1,0:T(8,128)(2,1)S(1)}, u32[]{:S(2)}, u32[]{:S(2)}) %collective-permute-start.5) | collective-permute-done | bytes 233504 | tf_op jit(solution)/shard_map/ppermute | solution.py:75
  132.6 1.0 add_bitcast_fusion.1
  134.5 2.1 %collective-permute-done.6 = f32[1,2,2,24,64]{4,3,2,1,0:T(8,128)S(1)} collective-permute-done((f32[1,2,2,24,64]{4,3,2,1,0:T(8,128)S(1)}, f32[1,2,2,24,64]{4,3,2,1,0:T(8,128)S(1)}, u32[]{:S(2)}, u32[]{:S(2)}) %collective-permute-start.6) | collective-permute-done | bytes 24608 | tf_op jit(solution)/shard_map/ppermute | solution.py:43
  136.6 2.4 %collective-permute-start.7 = (f32[2,1,2,2,24,64]{5,4,3,2,0,1:T(8,128)S(1)}, f32[2,1,2,2,24,64]{5,4,3,2,0,1:T(8,128)S(1)}, u32[]{:S(2)}, u32[]{:S(2)}) collective-permute-start(f32[2,1,2,2,24,64]{5,4,3,2,0,1:T(8,128)S(1)} %maximum_select_fusion.6), channel_id=1, source_target_pairs={{0,1},{1,0},{2,3},{3,2},{4,5},{5,4},{6,7},{7,6},{8,9},{9,8},{10,11... | collective-permute-start | bytes 147464 | tf_op jit(solution)/shard_map/ppermute | solution.py:43
  (108 shorter events, 21.6 us)
Async XLA Ops:
  7.2 11.5 %copy-start.4 = (bf16[8,24,608]{2,1,0:T(8,128)(2,1)S(1)}, bf16[8,24,608]{2,1,0:T(8,128)(2,1)}, u32[]{:S(2)}) copy-start(bf16[8,24,608]{2,1,0:T(8,128)(2,1)} %param.12) | copy-start | bytes 700420
  7.2 104.9 %all-gather.3.cloned.1.call-start = ((), (), s32[]{:S(2)}) async-start(), calls=%async_computation.2 | async-start | bytes 2662400 | tf_op jit(solution)/shard_map/all_gather | solution.py:110
  9.0 5.6 %collective-permute-start.2 = (bf16[1,80,608]{2,1,0:T(8,128)(2,1)S(1)}, bf16[1,80,608]{2,1,0:T(8,128)(2,1)S(1)}, u32[]{:S(2)}, u32[]{:S(2)}) collective-permute-start(bf16[1,80,608]{2,1,0:T(8,128)(2,1)S(1)} %get-tuple-element.23), channel_id=1, source_target_pairs={{0,2},{1,3},{2,0},{3,1},{4,6},{5,7},{6,4},{7,5},{8,10},{9,11},{10,... | collective-permute-start | bytes 291848 | tf_op jit(solution)/shard_map/ppermute | solution.py:43
  11.5 7.2 %collective-permute-start = (bf16[1,8,24,608]{3,2,1,0:T(8,128)(2,1)}, bf16[1,8,24,608]{3,2,1,0:T(8,128)(2,1)S(1)}, u32[]{:S(2)}, u32[]{:S(2)}) collective-permute-start(bf16[1,8,24,608]{3,2,1,0:T(8,128)(2,1)} %bitcast.184), channel_id=1, source_target_pairs={{0,2},{1,3},{2,0},{3,1},{4,6},{5,7},{6,4},{7,5},{8,10},{9,11},{10,... | collective-permute-start | bytes 700424 | tf_op jit(solution)/shard_map/ppermute | solution.py:43
  14.6 7.1 %collective-permute-start.3 = (bf16[2,1,80,608]{3,2,0,1:T(8,128)(2,1)S(1)}, bf16[2,1,80,608]{3,2,0,1:T(8,128)(2,1)S(1)}, u32[]{:S(2)}, u32[]{:S(2)}) collective-permute-start(bf16[2,1,80,608]{3,2,0,1:T(8,128)(2,1)S(1)} %maximum_select_fusion.4), channel_id=1, source_target_pairs={{0,1},{1,0},{2,3},{3,2},{4,5},{5,4},{6,7},{7,6},{8,9},{9,8},{10,11... | collective-permute-start | bytes 583688 | tf_op jit(solution)/shard_map/ppermute | solution.py:43
  18.8 8.3 %collective-permute-start.1 = (bf16[2,1,8,24,608]{4,3,2,0,1:T(8,128)(2,1)S(1)}, bf16[2,1,8,24,608]{4,3,2,0,1:T(8,128)(2,1)S(1)}, u32[]{:S(2)}, u32[]{:S(2)}) collective-permute-start(bf16[2,1,8,24,608]{4,3,2,0,1:T(8,128)(2,1)S(1)} %maximum_select_fusion.1), channel_id=1, source_target_pairs={{0,1},{1,0},{2,3},{3,2},{4,5},{5,4},{6,7},{7,6},{8,9},{9,8},{10,11... | collective-permute-start | bytes 1400840 | tf_op jit(solution)/shard_map/ppermute | solution.py:43
  21.9 0.8 copy-start.2
  41.3 1.8 %copy-start.1 = (bf16[8,24,8,64]{3,2,1,0:T(8,128)(2,1)S(1)}, bf16[8,24,8,64]{3,2,1,0:T(8,128)(2,1)}, u32[]{:S(2)}) copy-start(bf16[8,24,8,64]{3,2,1,0:T(8,128)(2,1)} %convert_element_type.99) | copy-start | bytes 589828
  43.5 16.2 %copy-start.6 = (s32[8]{0:T(128)S(1)}, s32[8]{0:T(128)}, u32[]{:S(2)}) copy-start(s32[8]{0:T(128)} %param.22) | copy-start | bytes 100
  46.0 36.7 %all-to-all-start = ((bf16[64,38,128]{2,1,0:T(8,128)(2,1)}), bf16[64,38,128]{2,1,0:T(8,128)(2,1)S(1)}, u32[]{:S(2)}, u32[]{:S(2)}) async-start(bf16[64,38,128]{2,1,0:T(8,128)(2,1)} %reshape.743), calls=%async_computation | async-start | bytes 1310720 | tf_op jit(solution)/shard_map/all_to_all | solution.py:152
  93.2 17.5 %all-to-all-start.1 = ((bf16[64,2,768]{2,1,0:T(2,128)(2,1)}), bf16[64,2,768]{2,1,0:T(2,128)(2,1)S(1)}, u32[]{:S(2)}, u32[]{:S(2)}) async-start(bf16[64,2,768]{2,1,0:T(2,128)(2,1)} %reshape.763), calls=%async_computation.1 | async-start | bytes 393216 | tf_op jit(solution)/shard_map/all_to_all | solution.py:167
  114.8 6.1 %copy-start.5 = (s32[8]{0:T(128)S(1)}, s32[8]{0:T(128)}, u32[]{:S(2)}) copy-start(s32[8]{0:T(128)} %param.23) | copy-start | bytes 100
  116.8 1.3 copy-start
  118.1 5.0 %collective-permute-start.4 = (f32[2,48,2432]{2,1,0:T(8,128)S(1)}, f32[2,48,2432]{2,1,0:T(8,128)S(1)}, u32[]{:S(2)}, u32[]{:S(2)}) collective-permute-start(f32[2,48,2432]{2,1,0:T(8,128)S(1)} %dynamic-slice_bitcast_fusion), channel_id=1, source_target_pairs={{0,1},{1,0},{2,3},{3,2},{4,5},{5,4},{6,7},{7,6},{8,9},{9,8},{10,11... | collective-permute-start | bytes 2801672 | tf_op jit(solution)/shard_map/ppermute | solution.py:71
  124.4 7.3 %collective-permute-start.5 = (bf16[48,2432]{1,0:T(8,128)(2,1)S(1)}, bf16[48,2432]{1,0:T(8,128)(2,1)S(1)}, u32[]{:S(2)}, u32[]{:S(2)}) collective-permute-start(bf16[48,2432]{1,0:T(8,128)(2,1)S(1)} %fusion.26), channel_id=1, source_target_pairs={{0,2},{1,3},{2,0},{3,1},{4,6},{5,7},{6,4},{7,5},{8,10},{9,11},{10,... | collective-permute-start | bytes 700424 | tf_op jit(solution)/shard_map/ppermute | solution.py:75
  128.0 4.6 %copy-start.3 = (bf16[2,2,80,608]{3,2,1,0:T(8,128)(2,1)S(1)}, bf16[2,2,80,608]{3,2,1,0:T(8,128)(2,1)}, u32[]{:S(2)}) copy-start(bf16[2,2,80,608]{3,2,1,0:T(8,128)(2,1)} %copy-done.2) | copy-start | bytes 1167364
  133.6 3.0 %collective-permute-start.6 = (f32[1,2,2,24,64]{4,3,2,1,0:T(8,128)S(1)}, f32[1,2,2,24,64]{4,3,2,1,0:T(8,128)S(1)}, u32[]{:S(2)}, u32[]{:S(2)}) collective-permute-start(f32[1,2,2,24,64]{4,3,2,1,0:T(8,128)S(1)} %get-tuple-element.26), channel_id=1, source_target_pairs={{0,2},{1,3},{2,0},{3,1},{4,6},{5,7},{6,4},{7,5},{8,10},{9,11},{10,... | collective-permute-start | bytes 73736 | tf_op jit(solution)/shard_map/ppermute | solution.py:43
  136.6 3.4 %collective-permute-start.7 = (f32[2,1,2,2,24,64]{5,4,3,2,0,1:T(8,128)S(1)}, f32[2,1,2,2,24,64]{5,4,3,2,0,1:T(8,128)S(1)}, u32[]{:S(2)}, u32[]{:S(2)}) collective-permute-start(f32[2,1,2,2,24,64]{5,4,3,2,0,1:T(8,128)S(1)} %maximum_select_fusion.6), channel_id=1, source_target_pairs={{0,1},{1,0},{2,3},{3,2},{4,5},{5,4},{6,7},{7,6},{8,9},{9,8},{10,11... | collective-permute-start | bytes 147464 | tf_op jit(solution)/shard_map/ppermute | solution.py:43
Sparse Core Ops, SparseCore 0:
  11.8 86.0 all-gather.2

commit v14 on v13

--- a/solution.py
+++ b/solution.py
@@ -165,16 +165,12 @@
 
     attended = attend_one(head_queries, keys, values, allowed).reshape(sources, patches, HD)
     attended = lax.all_to_all(attended, ROW, 0, 0, tiled=True)
-    attended = jnp.transpose(
-        attended.reshape(requests, heads_local, patches, HD), (0, 2, 1, 3)
-    ).reshape(requests * patches, cols_local)
-
-    partial_value = lax.dot_general(
-        attended,
-        weight_t,
-        (((1,), (1,)), ((), ())),
+    partial_value = jnp.einsum(
+        "rhtd,nhd->rtn",
+        attended.reshape(requests, heads_local, patches, HD),
+        weight_t.reshape(-1, heads_local, HD),
         preferred_element_type=jnp.float32,
-    )
+    ).reshape(requests * patches, -1)
     cols = lax.axis_size("col")
     col_index = lax.axis_index("col")
     shared_sum = halving_scatter(partial_value, cols, col_index)

time: 148 us -> 155 us (1.047)
  local copies, waits for them, and re-layouts: 26.9 us -> 31.2 us
  starting transfers between devices: 35.3 us -> 32.3 us
  waiting for transfers between devices: 43.2 us -> 45.7 us
  matrix products: 15.2 us -> 17.5 us
    reshape x0 -> x1, local copies, waits for them, and re-layouts: none -> 7.36 us  [per_device(): weight_t.reshape(-1, heads_local, HD)]
    ppermute x6, starting transfers between devices: 12.4 us -> 8.35 us  [doubling_gather(): received = lax.ppermute(buffer, axis, pairs)]
    unnamed x17 -> x14, local copies, waits for them, and re-layouts: 5.86 us -> 3.08 us
    ppermute x6, waiting for transfers between devices: 3.49 us -> 6.23 us  [doubling_gather(): received = lax.ppermute(buffer, axis, pairs)]
    dot_general x1, matrix products: 1.9 us -> 4.2 us  [per_device(): jnp.einsum('rhtd,nhd->rtn', attended.reshape(requests, heads_local, patch...]
    all_to_all x1, starting transfers between devices: 5.18 us -> 6.77 us  [per_device(): attended = lax.all_to_all(attended, ROW, 0, 0, tiled=True)]
  transfers between devices with their start and end apart: 11 -> 11, of which waited for: 7 -> 8; matrix products, arithmetic and copies ran while one was open for 29% -> 27% of each run, Pallas kernels for 0% -> 0%
where the time goes in v14:
time: 155 us; the launch traced here: 154 us
  waiting for transfers between devices  45.7 us (29%)
  starting transfers between devices  32.3 us (21%)
  local copies, waits for them, and re-layouts  31.2 us (20%)
  matrix products  17.5 us (11%)
  between operations  14.6 us (9%)
  other arithmetic  12.4 us (8%)
    all_to_all x1, waiting for transfers between devices, per_device(): bundle = lax.all_to_all(bundle, ROW, 0, 0, tiled=True)  20.6 us
    all_to_all x1, starting transfers between devices, per_device(): bundle = lax.all_to_all(bundle, ROW, 0, 0, tiled=True)  14.3 us
    all_to_all x1, waiting for transfers between devices, per_device(): attended = lax.all_to_all(attended, ROW, 0, 0, tiled=True)  12.4 us
    ppermute x6, starting transfers between devices, doubling_gather(): received = lax.ppermute(buffer, axis, pairs)  8.35 us
    reshape x1, local copies, waits for them, and re-layouts, per_device(): weight_t.reshape(-1, heads_local, HD)  7.36 us
    all_to_all x1, starting transfers between devices, per_device(): attended = lax.all_to_all(attended, ROW, 0, 0, tiled=True)  6.77 us
    ppermute x6, waiting for transfers between devices, doubling_gather(): received = lax.ppermute(buffer, axis, pairs)  6.23 us
    dot_general x1, matrix products, per_device(): jnp.einsum('td,cde->cte', flat_rows, qkv_weight, preferred_element_type=j...  4.81 us
  transfers between devices with their start and end apart: 11, of which 8 were waited for; matrix products, arithmetic and copies ran while one was open for 27% of the time, Pallas kernels for 0%

profile of v14, /device:TPU:1, one launch (start us, length us, event | category | flops | bytes accessed | tf_op | source)
XLA Modules:
  0.0 153.6 jit_solution(15342907084085209295)
XLA Ops:
  7.2 2.6 %collective-permute-start = (bf16[1,8,24,608]{3,2,1,0:T(8,128)(2,1)}, bf16[1,8,24,608]{3,2,1,0:T(8,128)(2,1)S(1)}, u32[]{:S(2)}, u32[]{:S(2)}) collective-permute-start(bf16[1,8,24,608]{3,2,1,0:T(8,128)(2,1)} %bitcast.182), channel_id=1, source_target_pairs={{0,2},{1,3},{2,0},{3,1},{4,6},{5,7},{6,4},{7,5},{8,10},{9,11},{10,... | collective-permute-start | bytes 700424 | tf_op jit(solution)/shard_map/ppermute | solution.py:43
  11.6 0.9 add_bitcast_fusion
  12.5 1.1 fusion.61
  14.5 2.3 %collective-permute-done.2 = bf16[1,80,608]{2,1,0:T(8,128)(2,1)S(1)} collective-permute-done((bf16[1,80,608]{2,1,0:T(8,128)(2,1)S(1)}, bf16[1,80,608]{2,1,0:T(8,128)(2,1)S(1)}, u32[]{:S(2)}, u32[]{:S(2)}) %collective-permute-start.2) | collective-permute-done | bytes 97312 | tf_op jit(solution)/shard_map/ppermute | solution.py:43
  16.9 2.4 %collective-permute-start.3 = (bf16[2,1,80,608]{3,2,0,1:T(8,128)(2,1)S(1)}, bf16[2,1,80,608]{3,2,0,1:T(8,128)(2,1)S(1)}, u32[]{:S(2)}, u32[]{:S(2)}) collective-permute-start(bf16[2,1,80,608]{3,2,0,1:T(8,128)(2,1)S(1)} %maximum_select_fusion.4), channel_id=1, source_target_pairs={{0,1},{1,0},{2,3},{3,2},{4,5},{5,4},{6,7},{7,6},{8,9},{9,8},{10,11... | collective-permute-start | bytes 583688 | tf_op jit(solution)/shard_map/ppermute | solution.py:43
  22.2 3.2 %fusion.19 = f32[2,8,2,512]{3,1,0,2:T(8,128)S(1)} fusion(bf16[2,2432,512]{2,1,0:T(8,128)(2,1)} %param.18, bf16[8,2,2432,1]{2,1,0,3:T(2,128)(2,1)S(1)} %fusion.38), kind=kOutput, calls=%fused_computation.19 | convolution fusion | flops 79691776 | bytes 5124096 | tf_op jit(solution)/shard_map/rtd,cde->crte/dot_general | solution.py:135
  27.0 2.6 %copy.97 = f32[8,24,4,608]{3,2,1,0:T(4,128)} copy(f32[8,24,4,608]{3,1,0,2:T(8,128)S(1)} %bitcast_convert_fusion) | data formatting | bytes 3735552 | tf_op jit(solution)/shard_map/convert_element_type | solution.py:124
  29.5 2.2 %reshape.753 = f32[192,2432]{1,0:T(8,128)S(1)} reshape(f32[8,24,4,608]{3,2,1,0:T(4,128)} %copy.97) | data formatting | bytes 3735552 | tf_op jit(solution)/shard_map/convert_element_type | solution.py:124
  32.3 4.8 %convolution_bitcast_fusion = f32[3,192,512]{2,1,0:T(8,128)S(1)} fusion(bf16[3,2432,512]{2,1,0:T(8,128)(2,1)} %param.17, bf16[192,2432]{1,0:T(8,128)(2,1)S(1)} %fusion.18), kind=kOutput, calls=%fused_computation.17 | convolution fusion | flops 1434451968 | bytes 9584640 | tf_op jit(solution)/shard_map/td,cde->cte/dot_general | solution.py:128
  39.6 1.2 convert_element_type.99
  42.4 1.6 %reshape.743 = bf16[64,38,128]{2,1,0:T(8,128)(2,1)} reshape(bf16[64,76,64]{2,1,0:T(8,128)(2,1)S(1)} %copy.116) | data formatting | bytes 1245184 | tf_op jit(solution)/shard_map/reshape | solution.py:151
  44.0 14.3 %all-to-all-start = ((bf16[64,38,128]{2,1,0:T(8,128)(2,1)}), bf16[64,38,128]{2,1,0:T(8,128)(2,1)S(1)}, u32[]{:S(2)}, u32[]{:S(2)}) async-start(bf16[64,38,128]{2,1,0:T(8,128)(2,1)} %reshape.743), calls=%async_computation | async-start | bytes 1310720 | tf_op jit(solution)/shard_map/all_to_all | solution.py:152
  59.6 20.6 %all-to-all-done = bf16[64,38,128]{2,1,0:T(8,128)(2,1)S(1)} async-done(((bf16[64,38,128]{2,1,0:T(8,128)(2,1)}), bf16[64,38,128]{2,1,0:T(8,128)(2,1)S(1)}, u32[]{:S(2)}, u32[]{:S(2)}) %all-to-all-start) | async-done | bytes 622624 | tf_op jit(solution)/shard_map/all_to_all | solution.py:152
  80.9 0.9 fusion.59
  81.8 1.2 reshape.746
  83.2 1.9 %fusion.62 = (f32[1536]{0:T(1024)S(1)}, f32[1536,1664]{1,0:T(8,128)S(1)}) fusion(bf16[1536,64]{1,0:T(8,128)(2,1)S(1)} %bitcast.172, bf16[1664,64]{1,0:T(8,128)(2,1)S(1)} %reshape.746, pred[1664]{0:T(1024)(128)(4,1)S(1)} %fusion.57), kind=kOutput, calls=%fused_computation.124 | convolution fusion | flops 334821888 | bytes 10641024 | tf_op jit(solution)/shard_map/dot_general | solution.py:80
  85.1 1.8 %fusion = f32[1536]{0:T(1024)S(1)} fusion(f32[1536,1664]{1,0:T(8,128)S(1)} %get-tuple-element.31, f32[1536]{0:T(1024)S(1)} %get-tuple-element.30, pred[1664]{0:T(1024)(128)(4,1)S(1)} %fusion.57), kind=kLoop, calls=%fused_computation.2 | loop fusion | flops 7666176 | bytes 10237568 | tf_op jit(solution)/shard_map/reduce_sum | solution.py:84
  86.9 2.4 %fusion.15 = bf16[1536,64]{0,1:T(8,128)(2,1)S(1)} fusion(bf16[1664,64]{1,0:T(8,128)(2,1)S(1)} %reshape.747, f32[1536,1664]{1,0:T(8,128)S(1)} %get-tuple-element.31, f32[1536]{0:T(1024)S(1)} %get-tuple-element.30, pred[1664]{0:T(1024)(128)(4,1)S(1)} %fusion.57, f32[1536]{0:T(1024)S(1)} %fusion), kind=kOutput, calls=%fused_computation.12 | convolution fusion | flops 335020032 | bytes 10647168 | tf_op jit(solution)/shard_map/dot_general | solution.py:85
  90.5 6.8 %all-to-all-start.1 = ((bf16[64,2,768]{2,1,0:T(2,128)(2,1)}), bf16[64,2,768]{2,1,0:T(2,128)(2,1)S(1)}, u32[]{:S(2)}, u32[]{:S(2)}) async-start(bf16[64,2,768]{2,1,0:T(2,128)(2,1)} %reshape.765), calls=%async_computation.1 | async-start | bytes 393216 | tf_op jit(solution)/shard_map/all_to_all | solution.py:167
  97.3 12.4 %all-to-all-done.1 = bf16[64,2,768]{2,1,0:T(2,128)(2,1)S(1)} async-done(((bf16[64,2,768]{2,1,0:T(2,128)(2,1)}), bf16[64,2,768]{2,1,0:T(2,128)(2,1)S(1)}, u32[]{:S(2)}, u32[]{:S(2)}) %all-to-all-start.1) | async-done | bytes 196640 | tf_op jit(solution)/shard_map/all_to_all | solution.py:167
  110.1 7.4 %reshape.750 = bf16[2432,8,64]{2,1,0:T(8,128)(2,1)} reshape(bf16[64,38,512]{2,1,0:T(8,128)(2,1)} %all-gather.3.cloned.1.call-done) | data formatting | bytes 4980736 | tf_op jit(solution)/shard_map/reshape | solution.py:171
  117.4 4.2 %fusion.9 = f32[2,2,48,2432]{3,2,1,0:T(8,128)S(1)} fusion(bf16[2432,8,64,1,1]{2,1,0,4,3:T(8,128)(2,1)} %bitcast.171, bf16[2,2,48,64,8]{3,4,2,1,0:T(8,128)(2,1)S(1)} %bitcast.195), kind=kOutput, calls=%fused_computation.10 | convolution fusion | flops 478150656 | bytes 4554752 | tf_op jit(solution)/shard_map/rhtd,nhd->rtn/dot_general | solution.py:168
  121.7 1.3 copy-done
  123.0 2.5 %collective-permute-start.4 = (f32[2,48,2432]{2,1,0:T(8,128)S(1)}, f32[2,48,2432]{2,1,0:T(8,128)S(1)}, u32[]{:S(2)}, u32[]{:S(2)}) collective-permute-start(f32[2,48,2432]{2,1,0:T(8,128)S(1)} %dynamic-slice_bitcast_fusion), channel_id=1, source_target_pairs={{0,1},{1,0},{2,3},{3,2},{4,5},{5,4},{6,7},{7,6},{8,9},{9,8},{10,11... | collective-permute-start | bytes 2801672 | tf_op jit(solution)/shard_map/ppermute | solution.py:71
  125.5 2.0 %collective-permute-done.4 = f32[2,48,2432]{2,1,0:T(8,128)S(1)} collective-permute-done((f32[2,48,2432]{2,1,0:T(8,128)S(1)}, f32[2,48,2432]{2,1,0:T(8,128)S(1)}, u32[]{:S(2)}, u32[]{:S(2)}) %collective-permute-start.4) | collective-permute-done | bytes 933920 | tf_op jit(solution)/shard_map/ppermute | solution.py:71
  127.6 1.3 bitcast_add_fusion.1
  130.0 1.0 dynamic-slice_bitcast_fusion.2
  132.5 4.3 %collective-permute-done.5 = bf16[48,2432]{1,0:T(8,128)(2,1)} collective-permute-done((bf16[48,2432]{1,0:T(8,128)(2,1)}, bf16[48,2432]{1,0:T(8,128)(2,1)}, u32[]{:S(2)}, u32[]{:S(2)}) %collective-permute-start.5) | collective-permute-done | bytes 233504 | tf_op jit(solution)/shard_map/ppermute | solution.py:75
  136.8 1.0 bitcast_add_fusion.2
  138.6 1.0 add_bitcast_fusion.1
  140.2 2.5 %collective-permute-done.6 = f32[1,2,2,24,64]{4,3,2,1,0:T(8,128)S(1)} collective-permute-done((f32[1,2,2,24,64]{4,3,2,1,0:T(8,128)S(1)}, f32[1,2,2,24,64]{4,3,2,1,0:T(8,128)S(1)}, u32[]{:S(2)}, u32[]{:S(2)}) %collective-permute-start.6) | collective-permute-done | bytes 24608 | tf_op jit(solution)/shard_map/ppermute | solution.py:43
  142.7 2.4 %collective-permute-start.7 = (f32[2,1,2,2,24,64]{5,4,3,2,0,1:T(8,128)S(1)}, f32[2,1,2,2,24,64]{5,4,3,2,0,1:T(8,128)S(1)}, u32[]{:S(2)}, u32[]{:S(2)}) collective-permute-start(f32[2,1,2,2,24,64]{5,4,3,2,0,1:T(8,128)S(1)} %maximum_select_fusion.6), channel_id=1, source_target_pairs={{0,1},{1,0},{2,3},{3,2},{4,5},{5,4},{6,7},{7,6},{8,9},{9,8},{10,11... | collective-permute-start | bytes 147464 | tf_op jit(solution)/shard_map/ppermute | solution.py:43
  (105 shorter events, 20.9 us)
Async XLA Ops:
  7.2 12.2 %copy-start.3 = (bf16[8,24,608]{2,1,0:T(8,128)(2,1)S(1)}, bf16[8,24,608]{2,1,0:T(8,128)(2,1)}, u32[]{:S(2)}) copy-start(bf16[8,24,608]{2,1,0:T(8,128)(2,1)} %param.12) | copy-start | bytes 700420
  7.2 102.9 %all-gather.3.cloned.1.call-start = ((), (), s32[]{:S(2)}) async-start(), calls=%async_computation.2 | async-start | bytes 2662400 | tf_op jit(solution)/shard_map/all_gather | solution.py:110
  7.2 12.1 %collective-permute-start = (bf16[1,8,24,608]{3,2,1,0:T(8,128)(2,1)}, bf16[1,8,24,608]{3,2,1,0:T(8,128)(2,1)S(1)}, u32[]{:S(2)}, u32[]{:S(2)}) collective-permute-start(bf16[1,8,24,608]{3,2,1,0:T(8,128)(2,1)} %bitcast.182), channel_id=1, source_target_pairs={{0,2},{1,3},{2,0},{3,1},{4,6},{5,7},{6,4},{7,5},{8,10},{9,11},{10,... | collective-permute-start | bytes 700424 | tf_op jit(solution)/shard_map/ppermute | solution.py:43
  11.4 5.4 %collective-permute-start.2 = (bf16[1,80,608]{2,1,0:T(8,128)(2,1)S(1)}, bf16[1,80,608]{2,1,0:T(8,128)(2,1)S(1)}, u32[]{:S(2)}, u32[]{:S(2)}) collective-permute-start(bf16[1,80,608]{2,1,0:T(8,128)(2,1)S(1)} %get-tuple-element.23), channel_id=1, source_target_pairs={{0,2},{1,3},{2,0},{3,1},{4,6},{5,7},{6,4},{7,5},{8,10},{9,11},{10,... | collective-permute-start | bytes 291848 | tf_op jit(solution)/shard_map/ppermute | solution.py:43
  16.9 3.5 %collective-permute-start.3 = (bf16[2,1,80,608]{3,2,0,1:T(8,128)(2,1)S(1)}, bf16[2,1,80,608]{3,2,0,1:T(8,128)(2,1)S(1)}, u32[]{:S(2)}, u32[]{:S(2)}) collective-permute-start(bf16[2,1,80,608]{3,2,0,1:T(8,128)(2,1)S(1)} %maximum_select_fusion.4), channel_id=1, source_target_pairs={{0,1},{1,0},{2,3},{3,2},{4,5},{5,4},{6,7},{7,6},{8,9},{9,8},{10,11... | collective-permute-start | bytes 583688 | tf_op jit(solution)/shard_map/ppermute | solution.py:43
  19.5 6.3 %collective-permute-start.1 = (bf16[2,1,8,24,608]{4,3,2,0,1:T(8,128)(2,1)S(1)}, bf16[2,1,8,24,608]{4,3,2,0,1:T(8,128)(2,1)S(1)}, u32[]{:S(2)}, u32[]{:S(2)}) collective-permute-start(bf16[2,1,8,24,608]{4,3,2,0,1:T(8,128)(2,1)S(1)} %maximum_select_fusion.1), channel_id=1, source_target_pairs={{0,1},{1,0},{2,3},{3,2},{4,5},{5,4},{6,7},{7,6},{8,9},{9,8},{10,11... | collective-permute-start | bytes 1400840 | tf_op jit(solution)/shard_map/ppermute | solution.py:43
  20.5 0.8 copy-start.1
  41.5 16.8 %copy-start.5 = (s32[8]{0:T(128)S(1)}, s32[8]{0:T(128)}, u32[]{:S(2)}) copy-start(s32[8]{0:T(128)} %param.22) | copy-start | bytes 100
  44.0 36.2 %all-to-all-start = ((bf16[64,38,128]{2,1,0:T(8,128)(2,1)}), bf16[64,38,128]{2,1,0:T(8,128)(2,1)S(1)}, u32[]{:S(2)}, u32[]{:S(2)}) async-start(bf16[64,38,128]{2,1,0:T(8,128)(2,1)} %reshape.743), calls=%async_computation | async-start | bytes 1310720 | tf_op jit(solution)/shard_map/all_to_all | solution.py:152
  90.5 19.2 %all-to-all-start.1 = ((bf16[64,2,768]{2,1,0:T(2,128)(2,1)}), bf16[64,2,768]{2,1,0:T(2,128)(2,1)S(1)}, u32[]{:S(2)}, u32[]{:S(2)}) async-start(bf16[64,2,768]{2,1,0:T(2,128)(2,1)} %reshape.765), calls=%async_computation.1 | async-start | bytes 393216 | tf_op jit(solution)/shard_map/all_to_all | solution.py:167
  117.4 8.0 %copy-start.4 = (s32[8]{0:T(128)S(1)}, s32[8]{0:T(128)}, u32[]{:S(2)}) copy-start(s32[8]{0:T(128)} %param.23) | copy-start | bytes 100
  121.6 1.3 copy-start
  123.0 4.6 %collective-permute-start.4 = (f32[2,48,2432]{2,1,0:T(8,128)S(1)}, f32[2,48,2432]{2,1,0:T(8,128)S(1)}, u32[]{:S(2)}, u32[]{:S(2)}) collective-permute-start(f32[2,48,2432]{2,1,0:T(8,128)S(1)} %dynamic-slice_bitcast_fusion), channel_id=1, source_target_pairs={{0,1},{1,0},{2,3},{3,2},{4,5},{5,4},{6,7},{7,6},{8,9},{9,8},{10,11... | collective-permute-start | bytes 2801672 | tf_op jit(solution)/shard_map/ppermute | solution.py:71
  129.6 7.2 %collective-permute-start.5 = (bf16[48,2432]{1,0:T(8,128)(2,1)}, bf16[48,2432]{1,0:T(8,128)(2,1)}, u32[]{:S(2)}, u32[]{:S(2)}) collective-permute-start(bf16[48,2432]{1,0:T(8,128)(2,1)} %fusion.30), channel_id=1, source_target_pairs={{0,2},{1,3},{2,0},{3,1},{4,6},{5,7},{6,4},{7,5},{8,10},{9,11},{10,... | collective-permute-start | bytes 700424 | tf_op jit(solution)/shard_map/ppermute | solution.py:75
  131.7 6.9 %copy-start.2 = (bf16[2,2,80,608]{3,2,1,0:T(8,128)(2,1)S(1)}, bf16[2,2,80,608]{3,2,1,0:T(8,128)(2,1)}, u32[]{:S(2)}) copy-start(bf16[2,2,80,608]{3,2,1,0:T(8,128)(2,1)} %copy-done.1) | copy-start | bytes 1167364
  139.6 3.0 %collective-permute-start.6 = (f32[1,2,2,24,64]{4,3,2,1,0:T(8,128)S(1)}, f32[1,2,2,24,64]{4,3,2,1,0:T(8,128)S(1)}, u32[]{:S(2)}, u32[]{:S(2)}) collective-permute-start(f32[1,2,2,24,64]{4,3,2,1,0:T(8,128)S(1)} %get-tuple-element.26), channel_id=1, source_target_pairs={{0,2},{1,3},{2,0},{3,1},{4,6},{5,7},{6,4},{7,5},{8,10},{9,11},{10,... | collective-permute-start | bytes 73736 | tf_op jit(solution)/shard_map/ppermute | solution.py:43
  142.7 3.4 %collective-permute-start.7 = (f32[2,1,2,2,24,64]{5,4,3,2,0,1:T(8,128)S(1)}, f32[2,1,2,2,24,64]{5,4,3,2,0,1:T(8,128)S(1)}, u32[]{:S(2)}, u32[]{:S(2)}) collective-permute-start(f32[2,1,2,2,24,64]{5,4,3,2,0,1:T(8,128)S(1)} %maximum_select_fusion.6), channel_id=1, source_target_pairs={{0,1},{1,0},{2,3},{3,2},{4,5},{5,4},{6,7},{7,6},{8,9},{9,8},{10,11... | collective-permute-start | bytes 147464 | tf_op jit(solution)/shard_map/ppermute | solution.py:43
Sparse Core Ops, SparseCore 0:
  11.7 87.4 all-gather.2

commit v15 on v13

--- a/solution.py
+++ b/solution.py
@@ -109,7 +109,7 @@
 
     weight_t = lax.all_gather(jnp.transpose(out_weight), ROW, axis=0, tiled=True)
 
-    img_full = gather_features(img_hidden)
+    img_full = lax.optimization_barrier(gather_features(img_hidden))
     txt_rows = txt_hidden.reshape(requests * text_rows, -1)
     packed = jnp.concatenate([txt_rows, jnp.transpose(final_weight)], 0)
     packed = doubling_gather(packed, "col", COL_ORDER)

time: 148 us -> 146 us (0.986)
  local copies, waits for them, and re-layouts: 26.9 us -> 21.9 us
  other arithmetic: 12.3 us -> 14.5 us
    convert_element_type x2 -> x0, local copies, waits for them, and re-layouts: 4.77 us -> none  [per_device(): img_full.astype(jnp.float32)]
    unnamed x17 -> x19, local copies, waits for them, and re-layouts: 5.86 us -> 5.84 us
  transfers between devices with their start and end apart: 11 -> 11, of which waited for: 7 -> 7; matrix products, arithmetic and copies ran while one was open for 29% -> 27% of each run, Pallas kernels for 0% -> 0%
where the time goes in v15:
time: 146 us; the launch traced here: 145 us
  waiting for transfers between devices  44.6 us (31%)
  starting transfers between devices  34.7 us (24%)
  local copies, waits for them, and re-layouts  21.9 us (15%)
  matrix products  15.2 us (10%)
  between operations  14.6 us (10%)
  other arithmetic  14.5 us (10%)
    all_to_all x1, waiting for transfers between devices, per_device(): bundle = lax.all_to_all(bundle, ROW, 0, 0, tiled=True)  22.4 us
    all_to_all x1, starting transfers between devices, per_device(): bundle = lax.all_to_all(bundle, ROW, 0, 0, tiled=True)  13.7 us
    all_to_all x1, waiting for transfers between devices, per_device(): attended = lax.all_to_all(attended, ROW, 0, 0, tiled=True)  11.9 us
    ppermute x6, starting transfers between devices, doubling_gather(): received = lax.ppermute(buffer, axis, pairs)  11.8 us
    unnamed x19, local copies, waits for them, and re-layouts  5.84 us
    all_to_all x1, starting transfers between devices, per_device(): attended = lax.all_to_all(attended, ROW, 0, 0, tiled=True)  5.38 us
    ppermute x1, waiting for transfers between devices, halving_scatter(): received = lax.ppermute(send.astype(jnp.bfloat16), 'col', pairs)  4.91 us
    dot_general x1, matrix products, per_device(): jnp.einsum('td,cde->cte', flat_rows, qkv_weight, preferred_element_type=j...  4.81 us
  transfers between devices with their start and end apart: 11, of which 7 were waited for; matrix products, arithmetic and copies ran while one was open for 27% of the time, Pallas kernels for 0%

profile of v15, /device:TPU:1, one launch (start us, length us, event | category | flops | bytes accessed | tf_op | source)
XLA Modules:
  0.0 145.4 jit_solution(10878925100560910617)
XLA Ops:
  9.0 2.6 %collective-permute-start.2 = (bf16[1,80,608]{2,1,0:T(8,128)(2,1)S(1)}, bf16[1,80,608]{2,1,0:T(8,128)(2,1)S(1)}, u32[]{:S(2)}, u32[]{:S(2)}) collective-permute-start(bf16[1,80,608]{2,1,0:T(8,128)(2,1)S(1)} %get-tuple-element.23), channel_id=1, source_target_pairs={{0,2},{1,3},{2,0},{3,1},{4,6},{5,7},{6,4},{7,5},{8,10},{9,11},{10,... | collective-permute-start | bytes 291848 | tf_op jit(solution)/shard_map/ppermute | solution.py:43
  11.6 1.1 fusion.61
  13.7 1.4 slice_bitcast_fusion.5
  15.2 3.0 %collective-permute-start.3 = (bf16[2,1,80,608]{3,2,0,1:T(8,128)(2,1)S(1)}, bf16[2,1,80,608]{3,2,0,1:T(8,128)(2,1)S(1)}, u32[]{:S(2)}, u32[]{:S(2)}) collective-permute-start(bf16[2,1,80,608]{3,2,0,1:T(8,128)(2,1)S(1)} %maximum_select_fusion.4), channel_id=1, source_target_pairs={{0,1},{1,0},{2,3},{3,2},{4,5},{5,4},{6,7},{7,6},{8,9},{9,8},{10,11... | collective-permute-start | bytes 583688 | tf_op jit(solution)/shard_map/ppermute | solution.py:43
  18.8 2.6 %collective-permute-start.1 = (bf16[2,1,8,24,608]{4,3,2,0,1:T(8,128)(2,1)S(1)}, bf16[2,1,8,24,608]{4,3,2,0,1:T(8,128)(2,1)S(1)}, u32[]{:S(2)}, u32[]{:S(2)}) collective-permute-start(bf16[2,1,8,24,608]{4,3,2,0,1:T(8,128)(2,1)S(1)} %maximum_select_fusion.1), channel_id=1, source_target_pairs={{0,1},{1,0},{2,3},{3,2},{4,5},{5,4},{6,7},{7,6},{8,9},{9,8},{10,11... | collective-permute-start | bytes 1400840 | tf_op jit(solution)/shard_map/ppermute | solution.py:43
  23.4 3.2 %fusion.21 = f32[2,8,2,512]{3,1,0,2:T(8,128)S(1)} fusion(bf16[2,2432,512]{2,1,0:T(8,128)(2,1)} %param.18, bf16[8,2,2432,1]{2,1,0,3:T(2,128)(2,1)S(1)} %fusion.38), kind=kOutput, calls=%fused_computation.22 | convolution fusion | flops 79691776 | bytes 5124096 | tf_op jit(solution)/shard_map/rtd,cde->crte/dot_general | solution.py:135
  30.5 4.8 %convolution_bitcast_fusion = f32[3,192,512]{2,1,0:T(8,128)S(1)} fusion(bf16[192,2432,1]{1,0,2:T(8,128)(2,1)S(1)} %bitcast.179, bf16[3,2432,512]{2,1,0:T(8,128)(2,1)} %param.17), kind=kOutput, calls=%fused_computation.20 | convolution fusion | flops 1434451968 | bytes 9584640 | tf_op jit(solution)/shard_map/td,cde->cte/dot_general | solution.py:128
  35.5 1.0 convert_element_type.88
  40.0 0.9 fusion.25
  42.3 1.6 %reshape.728 = bf16[64,38,128]{2,1,0:T(8,128)(2,1)} reshape(bf16[64,76,64]{2,1,0:T(8,128)(2,1)S(1)} %copy.110) | data formatting | bytes 1245184 | tf_op jit(solution)/shard_map/reshape | solution.py:151
  43.9 13.7 %all-to-all-start = ((bf16[64,38,128]{2,1,0:T(8,128)(2,1)}), bf16[64,38,128]{2,1,0:T(8,128)(2,1)S(1)}, u32[]{:S(2)}, u32[]{:S(2)}) async-start(bf16[64,38,128]{2,1,0:T(8,128)(2,1)} %reshape.728), calls=%async_computation | async-start | bytes 1310720 | tf_op jit(solution)/shard_map/all_to_all | solution.py:152
  58.9 22.4 %all-to-all-done = bf16[64,38,128]{2,1,0:T(8,128)(2,1)S(1)} async-done(((bf16[64,38,128]{2,1,0:T(8,128)(2,1)}), bf16[64,38,128]{2,1,0:T(8,128)(2,1)S(1)}, u32[]{:S(2)}, u32[]{:S(2)}) %all-to-all-start) | async-done | bytes 622624 | tf_op jit(solution)/shard_map/all_to_all | solution.py:152
  82.0 1.0 fusion.59
  83.0 1.2 reshape.732
  84.4 1.9 %fusion.62 = (f32[1536]{0:T(1024)S(1)}, f32[1536,1664]{1,0:T(8,128)S(1)}) fusion(bf16[1536,64]{1,0:T(8,128)(2,1)S(1)} %bitcast.163, bf16[1664,64]{1,0:T(8,128)(2,1)S(1)} %reshape.731, pred[1664]{0:T(1024)(128)(4,1)S(1)} %fusion.57), kind=kOutput, calls=%fused_computation.124 | convolution fusion | flops 334821888 | bytes 10641024 | tf_op jit(solution)/shard_map/dot_general | solution.py:80
  86.4 1.8 %fusion = f32[1536]{0:T(1024)S(1)} fusion(f32[1536,1664]{1,0:T(8,128)S(1)} %get-tuple-element.31, f32[1536]{0:T(1024)S(1)} %get-tuple-element.30, pred[1664]{0:T(1024)(128)(4,1)S(1)} %fusion.57), kind=kLoop, calls=%fused_computation.2 | loop fusion | flops 7666176 | bytes 10237568 | tf_op jit(solution)/shard_map/reduce_sum | solution.py:84
  88.2 2.4 %fusion.14 = bf16[1536,64]{0,1:T(8,128)(2,1)S(1)} fusion(bf16[1664,64]{1,0:T(8,128)(2,1)S(1)} %reshape.732, f32[1536,1664]{1,0:T(8,128)S(1)} %get-tuple-element.31, f32[1536]{0:T(1024)S(1)} %get-tuple-element.30, pred[1664]{0:T(1024)(128)(4,1)S(1)} %fusion.57, f32[1536]{0:T(1024)S(1)} %fusion), kind=kOutput, calls=%fused_computation.15 | convolution fusion | flops 335020032 | bytes 10647168 | tf_op jit(solution)/shard_map/dot_general | solution.py:85
  91.8 5.4 %all-to-all-start.1 = ((bf16[64,2,768]{2,1,0:T(2,128)(2,1)}), bf16[64,2,768]{2,1,0:T(2,128)(2,1)S(1)}, u32[]{:S(2)}, u32[]{:S(2)}) async-start(bf16[64,2,768]{2,1,0:T(2,128)(2,1)} %reshape.747), calls=%async_computation.1 | async-start | bytes 393216 | tf_op jit(solution)/shard_map/all_to_all | solution.py:167
  97.2 11.9 %all-to-all-done.1 = bf16[64,2,768]{2,1,0:T(2,128)(2,1)S(1)} async-done(((bf16[64,2,768]{2,1,0:T(2,128)(2,1)}), bf16[64,2,768]{2,1,0:T(2,128)(2,1)S(1)}, u32[]{:S(2)}, u32[]{:S(2)}) %all-to-all-start.1) | async-done | bytes 196640 | tf_op jit(solution)/shard_map/all_to_all | solution.py:167
  110.4 2.8 %reshape.743 = bf16[2432,512,1,1]{1,0,2,3:T(8,128)(2,1)S(1)} reshape(bf16[64,38,512]{2,1,0:T(8,128)(2,1)} %all-gather.3.cloned.1.call-done) | data formatting | bytes 4980736
  113.2 1.9 %fusion.7 = f32[2,2,48,2432]{3,2,1,0:T(8,128)S(1)} fusion(bf16[2,2,48,512]{3,2,1,0:T(8,128)(2,1)} %dot_general.26, bf16[2432,512,1,1]{1,0,2,3:T(8,128)(2,1)S(1)} %reshape.743), kind=kOutput, calls=%fused_computation.8 | convolution fusion | flops 478150656 | bytes 4554752 | tf_op jit(solution)/shard_map/dot_general | solution.py:172
  115.1 1.3 copy-done
  116.4 2.6 %collective-permute-start.4 = (f32[2,48,2432]{2,1,0:T(8,128)S(1)}, f32[2,48,2432]{2,1,0:T(8,128)S(1)}, u32[]{:S(2)}, u32[]{:S(2)}) collective-permute-start(f32[2,48,2432]{2,1,0:T(8,128)S(1)} %dynamic-slice_bitcast_fusion), channel_id=1, source_target_pairs={{0,1},{1,0},{2,3},{3,2},{4,5},{5,4},{6,7},{7,6},{8,9},{9,8},{10,11... | collective-permute-start | bytes 2801672 | tf_op jit(solution)/shard_map/ppermute | solution.py:71
  119.1 2.0 %collective-permute-done.4 = f32[2,48,2432]{2,1,0:T(8,128)S(1)} collective-permute-done((f32[2,48,2432]{2,1,0:T(8,128)S(1)}, f32[2,48,2432]{2,1,0:T(8,128)S(1)}, u32[]{:S(2)}, u32[]{:S(2)}) %collective-permute-start.4) | collective-permute-done | bytes 933920 | tf_op jit(solution)/shard_map/ppermute | solution.py:71
  121.2 1.3 bitcast_add_fusion
  122.5 1.1 collective-permute-start.5
  123.6 1.0 dynamic-slice_bitcast_fusion.2
  124.6 4.9 %collective-permute-done.5 = bf16[48,2432]{1,0:T(8,128)(2,1)S(1)} collective-permute-done((bf16[48,2432]{1,0:T(8,128)(2,1)S(1)}, bf16[48,2432]{1,0:T(8,128)(2,1)S(1)}, u32[]{:S(2)}, u32[]{:S(2)}) %collective-permute-start.5) | collective-permute-done | bytes 233504 | tf_op jit(solution)/shard_map/ppermute | solution.py:75
  130.4 1.0 add_bitcast_fusion.1
  131.4 1.1 collective-permute-start.6
  132.5 1.9 %collective-permute-done.6 = f32[1,2,2,24,64]{4,3,2,1,0:T(8,128)S(1)} collective-permute-done((f32[1,2,2,24,64]{4,3,2,1,0:T(8,128)S(1)}, f32[1,2,2,24,64]{4,3,2,1,0:T(8,128)S(1)}, u32[]{:S(2)}, u32[]{:S(2)}) %collective-permute-start.6) | collective-permute-done | bytes 24608 | tf_op jit(solution)/shard_map/ppermute | solution.py:43
  134.4 2.4 %collective-permute-start.7 = (f32[2,1,2,2,24,64]{5,4,3,2,0,1:T(8,128)S(1)}, f32[2,1,2,2,24,64]{5,4,3,2,0,1:T(8,128)S(1)}, u32[]{:S(2)}, u32[]{:S(2)}) collective-permute-start(f32[2,1,2,2,24,64]{5,4,3,2,0,1:T(8,128)S(1)} %maximum_select_fusion.6), channel_id=1, source_target_pairs={{0,1},{1,0},{2,3},{3,2},{4,5},{5,4},{6,7},{7,6},{8,9},{9,8},{10,11... | collective-permute-start | bytes 147464 | tf_op jit(solution)/shard_map/ppermute | solution.py:43
  (105 shorter events, 21.5 us)
Async XLA Ops:
  7.2 11.5 %copy-start.4 = (bf16[8,24,608]{2,1,0:T(8,128)(2,1)S(1)}, bf16[8,24,608]{2,1,0:T(8,128)(2,1)}, u32[]{:S(2)}) copy-start(bf16[8,24,608]{2,1,0:T(8,128)(2,1)} %param.12) | copy-start | bytes 700420
  7.2 103.2 %all-gather.3.cloned.1.call-start = ((), (), s32[]{:S(2)}) async-start(), calls=%async_computation.2 | async-start | bytes 2662400 | tf_op jit(solution)/shard_map/all_gather | solution.py:110
  9.0 6.2 %collective-permute-start.2 = (bf16[1,80,608]{2,1,0:T(8,128)(2,1)S(1)}, bf16[1,80,608]{2,1,0:T(8,128)(2,1)S(1)}, u32[]{:S(2)}, u32[]{:S(2)}) collective-permute-start(bf16[1,80,608]{2,1,0:T(8,128)(2,1)S(1)} %get-tuple-element.23), channel_id=1, source_target_pairs={{0,2},{1,3},{2,0},{3,1},{4,6},{5,7},{6,4},{7,5},{8,10},{9,11},{10,... | collective-permute-start | bytes 291848 | tf_op jit(solution)/shard_map/ppermute | solution.py:43
  11.5 7.2 %collective-permute-start = (bf16[1,8,24,608]{3,2,1,0:T(8,128)(2,1)}, bf16[1,8,24,608]{3,2,1,0:T(8,128)(2,1)S(1)}, u32[]{:S(2)}, u32[]{:S(2)}) collective-permute-start(bf16[1,8,24,608]{3,2,1,0:T(8,128)(2,1)} %bitcast.174), channel_id=1, source_target_pairs={{0,2},{1,3},{2,0},{3,1},{4,6},{5,7},{6,4},{7,5},{8,10},{9,11},{10,... | collective-permute-start | bytes 700424 | tf_op jit(solution)/shard_map/ppermute | solution.py:43
  15.2 6.4 %collective-permute-start.3 = (bf16[2,1,80,608]{3,2,0,1:T(8,128)(2,1)S(1)}, bf16[2,1,80,608]{3,2,0,1:T(8,128)(2,1)S(1)}, u32[]{:S(2)}, u32[]{:S(2)}) collective-permute-start(bf16[2,1,80,608]{3,2,0,1:T(8,128)(2,1)S(1)} %maximum_select_fusion.4), channel_id=1, source_target_pairs={{0,1},{1,0},{2,3},{3,2},{4,5},{5,4},{6,7},{7,6},{8,9},{9,8},{10,11... | collective-permute-start | bytes 583688 | tf_op jit(solution)/shard_map/ppermute | solution.py:43
  18.8 8.7 %collective-permute-start.1 = (bf16[2,1,8,24,608]{4,3,2,0,1:T(8,128)(2,1)S(1)}, bf16[2,1,8,24,608]{4,3,2,0,1:T(8,128)(2,1)S(1)}, u32[]{:S(2)}, u32[]{:S(2)}) collective-permute-start(bf16[2,1,8,24,608]{4,3,2,0,1:T(8,128)(2,1)S(1)} %maximum_select_fusion.1), channel_id=1, source_target_pairs={{0,1},{1,0},{2,3},{3,2},{4,5},{5,4},{6,7},{7,6},{8,9},{9,8},{10,11... | collective-permute-start | bytes 1400840 | tf_op jit(solution)/shard_map/ppermute | solution.py:43
  21.7 0.7 copy-start.2
  37.5 3.5 %copy-start.1 = (bf16[8,24,8,64]{3,2,1,0:T(8,128)(2,1)S(1)}, bf16[8,24,8,64]{3,2,1,0:T(8,128)(2,1)}, u32[]{:S(2)}) copy-start(bf16[8,24,8,64]{3,2,1,0:T(8,128)(2,1)} %convert_element_type.88) | copy-start | bytes 589828
  38.2 2.7 %copy-start.5 = (bf16[8,2,8,64]{3,2,0,1:T(8,128)(2,1)S(1)}, bf16[8,2,8,64]{3,2,0,1:T(8,128)(2,1)}, u32[]{:S(2)}) copy-start(bf16[8,2,8,64]{3,2,0,1:T(8,128)(2,1)} %multiply_convert_fusion) | copy-start | bytes 49156
  41.4 16.2 %copy-start.7 = (s32[8]{0:T(128)S(1)}, s32[8]{0:T(128)}, u32[]{:S(2)}) copy-start(s32[8]{0:T(128)} %param.22) | copy-start | bytes 100
  43.9 37.4 %all-to-all-start = ((bf16[64,38,128]{2,1,0:T(8,128)(2,1)}), bf16[64,38,128]{2,1,0:T(8,128)(2,1)S(1)}, u32[]{:S(2)}, u32[]{:S(2)}) async-start(bf16[64,38,128]{2,1,0:T(8,128)(2,1)} %reshape.728), calls=%async_computation | async-start | bytes 1310720 | tf_op jit(solution)/shard_map/all_to_all | solution.py:152
  91.8 17.3 %all-to-all-start.1 = ((bf16[64,2,768]{2,1,0:T(2,128)(2,1)}), bf16[64,2,768]{2,1,0:T(2,128)(2,1)S(1)}, u32[]{:S(2)}, u32[]{:S(2)}) async-start(bf16[64,2,768]{2,1,0:T(2,128)(2,1)} %reshape.747), calls=%async_computation.1 | async-start | bytes 393216 | tf_op jit(solution)/shard_map/all_to_all | solution.py:167
  113.2 5.8 %copy-start.6 = (s32[8]{0:T(128)S(1)}, s32[8]{0:T(128)}, u32[]{:S(2)}) copy-start(s32[8]{0:T(128)} %param.23) | copy-start | bytes 100
  115.1 1.3 copy-start
  116.4 4.7 %collective-permute-start.4 = (f32[2,48,2432]{2,1,0:T(8,128)S(1)}, f32[2,48,2432]{2,1,0:T(8,128)S(1)}, u32[]{:S(2)}, u32[]{:S(2)}) collective-permute-start(f32[2,48,2432]{2,1,0:T(8,128)S(1)} %dynamic-slice_bitcast_fusion), channel_id=1, source_target_pairs={{0,1},{1,0},{2,3},{3,2},{4,5},{5,4},{6,7},{7,6},{8,9},{9,8},{10,11... | collective-permute-start | bytes 2801672 | tf_op jit(solution)/shard_map/ppermute | solution.py:71
  122.4 7.9 %copy-start.3 = (bf16[2,2,80,608]{3,2,1,0:T(8,128)(2,1)S(1)}, bf16[2,2,80,608]{3,2,1,0:T(8,128)(2,1)}, u32[]{:S(2)}) copy-start(bf16[2,2,80,608]{3,2,1,0:T(8,128)(2,1)} %copy-done.2) | copy-start | bytes 1167364
  122.5 7.0 %collective-permute-start.5 = (bf16[48,2432]{1,0:T(8,128)(2,1)S(1)}, bf16[48,2432]{1,0:T(8,128)(2,1)S(1)}, u32[]{:S(2)}, u32[]{:S(2)}) collective-permute-start(bf16[48,2432]{1,0:T(8,128)(2,1)S(1)} %fusion.30), channel_id=1, source_target_pairs={{0,2},{1,3},{2,0},{3,1},{4,6},{5,7},{6,4},{7,5},{8,10},{9,11},{10,... | collective-permute-start | bytes 700424 | tf_op jit(solution)/shard_map/ppermute | solution.py:75
  131.4 3.0 %collective-permute-start.6 = (f32[1,2,2,24,64]{4,3,2,1,0:T(8,128)S(1)}, f32[1,2,2,24,64]{4,3,2,1,0:T(8,128)S(1)}, u32[]{:S(2)}, u32[]{:S(2)}) collective-permute-start(f32[1,2,2,24,64]{4,3,2,1,0:T(8,128)S(1)} %get-tuple-element.26), channel_id=1, source_target_pairs={{0,2},{1,3},{2,0},{3,1},{4,6},{5,7},{6,4},{7,5},{8,10},{9,11},{10,... | collective-permute-start | bytes 73736 | tf_op jit(solution)/shard_map/ppermute | solution.py:43
  134.4 3.4 %collective-permute-start.7 = (f32[2,1,2,2,24,64]{5,4,3,2,0,1:T(8,128)S(1)}, f32[2,1,2,2,24,64]{5,4,3,2,0,1:T(8,128)S(1)}, u32[]{:S(2)}, u32[]{:S(2)}) collective-permute-start(f32[2,1,2,2,24,64]{5,4,3,2,0,1:T(8,128)S(1)} %maximum_select_fusion.6), channel_id=1, source_target_pairs={{0,1},{1,0},{2,3},{3,2},{4,5},{5,4},{6,7},{7,6},{8,9},{9,8},{10,11... | collective-permute-start | bytes 147464 | tf_op jit(solution)/shard_map/ppermute | solution.py:43
Sparse Core Ops, SparseCore 0:
  11.8 88.5 all-gather.2

commit v16 on v15

--- a/solution.py
+++ b/solution.py
@@ -68,7 +68,7 @@
     keep = lax.dynamic_index_in_dim(chunks, low, 1, keepdims=False)
     send = lax.dynamic_index_in_dim(chunks, 1 - low, 1, keepdims=False)
     pairs = [(i, i ^ 1) for i in range(cols)]
-    halves = keep + lax.ppermute(send, "col", pairs)
+    halves = keep + lax.ppermute(send.astype(jnp.bfloat16), "col", pairs).astype(jnp.float32)
     keep = lax.dynamic_index_in_dim(halves, high, 0, keepdims=False)
     send = lax.dynamic_index_in_dim(halves, 1 - high, 0, keepdims=False)
     pairs = [(i, i ^ 2) for i in range(cols)]

time: 146 us -> 145 us (level)
  no operation moved by 1% of the time
where the time goes in v16:
time: 145 us
  waiting for transfers between devices  43.9 us (30%)
  starting transfers between devices  34.7 us (24%)
  local copies, waits for them, and re-layouts  21.9 us (15%)
  matrix products  15.2 us (10%)
  between operations  14.6 us (10%)
  other arithmetic  14.5 us (10%)
    all_to_all x1, waiting for transfers between devices, per_device(): bundle = lax.all_to_all(bundle, ROW, 0, 0, tiled=True)  22.4 us
    all_to_all x1, starting transfers between devices, per_device(): bundle = lax.all_to_all(bundle, ROW, 0, 0, tiled=True)  13.7 us
    all_to_all x1, waiting for transfers between devices, per_device(): attended = lax.all_to_all(attended, ROW, 0, 0, tiled=True)  11.9 us
    ppermute x6, starting transfers between devices, doubling_gather(): received = lax.ppermute(buffer, axis, pairs)  11.8 us
    unnamed x19, local copies, waits for them, and re-layouts  5.84 us
    all_to_all x1, starting transfers between devices, per_device(): attended = lax.all_to_all(attended, ROW, 0, 0, tiled=True)  5.38 us
    ppermute x1, waiting for transfers between devices, halving_scatter(): received = lax.ppermute(send.astype(jnp.bfloat16), 'col', pairs)  4.91 us
    dot_general x1, matrix products, per_device(): jnp.einsum('td,cde->cte', flat_rows, qkv_weight, preferred_element_type=j...  4.81 us
  transfers between devices with their start and end apart: 11, of which 7 were waited for; matrix products, arithmetic and copies ran while one was open for 27% of the time, Pallas kernels for 0%

profile of v16, /device:TPU:1, one launch (start us, length us, event | category | flops | bytes accessed | tf_op | source)
XLA Modules:
  0.0 144.7 jit_solution(14507552605795376340)
XLA Ops:
  9.0 2.6 %collective-permute-start.2 = (bf16[1,80,608]{2,1,0:T(8,128)(2,1)S(1)}, bf16[1,80,608]{2,1,0:T(8,128)(2,1)S(1)}, u32[]{:S(2)}, u32[]{:S(2)}) collective-permute-start(bf16[1,80,608]{2,1,0:T(8,128)(2,1)S(1)} %get-tuple-element.23), channel_id=1, source_target_pairs={{0,2},{1,3},{2,0},{3,1},{4,6},{5,7},{6,4},{7,5},{8,10},{9,11},{10,... | collective-permute-start | bytes 291848 | tf_op jit(solution)/shard_map/ppermute | solution.py:43
  11.6 1.1 fusion.62
  13.7 1.4 slice_bitcast_fusion.5
  15.2 3.0 %collective-permute-start.3 = (bf16[2,1,80,608]{3,2,0,1:T(8,128)(2,1)S(1)}, bf16[2,1,80,608]{3,2,0,1:T(8,128)(2,1)S(1)}, u32[]{:S(2)}, u32[]{:S(2)}) collective-permute-start(bf16[2,1,80,608]{3,2,0,1:T(8,128)(2,1)S(1)} %maximum_select_fusion.4), channel_id=1, source_target_pairs={{0,1},{1,0},{2,3},{3,2},{4,5},{5,4},{6,7},{7,6},{8,9},{9,8},{10,11... | collective-permute-start | bytes 583688 | tf_op jit(solution)/shard_map/ppermute | solution.py:43
  18.8 2.6 %collective-permute-start.1 = (bf16[2,1,8,24,608]{4,3,2,0,1:T(8,128)(2,1)S(1)}, bf16[2,1,8,24,608]{4,3,2,0,1:T(8,128)(2,1)S(1)}, u32[]{:S(2)}, u32[]{:S(2)}) collective-permute-start(bf16[2,1,8,24,608]{4,3,2,0,1:T(8,128)(2,1)S(1)} %maximum_select_fusion.1), channel_id=1, source_target_pairs={{0,1},{1,0},{2,3},{3,2},{4,5},{5,4},{6,7},{7,6},{8,9},{9,8},{10,11... | collective-permute-start | bytes 1400840 | tf_op jit(solution)/shard_map/ppermute | solution.py:43
  23.4 3.2 %fusion.21 = f32[2,8,2,512]{3,1,0,2:T(8,128)S(1)} fusion(bf16[2,2432,512]{2,1,0:T(8,128)(2,1)} %param.18, bf16[8,2,2432,1]{2,1,0,3:T(2,128)(2,1)S(1)} %fusion.39), kind=kOutput, calls=%fused_computation.22 | convolution fusion | flops 79691776 | bytes 5124096 | tf_op jit(solution)/shard_map/rtd,cde->crte/dot_general | solution.py:135
  30.5 4.8 %convolution_bitcast_fusion = f32[3,192,512]{2,1,0:T(8,128)S(1)} fusion(bf16[192,2432,1]{1,0,2:T(8,128)(2,1)S(1)} %bitcast.179, bf16[3,2432,512]{2,1,0:T(8,128)(2,1)} %param.17), kind=kOutput, calls=%fused_computation.20 | convolution fusion | flops 1434451968 | bytes 9584640 | tf_op jit(solution)/shard_map/td,cde->cte/dot_general | solution.py:128
  35.5 1.0 convert_element_type.97
  40.0 0.9 fusion.25
  42.3 1.6 %reshape.729 = bf16[64,38,128]{2,1,0:T(8,128)(2,1)} reshape(bf16[64,76,64]{2,1,0:T(8,128)(2,1)S(1)} %copy.110) | data formatting | bytes 1245184 | tf_op jit(solution)/shard_map/reshape | solution.py:151
  43.9 13.7 %all-to-all-start = ((bf16[64,38,128]{2,1,0:T(8,128)(2,1)}), bf16[64,38,128]{2,1,0:T(8,128)(2,1)S(1)}, u32[]{:S(2)}, u32[]{:S(2)}) async-start(bf16[64,38,128]{2,1,0:T(8,128)(2,1)} %reshape.729), calls=%async_computation | async-start | bytes 1310720 | tf_op jit(solution)/shard_map/all_to_all | solution.py:152
  58.9 22.4 %all-to-all-done = bf16[64,38,128]{2,1,0:T(8,128)(2,1)S(1)} async-done(((bf16[64,38,128]{2,1,0:T(8,128)(2,1)}), bf16[64,38,128]{2,1,0:T(8,128)(2,1)S(1)}, u32[]{:S(2)}, u32[]{:S(2)}) %all-to-all-start) | async-done | bytes 622624 | tf_op jit(solution)/shard_map/all_to_all | solution.py:152
  82.0 1.0 fusion.60
  83.0 1.2 reshape.733
  84.4 1.9 %fusion.63 = (f32[1536]{0:T(1024)S(1)}, f32[1536,1664]{1,0:T(8,128)S(1)}) fusion(bf16[1536,64]{1,0:T(8,128)(2,1)S(1)} %bitcast.163, bf16[1664,64]{1,0:T(8,128)(2,1)S(1)} %reshape.732, pred[1664]{0:T(1024)(128)(4,1)S(1)} %fusion.58), kind=kOutput, calls=%fused_computation.125 | convolution fusion | flops 334821888 | bytes 10641024 | tf_op jit(solution)/shard_map/dot_general | solution.py:80
  86.4 1.8 %fusion = f32[1536]{0:T(1024)S(1)} fusion(f32[1536,1664]{1,0:T(8,128)S(1)} %get-tuple-element.31, f32[1536]{0:T(1024)S(1)} %get-tuple-element.30, pred[1664]{0:T(1024)(128)(4,1)S(1)} %fusion.58), kind=kLoop, calls=%fused_computation.2 | loop fusion | flops 7666176 | bytes 10237568 | tf_op jit(solution)/shard_map/reduce_sum | solution.py:84
  88.2 2.4 %fusion.14 = bf16[1536,64]{0,1:T(8,128)(2,1)S(1)} fusion(bf16[1664,64]{1,0:T(8,128)(2,1)S(1)} %reshape.733, f32[1536,1664]{1,0:T(8,128)S(1)} %get-tuple-element.31, f32[1536]{0:T(1024)S(1)} %get-tuple-element.30, pred[1664]{0:T(1024)(128)(4,1)S(1)} %fusion.58, f32[1536]{0:T(1024)S(1)} %fusion), kind=kOutput, calls=%fused_computation.15 | convolution fusion | flops 335020032 | bytes 10647168 | tf_op jit(solution)/shard_map/dot_general | solution.py:85
  91.8 5.4 %all-to-all-start.1 = ((bf16[64,2,768]{2,1,0:T(2,128)(2,1)}), bf16[64,2,768]{2,1,0:T(2,128)(2,1)S(1)}, u32[]{:S(2)}, u32[]{:S(2)}) async-start(bf16[64,2,768]{2,1,0:T(2,128)(2,1)} %reshape.748), calls=%async_computation.1 | async-start | bytes 393216 | tf_op jit(solution)/shard_map/all_to_all | solution.py:167
  97.2 11.9 %all-to-all-done.1 = bf16[64,2,768]{2,1,0:T(2,128)(2,1)S(1)} async-done(((bf16[64,2,768]{2,1,0:T(2,128)(2,1)}), bf16[64,2,768]{2,1,0:T(2,128)(2,1)S(1)}, u32[]{:S(2)}, u32[]{:S(2)}) %all-to-all-start.1) | async-done | bytes 196640 | tf_op jit(solution)/shard_map/all_to_all | solution.py:167
  110.4 2.8 %reshape.744 = bf16[2432,512,1,1]{1,0,2,3:T(8,128)(2,1)S(1)} reshape(bf16[64,38,512]{2,1,0:T(8,128)(2,1)} %all-gather.3.cloned.1.call-done) | data formatting | bytes 4980736
  113.2 1.9 %fusion.7 = f32[2,2,48,2432]{3,2,1,0:T(8,128)S(1)} fusion(bf16[2,2,48,512]{3,2,1,0:T(8,128)(2,1)} %dot_general.26, bf16[2432,512,1,1]{1,0,2,3:T(8,128)(2,1)S(1)} %reshape.744), kind=kOutput, calls=%fused_computation.8 | convolution fusion | flops 478150656 | bytes 4554752 | tf_op jit(solution)/shard_map/dot_general | solution.py:172
  115.1 1.3 copy-done
  116.4 2.6 %collective-permute-start.4 = (bf16[2,48,2432]{2,1,0:T(8,128)(2,1)S(1)}, bf16[2,48,2432]{2,1,0:T(8,128)(2,1)S(1)}, u32[]{:S(2)}, u32[]{:S(2)}) collective-permute-start(bf16[2,48,2432]{2,1,0:T(8,128)(2,1)S(1)} %fusion.28), channel_id=1, source_target_pairs={{0,1},{1,0},{2,3},{3,2},{4,5},{5,4},{6,7},{7,6},{8,9},{9,8},{10,11... | collective-permute-start | bytes 1400840 | tf_op jit(solution)/shard_map/ppermute | solution.py:71
  119.1 1.4 collective-permute-done.4
  120.5 1.3 bitcast_add_fusion
  121.8 1.1 collective-permute-start.5
  122.9 1.0 dynamic-slice_bitcast_fusion.1
  123.9 4.9 %collective-permute-done.5 = bf16[48,2432]{1,0:T(8,128)(2,1)S(1)} collective-permute-done((bf16[48,2432]{1,0:T(8,128)(2,1)S(1)}, bf16[48,2432]{1,0:T(8,128)(2,1)S(1)}, u32[]{:S(2)}, u32[]{:S(2)}) %collective-permute-start.5) | collective-permute-done | bytes 233504 | tf_op jit(solution)/shard_map/ppermute | solution.py:75
  129.7 1.0 add_bitcast_fusion.1
  130.7 1.1 collective-permute-start.6
  131.8 1.9 %collective-permute-done.6 = f32[1,2,2,24,64]{4,3,2,1,0:T(8,128)S(1)} collective-permute-done((f32[1,2,2,24,64]{4,3,2,1,0:T(8,128)S(1)}, f32[1,2,2,24,64]{4,3,2,1,0:T(8,128)S(1)}, u32[]{:S(2)}, u32[]{:S(2)}) %collective-permute-start.6) | collective-permute-done | bytes 24608 | tf_op jit(solution)/shard_map/ppermute | solution.py:43
  133.7 2.4 %collective-permute-start.7 = (f32[2,1,2,2,24,64]{5,4,3,2,0,1:T(8,128)S(1)}, f32[2,1,2,2,24,64]{5,4,3,2,0,1:T(8,128)S(1)}, u32[]{:S(2)}, u32[]{:S(2)}) collective-permute-start(f32[2,1,2,2,24,64]{5,4,3,2,0,1:T(8,128)S(1)} %maximum_select_fusion.6), channel_id=1, source_target_pairs={{0,1},{1,0},{2,3},{3,2},{4,5},{5,4},{6,7},{7,6},{8,9},{9,8},{10,11... | collective-permute-start | bytes 147464 | tf_op jit(solution)/shard_map/ppermute | solution.py:43
  (105 shorter events, 21.4 us)
Async XLA Ops:
  7.2 11.5 %copy-start.4 = (bf16[8,24,608]{2,1,0:T(8,128)(2,1)S(1)}, bf16[8,24,608]{2,1,0:T(8,128)(2,1)}, u32[]{:S(2)}) copy-start(bf16[8,24,608]{2,1,0:T(8,128)(2,1)} %param.12) | copy-start | bytes 700420
  7.2 103.2 %all-gather.3.cloned.1.call-start = ((), (), s32[]{:S(2)}) async-start(), calls=%async_computation.2 | async-start | bytes 2662400 | tf_op jit(solution)/shard_map/all_gather | solution.py:110
  9.0 6.2 %collective-permute-start.2 = (bf16[1,80,608]{2,1,0:T(8,128)(2,1)S(1)}, bf16[1,80,608]{2,1,0:T(8,128)(2,1)S(1)}, u32[]{:S(2)}, u32[]{:S(2)}) collective-permute-start(bf16[1,80,608]{2,1,0:T(8,128)(2,1)S(1)} %get-tuple-element.23), channel_id=1, source_target_pairs={{0,2},{1,3},{2,0},{3,1},{4,6},{5,7},{6,4},{7,5},{8,10},{9,11},{10,... | collective-permute-start | bytes 291848 | tf_op jit(solution)/shard_map/ppermute | solution.py:43
  11.5 7.2 %collective-permute-start = (bf16[1,8,24,608]{3,2,1,0:T(8,128)(2,1)}, bf16[1,8,24,608]{3,2,1,0:T(8,128)(2,1)S(1)}, u32[]{:S(2)}, u32[]{:S(2)}) collective-permute-start(bf16[1,8,24,608]{3,2,1,0:T(8,128)(2,1)} %bitcast.174), channel_id=1, source_target_pairs={{0,2},{1,3},{2,0},{3,1},{4,6},{5,7},{6,4},{7,5},{8,10},{9,11},{10,... | collective-permute-start | bytes 700424 | tf_op jit(solution)/shard_map/ppermute | solution.py:43
  15.2 6.4 %collective-permute-start.3 = (bf16[2,1,80,608]{3,2,0,1:T(8,128)(2,1)S(1)}, bf16[2,1,80,608]{3,2,0,1:T(8,128)(2,1)S(1)}, u32[]{:S(2)}, u32[]{:S(2)}) collective-permute-start(bf16[2,1,80,608]{3,2,0,1:T(8,128)(2,1)S(1)} %maximum_select_fusion.4), channel_id=1, source_target_pairs={{0,1},{1,0},{2,3},{3,2},{4,5},{5,4},{6,7},{7,6},{8,9},{9,8},{10,11... | collective-permute-start | bytes 583688 | tf_op jit(solution)/shard_map/ppermute | solution.py:43
  18.8 8.7 %collective-permute-start.1 = (bf16[2,1,8,24,608]{4,3,2,0,1:T(8,128)(2,1)S(1)}, bf16[2,1,8,24,608]{4,3,2,0,1:T(8,128)(2,1)S(1)}, u32[]{:S(2)}, u32[]{:S(2)}) collective-permute-start(bf16[2,1,8,24,608]{4,3,2,0,1:T(8,128)(2,1)S(1)} %maximum_select_fusion.1), channel_id=1, source_target_pairs={{0,1},{1,0},{2,3},{3,2},{4,5},{5,4},{6,7},{7,6},{8,9},{9,8},{10,11... | collective-permute-start | bytes 1400840 | tf_op jit(solution)/shard_map/ppermute | solution.py:43
  21.7 0.7 copy-start.2
  37.5 3.5 %copy-start.1 = (bf16[8,24,8,64]{3,2,1,0:T(8,128)(2,1)S(1)}, bf16[8,24,8,64]{3,2,1,0:T(8,128)(2,1)}, u32[]{:S(2)}) copy-start(bf16[8,24,8,64]{3,2,1,0:T(8,128)(2,1)} %convert_element_type.97) | copy-start | bytes 589828
  38.2 2.7 %copy-start.5 = (bf16[8,2,8,64]{3,2,0,1:T(8,128)(2,1)S(1)}, bf16[8,2,8,64]{3,2,0,1:T(8,128)(2,1)}, u32[]{:S(2)}) copy-start(bf16[8,2,8,64]{3,2,0,1:T(8,128)(2,1)} %multiply_convert_fusion) | copy-start | bytes 49156
  41.4 16.2 %copy-start.7 = (s32[8]{0:T(128)S(1)}, s32[8]{0:T(128)}, u32[]{:S(2)}) copy-start(s32[8]{0:T(128)} %param.22) | copy-start | bytes 100
  43.9 37.4 %all-to-all-start = ((bf16[64,38,128]{2,1,0:T(8,128)(2,1)}), bf16[64,38,128]{2,1,0:T(8,128)(2,1)S(1)}, u32[]{:S(2)}, u32[]{:S(2)}) async-start(bf16[64,38,128]{2,1,0:T(8,128)(2,1)} %reshape.729), calls=%async_computation | async-start | bytes 1310720 | tf_op jit(solution)/shard_map/all_to_all | solution.py:152
  91.8 17.3 %all-to-all-start.1 = ((bf16[64,2,768]{2,1,0:T(2,128)(2,1)}), bf16[64,2,768]{2,1,0:T(2,128)(2,1)S(1)}, u32[]{:S(2)}, u32[]{:S(2)}) async-start(bf16[64,2,768]{2,1,0:T(2,128)(2,1)} %reshape.748), calls=%async_computation.1 | async-start | bytes 393216 | tf_op jit(solution)/shard_map/all_to_all | solution.py:167
  113.2 5.8 %copy-start.6 = (s32[8]{0:T(128)S(1)}, s32[8]{0:T(128)}, u32[]{:S(2)}) copy-start(s32[8]{0:T(128)} %param.23) | copy-start | bytes 100
  115.1 1.3 copy-start
  116.4 4.1 %collective-permute-start.4 = (bf16[2,48,2432]{2,1,0:T(8,128)(2,1)S(1)}, bf16[2,48,2432]{2,1,0:T(8,128)(2,1)S(1)}, u32[]{:S(2)}, u32[]{:S(2)}) collective-permute-start(bf16[2,48,2432]{2,1,0:T(8,128)(2,1)S(1)} %fusion.28), channel_id=1, source_target_pairs={{0,1},{1,0},{2,3},{3,2},{4,5},{5,4},{6,7},{7,6},{8,9},{9,8},{10,11... | collective-permute-start | bytes 1400840 | tf_op jit(solution)/shard_map/ppermute | solution.py:71
  121.7 7.9 %copy-start.3 = (bf16[2,2,80,608]{3,2,1,0:T(8,128)(2,1)S(1)}, bf16[2,2,80,608]{3,2,1,0:T(8,128)(2,1)}, u32[]{:S(2)}) copy-start(bf16[2,2,80,608]{3,2,1,0:T(8,128)(2,1)} %copy-done.2) | copy-start | bytes 1167364
  121.8 7.0 %collective-permute-start.5 = (bf16[48,2432]{1,0:T(8,128)(2,1)S(1)}, bf16[48,2432]{1,0:T(8,128)(2,1)S(1)}, u32[]{:S(2)}, u32[]{:S(2)}) collective-permute-start(bf16[48,2432]{1,0:T(8,128)(2,1)S(1)} %fusion.31), channel_id=1, source_target_pairs={{0,2},{1,3},{2,0},{3,1},{4,6},{5,7},{6,4},{7,5},{8,10},{9,11},{10,... | collective-permute-start | bytes 700424 | tf_op jit(solution)/shard_map/ppermute | solution.py:75
  130.7 3.0 %collective-permute-start.6 = (f32[1,2,2,24,64]{4,3,2,1,0:T(8,128)S(1)}, f32[1,2,2,24,64]{4,3,2,1,0:T(8,128)S(1)}, u32[]{:S(2)}, u32[]{:S(2)}) collective-permute-start(f32[1,2,2,24,64]{4,3,2,1,0:T(8,128)S(1)} %get-tuple-element.26), channel_id=1, source_target_pairs={{0,2},{1,3},{2,0},{3,1},{4,6},{5,7},{6,4},{7,5},{8,10},{9,11},{10,... | collective-permute-start | bytes 73736 | tf_op jit(solution)/shard_map/ppermute | solution.py:43
  133.7 3.4 %collective-permute-start.7 = (f32[2,1,2,2,24,64]{5,4,3,2,0,1:T(8,128)S(1)}, f32[2,1,2,2,24,64]{5,4,3,2,0,1:T(8,128)S(1)}, u32[]{:S(2)}, u32[]{:S(2)}) collective-permute-start(f32[2,1,2,2,24,64]{5,4,3,2,0,1:T(8,128)S(1)} %maximum_select_fusion.6), channel_id=1, source_target_pairs={{0,1},{1,0},{2,3},{3,2},{4,5},{5,4},{6,7},{7,6},{8,9},{9,8},{10,11... | collective-permute-start | bytes 147464 | tf_op jit(solution)/shard_map/ppermute | solution.py:43
Sparse Core Ops, SparseCore 0:
  11.8 88.5 all-gather.2

commit v17 on v15

--- a/solution.py
+++ b/solution.py
@@ -142,13 +142,13 @@
 
     def by_head(values, length):
         split = values.reshape(requests, length, heads_local, HD)
-        return jnp.transpose(split, (0, 2, 1, 3)).reshape(requests * heads_local, length, HD)
+        moved = jnp.transpose(split, (0, 2, 1, 3))
+        return moved.reshape(requests * heads_local, length // 2, 2 * HD)
 
     bundle = jnp.concatenate(
         [by_head(queries, patches), by_head(key_rows, block_len), by_head(value_rows, block_len)], 1
     )
-    sources, bundle_rows = bundle.shape[0], bundle.shape[1]
-    bundle = bundle.reshape(sources, bundle_rows // 2, 2 * HD)
+    sources, bundle_rows = bundle.shape[0], 2 * bundle.shape[1]
     bundle = lax.all_to_all(bundle, ROW, 0, 0, tiled=True)
     bundle = bundle.reshape(sources, bundle_rows, HD)
     head_queries = bundle[:, :patches].reshape(sources * patches, HD)

time: 146 us -> 144 us (0.986)
    convert_element_type x3 -> x2, other arithmetic: 2.53 us -> 0.56 us  [rms_heads(): return (reshaped * inverse * scaling).astype(jnp.bfloat16)]
  transfers between devices with their start and end apart: 11 -> 11, of which waited for: 7 -> 7; matrix products, arithmetic and copies ran while one was open for 27% -> 25% of each run, Pallas kernels for 0% -> 0%
where the time goes in v17:
time: 144 us
  waiting for transfers between devices  44.9 us (31%)
  starting transfers between devices  35.2 us (24%)
  local copies, waits for them, and re-layouts  20.6 us (14%)
  matrix products  15.2 us (11%)
  between operations  14.6 us (10%)
  other arithmetic  13.2 us (9%)
    all_to_all x1, waiting for transfers between devices, per_device(): bundle = lax.all_to_all(bundle, ROW, 0, 0, tiled=True)  23.2 us
    all_to_all x1, starting transfers between devices, per_device(): bundle = lax.all_to_all(bundle, ROW, 0, 0, tiled=True)  13.5 us
    ppermute x6, starting transfers between devices, doubling_gather(): received = lax.ppermute(buffer, axis, pairs)  12.7 us
    all_to_all x1, waiting for transfers between devices, per_device(): attended = lax.all_to_all(attended, ROW, 0, 0, tiled=True)  12.1 us
    unnamed x19, local copies, waits for them, and re-layouts  6.89 us
    all_to_all x1, starting transfers between devices, per_device(): attended = lax.all_to_all(attended, ROW, 0, 0, tiled=True)  5.24 us
    dot_general x1, matrix products, per_device(): jnp.einsum('td,cde->cte', flat_rows, qkv_weight, preferred_element_type=j...  4.81 us
    ppermute x1, waiting for transfers between devices, halving_scatter(): received = lax.ppermute(send.astype(jnp.bfloat16), 'col', pairs)  4.6 us
  transfers between devices with their start and end apart: 11, of which 7 were waited for; matrix products, arithmetic and copies ran while one was open for 25% of the time, Pallas kernels for 0%

profile of v17, /device:TPU:1, one launch (start us, length us, event | category | flops | bytes accessed | tf_op | source)
XLA Modules:
  0.0 143.7 jit_solution(14056078315266861676)
XLA Ops:
  9.0 2.6 %collective-permute-start.2 = (bf16[1,80,608]{2,1,0:T(8,128)(2,1)S(1)}, bf16[1,80,608]{2,1,0:T(8,128)(2,1)S(1)}, u32[]{:S(2)}, u32[]{:S(2)}) collective-permute-start(bf16[1,80,608]{2,1,0:T(8,128)(2,1)S(1)} %get-tuple-element.23), channel_id=1, source_target_pairs={{0,2},{1,3},{2,0},{3,1},{4,6},{5,7},{6,4},{7,5},{8,10},{9,11},{10,... | collective-permute-start | bytes 291848 | tf_op jit(solution)/shard_map/ppermute | solution.py:43
  11.6 1.1 fusion.64
  14.6 3.6 %collective-permute-start.3 = (bf16[2,1,80,608]{3,2,0,1:T(8,128)(2,1)S(1)}, bf16[2,1,80,608]{3,2,0,1:T(8,128)(2,1)S(1)}, u32[]{:S(2)}, u32[]{:S(2)}) collective-permute-start(bf16[2,1,80,608]{3,2,0,1:T(8,128)(2,1)S(1)} %maximum_select_fusion.4), channel_id=1, source_target_pairs={{0,1},{1,0},{2,3},{3,2},{4,5},{5,4},{6,7},{7,6},{8,9},{9,8},{10,11... | collective-permute-start | bytes 583688 | tf_op jit(solution)/shard_map/ppermute | solution.py:43
  18.8 2.6 %collective-permute-start.1 = (bf16[2,1,8,24,608]{4,3,2,0,1:T(8,128)(2,1)S(1)}, bf16[2,1,8,24,608]{4,3,2,0,1:T(8,128)(2,1)S(1)}, u32[]{:S(2)}, u32[]{:S(2)}) collective-permute-start(bf16[2,1,8,24,608]{4,3,2,0,1:T(8,128)(2,1)S(1)} %maximum_select_fusion.1), channel_id=1, source_target_pairs={{0,1},{1,0},{2,3},{3,2},{4,5},{5,4},{6,7},{7,6},{8,9},{9,8},{10,11... | collective-permute-start | bytes 1400840 | tf_op jit(solution)/shard_map/ppermute | solution.py:43
  23.4 3.2 %fusion.21 = f32[2,8,2,512]{3,1,0,2:T(8,128)S(1)} fusion(bf16[2,2432,512]{2,1,0:T(8,128)(2,1)} %param.18, bf16[8,2,2432,1]{2,1,0,3:T(2,128)(2,1)S(1)} %fusion.39), kind=kOutput, calls=%fused_computation.21 | convolution fusion | flops 79691776 | bytes 5124096 | tf_op jit(solution)/shard_map/rtd,cde->crte/dot_general | solution.py:135
  30.0 4.8 %convolution_bitcast_fusion = f32[3,192,512]{2,1,0:T(8,128)S(1)} fusion(bf16[192,2432,1]{1,0,2:T(8,128)(2,1)S(1)} %bitcast.171, bf16[3,2432,512]{2,1,0:T(8,128)(2,1)} %param.17), kind=kOutput, calls=%fused_computation.20 | convolution fusion | flops 1434451968 | bytes 9584640 | tf_op jit(solution)/shard_map/td,cde->cte/dot_general | solution.py:128
  34.8 1.0 copy-done.5
  36.3 1.0 reshape.724
  37.3 1.3 slice_multiply_fusion.1
  40.8 1.1 pad_maximum_fusion
  41.9 13.5 %all-to-all-start = ((bf16[64,38,128]{2,1,0:T(8,128)(2,1)}), bf16[64,38,128]{2,1,0:T(8,128)(2,1)S(1)}, u32[]{:S(2)}, u32[]{:S(2)}) async-start(bf16[64,38,128]{2,1,0:T(8,128)(2,1)} %pad_maximum_fusion), calls=%async_computation | async-start | bytes 1310720 | tf_op jit(solution)/shard_map/all_to_all | solution.py:152
  56.8 23.2 %all-to-all-done = bf16[64,38,128]{2,1,0:T(8,128)(2,1)S(1)} async-done(((bf16[64,38,128]{2,1,0:T(8,128)(2,1)}), bf16[64,38,128]{2,1,0:T(8,128)(2,1)S(1)}, u32[]{:S(2)}, u32[]{:S(2)}) %all-to-all-start) | async-done | bytes 622624 | tf_op jit(solution)/shard_map/all_to_all | solution.py:152
  80.7 1.0 fusion.62
  81.8 1.2 reshape.728
  83.2 1.9 %fusion.65 = (f32[1536]{0:T(1024)S(1)}, f32[1536,1664]{1,0:T(8,128)S(1)}) fusion(bf16[1536,64]{1,0:T(8,128)(2,1)S(1)} %bitcast.156, bf16[1664,64]{1,0:T(8,128)(2,1)S(1)} %reshape.727, pred[1664]{0:T(1024)(128)(4,1)S(1)} %fusion.60), kind=kOutput, calls=%fused_computation.127 | convolution fusion | flops 334821888 | bytes 10641024 | tf_op jit(solution)/shard_map/dot_general | solution.py:80
  85.1 1.8 %fusion = f32[1536]{0:T(1024)S(1)} fusion(f32[1536,1664]{1,0:T(8,128)S(1)} %get-tuple-element.31, f32[1536]{0:T(1024)S(1)} %get-tuple-element.30, pred[1664]{0:T(1024)(128)(4,1)S(1)} %fusion.60), kind=kLoop, calls=%fused_computation.2 | loop fusion | flops 7666176 | bytes 10237568 | tf_op jit(solution)/shard_map/reduce_sum | solution.py:84
  86.9 2.4 %fusion.14 = bf16[1536,64]{0,1:T(8,128)(2,1)S(1)} fusion(bf16[1664,64]{1,0:T(8,128)(2,1)S(1)} %reshape.728, f32[1536,1664]{1,0:T(8,128)S(1)} %get-tuple-element.31, f32[1536]{0:T(1024)S(1)} %get-tuple-element.30, pred[1664]{0:T(1024)(128)(4,1)S(1)} %fusion.60, f32[1536]{0:T(1024)S(1)} %fusion), kind=kOutput, calls=%fused_computation.15 | convolution fusion | flops 335020032 | bytes 10647168 | tf_op jit(solution)/shard_map/dot_general | solution.py:85
  90.5 5.2 %all-to-all-start.1 = ((bf16[64,2,768]{2,1,0:T(2,128)(2,1)}), bf16[64,2,768]{2,1,0:T(2,128)(2,1)S(1)}, u32[]{:S(2)}, u32[]{:S(2)}) async-start(bf16[64,2,768]{2,1,0:T(2,128)(2,1)} %reshape.743), calls=%async_computation.1 | async-start | bytes 393216 | tf_op jit(solution)/shard_map/all_to_all | solution.py:167
  95.7 12.1 %all-to-all-done.1 = bf16[64,2,768]{2,1,0:T(2,128)(2,1)S(1)} async-done(((bf16[64,2,768]{2,1,0:T(2,128)(2,1)}), bf16[64,2,768]{2,1,0:T(2,128)(2,1)S(1)}, u32[]{:S(2)}, u32[]{:S(2)}) %all-to-all-start.1) | async-done | bytes 196640 | tf_op jit(solution)/shard_map/all_to_all | solution.py:167
  109.1 2.8 %reshape.739 = bf16[2432,512,1,1]{1,0,2,3:T(8,128)(2,1)S(1)} reshape(bf16[64,38,512]{2,1,0:T(8,128)(2,1)} %all-gather.3.cloned.1.call-done) | data formatting | bytes 4980736
  111.9 1.9 %fusion.7 = f32[2,2,48,2432]{3,2,1,0:T(8,128)S(1)} fusion(bf16[2,2,48,512]{3,2,1,0:T(8,128)(2,1)} %dot_general.26, bf16[2432,512,1,1]{1,0,2,3:T(8,128)(2,1)S(1)} %reshape.739), kind=kOutput, calls=%fused_computation.8 | convolution fusion | flops 478150656 | bytes 4554752 | tf_op jit(solution)/shard_map/dot_general | solution.py:172
  113.8 1.2 copy-done
  115.1 2.2 %collective-permute-start.4 = (f32[2,48,2432]{2,1,0:T(8,128)S(1)}, f32[2,48,2432]{2,1,0:T(8,128)S(1)}, u32[]{:S(2)}, u32[]{:S(2)}) collective-permute-start(f32[2,48,2432]{2,1,0:T(8,128)S(1)} %dynamic-slice_bitcast_fusion), channel_id=1, source_target_pairs={{0,1},{1,0},{2,3},{3,2},{4,5},{5,4},{6,7},{7,6},{8,9},{9,8},{10,11... | collective-permute-start | bytes 2801672 | tf_op jit(solution)/shard_map/ppermute | solution.py:71
  117.4 2.0 %collective-permute-done.4 = f32[2,48,2432]{2,1,0:T(8,128)S(1)} collective-permute-done((f32[2,48,2432]{2,1,0:T(8,128)S(1)}, f32[2,48,2432]{2,1,0:T(8,128)S(1)}, u32[]{:S(2)}, u32[]{:S(2)}) %collective-permute-start.4) | collective-permute-done | bytes 933920 | tf_op jit(solution)/shard_map/ppermute | solution.py:71
  119.5 1.3 bitcast_add_fusion
  120.8 1.4 collective-permute-start.5
  122.2 1.0 dynamic-slice_bitcast_fusion.2
  123.2 4.6 %collective-permute-done.5 = bf16[48,2432]{1,0:T(8,128)(2,1)S(1)} collective-permute-done((bf16[48,2432]{1,0:T(8,128)(2,1)S(1)}, bf16[48,2432]{1,0:T(8,128)(2,1)S(1)}, u32[]{:S(2)}, u32[]{:S(2)}) %collective-permute-start.5) | collective-permute-done | bytes 233504 | tf_op jit(solution)/shard_map/ppermute | solution.py:75
  128.7 1.0 add_bitcast_fusion.1
  129.7 1.4 collective-permute-start.6
  131.1 1.6 %collective-permute-done.6 = f32[1,2,2,24,64]{4,3,2,1,0:T(8,128)S(1)} collective-permute-done((f32[1,2,2,24,64]{4,3,2,1,0:T(8,128)S(1)}, f32[1,2,2,24,64]{4,3,2,1,0:T(8,128)S(1)}, u32[]{:S(2)}, u32[]{:S(2)}) %collective-permute-start.6) | collective-permute-done | bytes 24608 | tf_op jit(solution)/shard_map/ppermute | solution.py:43
  132.7 2.4 %collective-permute-start.7 = (f32[2,1,2,2,24,64]{5,4,3,2,0,1:T(8,128)S(1)}, f32[2,1,2,2,24,64]{5,4,3,2,0,1:T(8,128)S(1)}, u32[]{:S(2)}, u32[]{:S(2)}) collective-permute-start(f32[2,1,2,2,24,64]{5,4,3,2,0,1:T(8,128)S(1)} %maximum_select_fusion.6), channel_id=1, source_target_pairs={{0,1},{1,0},{2,3},{3,2},{4,5},{5,4},{6,7},{7,6},{8,9},{9,8},{10,11... | collective-permute-start | bytes 147464 | tf_op jit(solution)/shard_map/ppermute | solution.py:43
  (109 shorter events, 19.5 us)
Async XLA Ops:
  7.2 11.5 %copy-start.4 = (bf16[8,24,608]{2,1,0:T(8,128)(2,1)S(1)}, bf16[8,24,608]{2,1,0:T(8,128)(2,1)}, u32[]{:S(2)}) copy-start(bf16[8,24,608]{2,1,0:T(8,128)(2,1)} %param.12) | copy-start | bytes 700420
  7.2 101.9 %all-gather.3.cloned.1.call-start = ((), (), s32[]{:S(2)}) async-start(), calls=%async_computation.2 | async-start | bytes 2662400 | tf_op jit(solution)/shard_map/all_gather | solution.py:110
  9.0 5.6 %collective-permute-start.2 = (bf16[1,80,608]{2,1,0:T(8,128)(2,1)S(1)}, bf16[1,80,608]{2,1,0:T(8,128)(2,1)S(1)}, u32[]{:S(2)}, u32[]{:S(2)}) collective-permute-start(bf16[1,80,608]{2,1,0:T(8,128)(2,1)S(1)} %get-tuple-element.23), channel_id=1, source_target_pairs={{0,2},{1,3},{2,0},{3,1},{4,6},{5,7},{6,4},{7,5},{8,10},{9,11},{10,... | collective-permute-start | bytes 291848 | tf_op jit(solution)/shard_map/ppermute | solution.py:43
  11.5 7.2 %collective-permute-start = (bf16[1,8,24,608]{3,2,1,0:T(8,128)(2,1)}, bf16[1,8,24,608]{3,2,1,0:T(8,128)(2,1)S(1)}, u32[]{:S(2)}, u32[]{:S(2)}) collective-permute-start(bf16[1,8,24,608]{3,2,1,0:T(8,128)(2,1)} %bitcast.166), channel_id=1, source_target_pairs={{0,2},{1,3},{2,0},{3,1},{4,6},{5,7},{6,4},{7,5},{8,10},{9,11},{10,... | collective-permute-start | bytes 700424 | tf_op jit(solution)/shard_map/ppermute | solution.py:43
  14.6 6.9 %collective-permute-start.3 = (bf16[2,1,80,608]{3,2,0,1:T(8,128)(2,1)S(1)}, bf16[2,1,80,608]{3,2,0,1:T(8,128)(2,1)S(1)}, u32[]{:S(2)}, u32[]{:S(2)}) collective-permute-start(bf16[2,1,80,608]{3,2,0,1:T(8,128)(2,1)S(1)} %maximum_select_fusion.4), channel_id=1, source_target_pairs={{0,1},{1,0},{2,3},{3,2},{4,5},{5,4},{6,7},{7,6},{8,9},{9,8},{10,11... | collective-permute-start | bytes 583688 | tf_op jit(solution)/shard_map/ppermute | solution.py:43
  18.8 8.3 %collective-permute-start.1 = (bf16[2,1,8,24,608]{4,3,2,0,1:T(8,128)(2,1)S(1)}, bf16[2,1,8,24,608]{4,3,2,0,1:T(8,128)(2,1)S(1)}, u32[]{:S(2)}, u32[]{:S(2)}) collective-permute-start(bf16[2,1,8,24,608]{4,3,2,0,1:T(8,128)(2,1)S(1)} %maximum_select_fusion.1), channel_id=1, source_target_pairs={{0,1},{1,0},{2,3},{3,2},{4,5},{5,4},{6,7},{7,6},{8,9},{9,8},{10,11... | collective-permute-start | bytes 1400840 | tf_op jit(solution)/shard_map/ppermute | solution.py:43
  21.7 0.8 copy-start.1
  34.8 1.0 copy-start.5
  39.7 1.1 copy-start.3
  40.2 15.3 %copy-start.7 = (s32[8]{0:T(128)S(1)}, s32[8]{0:T(128)}, u32[]{:S(2)}) copy-start(s32[8]{0:T(128)} %param.22) | copy-start | bytes 100
  41.9 38.1 %all-to-all-start = ((bf16[64,38,128]{2,1,0:T(8,128)(2,1)}), bf16[64,38,128]{2,1,0:T(8,128)(2,1)S(1)}, u32[]{:S(2)}, u32[]{:S(2)}) async-start(bf16[64,38,128]{2,1,0:T(8,128)(2,1)} %pad_maximum_fusion), calls=%async_computation | async-start | bytes 1310720 | tf_op jit(solution)/shard_map/all_to_all | solution.py:152
  90.5 17.3 %all-to-all-start.1 = ((bf16[64,2,768]{2,1,0:T(2,128)(2,1)}), bf16[64,2,768]{2,1,0:T(2,128)(2,1)S(1)}, u32[]{:S(2)}, u32[]{:S(2)}) async-start(bf16[64,2,768]{2,1,0:T(2,128)(2,1)} %reshape.743), calls=%async_computation.1 | async-start | bytes 393216 | tf_op jit(solution)/shard_map/all_to_all | solution.py:167
  111.9 5.5 %copy-start.6 = (s32[8]{0:T(128)S(1)}, s32[8]{0:T(128)}, u32[]{:S(2)}) copy-start(s32[8]{0:T(128)} %param.23) | copy-start | bytes 100
  113.8 1.3 copy-start
  115.1 4.3 %collective-permute-start.4 = (f32[2,48,2432]{2,1,0:T(8,128)S(1)}, f32[2,48,2432]{2,1,0:T(8,128)S(1)}, u32[]{:S(2)}, u32[]{:S(2)}) collective-permute-start(f32[2,48,2432]{2,1,0:T(8,128)S(1)} %dynamic-slice_bitcast_fusion), channel_id=1, source_target_pairs={{0,1},{1,0},{2,3},{3,2},{4,5},{5,4},{6,7},{7,6},{8,9},{9,8},{10,11... | collective-permute-start | bytes 2801672 | tf_op jit(solution)/shard_map/ppermute | solution.py:71
  120.8 7.9 %copy-start.2 = (bf16[2,2,80,608]{3,2,1,0:T(8,128)(2,1)S(1)}, bf16[2,2,80,608]{3,2,1,0:T(8,128)(2,1)}, u32[]{:S(2)}) copy-start(bf16[2,2,80,608]{3,2,1,0:T(8,128)(2,1)} %copy-done.1) | copy-start | bytes 1167364
  120.8 7.0 %collective-permute-start.5 = (bf16[48,2432]{1,0:T(8,128)(2,1)S(1)}, bf16[48,2432]{1,0:T(8,128)(2,1)S(1)}, u32[]{:S(2)}, u32[]{:S(2)}) collective-permute-start(bf16[48,2432]{1,0:T(8,128)(2,1)S(1)} %fusion.31), channel_id=1, source_target_pairs={{0,2},{1,3},{2,0},{3,1},{4,6},{5,7},{6,4},{7,5},{8,10},{9,11},{10,... | collective-permute-start | bytes 700424 | tf_op jit(solution)/shard_map/ppermute | solution.py:75
  129.7 3.0 %collective-permute-start.6 = (f32[1,2,2,24,64]{4,3,2,1,0:T(8,128)S(1)}, f32[1,2,2,24,64]{4,3,2,1,0:T(8,128)S(1)}, u32[]{:S(2)}, u32[]{:S(2)}) collective-permute-start(f32[1,2,2,24,64]{4,3,2,1,0:T(8,128)S(1)} %get-tuple-element.26), channel_id=1, source_target_pairs={{0,2},{1,3},{2,0},{3,1},{4,6},{5,7},{6,4},{7,5},{8,10},{9,11},{10,... | collective-permute-start | bytes 73736 | tf_op jit(solution)/shard_map/ppermute | solution.py:43
  132.7 3.4 %collective-permute-start.7 = (f32[2,1,2,2,24,64]{5,4,3,2,0,1:T(8,128)S(1)}, f32[2,1,2,2,24,64]{5,4,3,2,0,1:T(8,128)S(1)}, u32[]{:S(2)}, u32[]{:S(2)}) collective-permute-start(f32[2,1,2,2,24,64]{5,4,3,2,0,1:T(8,128)S(1)} %maximum_select_fusion.6), channel_id=1, source_target_pairs={{0,1},{1,0},{2,3},{3,2},{4,5},{5,4},{6,7},{7,6},{8,9},{9,8},{10,11... | collective-permute-start | bytes 147464 | tf_op jit(solution)/shard_map/ppermute | solution.py:43
Sparse Core Ops, SparseCore 0:
  11.8 87.3 all-gather.2

commit v18 on v17

--- a/solution.py
+++ b/solution.py
@@ -115,10 +115,8 @@
     packed = doubling_gather(packed, "col", COL_ORDER)
     slabs = packed.shape[0]
     txt_count = requests * text_rows
-    txt_full = (
-        jnp.moveaxis(packed[:, :txt_count], 0, -2)
-        .reshape(txt_count, D)
-        .reshape(requests, text_rows, D)
+    txt_full = lax.optimization_barrier(
+        jnp.moveaxis(packed[:, :txt_count], 0, -2).reshape(requests, text_rows, D)
     )
     final_slabs = packed[:, txt_count:]
     normed = (layer_norm(img_full.astype(jnp.float32)) * (1.0 + img_mod[:, 1:2, :]) + img_mod[:, 0:1, :]).astype(

time: 144 us -> 144 us (level)
  no operation moved by 1% of the time
where the time goes in v18:
time: 144 us
  waiting for transfers between devices  45.4 us (32%)
  starting transfers between devices  34.7 us (24%)
  local copies, waits for them, and re-layouts  20.5 us (14%)
  matrix products  15.2 us (11%)
  between operations  14.6 us (10%)
  other arithmetic  13.3 us (9%)
    all_to_all x1, waiting for transfers between devices, per_device(): bundle = lax.all_to_all(bundle, ROW, 0, 0, tiled=True)  23.4 us
    all_to_all x1, starting transfers between devices, per_device(): bundle = lax.all_to_all(bundle, ROW, 0, 0, tiled=True)  13.6 us
    ppermute x6, starting transfers between devices, doubling_gather(): received = lax.ppermute(buffer, axis, pairs)  12.4 us
    all_to_all x1, waiting for transfers between devices, per_device(): attended = lax.all_to_all(attended, ROW, 0, 0, tiled=True)  11.8 us
    unnamed x19, local copies, waits for them, and re-layouts  7.04 us
    all_to_all x1, starting transfers between devices, per_device(): attended = lax.all_to_all(attended, ROW, 0, 0, tiled=True)  4.97 us
    ppermute x1, waiting for transfers between devices, halving_scatter(): received = lax.ppermute(send.astype(jnp.bfloat16), 'col', pairs)  4.93 us
    dot_general x1, matrix products, per_device(): jnp.einsum('td,cde->cte', flat_rows, qkv_weight, preferred_element_type=j...  4.8 us
  transfers between devices with their start and end apart: 11, of which 7 were waited for; matrix products, arithmetic and copies ran while one was open for 25% of the time, Pallas kernels for 0%

profile of v18, /device:TPU:1, one launch (start us, length us, event | category | flops | bytes accessed | tf_op | source)
XLA Modules:
  0.0 143.7 jit_solution(17153448544769521715)
XLA Ops:
  9.0 2.6 %collective-permute-start.2 = (bf16[1,80,608]{2,1,0:T(8,128)(2,1)S(1)}, bf16[1,80,608]{2,1,0:T(8,128)(2,1)S(1)}, u32[]{:S(2)}, u32[]{:S(2)}) collective-permute-start(bf16[1,80,608]{2,1,0:T(8,128)(2,1)S(1)} %get-tuple-element.23), channel_id=1, source_target_pairs={{0,2},{1,3},{2,0},{3,1},{4,6},{5,7},{6,4},{7,5},{8,10},{9,11},{10,... | collective-permute-start | bytes 291848 | tf_op jit(solution)/shard_map/ppermute | solution.py:43
  11.6 1.1 fusion.68
  14.6 3.6 %collective-permute-start.3 = (bf16[2,1,80,608]{3,2,0,1:T(8,128)(2,1)S(1)}, bf16[2,1,80,608]{3,2,0,1:T(8,128)(2,1)S(1)}, u32[]{:S(2)}, u32[]{:S(2)}) collective-permute-start(bf16[2,1,80,608]{3,2,0,1:T(8,128)(2,1)S(1)} %maximum_select_fusion.4), channel_id=1, source_target_pairs={{0,1},{1,0},{2,3},{3,2},{4,5},{5,4},{6,7},{7,6},{8,9},{9,8},{10,11... | collective-permute-start | bytes 583688 | tf_op jit(solution)/shard_map/ppermute | solution.py:43
  18.8 2.6 %collective-permute-start.1 = (bf16[2,1,8,24,608]{4,3,2,0,1:T(8,128)(2,1)S(1)}, bf16[2,1,8,24,608]{4,3,2,0,1:T(8,128)(2,1)S(1)}, u32[]{:S(2)}, u32[]{:S(2)}) collective-permute-start(bf16[2,1,8,24,608]{4,3,2,0,1:T(8,128)(2,1)S(1)} %maximum_select_fusion.1), channel_id=1, source_target_pairs={{0,1},{1,0},{2,3},{3,2},{4,5},{5,4},{6,7},{7,6},{8,9},{9,8},{10,11... | collective-permute-start | bytes 1400840 | tf_op jit(solution)/shard_map/ppermute | solution.py:43
  23.3 3.2 %fusion.21 = f32[2,8,2,512]{3,1,0,2:T(8,128)S(1)} fusion(bf16[2,2432,512]{2,1,0:T(8,128)(2,1)} %param.18, bf16[8,2,2432,1]{2,1,0,3:T(2,128)(2,1)S(1)} %fusion.41), kind=kOutput, calls=%fused_computation.21 | convolution fusion | flops 79691776 | bytes 5124096 | tf_op jit(solution)/shard_map/rtd,cde->crte/dot_general | solution.py:133
  30.0 4.8 %convolution_bitcast_fusion = f32[3,192,512]{2,1,0:T(8,128)S(1)} fusion(bf16[192,2432,1]{1,0,2:T(8,128)(2,1)S(1)} %bitcast.167, bf16[3,2432,512]{2,1,0:T(8,128)(2,1)} %param.17), kind=kOutput, calls=%fused_computation.20 | convolution fusion | flops 1434451968 | bytes 9584640 | tf_op jit(solution)/shard_map/td,cde->cte/dot_general | solution.py:126
  34.8 1.0 copy-done.3
  36.3 1.0 reshape.709
  37.2 1.3 slice_multiply_fusion.1
  40.8 1.1 pad_maximum_fusion
  41.9 13.6 %all-to-all-start = ((bf16[64,38,128]{2,1,0:T(8,128)(2,1)}), bf16[64,38,128]{2,1,0:T(8,128)(2,1)S(1)}, u32[]{:S(2)}, u32[]{:S(2)}) async-start(bf16[64,38,128]{2,1,0:T(8,128)(2,1)} %pad_maximum_fusion), calls=%async_computation | async-start | bytes 1310720 | tf_op jit(solution)/shard_map/all_to_all | solution.py:150
  56.7 23.4 %all-to-all-done = bf16[64,38,128]{2,1,0:T(8,128)(2,1)S(1)} async-done(((bf16[64,38,128]{2,1,0:T(8,128)(2,1)}), bf16[64,38,128]{2,1,0:T(8,128)(2,1)S(1)}, u32[]{:S(2)}, u32[]{:S(2)}) %all-to-all-start) | async-done | bytes 622624 | tf_op jit(solution)/shard_map/all_to_all | solution.py:150
  80.8 1.0 fusion.66
  81.8 1.2 reshape.713
  83.2 1.9 %fusion.69 = (f32[1536]{0:T(1024)S(1)}, f32[1536,1664]{1,0:T(8,128)S(1)}) fusion(bf16[1536,64]{1,0:T(8,128)(2,1)S(1)} %bitcast.156, bf16[1664,64]{1,0:T(8,128)(2,1)S(1)} %reshape.712, pred[1664]{0:T(1024)(128)(4,1)S(1)} %fusion.64), kind=kOutput, calls=%fused_computation.130 | convolution fusion | flops 334821888 | bytes 10641024 | tf_op jit(solution)/shard_map/dot_general | solution.py:80
  85.1 1.8 %fusion = f32[1536]{0:T(1024)S(1)} fusion(f32[1536,1664]{1,0:T(8,128)S(1)} %get-tuple-element.31, f32[1536]{0:T(1024)S(1)} %get-tuple-element.30, pred[1664]{0:T(1024)(128)(4,1)S(1)} %fusion.64), kind=kLoop, calls=%fused_computation.2 | loop fusion | flops 7666176 | bytes 10237568 | tf_op jit(solution)/shard_map/reduce_sum | solution.py:84
  87.0 2.4 %fusion.14 = bf16[1536,64]{0,1:T(8,128)(2,1)S(1)} fusion(bf16[1664,64]{1,0:T(8,128)(2,1)S(1)} %reshape.713, f32[1536,1664]{1,0:T(8,128)S(1)} %get-tuple-element.31, f32[1536]{0:T(1024)S(1)} %get-tuple-element.30, pred[1664]{0:T(1024)(128)(4,1)S(1)} %fusion.64, f32[1536]{0:T(1024)S(1)} %fusion), kind=kOutput, calls=%fused_computation.15 | convolution fusion | flops 335020032 | bytes 10647168 | tf_op jit(solution)/shard_map/dot_general | solution.py:85
  90.5 5.0 %all-to-all-start.1 = ((bf16[64,2,768]{2,1,0:T(2,128)(2,1)}), bf16[64,2,768]{2,1,0:T(2,128)(2,1)S(1)}, u32[]{:S(2)}, u32[]{:S(2)}) async-start(bf16[64,2,768]{2,1,0:T(2,128)(2,1)} %reshape.727), calls=%async_computation.1 | async-start | bytes 393216 | tf_op jit(solution)/shard_map/all_to_all | solution.py:165
  95.5 11.8 %all-to-all-done.1 = bf16[64,2,768]{2,1,0:T(2,128)(2,1)S(1)} async-done(((bf16[64,2,768]{2,1,0:T(2,128)(2,1)}), bf16[64,2,768]{2,1,0:T(2,128)(2,1)S(1)}, u32[]{:S(2)}, u32[]{:S(2)}) %all-to-all-start.1) | async-done | bytes 196640 | tf_op jit(solution)/shard_map/all_to_all | solution.py:165
  108.6 2.8 %reshape.723 = bf16[2432,512,1,1]{1,0,2,3:T(8,128)(2,1)S(1)} reshape(bf16[64,38,512]{2,1,0:T(8,128)(2,1)} %all-gather.3.cloned.1.call-done) | data formatting | bytes 4980736
  111.4 1.9 %fusion.7 = f32[2,2,48,2432]{3,2,1,0:T(8,128)S(1)} fusion(bf16[2,2,48,512]{3,2,1,0:T(8,128)(2,1)} %dot_general.26, bf16[2432,512,1,1]{1,0,2,3:T(8,128)(2,1)S(1)} %reshape.723), kind=kOutput, calls=%fused_computation.8 | convolution fusion | flops 478150656 | bytes 4554752 | tf_op jit(solution)/shard_map/dot_general | solution.py:170
  113.3 1.2 copy-done
  114.6 2.7 %collective-permute-start.4 = (f32[2,48,2432]{2,1,0:T(8,128)S(1)}, f32[2,48,2432]{2,1,0:T(8,128)S(1)}, u32[]{:S(2)}, u32[]{:S(2)}) collective-permute-start(f32[2,48,2432]{2,1,0:T(8,128)S(1)} %dynamic-slice_bitcast_fusion), channel_id=1, source_target_pairs={{0,1},{1,0},{2,3},{3,2},{4,5},{5,4},{6,7},{7,6},{8,9},{9,8},{10,11... | collective-permute-start | bytes 2801672 | tf_op jit(solution)/shard_map/ppermute | solution.py:71
  117.4 2.0 %collective-permute-done.4 = f32[2,48,2432]{2,1,0:T(8,128)S(1)} collective-permute-done((f32[2,48,2432]{2,1,0:T(8,128)S(1)}, f32[2,48,2432]{2,1,0:T(8,128)S(1)}, u32[]{:S(2)}, u32[]{:S(2)}) %collective-permute-start.4) | collective-permute-done | bytes 933920 | tf_op jit(solution)/shard_map/ppermute | solution.py:71
  119.5 1.3 bitcast_add_fusion
  120.8 1.1 collective-permute-start.5
  121.9 1.0 dynamic-slice_bitcast_fusion.2
  122.9 4.9 %collective-permute-done.5 = bf16[48,2432]{1,0:T(8,128)(2,1)S(1)} collective-permute-done((bf16[48,2432]{1,0:T(8,128)(2,1)S(1)}, bf16[48,2432]{1,0:T(8,128)(2,1)S(1)}, u32[]{:S(2)}, u32[]{:S(2)}) %collective-permute-start.5) | collective-permute-done | bytes 233504 | tf_op jit(solution)/shard_map/ppermute | solution.py:75
  128.7 1.0 add_bitcast_fusion.1
  129.7 1.1 collective-permute-start.6
  130.8 1.9 %collective-permute-done.6 = f32[1,2,2,24,64]{4,3,2,1,0:T(8,128)S(1)} collective-permute-done((f32[1,2,2,24,64]{4,3,2,1,0:T(8,128)S(1)}, f32[1,2,2,24,64]{4,3,2,1,0:T(8,128)S(1)}, u32[]{:S(2)}, u32[]{:S(2)}) %collective-permute-start.6) | collective-permute-done | bytes 24608 | tf_op jit(solution)/shard_map/ppermute | solution.py:43
  132.7 2.4 %collective-permute-start.7 = (f32[2,1,2,2,24,64]{5,4,3,2,0,1:T(8,128)S(1)}, f32[2,1,2,2,24,64]{5,4,3,2,0,1:T(8,128)S(1)}, u32[]{:S(2)}, u32[]{:S(2)}) collective-permute-start(f32[2,1,2,2,24,64]{5,4,3,2,0,1:T(8,128)S(1)} %maximum_select_fusion.6), channel_id=1, source_target_pairs={{0,1},{1,0},{2,3},{3,2},{4,5},{5,4},{6,7},{7,6},{8,9},{9,8},{10,11... | collective-permute-start | bytes 147464 | tf_op jit(solution)/shard_map/ppermute | solution.py:43
  (107 shorter events, 19.4 us)
Async XLA Ops:
  7.2 11.5 %copy-start.2 = (bf16[8,24,608]{2,1,0:T(8,128)(2,1)S(1)}, bf16[8,24,608]{2,1,0:T(8,128)(2,1)}, u32[]{:S(2)}) copy-start(bf16[8,24,608]{2,1,0:T(8,128)(2,1)} %param.12) | copy-start | bytes 700420
  7.2 101.4 %all-gather.3.cloned.1.call-start = ((), (), s32[]{:S(2)}) async-start(), calls=%async_computation.2 | async-start | bytes 2662400 | tf_op jit(solution)/shard_map/all_gather | solution.py:110
  9.0 5.6 %collective-permute-start.2 = (bf16[1,80,608]{2,1,0:T(8,128)(2,1)S(1)}, bf16[1,80,608]{2,1,0:T(8,128)(2,1)S(1)}, u32[]{:S(2)}, u32[]{:S(2)}) collective-permute-start(bf16[1,80,608]{2,1,0:T(8,128)(2,1)S(1)} %get-tuple-element.23), channel_id=1, source_target_pairs={{0,2},{1,3},{2,0},{3,1},{4,6},{5,7},{6,4},{7,5},{8,10},{9,11},{10,... | collective-permute-start | bytes 291848 | tf_op jit(solution)/shard_map/ppermute | solution.py:43
  11.5 7.2 %collective-permute-start = (bf16[1,8,24,608]{3,2,1,0:T(8,128)(2,1)}, bf16[1,8,24,608]{3,2,1,0:T(8,128)(2,1)S(1)}, u32[]{:S(2)}, u32[]{:S(2)}) collective-permute-start(bf16[1,8,24,608]{3,2,1,0:T(8,128)(2,1)} %bitcast.162), channel_id=1, source_target_pairs={{0,2},{1,3},{2,0},{3,1},{4,6},{5,7},{6,4},{7,5},{8,10},{9,11},{10,... | collective-permute-start | bytes 700424 | tf_op jit(solution)/shard_map/ppermute | solution.py:43
  14.6 6.9 %collective-permute-start.3 = (bf16[2,1,80,608]{3,2,0,1:T(8,128)(2,1)S(1)}, bf16[2,1,80,608]{3,2,0,1:T(8,128)(2,1)S(1)}, u32[]{:S(2)}, u32[]{:S(2)}) collective-permute-start(bf16[2,1,80,608]{3,2,0,1:T(8,128)(2,1)S(1)} %maximum_select_fusion.4), channel_id=1, source_target_pairs={{0,1},{1,0},{2,3},{3,2},{4,5},{5,4},{6,7},{7,6},{8,9},{9,8},{10,11... | collective-permute-start | bytes 583688 | tf_op jit(solution)/shard_map/ppermute | solution.py:43
  18.8 8.2 %collective-permute-start.1 = (bf16[2,1,8,24,608]{4,3,2,0,1:T(8,128)(2,1)S(1)}, bf16[2,1,8,24,608]{4,3,2,0,1:T(8,128)(2,1)S(1)}, u32[]{:S(2)}, u32[]{:S(2)}) collective-permute-start(bf16[2,1,8,24,608]{4,3,2,0,1:T(8,128)(2,1)S(1)} %maximum_select_fusion.1), channel_id=1, source_target_pairs={{0,1},{1,0},{2,3},{3,2},{4,5},{5,4},{6,7},{7,6},{8,9},{9,8},{10,11... | collective-permute-start | bytes 1400840 | tf_op jit(solution)/shard_map/ppermute | solution.py:43
  21.7 0.8 copy-start.4
  34.8 1.0 copy-start.3
  39.6 1.1 copy-start.1
  40.1 15.3 %copy-start.7 = (s32[8]{0:T(128)S(1)}, s32[8]{0:T(128)}, u32[]{:S(2)}) copy-start(s32[8]{0:T(128)} %param.22) | copy-start | bytes 100
  41.9 38.2 %all-to-all-start = ((bf16[64,38,128]{2,1,0:T(8,128)(2,1)}), bf16[64,38,128]{2,1,0:T(8,128)(2,1)S(1)}, u32[]{:S(2)}, u32[]{:S(2)}) async-start(bf16[64,38,128]{2,1,0:T(8,128)(2,1)} %pad_maximum_fusion), calls=%async_computation | async-start | bytes 1310720 | tf_op jit(solution)/shard_map/all_to_all | solution.py:150
  90.5 16.8 %all-to-all-start.1 = ((bf16[64,2,768]{2,1,0:T(2,128)(2,1)}), bf16[64,2,768]{2,1,0:T(2,128)(2,1)S(1)}, u32[]{:S(2)}, u32[]{:S(2)}) async-start(bf16[64,2,768]{2,1,0:T(2,128)(2,1)} %reshape.727), calls=%async_computation.1 | async-start | bytes 393216 | tf_op jit(solution)/shard_map/all_to_all | solution.py:165
  111.4 5.9 %copy-start.6 = (s32[8]{0:T(128)S(1)}, s32[8]{0:T(128)}, u32[]{:S(2)}) copy-start(s32[8]{0:T(128)} %param.23) | copy-start | bytes 100
  113.3 1.3 copy-start
  114.6 4.8 %collective-permute-start.4 = (f32[2,48,2432]{2,1,0:T(8,128)S(1)}, f32[2,48,2432]{2,1,0:T(8,128)S(1)}, u32[]{:S(2)}, u32[]{:S(2)}) collective-permute-start(f32[2,48,2432]{2,1,0:T(8,128)S(1)} %dynamic-slice_bitcast_fusion), channel_id=1, source_target_pairs={{0,1},{1,0},{2,3},{3,2},{4,5},{5,4},{6,7},{7,6},{8,9},{9,8},{10,11... | collective-permute-start | bytes 2801672 | tf_op jit(solution)/shard_map/ppermute | solution.py:71
  120.7 7.9 %copy-start.5 = (bf16[2,2,80,608]{3,2,1,0:T(8,128)(2,1)S(1)}, bf16[2,2,80,608]{3,2,1,0:T(8,128)(2,1)}, u32[]{:S(2)}) copy-start(bf16[2,2,80,608]{3,2,1,0:T(8,128)(2,1)} %copy-done.4) | copy-start | bytes 1167364
  120.8 7.0 %collective-permute-start.5 = (bf16[48,2432]{1,0:T(8,128)(2,1)S(1)}, bf16[48,2432]{1,0:T(8,128)(2,1)S(1)}, u32[]{:S(2)}, u32[]{:S(2)}) collective-permute-start(bf16[48,2432]{1,0:T(8,128)(2,1)S(1)} %fusion.31), channel_id=1, source_target_pairs={{0,2},{1,3},{2,0},{3,1},{4,6},{5,7},{6,4},{7,5},{8,10},{9,11},{10,... | collective-permute-start | bytes 700424 | tf_op jit(solution)/shard_map/ppermute | solution.py:75
  129.7 3.0 %collective-permute-start.6 = (f32[1,2,2,24,64]{4,3,2,1,0:T(8,128)S(1)}, f32[1,2,2,24,64]{4,3,2,1,0:T(8,128)S(1)}, u32[]{:S(2)}, u32[]{:S(2)}) collective-permute-start(f32[1,2,2,24,64]{4,3,2,1,0:T(8,128)S(1)} %get-tuple-element.26), channel_id=1, source_target_pairs={{0,2},{1,3},{2,0},{3,1},{4,6},{5,7},{6,4},{7,5},{8,10},{9,11},{10,... | collective-permute-start | bytes 73736 | tf_op jit(solution)/shard_map/ppermute | solution.py:43
  132.7 3.4 %collective-permute-start.7 = (f32[2,1,2,2,24,64]{5,4,3,2,0,1:T(8,128)S(1)}, f32[2,1,2,2,24,64]{5,4,3,2,0,1:T(8,128)S(1)}, u32[]{:S(2)}, u32[]{:S(2)}) collective-permute-start(f32[2,1,2,2,24,64]{5,4,3,2,0,1:T(8,128)S(1)} %maximum_select_fusion.6), channel_id=1, source_target_pairs={{0,1},{1,0},{2,3},{3,2},{4,5},{5,4},{6,7},{7,6},{8,9},{9,8},{10,11... | collective-permute-start | bytes 147464 | tf_op jit(solution)/shard_map/ppermute | solution.py:43
Sparse Core Ops, SparseCore 0:
  11.8 87.3 all-gather.2
